TPU v7x, 128 devices: a whole 4x4x4 slice. The times are simulated.
128 devices in a mesh: row: 8 (over y, core), col: 16 (over z, x).
Axes of the slice: x: 4, y: 4, z: 4, core: 2. Of those that a mesh axis runs over, the one named last changes fastest.
Arguments:
- constraint_features: bfloat16 [32768, 768], P(('row', 'col')), may hold values from -6 to 6
- variable_features: bfloat16 [32768, 768], P(('row', 'col')), may hold values from -6 to 6
- variable_cotangent: bfloat16 [32768, 768], P(('row', 'col')), may hold values from -6 to 6
- constraint_weight: bfloat16 [768, 768], replicated, may hold values from -0.21875 to 0.21875
- variable_weight: bfloat16 [768, 768], replicated, may hold values from -0.21875 to 0.21875
- bias: float32 [768], replicated, may hold values from -4 to 4
- send_rows: int32 [2, 128, 512], P(None, ('row', 'col')), may hold values from 0 to 255
- recv_count: int32 [2, 128, 128], P(None, ('row', 'col')), may hold values from 2 to 4, as said below
- edge_slots: int32 [2, 262144], P(None, ('row', 'col')), may hold values from 0 to 511
Outputs:
- grad_con: bfloat16 [32768, 768], P(('row', 'col'))
- grad_var: bfloat16 [32768, 768], P(('row', 'col'))
- grad_wcon: float32 [768, 768], P(('row', 'col'))
- grad_wvar: float32 [768, 768], P(('row', 'col'))
- grad_bias: float32 [768], P(('row', 'col'))
Inputs may be any that keep to these rules, and one draw needn't show every extreme that they name: `recv_count`: every device holds exactly 4 live slots from some peer, for each side.
All inputs are finite; a program needn't handle non-finite values.
Results may differ from a plain program's by a relative error of at most 0.0063.
Values may be sent and summed in bfloat16 or wider, within the bound.
No kernel may reach another device: no remote copies, remote signals or barrier semaphores. Data moves between devices by JAX's collectives and lax.ppermute only.
A program may use at most 128 MiB of HBM per device.

v0:
```python
import jax
import jax.numpy as jnp
from jax import lax
from jax.sharding import PartitionSpec as P


def one_hot_table(indices, width):
    columns = lax.broadcasted_iota(jnp.int32, (indices.shape[0], width), 1)
    return jnp.where(columns == indices[:, None], 1.0, 0.0).astype(jnp.bfloat16)


def pick_rows(table, values):
    return jnp.dot(table, values, preferred_element_type=jnp.float32).astype(jnp.bfloat16)


def on_device(
    constraint_features,
    variable_features,
    variable_cotangent,
    constraint_weight,
    variable_weight,
    bias,
    send_rows,
    recv_count,
    edge_slots,
):
    device_count = lax.axis_size(("row", "col"))
    slot_cap = send_rows.shape[2] // device_count
    embedding_width = constraint_features.shape[1]
    replica_rows = device_count * slot_cap
    master_rows = constraint_features.shape[0]
    select_con = one_hot_table(send_rows[0, 0], master_rows)
    select_var = one_hot_table(send_rows[1, 0], master_rows)
    out_con = pick_rows(select_con, constraint_features).reshape(
        device_count, slot_cap, embedding_width
    )
    out_var = pick_rows(select_var, variable_features).reshape(
        device_count, slot_cap, embedding_width
    )
    out_cot = pick_rows(select_var, variable_cotangent).reshape(
        device_count, slot_cap, embedding_width
    )
    constraint_mirror_rows, variable_mirror_rows, cotangent_mirror_rows = (
        lax.all_to_all(out_con, ("row", "col"), split_axis=0, concat_axis=0, tiled=True),
        lax.all_to_all(out_var, ("row", "col"), split_axis=0, concat_axis=0, tiled=True),
        lax.all_to_all(out_cot, ("row", "col"), split_axis=0, concat_axis=0, tiled=True),
    )
    constraint_mirror_rows = constraint_mirror_rows.reshape(replica_rows, embedding_width)
    variable_mirror_rows = variable_mirror_rows.reshape(replica_rows, embedding_width)
    cotangent_mirror_rows = cotangent_mirror_rows.reshape(replica_rows, embedding_width)
    slot_pos = lax.broadcasted_iota(jnp.int32, (2, replica_rows), 1) % slot_cap
    slot_live = jnp.where(
        slot_pos < jnp.repeat(recv_count[:, 0], slot_cap, axis=1), 1.0, 0.0
    ).astype(jnp.bfloat16)
    table_con = one_hot_table(edge_slots[0], replica_rows)
    table_var = one_hot_table(edge_slots[1], replica_rows)
    live_con = jnp.dot(table_con, slot_live[0], preferred_element_type=jnp.float32)
    live_var = jnp.dot(table_var, slot_live[1], preferred_element_type=jnp.float32)
    edge_active_mask = live_con * live_var
    edge_con = pick_rows(table_con, constraint_mirror_rows)
    edge_var = pick_rows(table_var, variable_mirror_rows)
    upstream_gradient = jnp.dot(
        table_var, cotangent_mirror_rows, preferred_element_type=jnp.float32
    )
    pre_act = (
        jnp.dot(edge_con, constraint_weight, preferred_element_type=jnp.float32)
        + jnp.dot(edge_var, variable_weight, preferred_element_type=jnp.float32)
        + bias[None, :]
    )
    sigmoid_pre = jax.nn.sigmoid(pre_act)
    message_derivative = sigmoid_pre * (1.0 + pre_act * (1.0 - sigmoid_pre))
    edge_delta = (upstream_gradient * message_derivative * edge_active_mask[:, None]).astype(
        jnp.bfloat16
    )
    sum_dims = (((0,), (0,)), ((), ()))
    constraint_projection_gradient = lax.dot_general(
        table_con, edge_delta, sum_dims, preferred_element_type=jnp.float32
    ).astype(jnp.bfloat16)
    variable_projection_gradient = lax.dot_general(
        table_var, edge_delta, sum_dims, preferred_element_type=jnp.float32
    ).astype(jnp.bfloat16)
    back_con = jnp.dot(
        constraint_projection_gradient, constraint_weight.T, preferred_element_type=jnp.float32
    ).astype(jnp.bfloat16)
    back_var = jnp.dot(
        variable_projection_gradient, variable_weight.T, preferred_element_type=jnp.float32
    ).astype(jnp.bfloat16)
    back_con = back_con.reshape(device_count, slot_cap, embedding_width)
    back_var = back_var.reshape(device_count, slot_cap, embedding_width)
    home_con, home_var = (
        lax.all_to_all(back_con, ("row", "col"), split_axis=0, concat_axis=0, tiled=True),
        lax.all_to_all(back_var, ("row", "col"), split_axis=0, concat_axis=0, tiled=True),
    )
    grad_con = lax.dot_general(
        select_con,
        home_con.reshape(replica_rows, embedding_width),
        sum_dims,
        preferred_element_type=jnp.float32,
    )
    grad_var = lax.dot_general(
        select_var,
        home_var.reshape(replica_rows, embedding_width),
        sum_dims,
        preferred_element_type=jnp.float32,
    )
    grad_var = variable_cotangent.astype(jnp.float32) + grad_var
    constraint_term = lax.dot_general(
        constraint_mirror_rows,
        constraint_projection_gradient,
        sum_dims,
        preferred_element_type=jnp.float32,
    )
    variable_term = lax.dot_general(
        variable_mirror_rows,
        variable_projection_gradient,
        sum_dims,
        preferred_element_type=jnp.float32,
    )
    term_bias = jnp.sum(edge_delta.astype(jnp.float32), axis=0)
    factor = float(device_count * edge_slots.shape[1]) ** (-0.5)
    sum_con, sum_var, sum_bias = lax.psum(
        (constraint_term, variable_term, term_bias), ("row", "col")
    )
    share = embedding_width // device_count
    my_index = lax.axis_index(("row", "col"))
    sum_con = lax.dynamic_slice_in_dim(sum_con, my_index * share, share, 0)
    sum_var = lax.dynamic_slice_in_dim(sum_var, my_index * share, share, 0)
    sum_bias = lax.dynamic_slice_in_dim(sum_bias, my_index * share, share, 0)
    return (
        grad_con.astype(jnp.bfloat16),
        grad_var.astype(jnp.bfloat16),
        sum_con * factor,
        sum_var * factor,
        sum_bias * factor,
    )


def solution(mesh):
    placed = (
        P(("row", "col"), None),
        P(("row", "col"), None),
        P(("row", "col"), None),
        P(),
        P(),
        P(),
        P(None, ("row", "col"), None),
        P(None, ("row", "col"), None),
        P(None, ("row", "col")),
    )
    return jax.shard_map(
        on_device,
        mesh=mesh,
        in_specs=placed,
        out_specs=(
            P(("row", "col"), None),
            P(("row", "col"), None),
            P(("row", "col"), None),
            P(("row", "col"), None),
            P(("row", "col")),
        ),
        check_vma=False,
    )
```

profile of v0, /device:TPU:0, one launch (start us, length us, event | category | flops | bytes accessed | tf_op | source)
XLA Modules:
  0.0 276.4 jit_solution(17661041611296465964)
XLA Ops:
  8.0 1.4 convolution_convert_fusion.3
  9.5 1.1 reshape.53
  10.6 11.2 %all-to-all-start.2 = ((bf16[128,4,768]{2,1,0:T(4,128)(2,1)}), bf16[128,4,768]{2,1,0:T(4,128)(2,1)S(1)}, u32[]{:S(2)}, u32[]{:S(2)}) async-start(bf16[128,4,768]{2,1,0:T(4,128)(2,1)} %reshape.53), calls=%async_computation.2 | async-start | bytes 1572864 | tf_op jit(solution)/shard_map/all_to_all | solution.py:45
  22.4 1.1 reshape.51
  23.5 1.4 convolution_convert_fusion.5
  24.9 1.1 reshape.49
  26.1 12.0 %all-to-all-done.2 = bf16[128,4,768]{2,1,0:T(4,128)(2,1)S(1)} async-done(((bf16[128,4,768]{2,1,0:T(4,128)(2,1)}), bf16[128,4,768]{2,1,0:T(4,128)(2,1)S(1)}, u32[]{:S(2)}, u32[]{:S(2)}) %all-to-all-start.2) | async-done | bytes 786464 | tf_op jit(solution)/shard_map/all_to_all | solution.py:45
  38.1 4.6 %all-to-all-start.1 = ((bf16[128,4,768]{2,1,0:T(4,128)(2,1)}), bf16[128,4,768]{2,1,0:T(4,128)(2,1)S(1)}, u32[]{:S(2)}, u32[]{:S(2)}) async-start(bf16[128,4,768]{2,1,0:T(4,128)(2,1)} %reshape.51), calls=%async_computation.1 | async-start | bytes 1572864 | tf_op jit(solution)/shard_map/all_to_all | solution.py:44
  42.7 1.0 fusion.1
  44.9 14.1 %all-to-all-done.1 = bf16[128,4,768]{2,1,0:T(4,128)(2,1)S(1)} async-done(((bf16[128,4,768]{2,1,0:T(4,128)(2,1)}), bf16[128,4,768]{2,1,0:T(4,128)(2,1)S(1)}, u32[]{:S(2)}, u32[]{:S(2)}) %all-to-all-start.1) | async-done | bytes 786464 | tf_op jit(solution)/shard_map/all_to_all | solution.py:44
  59.0 5.7 %all-to-all-start = ((bf16[128,4,768]{2,1,0:T(4,128)(2,1)}), bf16[128,4,768]{2,1,0:T(4,128)(2,1)}, u32[]{:S(2)}, u32[]{:S(2)}) async-start(bf16[128,4,768]{2,1,0:T(4,128)(2,1)} %reshape.49), calls=%async_computation | async-start | bytes 1572864 | tf_op jit(solution)/shard_map/all_to_all | solution.py:46
  64.9 7.1 %fusion.30 = f32[2048,768]{1,0:T(8,128)} fusion(bf16[768,768]{1,0:T(8,128)(2,1)S(1)} %copy-done, bf16[512,768]{1,0:T(8,128)(2,1)S(1)} %reshape.54, s32[2048]{0:T(1024)} %bitcast.39), kind=kOutput, calls=%fused_computation.44 | convolution fusion | flops 4031250432 | bytes 8265728 | tf_op jit(solution)/shard_map/dot_general | solution.py:67
  72.2 7.7 %fusion.31 = f32[2048,768]{1,0:T(8,128)} fusion(bf16[768,768]{1,0:T(8,128)(2,1)} %param.12, bf16[512,768]{1,0:T(8,128)(2,1)S(1)} %reshape.52, s32[2048]{0:T(1024)S(1)} %bitcast.36), kind=kOutput, calls=%fused_computation.45 | convolution fusion | flops 4031250432 | bytes 8265728 | tf_op jit(solution)/shard_map/dot_general | solution.py:66
  80.7 1.6 reshape.50
  82.3 7.9 %convert_reduce_fusion = (f32[768]{0:T(1024)}, bf16[2048,768]{1,0:T(8,128)(2,1)S(1)}) fusion(f32[2048]{0:T(1024)S(1)} %mul.40, f32[768]{0:T(1024)} %param.14, f32[2048,768]{1,0:T(8,128)} %fusion.31, f32[2048,768]{1,0:T(8,128)} %fusion.30, bf16[512,768]{1,0:T(8,128)(2,1)S(1)} %reshape.50, s32[2048]{0:T(1024)} %bitcast.40), kind=kOutput, calls=%fused_computation | convolution fusion | flops 1635777792 | bytes 16537600 | tf_op jit(solution)/shard_map/dot_general | solution.py:62
  90.2 2.0 fusion.28
  92.2 2.0 fusion.27
  94.3 2.3 fusion.83
  96.6 2.2 fusion.82
  98.8 1.1 copy-done.2
  100.7 1.1 reshape.58
  101.8 9.0 %all-to-all-start.4 = ((bf16[128,4,768]{2,1,0:T(4,128)(2,1)}), bf16[128,4,768]{2,1,0:T(4,128)(2,1)S(1)}, u32[]{:S(2)}, u32[]{:S(2)}) async-start(bf16[128,4,768]{2,1,0:T(4,128)(2,1)} %reshape.58), calls=%async_computation.4 | async-start | bytes 1572864 | tf_op jit(solution)/shard_map/all_to_all | solution.py:92
  110.8 2.1 convolution_convert_fusion.2
  112.9 1.1 reshape.56
  114.0 15.1 %all-to-all-done.4 = bf16[128,4,768]{2,1,0:T(4,128)(2,1)S(1)} async-done(((bf16[128,4,768]{2,1,0:T(4,128)(2,1)}), bf16[128,4,768]{2,1,0:T(4,128)(2,1)S(1)}, u32[]{:S(2)}, u32[]{:S(2)}) %all-to-all-start.4) | async-done | bytes 786464 | tf_op jit(solution)/shard_map/all_to_all | solution.py:92
  129.1 4.6 %all-to-all-start.3 = ((bf16[128,4,768]{2,1,0:T(4,128)(2,1)}), bf16[128,4,768]{2,1,0:T(4,128)(2,1)S(1)}, u32[]{:S(2)}, u32[]{:S(2)}) async-start(bf16[128,4,768]{2,1,0:T(4,128)(2,1)} %reshape.56), calls=%async_computation.3 | async-start | bytes 1572864 | tf_op jit(solution)/shard_map/all_to_all | solution.py:91
  133.8 68.2 %psum.23 = f32[768]{0:T(1024)S(1)} all-reduce(f32[768]{0:T(1024)S(1)} %copy-done.6), channel_id=1, replica_groups=mesh['row'=8,'col'=16] {'row','col'}, use_global_device_ids=true, to_apply=%region_3.4 | all-reduce | flops 768 | bytes 6144 | tf_op jit(solution)/shard_map/psum | solution.py:121
  202.9 1.3 convolution_convert_fusion.6
  204.2 2.2 fusion.29
  206.4 60.3 %all-reduce.3.cloned.1.call-done = (f32[768,768]{1,0:T(8,128)}, f32[768,768]{1,0:T(8,128)}) async-done(((f32[768,768]{1,0:T(8,128)}, f32[768,768]{1,0:T(8,128)}), (f32[768,768]{1,0:T(8,128)}, f32[768,768]{1,0:T(8,128)})) %all-reduce.3.cloned.1.call-update) | async-done | bytes 4718608 | tf_op jit(solution)/shard_map/psum | solution.py:121
  266.7 1.4 dynamic-slice_multiply_fusion
  268.1 1.4 dynamic-slice_multiply_fusion.1
  (45 shorter events, 5.6 us)
Async XLA Ops:
  7.2 57.8 %copy-start = (bf16[768,768]{1,0:T(8,128)(2,1)S(1)}, bf16[768,768]{1,0:T(8,128)(2,1)}, u32[]{:S(2)}) copy-start(bf16[768,768]{1,0:T(8,128)(2,1)} %param.13) | copy-start | bytes 3538948
  7.2 14.6 %copy-start.11 = (s32[2,1,128]{2,1,0:T(1,128)S(1)}, s32[2,1,128]{2,1,0:T(1,128)}, u32[]{:S(2)}) copy-start(s32[2,1,128]{2,1,0:T(1,128)} %param.16) | copy-start | bytes 3076
  7.2 14.8 %copy-start.12 = (bf16[256,768]{1,0:T(8,128)(2,1)S(1)}, bf16[256,768]{1,0:T(8,128)(2,1)}, u32[]{:S(2)}) copy-start(bf16[256,768]{1,0:T(8,128)(2,1)} %param.9) | copy-start | bytes 1179652
  8.0 16.9 %copy-start.7 = (s32[1,1,512]{2,1,0:T(1,128)}, s32[1,1,512]{2,1,0:T(1,128)S(1)}, u32[]{:S(2)}) copy-start(s32[1,1,512]{2,1,0:T(1,128)S(1)} %get-tuple-element.9) | copy-start | bytes 6148
  8.0 16.9 %copy-start.9 = (s32[1,1,512]{2,1,0:T(1,128)}, s32[1,1,512]{2,1,0:T(1,128)S(1)}, u32[]{:S(2)}) copy-start(s32[1,1,512]{2,1,0:T(1,128)S(1)} %get-tuple-element.10) | copy-start | bytes 6148
  9.4 16.6 %copy-start.3 = (s32[2,2048]{1,0:T(2,128)S(1)}, s32[2,2048]{1,0:T(2,128)}, u32[]{:S(2)}) copy-start(s32[2,2048]{1,0:T(2,128)} %param.17) | copy-start | bytes 49156
  10.6 27.5 %all-to-all-start.2 = ((bf16[128,4,768]{2,1,0:T(4,128)(2,1)}), bf16[128,4,768]{2,1,0:T(4,128)(2,1)S(1)}, u32[]{:S(2)}, u32[]{:S(2)}) async-start(bf16[128,4,768]{2,1,0:T(4,128)(2,1)} %reshape.53), calls=%async_computation.2 | async-start | bytes 1572864 | tf_op jit(solution)/shard_map/all_to_all | solution.py:45
  26.0 17.7 %copy-start.4 = (s32[1,2048]{1,0:T(1,128)}, s32[1,2048]{1,0:T(1,128)S(1)}, u32[]{:S(2)}) copy-start(s32[1,2048]{1,0:T(1,128)S(1)} %get-tuple-element.7) | copy-start | bytes 24580
  38.1 21.0 %all-to-all-start.1 = ((bf16[128,4,768]{2,1,0:T(4,128)(2,1)}), bf16[128,4,768]{2,1,0:T(4,128)(2,1)S(1)}, u32[]{:S(2)}, u32[]{:S(2)}) async-start(bf16[128,4,768]{2,1,0:T(4,128)(2,1)} %reshape.51), calls=%async_computation.1 | async-start | bytes 1572864 | tf_op jit(solution)/shard_map/all_to_all | solution.py:44
  59.0 21.6 %all-to-all-start = ((bf16[128,4,768]{2,1,0:T(4,128)(2,1)}), bf16[128,4,768]{2,1,0:T(4,128)(2,1)}, u32[]{:S(2)}, u32[]{:S(2)}) async-start(bf16[128,4,768]{2,1,0:T(4,128)(2,1)} %reshape.49), calls=%async_computation | async-start | bytes 1572864 | tf_op jit(solution)/shard_map/all_to_all | solution.py:46
  64.7 202.0 %all-reduce.3.cloned.1.call-start = ((), (), s32[]{:S(2)}) async-start(), calls=%async_computation.5 | async-start | bytes 9437184 | tf_op jit(solution)/shard_map/psum | solution.py:121
  82.2 7.9 %copy-start.5 = (s32[1,2048]{1,0:T(1,128)S(1)}, s32[1,2048]{1,0:T(1,128)}, u32[]{:S(2)}) copy-start(s32[1,2048]{1,0:T(1,128)} %copy-done.4) | copy-start | bytes 24580
  92.2 4.3 %copy-start.1 = (bf16[512,768]{1,0:T(8,128)(2,1)}, bf16[512,768]{1,0:T(8,128)(2,1)S(1)}, u32[]{:S(2)}) copy-start(bf16[512,768]{1,0:T(8,128)(2,1)S(1)} %fusion.28) | copy-start | bytes 2359300
  98.8 1.1 copy-start.2
  101.8 31.9 %copy-start.6 = (f32[768]{0:T(1024)S(1)}, f32[768]{0:T(1024)}, u32[]{:S(2)}) copy-start(f32[768]{0:T(1024)} %get-tuple-element.11) | copy-start | bytes 9220
  101.8 27.3 %all-to-all-start.4 = ((bf16[128,4,768]{2,1,0:T(4,128)(2,1)}), bf16[128,4,768]{2,1,0:T(4,128)(2,1)S(1)}, u32[]{:S(2)}, u32[]{:S(2)}) async-start(bf16[128,4,768]{2,1,0:T(4,128)(2,1)} %reshape.58), calls=%async_computation.4 | async-start | bytes 1572864 | tf_op jit(solution)/shard_map/all_to_all | solution.py:92
  110.8 92.1 %copy-start.10 = (s32[1,1,512]{2,1,0:T(1,128)S(1)}, s32[1,1,512]{2,1,0:T(1,128)}, u32[]{:S(2)}) copy-start(s32[1,1,512]{2,1,0:T(1,128)} %copy-done.9) | copy-start | bytes 6148
  112.9 91.2 %copy-start.8 = (s32[1,1,512]{2,1,0:T(1,128)S(1)}, s32[1,1,512]{2,1,0:T(1,128)}, u32[]{:S(2)}) copy-start(s32[1,1,512]{2,1,0:T(1,128)} %copy-done.7) | copy-start | bytes 6148
  129.1 73.6 %all-to-all-start.3 = ((bf16[128,4,768]{2,1,0:T(4,128)(2,1)}), bf16[128,4,768]{2,1,0:T(4,128)(2,1)S(1)}, u32[]{:S(2)}, u32[]{:S(2)}) async-start(bf16[128,4,768]{2,1,0:T(4,128)(2,1)} %reshape.56), calls=%async_computation.3 | async-start | bytes 1572864 | tf_op jit(solution)/shard_map/all_to_all | solution.py:91
Sparse Core Ops, SparseCore 0:
  98.9 167.7 all-reduce.2
where the time goes:
time: 278 us; the launch traced here: 276 us
  waiting for transfers between devices  102 us (37%)
  blocking collectives  68.2 us (25%)
  matrix products  42.9 us (15%)
  starting transfers between devices  35.3 us (13%)
  between operations  14.3 us (5%)
  local copies, waits for them, and re-layouts  9.91 us (4%)
  other arithmetic  3.44 us (1%)
    psum x1, blocking collectives, on_device(): lax.psum((constraint_term, variable_term, term_bias), ('row', 'col'))  68.2 us
    psum x1, waiting for transfers between devices, on_device(): lax.psum((constraint_term, variable_term, term_bias), ('row', 'col'))  60.3 us
    all_to_all x1, waiting for transfers between devices, on_device(): lax.all_to_all(back_var, ('row', 'col'), split_axis=0, concat_axis=0, til...  15.1 us
    all_to_all x1, waiting for transfers between devices, on_device(): lax.all_to_all(out_con, ('row', 'col'), split_axis=0, concat_axis=0, tile...  14.1 us
    all_to_all x1, waiting for transfers between devices, on_device(): lax.all_to_all(out_var, ('row', 'col'), split_axis=0, concat_axis=0, tile...  12 us
    all_to_all x1, starting transfers between devices, on_device(): lax.all_to_all(out_var, ('row', 'col'), split_axis=0, concat_axis=0, tile...  11.2 us
    all_to_all x1, starting transfers between devices, on_device(): lax.all_to_all(back_var, ('row', 'col'), split_axis=0, concat_axis=0, til...  9 us
    dot_general x1, matrix products, on_device(): jnp.dot(table_var, cotangent_mirror_rows, preferred_element_type=jnp.floa...  7.93 us
  transfers between devices with their start and end apart: 6, of which 5 were waited for; matrix products, arithmetic and copies ran while one was open for 11% of the time, Pallas kernels for 0%

commit v1 on v0

--- a/solution.py
+++ b/solution.py
@@ -118,14 +118,13 @@
     )
     term_bias = jnp.sum(edge_delta.astype(jnp.float32), axis=0)
     factor = float(device_count * edge_slots.shape[1]) ** (-0.5)
-    sum_con, sum_var, sum_bias = lax.psum(
-        (constraint_term, variable_term, term_bias), ("row", "col")
-    )
+    bias_block = jnp.zeros((embedding_width, 128), jnp.float32).at[:, 0].set(term_bias)
+    partials = jnp.concatenate([constraint_term, variable_term, bias_block], axis=1)
     share = embedding_width // device_count
-    my_index = lax.axis_index(("row", "col"))
-    sum_con = lax.dynamic_slice_in_dim(sum_con, my_index * share, share, 0)
-    sum_var = lax.dynamic_slice_in_dim(sum_var, my_index * share, share, 0)
-    sum_bias = lax.dynamic_slice_in_dim(sum_bias, my_index * share, share, 0)
+    summed = lax.psum_scatter(partials.reshape(device_count, share, -1), ("row", "col"), scatter_dimension=0, tiled=True).reshape(share, -1)
+    sum_con = summed[:, :embedding_width]
+    sum_var = summed[:, embedding_width : 2 * embedding_width]
+    sum_bias = summed[:, 2 * embedding_width]
     return (
         grad_con.astype(jnp.bfloat16),
         grad_var.astype(jnp.bfloat16),

time: 278 us -> 783 us (2.82)
  waiting for transfers between devices: 102 us -> 664 us
  blocking collectives: 68.2 us -> 0 us
  local copies, waits for them, and re-layouts: 9.91 us -> 22.7 us
    unnamed x1 -> x2, waiting for transfers between devices: 0.02 us -> 606 us
    psum x1 -> x0, blocking collectives: 68.2 us -> none  [on_device(): lax.psum((constraint_term, variable_term, term_bias), ('row', 'col'))]
    psum x1 -> x0, waiting for transfers between devices: 60.3 us -> none  [on_device(): lax.psum((constraint_term, variable_term, term_bias), ('row', 'col'))]
    all_to_all x1, waiting for transfers between devices: 0.01 us -> 17.2 us  [on_device(): lax.all_to_all(back_con, ('row', 'col'), split_axis=0, concat_axis=0, til...]
  transfers between devices with their start and end apart: 6 -> 6, of which waited for: 5 -> 6; matrix products, arithmetic and copies ran while one was open for 11% -> 4% of each run, Pallas kernels for 0% -> 0%
where the time goes in v1:
time: 783 us; the launch traced here: 782 us
  waiting for transfers between devices  664 us (85%)
  matrix products  39.4 us (5%)
  starting transfers between devices  35.3 us (5%)
  local copies, waits for them, and re-layouts  22.7 us (3%)
  between operations  14.4 us (2%)
    unnamed x2, waiting for transfers between devices  606 us
    all_to_all x1, waiting for transfers between devices, on_device(): lax.all_to_all(back_con, ('row', 'col'), split_axis=0, concat_axis=0, til...  17.2 us
  transfers between devices with their start and end apart: 6, of which 6 were waited for; matrix products, arithmetic and copies ran while one was open for 4% of the time, Pallas kernels for 0%

profile of v1, /device:TPU:0, one launch (start us, length us, event | category | flops | bytes accessed | tf_op | source)
XLA Modules:
  0.0 782.4 jit_solution(15963690538416077669)
XLA Ops:
  8.0 1.4 convolution_convert_fusion.3
  9.5 1.1 reshape.97
  10.5 11.2 %all-to-all-start.2 = ((bf16[128,4,768]{2,1,0:T(4,128)(2,1)}), bf16[128,4,768]{2,1,0:T(4,128)(2,1)S(1)}, u32[]{:S(2)}, u32[]{:S(2)}) async-start(bf16[128,4,768]{2,1,0:T(4,128)(2,1)} %reshape.97), calls=%async_computation.2 | async-start | bytes 1572864 | tf_op jit(solution)/shard_map/all_to_all | solution.py:45
  22.4 1.1 reshape.95
  23.5 1.4 convolution_convert_fusion.5
  24.9 1.1 reshape.93
  26.1 12.0 %all-to-all-done.2 = bf16[128,4,768]{2,1,0:T(4,128)(2,1)S(1)} async-done(((bf16[128,4,768]{2,1,0:T(4,128)(2,1)}), bf16[128,4,768]{2,1,0:T(4,128)(2,1)S(1)}, u32[]{:S(2)}, u32[]{:S(2)}) %all-to-all-start.2) | async-done | bytes 786464 | tf_op jit(solution)/shard_map/all_to_all | solution.py:45
  38.0 4.6 all-to-all-start.1
  45.5 13.5 %all-to-all-done.1 = bf16[128,4,768]{2,1,0:T(4,128)(2,1)S(1)} async-done(((bf16[128,4,768]{2,1,0:T(4,128)(2,1)}), bf16[128,4,768]{2,1,0:T(4,128)(2,1)S(1)}, u32[]{:S(2)}, u32[]{:S(2)}) %all-to-all-start.1) | async-done | bytes 786464 | tf_op jit(solution)/shard_map/all_to_all | solution.py:44
  59.0 5.7 all-to-all-start
  64.9 7.1 fusion.30
  72.2 7.7 fusion.31
  80.7 1.6 reshape.94
  82.3 7.4 convert_reduce_fusion
  89.6 2.0 fusion.28
  91.6 2.0 fusion.27
  96.0 2.6 select_maximum_fusion
  98.6 6.0 copy.17
  104.6 6.7 reshape.105
  111.4 1.1 copy-done.2
  113.3 1.1 reshape.102
  114.4 9.0 %all-to-all-start.4 = ((bf16[128,4,768]{2,1,0:T(4,128)(2,1)}), bf16[128,4,768]{2,1,0:T(4,128)(2,1)S(1)}, u32[]{:S(2)}, u32[]{:S(2)}) async-start(bf16[128,4,768]{2,1,0:T(4,128)(2,1)} %reshape.102), calls=%async_computation.4 | async-start | bytes 1572864 | tf_op jit(solution)/shard_map/all_to_all | solution.py:92
  123.4 2.1 convolution_convert_fusion.2
  125.5 1.1 reshape.100
  126.6 14.8 %all-to-all-done.4 = bf16[128,4,768]{2,1,0:T(4,128)(2,1)S(1)} async-done(((bf16[128,4,768]{2,1,0:T(4,128)(2,1)}), bf16[128,4,768]{2,1,0:T(4,128)(2,1)S(1)}, u32[]{:S(2)}, u32[]{:S(2)}) %all-to-all-start.4) | async-done | bytes 786464 | tf_op jit(solution)/shard_map/all_to_all | solution.py:92
  141.3 4.6 all-to-all-start.3
  146.2 17.2 %all-to-all-done.3 = bf16[128,4,768]{2,1,0:T(4,128)(2,1)S(1)} async-done(((bf16[128,4,768]{2,1,0:T(4,128)(2,1)}), bf16[128,4,768]{2,1,0:T(4,128)(2,1)S(1)}, u32[]{:S(2)}, u32[]{:S(2)}) %all-to-all-start.3) | async-done | bytes 786464 | tf_op jit(solution)/shard_map/all_to_all | solution.py:91
  163.5 1.2 convolution_convert_fusion.6
  164.8 2.2 fusion.29
  167.0 605.8 %reduce-scatter.5.cloned.1.call-done = f32[1,6,1664]{2,1,0:T(8,128)} async-done(((f32[128,6,1664]{2,1,0:T(8,128)}), f32[1,6,1664]{2,1,0:T(8,128)}) %reduce-scatter.5.cloned.1.call-update) | async-done | bytes 39952
  772.8 1.4 slice_multiply_fusion
  774.2 1.3 fusion.48
  (47 shorter events, 9.0 us)
Async XLA Ops:
  7.2 57.8 %copy-start = (bf16[768,768]{1,0:T(8,128)(2,1)S(1)}, bf16[768,768]{1,0:T(8,128)(2,1)}, u32[]{:S(2)}) copy-start(bf16[768,768]{1,0:T(8,128)(2,1)} %param.15) | copy-start | bytes 3538948
  7.2 14.5 %copy-start.10 = (s32[2,1,128]{2,1,0:T(1,128)S(1)}, s32[2,1,128]{2,1,0:T(1,128)}, u32[]{:S(2)}) copy-start(s32[2,1,128]{2,1,0:T(1,128)} %param.18) | copy-start | bytes 3076
  7.2 14.8 %copy-start.11 = (bf16[256,768]{1,0:T(8,128)(2,1)S(1)}, bf16[256,768]{1,0:T(8,128)(2,1)}, u32[]{:S(2)}) copy-start(bf16[256,768]{1,0:T(8,128)(2,1)} %param.11) | copy-start | bytes 1179652
  8.0 16.9 %copy-start.6 = (s32[1,1,512]{2,1,0:T(1,128)}, s32[1,1,512]{2,1,0:T(1,128)S(1)}, u32[]{:S(2)}) copy-start(s32[1,1,512]{2,1,0:T(1,128)S(1)} %get-tuple-element.21) | copy-start | bytes 6148
  8.0 16.9 %copy-start.8 = (s32[1,1,512]{2,1,0:T(1,128)}, s32[1,1,512]{2,1,0:T(1,128)S(1)}, u32[]{:S(2)}) copy-start(s32[1,1,512]{2,1,0:T(1,128)S(1)} %get-tuple-element.22) | copy-start | bytes 6148
  9.4 16.6 %copy-start.3 = (s32[2,2048]{1,0:T(2,128)S(1)}, s32[2,2048]{1,0:T(2,128)}, u32[]{:S(2)}) copy-start(s32[2,2048]{1,0:T(2,128)} %param.19) | copy-start | bytes 49156
  10.5 27.5 %all-to-all-start.2 = ((bf16[128,4,768]{2,1,0:T(4,128)(2,1)}), bf16[128,4,768]{2,1,0:T(4,128)(2,1)S(1)}, u32[]{:S(2)}, u32[]{:S(2)}) async-start(bf16[128,4,768]{2,1,0:T(4,128)(2,1)} %reshape.97), calls=%async_computation.2 | async-start | bytes 1572864 | tf_op jit(solution)/shard_map/all_to_all | solution.py:45
  26.1 18.6 %copy-start.4 = (s32[1,2048]{1,0:T(1,128)}, s32[1,2048]{1,0:T(1,128)S(1)}, u32[]{:S(2)}) copy-start(s32[1,2048]{1,0:T(1,128)S(1)} %get-tuple-element.19) | copy-start | bytes 24580
  38.0 21.0 %all-to-all-start.1 = ((bf16[128,4,768]{2,1,0:T(4,128)(2,1)}), bf16[128,4,768]{2,1,0:T(4,128)(2,1)S(1)}, u32[]{:S(2)}, u32[]{:S(2)}) async-start(bf16[128,4,768]{2,1,0:T(4,128)(2,1)} %reshape.95), calls=%async_computation.1 | async-start | bytes 1572864 | tf_op jit(solution)/shard_map/all_to_all | solution.py:44
  59.0 21.7 %all-to-all-start = ((bf16[128,4,768]{2,1,0:T(4,128)(2,1)}), bf16[128,4,768]{2,1,0:T(4,128)(2,1)}, u32[]{:S(2)}, u32[]{:S(2)}) async-start(bf16[128,4,768]{2,1,0:T(4,128)(2,1)} %reshape.93), calls=%async_computation | async-start | bytes 1572864 | tf_op jit(solution)/shard_map/all_to_all | solution.py:46
  64.7 708.1 %reduce-scatter.5.cloned.1.call-start = ((), (), s32[]{:S(2)}) async-start(), calls=%async_computation.6 | async-start | bytes 6868992
  82.2 7.4 copy-start.5
  91.6 2.9 copy-start.1
  111.3 1.1 copy-start.2
  114.4 26.9 %all-to-all-start.4 = ((bf16[128,4,768]{2,1,0:T(4,128)(2,1)}), bf16[128,4,768]{2,1,0:T(4,128)(2,1)S(1)}, u32[]{:S(2)}, u32[]{:S(2)}) async-start(bf16[128,4,768]{2,1,0:T(4,128)(2,1)} %reshape.102), calls=%async_computation.4 | async-start | bytes 1572864 | tf_op jit(solution)/shard_map/all_to_all | solution.py:92
  123.4 40.1 %copy-start.9 = (s32[1,1,512]{2,1,0:T(1,128)S(1)}, s32[1,1,512]{2,1,0:T(1,128)}, u32[]{:S(2)}) copy-start(s32[1,1,512]{2,1,0:T(1,128)} %copy-done.8) | copy-start | bytes 6148
  125.5 39.3 %copy-start.7 = (s32[1,1,512]{2,1,0:T(1,128)S(1)}, s32[1,1,512]{2,1,0:T(1,128)}, u32[]{:S(2)}) copy-start(s32[1,1,512]{2,1,0:T(1,128)} %copy-done.6) | copy-start | bytes 6148
  141.3 22.0 %all-to-all-start.3 = ((bf16[128,4,768]{2,1,0:T(4,128)(2,1)}), bf16[128,4,768]{2,1,0:T(4,128)(2,1)S(1)}, u32[]{:S(2)}, u32[]{:S(2)}) async-start(bf16[128,4,768]{2,1,0:T(4,128)(2,1)} %reshape.100), calls=%async_computation.3 | async-start | bytes 1572864 | tf_op jit(solution)/shard_map/all_to_all | solution.py:91
Sparse Core Ops, SparseCore 0:
  111.5 661.2 reduce-scatter.4

commit v2 on v1

--- a/solution.py
+++ b/solution.py
@@ -118,13 +118,24 @@
     )
     term_bias = jnp.sum(edge_delta.astype(jnp.float32), axis=0)
     factor = float(device_count * edge_slots.shape[1]) ** (-0.5)
-    bias_block = jnp.zeros((embedding_width, 128), jnp.float32).at[:, 0].set(term_bias)
-    partials = jnp.concatenate([constraint_term, variable_term, bias_block], axis=1)
     share = embedding_width // device_count
-    summed = lax.psum_scatter(partials.reshape(device_count, share, -1), ("row", "col"), scatter_dimension=0, tiled=True).reshape(share, -1)
-    sum_con = summed[:, :embedding_width]
-    sum_var = summed[:, embedding_width : 2 * embedding_width]
-    sum_bias = summed[:, 2 * embedding_width]
+    lanes = 128
+    bias_rows = jnp.zeros((device_count, 8, lanes), jnp.float32)
+    bias_rows = bias_rows.at[:, 0, :share].set(term_bias.reshape(device_count, share))
+    partials = jnp.concatenate(
+        [
+            constraint_term.reshape(device_count, -1, lanes),
+            variable_term.reshape(device_count, -1, lanes),
+            bias_rows,
+        ],
+        axis=1,
+    )
+    gathered = lax.all_to_all(partials, ("row", "col"), split_axis=0, concat_axis=0, tiled=True)
+    summed = jnp.sum(gathered, axis=0)
+    term_rows = share * embedding_width // lanes
+    sum_con = summed[:term_rows].reshape(share, embedding_width)
+    sum_var = summed[term_rows : 2 * term_rows].reshape(share, embedding_width)
+    sum_bias = summed[2 * term_rows, :share]
     return (
         grad_con.astype(jnp.bfloat16),
         grad_var.astype(jnp.bfloat16),

time: 783 us -> 216 us (0.28)
  waiting for transfers between devices: 664 us -> 96 us
  between operations: 14.4 us -> 1.01 us
  starting transfers between devices: 35.3 us -> 43.9 us
    unnamed x2 -> x0, waiting for transfers between devices: 606 us -> none
    all_to_all x0 -> x1, waiting for transfers between devices: none -> 57.3 us  [on_device(): lax.all_to_all(partials, ('row', 'col'), split_axis=0, concat_axis=0, til...]
    all_to_all x1, waiting for transfers between devices: 14.8 us -> 2.67 us  [on_device(): lax.all_to_all(back_var, ('row', 'col'), split_axis=0, concat_axis=0, til...]
    all_to_all x1, waiting for transfers between devices: 17.2 us -> 9.27 us  [on_device(): lax.all_to_all(back_con, ('row', 'col'), split_axis=0, concat_axis=0, til...]
  transfers between devices with their start and end apart: 6 -> 6, of which waited for: 6 -> 6; matrix products, arithmetic and copies ran while one was open for 4% -> 21% of each run, Pallas kernels for 0% -> 0%
where the time goes in v2:
time: 216 us; the launch traced here: 214 us
  waiting for transfers between devices  96 us (44%)
  matrix products  45.5 us (21%)
  starting transfers between devices  43.9 us (20%)
  local copies, waits for them, and re-layouts  18.4 us (9%)
  other arithmetic  8.76 us (4%)
    all_to_all x1, waiting for transfers between devices, on_device(): lax.all_to_all(partials, ('row', 'col'), split_axis=0, concat_axis=0, til...  57.3 us
    all_to_all x1, waiting for transfers between devices, on_device(): lax.all_to_all(out_con, ('row', 'col'), split_axis=0, concat_axis=0, tile...  14.1 us
    all_to_all x1, waiting for transfers between devices, on_device(): lax.all_to_all(out_var, ('row', 'col'), split_axis=0, concat_axis=0, tile...  12 us
    all_to_all x1, starting transfers between devices, on_device(): lax.all_to_all(out_var, ('row', 'col'), split_axis=0, concat_axis=0, tile...  11.2 us
    all_to_all x1, waiting for transfers between devices, on_device(): lax.all_to_all(back_con, ('row', 'col'), split_axis=0, concat_axis=0, til...  9.27 us
    all_to_all x1, starting transfers between devices, on_device(): lax.all_to_all(back_con, ('row', 'col'), split_axis=0, concat_axis=0, til...  9.11 us
    dot_general x1, matrix products, on_device(): jnp.dot(table_var, cotangent_mirror_rows, preferred_element_type=jnp.floa...  9.1 us
    dot_general x1, matrix products, on_device(): jnp.dot(edge_var, variable_weight, preferred_element_type=jnp.float32)  7.72 us
  transfers between devices with their start and end apart: 6, of which 6 were waited for; matrix products, arithmetic and copies ran while one was open for 21% of the time, Pallas kernels for 0%

profile of v2, /device:TPU:0, one launch (start us, length us, event | category | flops | bytes accessed | tf_op | source)
XLA Modules:
  0.0 213.7 jit_solution(17116410378237824049)
XLA Ops:
  1.5 1.4 convolution_convert_fusion.3
  2.9 1.1 reshape.108
  4.0 11.2 %all-to-all-start.2 = ((bf16[128,4,768]{2,1,0:T(4,128)(2,1)}), bf16[128,4,768]{2,1,0:T(4,128)(2,1)S(1)}, u32[]{:S(2)}, u32[]{:S(2)}) async-start(bf16[128,4,768]{2,1,0:T(4,128)(2,1)} %reshape.108), calls=%async_computation.2 | async-start | bytes 1572864 | tf_op jit(solution)/shard_map/all_to_all | solution.py:45
  15.8 1.1 reshape.106
  16.9 1.4 convolution_convert_fusion.5
  18.3 1.1 reshape.104
  19.5 12.0 %all-to-all-done.2 = bf16[128,4,768]{2,1,0:T(4,128)(2,1)S(1)} async-done(((bf16[128,4,768]{2,1,0:T(4,128)(2,1)}), bf16[128,4,768]{2,1,0:T(4,128)(2,1)S(1)}, u32[]{:S(2)}, u32[]{:S(2)}) %all-to-all-start.2) | async-done | bytes 786464 | tf_op jit(solution)/shard_map/all_to_all | solution.py:45
  31.5 4.6 %all-to-all-start.1 = ((bf16[128,4,768]{2,1,0:T(4,128)(2,1)}), bf16[128,4,768]{2,1,0:T(4,128)(2,1)S(1)}, u32[]{:S(2)}, u32[]{:S(2)}) async-start(bf16[128,4,768]{2,1,0:T(4,128)(2,1)} %reshape.106), calls=%async_computation.1 | async-start | bytes 1572864 | tf_op jit(solution)/shard_map/all_to_all | solution.py:44
  38.4 14.1 %all-to-all-done.1 = bf16[128,4,768]{2,1,0:T(4,128)(2,1)S(1)} async-done(((bf16[128,4,768]{2,1,0:T(4,128)(2,1)}), bf16[128,4,768]{2,1,0:T(4,128)(2,1)S(1)}, u32[]{:S(2)}, u32[]{:S(2)}) %all-to-all-start.1) | async-done | bytes 786464 | tf_op jit(solution)/shard_map/all_to_all | solution.py:44
  52.5 5.9 %all-to-all-start = ((bf16[128,4,768]{2,1,0:T(4,128)(2,1)}), bf16[128,4,768]{2,1,0:T(4,128)(2,1)}, u32[]{:S(2)}, u32[]{:S(2)}) async-start(bf16[128,4,768]{2,1,0:T(4,128)(2,1)} %reshape.104), calls=%async_computation | async-start | bytes 1572864 | tf_op jit(solution)/shard_map/all_to_all | solution.py:46
  58.3 7.7 %fusion.30 = f32[2048,768]{1,0:T(8,128)} fusion(bf16[768,768]{1,0:T(8,128)(2,1)} %param.15, bf16[512,768]{1,0:T(8,128)(2,1)S(1)} %reshape.109, s32[2048]{0:T(1024)S(1)} %bitcast.40), kind=kOutput, calls=%fused_computation.46 | convolution fusion | flops 4031250432 | bytes 8265728 | tf_op jit(solution)/shard_map/dot_general | solution.py:67
  66.3 7.2 %fusion.31 = f32[2048,768]{1,0:T(8,128)} fusion(bf16[768,768]{1,0:T(8,128)(2,1)S(1)} %copy-done, bf16[512,768]{1,0:T(8,128)(2,1)S(1)} %reshape.107, s32[2048]{0:T(1024)} %bitcast.44), kind=kOutput, calls=%fused_computation.47 | convolution fusion | flops 4031250432 | bytes 8265728 | tf_op jit(solution)/shard_map/dot_general | solution.py:66
  74.1 1.6 reshape.105
  75.7 9.1 %convert_reduce_fusion = (f32[768]{0:T(1024)S(1)}, bf16[2048,768]{1,0:T(8,128)(2,1)}) fusion(f32[2048]{0:T(1024)S(1)} %mul.41, f32[768]{0:T(1024)S(1)} %copy-done.18, f32[2048,768]{1,0:T(8,128)} %fusion.31, f32[2048,768]{1,0:T(8,128)} %fusion.30, bf16[512,768]{1,0:T(8,128)(2,1)S(1)} %reshape.105, s32[2048]{0:T(1024)S(1)} %bitcast.41), kind=kOutput, calls=%fused_computation | convolution fusion | flops 1635777792 | bytes 16537600 | tf_op jit(solution)/shard_map/dot_general | solution.py:62
  85.6 3.9 %fusion.27 = bf16[512,768]{1,0:T(8,128)(2,1)S(1)} fusion(bf16[2048,768]{1,0:T(8,128)(2,1)} %get-tuple-element.24, s32[2048]{0:T(1024)S(1)} %bitcast.45), kind=kOutput, calls=%fused_computation.38 | convolution fusion | flops 1614151680 | bytes 3940352 | tf_op jit(solution)/shard_map/dot_general | solution.py:76
  92.2 9.1 %all-to-all-start.3 = ((bf16[128,4,768]{2,1,0:T(4,128)(2,1)}), bf16[128,4,768]{2,1,0:T(4,128)(2,1)S(1)}, u32[]{:S(2)}, u32[]{:S(2)}) async-start(bf16[128,4,768]{2,1,0:T(4,128)(2,1)} %reshape.111), calls=%async_computation.3 | async-start | bytes 1572864 | tf_op jit(solution)/shard_map/all_to_all | solution.py:91
  101.4 4.0 %fusion.28 = bf16[512,768]{1,0:T(8,128)(2,1)S(1)} fusion(bf16[2048,768]{1,0:T(8,128)(2,1)} %get-tuple-element.24, s32[2048]{0:T(1024)S(1)} %bitcast.42), kind=kOutput, calls=%fused_computation.39 | convolution fusion | flops 1614151680 | bytes 3940352 | tf_op jit(solution)/shard_map/dot_general | solution.py:79
  107.1 1.1 reshape.113
  108.2 9.3 %all-to-all-done.3 = bf16[128,4,768]{2,1,0:T(4,128)(2,1)S(1)} async-done(((bf16[128,4,768]{2,1,0:T(4,128)(2,1)}), bf16[128,4,768]{2,1,0:T(4,128)(2,1)S(1)}, u32[]{:S(2)}, u32[]{:S(2)}) %all-to-all-start.3) | async-done | bytes 786464 | tf_op jit(solution)/shard_map/all_to_all | solution.py:91
  118.4 5.7 %all-to-all-start.4 = ((bf16[128,4,768]{2,1,0:T(4,128)(2,1)}), bf16[128,4,768]{2,1,0:T(4,128)(2,1)}, u32[]{:S(2)}, u32[]{:S(2)}) async-start(bf16[128,4,768]{2,1,0:T(4,128)(2,1)} %reshape.113), calls=%async_computation.4 | async-start | bytes 1572864 | tf_op jit(solution)/shard_map/all_to_all | solution.py:92
  124.1 2.2 %fusion.83 = f32[768,768]{1,0:T(8,128)S(1)} fusion(bf16[512,768]{1,0:T(8,128)(2,1)} %copy-done.2, bf16[512,768]{1,0:T(8,128)(2,1)} %copy-done.5), kind=kOutput, calls=%fused_computation.106 | convolution fusion | flops 603979776 | bytes 3932160 | tf_op jit(solution)/shard_map/dot_general | solution.py:107
  126.2 1.7 reshape.115
  127.9 2.2 %fusion.84 = f32[768,768]{1,0:T(8,128)S(1)} fusion(bf16[512,768]{1,0:T(8,128)(2,1)} %copy-done.1, bf16[512,768]{1,0:T(8,128)(2,1)} %copy-done.6), kind=kOutput, calls=%fused_computation.107 | convolution fusion | flops 603979776 | bytes 3932160 | tf_op jit(solution)/shard_map/dot_general | solution.py:113
  130.1 1.8 reshape.116
  131.9 5.4 %select_maximum_fusion = f32[128,80,128]{2,1,0:T(8,128)} fusion(f32[128,1,6]{2,1,0:T(1,128)} %bitcast.36, f32[128,36,128]{2,1,0:T(8,128)} %reshape.116, f32[128,36,128]{2,1,0:T(8,128)} %reshape.115), kind=kLoop, calls=%fused_computation.2 | loop fusion | flops 5242880 | bytes 9964544 | tf_op jit(solution)/shard_map/concatenate | solution.py:125
  137.3 2.7 %all-to-all-done.4 = bf16[128,4,768]{2,1,0:T(4,128)(2,1)} async-done(((bf16[128,4,768]{2,1,0:T(4,128)(2,1)}), bf16[128,4,768]{2,1,0:T(4,128)(2,1)}, u32[]{:S(2)}, u32[]{:S(2)}) %all-to-all-start.4) | async-done | bytes 786464 | tf_op jit(solution)/shard_map/all_to_all | solution.py:92
  140.0 7.5 %all-to-all-start.5 = ((f32[128,80,128]{2,1,0:T(8,128)}), f32[128,80,128]{2,1,0:T(8,128)}, u32[]{:S(2)}, u32[]{:S(2)}) async-start(f32[128,80,128]{2,1,0:T(8,128)} %select_maximum_fusion), calls=%async_computation.5 | async-start | bytes 10485760 | tf_op jit(solution)/shard_map/all_to_all | solution.py:133
  147.7 1.6 reshape.114
  149.3 1.3 convolution_convert_fusion.6
  150.6 1.3 fusion.29
  151.8 57.3 %all-to-all-done.5 = f32[128,80,128]{2,1,0:T(8,128)} async-done(((f32[128,80,128]{2,1,0:T(8,128)}), f32[128,80,128]{2,1,0:T(8,128)}, u32[]{:S(2)}, u32[]{:S(2)}) %all-to-all-start.5) | async-done | bytes 5242912 | tf_op jit(solution)/shard_map/all_to_all | solution.py:133
  209.2 2.8 %reduce_sum.19 = f32[80,128]{1,0:T(8,128)S(1)} reduce(f32[128,80,128]{2,1,0:T(8,128)} %all-to-all-done.5, f32[]{:T(128)} %constant.48.clone.1), dimensions={0}, to_apply=%region_1.2 | reduce | flops 1300480 | bytes 5283844 | tf_op jit(solution)/shard_map/reduce_sum | solution.py:134
  (61 shorter events, 12.6 us)
Async XLA Ops:
  0.6 65.6 %copy-start = (bf16[768,768]{1,0:T(8,128)(2,1)S(1)}, bf16[768,768]{1,0:T(8,128)(2,1)}, u32[]{:S(2)}) copy-start(bf16[768,768]{1,0:T(8,128)(2,1)} %param.14) | copy-start | bytes 3538948
  0.6 14.5 %copy-start.14 = (s32[2,1,128]{2,1,0:T(1,128)S(1)}, s32[2,1,128]{2,1,0:T(1,128)}, u32[]{:S(2)}) copy-start(s32[2,1,128]{2,1,0:T(1,128)} %param.18) | copy-start | bytes 3076
  0.7 14.8 %copy-start.16 = (bf16[256,768]{1,0:T(8,128)(2,1)S(1)}, bf16[256,768]{1,0:T(8,128)(2,1)}, u32[]{:S(2)}) copy-start(bf16[256,768]{1,0:T(8,128)(2,1)} %param.11) | copy-start | bytes 1179652
  1.5 16.8 %copy-start.10 = (s32[1,1,512]{2,1,0:T(1,128)}, s32[1,1,512]{2,1,0:T(1,128)S(1)}, u32[]{:S(2)}) copy-start(s32[1,1,512]{2,1,0:T(1,128)S(1)} %get-tuple-element.21) | copy-start | bytes 6148
  1.5 16.9 %copy-start.12 = (s32[1,1,512]{2,1,0:T(1,128)}, s32[1,1,512]{2,1,0:T(1,128)S(1)}, u32[]{:S(2)}) copy-start(s32[1,1,512]{2,1,0:T(1,128)S(1)} %get-tuple-element.22) | copy-start | bytes 6148
  2.9 16.6 %copy-start.7 = (s32[2,2048]{1,0:T(2,128)S(1)}, s32[2,2048]{1,0:T(2,128)}, u32[]{:S(2)}) copy-start(s32[2,2048]{1,0:T(2,128)} %param.19) | copy-start | bytes 49156
  4.0 27.5 %all-to-all-start.2 = ((bf16[128,4,768]{2,1,0:T(4,128)(2,1)}), bf16[128,4,768]{2,1,0:T(4,128)(2,1)S(1)}, u32[]{:S(2)}, u32[]{:S(2)}) async-start(bf16[128,4,768]{2,1,0:T(4,128)(2,1)} %reshape.108), calls=%async_computation.2 | async-start | bytes 1572864 | tf_op jit(solution)/shard_map/all_to_all | solution.py:45
  19.5 18.6 %copy-start.8 = (s32[1,2048]{1,0:T(1,128)}, s32[1,2048]{1,0:T(1,128)S(1)}, u32[]{:S(2)}) copy-start(s32[1,2048]{1,0:T(1,128)S(1)} %get-tuple-element.20) | copy-start | bytes 24580
  31.5 21.0 %all-to-all-start.1 = ((bf16[128,4,768]{2,1,0:T(4,128)(2,1)}), bf16[128,4,768]{2,1,0:T(4,128)(2,1)S(1)}, u32[]{:S(2)}, u32[]{:S(2)}) async-start(bf16[128,4,768]{2,1,0:T(4,128)(2,1)} %reshape.106), calls=%async_computation.1 | async-start | bytes 1572864 | tf_op jit(solution)/shard_map/all_to_all | solution.py:44
  38.4 27.7 %copy-start.1 = (bf16[512,768]{1,0:T(8,128)(2,1)}, bf16[512,768]{1,0:T(8,128)(2,1)S(1)}, u32[]{:S(2)}) copy-start(bf16[512,768]{1,0:T(8,128)(2,1)S(1)} %reshape.109) | copy-start | bytes 2359300
  52.5 21.7 %all-to-all-start = ((bf16[128,4,768]{2,1,0:T(4,128)(2,1)}), bf16[128,4,768]{2,1,0:T(4,128)(2,1)}, u32[]{:S(2)}, u32[]{:S(2)}) async-start(bf16[128,4,768]{2,1,0:T(4,128)(2,1)} %reshape.104), calls=%async_computation | async-start | bytes 1572864 | tf_op jit(solution)/shard_map/all_to_all | solution.py:46
  66.3 7.2 %copy-start.2 = (bf16[512,768]{1,0:T(8,128)(2,1)}, bf16[512,768]{1,0:T(8,128)(2,1)S(1)}, u32[]{:S(2)}) copy-start(bf16[512,768]{1,0:T(8,128)(2,1)S(1)} %reshape.107) | copy-start | bytes 2359300
  66.3 9.4 %copy-start.18 = (f32[768]{0:T(1024)S(1)}, f32[768]{0:T(1024)}, u32[]{:S(2)}) copy-start(f32[768]{0:T(1024)} %param.16) | copy-start | bytes 9220
  75.7 9.9 %copy-start.9 = (s32[1,2048]{1,0:T(1,128)S(1)}, s32[1,2048]{1,0:T(1,128)}, u32[]{:S(2)}) copy-start(s32[1,2048]{1,0:T(1,128)} %copy-done.8) | copy-start | bytes 24580
  89.5 0.9 copy-start.5
  92.2 25.2 %all-to-all-start.3 = ((bf16[128,4,768]{2,1,0:T(4,128)(2,1)}), bf16[128,4,768]{2,1,0:T(4,128)(2,1)S(1)}, u32[]{:S(2)}, u32[]{:S(2)}) async-start(bf16[128,4,768]{2,1,0:T(4,128)(2,1)} %reshape.111), calls=%async_computation.3 | async-start | bytes 1572864 | tf_op jit(solution)/shard_map/all_to_all | solution.py:91
  101.4 4.9 %copy-start.15 = (bf16[768,768]{1,0:T(8,128)(2,1)S(1)}, bf16[768,768]{1,0:T(8,128)(2,1)}, u32[]{:S(2)}) copy-start(bf16[768,768]{1,0:T(8,128)(2,1)} %param.15) | copy-start | bytes 3538948
  105.3 0.9 copy-start.6
  117.5 0.9 copy-start.3
  118.4 21.7 %all-to-all-start.4 = ((bf16[128,4,768]{2,1,0:T(4,128)(2,1)}), bf16[128,4,768]{2,1,0:T(4,128)(2,1)}, u32[]{:S(2)}, u32[]{:S(2)}) async-start(bf16[128,4,768]{2,1,0:T(4,128)(2,1)} %reshape.113), calls=%async_computation.4 | async-start | bytes 1572864 | tf_op jit(solution)/shard_map/all_to_all | solution.py:92
  137.3 10.2 %copy-start.4 = (bf16[128,4,768]{2,1,0:T(4,128)(2,1)S(1)}, bf16[128,4,768]{2,1,0:T(4,128)(2,1)}, u32[]{:S(2)}) copy-start(bf16[128,4,768]{2,1,0:T(4,128)(2,1)} %copy-done.3) | copy-start | bytes 2359300
  137.3 12.0 %copy-start.13 = (s32[1,1,512]{2,1,0:T(1,128)S(1)}, s32[1,1,512]{2,1,0:T(1,128)}, u32[]{:S(2)}) copy-start(s32[1,1,512]{2,1,0:T(1,128)} %copy-done.12) | copy-start | bytes 6148
  140.0 69.2 %all-to-all-start.5 = ((f32[128,80,128]{2,1,0:T(8,128)}), f32[128,80,128]{2,1,0:T(8,128)}, u32[]{:S(2)}, u32[]{:S(2)}) async-start(f32[128,80,128]{2,1,0:T(8,128)} %select_maximum_fusion), calls=%async_computation.5 | async-start | bytes 10485760 | tf_op jit(solution)/shard_map/all_to_all | solution.py:133
  147.5 3.0 %copy-start.11 = (s32[1,1,512]{2,1,0:T(1,128)S(1)}, s32[1,1,512]{2,1,0:T(1,128)}, u32[]{:S(2)}) copy-start(s32[1,1,512]{2,1,0:T(1,128)} %copy-done.10) | copy-start | bytes 6148
  147.5 3.0 %copy-start.17 = (bf16[256,768]{1,0:T(8,128)(2,1)S(1)}, bf16[256,768]{1,0:T(8,128)(2,1)}, u32[]{:S(2)}) copy-start(bf16[256,768]{1,0:T(8,128)(2,1)} %param.13) | copy-start | bytes 1179652

commit v3 on v2

--- a/solution.py
+++ b/solution.py
@@ -1,7 +1,9 @@
 import jax
 import jax.numpy as jnp
 from jax import lax
-from jax.sharding import PartitionSpec as P
+from jax.sharding import Mesh, PartitionSpec as P
+
+DEVICE_AXES = ("y", "c", "z", "x")
 
 
 def one_hot_table(indices, width):
@@ -24,7 +26,7 @@
     recv_count,
     edge_slots,
 ):
-    device_count = lax.axis_size(("row", "col"))
+    device_count = lax.axis_size(DEVICE_AXES)
     slot_cap = send_rows.shape[2] // device_count
     embedding_width = constraint_features.shape[1]
     replica_rows = device_count * slot_cap
@@ -41,9 +43,9 @@
         device_count, slot_cap, embedding_width
     )
     constraint_mirror_rows, variable_mirror_rows, cotangent_mirror_rows = (
-        lax.all_to_all(out_con, ("row", "col"), split_axis=0, concat_axis=0, tiled=True),
-        lax.all_to_all(out_var, ("row", "col"), split_axis=0, concat_axis=0, tiled=True),
-        lax.all_to_all(out_cot, ("row", "col"), split_axis=0, concat_axis=0, tiled=True),
+        lax.all_to_all(out_con, DEVICE_AXES, split_axis=0, concat_axis=0, tiled=True),
+        lax.all_to_all(out_var, DEVICE_AXES, split_axis=0, concat_axis=0, tiled=True),
+        lax.all_to_all(out_cot, DEVICE_AXES, split_axis=0, concat_axis=0, tiled=True),
     )
     constraint_mirror_rows = constraint_mirror_rows.reshape(replica_rows, embedding_width)
     variable_mirror_rows = variable_mirror_rows.reshape(replica_rows, embedding_width)
@@ -88,8 +90,8 @@
     back_con = back_con.reshape(device_count, slot_cap, embedding_width)
     back_var = back_var.reshape(device_count, slot_cap, embedding_width)
     home_con, home_var = (
-        lax.all_to_all(back_con, ("row", "col"), split_axis=0, concat_axis=0, tiled=True),
-        lax.all_to_all(back_var, ("row", "col"), split_axis=0, concat_axis=0, tiled=True),
+        lax.all_to_all(back_con, DEVICE_AXES, split_axis=0, concat_axis=0, tiled=True),
+        lax.all_to_all(back_var, DEVICE_AXES, split_axis=0, concat_axis=0, tiled=True),
     )
     grad_con = lax.dot_general(
         select_con,
@@ -130,8 +132,12 @@
         ],
         axis=1,
     )
-    gathered = lax.all_to_all(partials, ("row", "col"), split_axis=0, concat_axis=0, tiled=True)
-    summed = jnp.sum(gathered, axis=0)
+    summed = partials.reshape(*(lax.axis_size(name) for name in DEVICE_AXES), -1, lanes)
+    for axis_name, position in (("c", 1), ("x", 3), ("z", 2), ("y", 0)):
+        sent = summed if axis_name == "c" else summed.astype(jnp.bfloat16)
+        gathered = lax.all_to_all(sent, axis_name, position, position, tiled=True)
+        summed = jnp.sum(gathered.astype(jnp.float32), axis=position, keepdims=True)
+    summed = summed.reshape(-1, lanes)
     term_rows = share * embedding_width // lanes
     sum_con = summed[:term_rows].reshape(share, embedding_width)
     sum_var = summed[term_rows : 2 * term_rows].reshape(share, embedding_width)
@@ -147,26 +153,28 @@
 
 def solution(mesh):
     placed = (
-        P(("row", "col"), None),
-        P(("row", "col"), None),
-        P(("row", "col"), None),
+        P(DEVICE_AXES, None),
+        P(DEVICE_AXES, None),
+        P(DEVICE_AXES, None),
         P(),
         P(),
         P(),
-        P(None, ("row", "col"), None),
-        P(None, ("row", "col"), None),
-        P(None, ("row", "col")),
+        P(None, DEVICE_AXES, None),
+        P(None, DEVICE_AXES, None),
+        P(None, DEVICE_AXES),
     )
+    rows, cols = mesh.devices.shape
+    torus = Mesh(mesh.devices.reshape(rows // 2, 2, cols // 4, 4), DEVICE_AXES)
     return jax.shard_map(
         on_device,
-        mesh=mesh,
+        mesh=torus,
         in_specs=placed,
         out_specs=(
-            P(("row", "col"), None),
-            P(("row", "col"), None),
-            P(("row", "col"), None),
-            P(("row", "col"), None),
-            P(("row", "col")),
+            P(DEVICE_AXES, None),
+            P(DEVICE_AXES, None),
+            P(DEVICE_AXES, None),
+            P(DEVICE_AXES, None),
+            P(DEVICE_AXES),
         ),
         check_vma=False,
     )

time: 216 us -> 205 us (0.949)
  waiting for transfers between devices: 96 us -> 74.8 us
  blocking collectives: 0 us -> 9.07 us
  local copies, waits for them, and re-layouts: 18.4 us -> 22 us
    all_to_all x6 -> x8, waiting for transfers between devices: 96 us -> 74.8 us  [the longest x3 22.6 us: on_device(): gathered = lax.all_to_all(sent, axis_name, position, position, tiled=True)]
    all_to_all x0 -> x1, blocking collectives: none -> 9.07 us  [on_device(): gathered = lax.all_to_all(sent, axis_name, position, position, tiled=True)]
    concatenate x0 -> x3, local copies, waits for them, and re-layouts: none -> 4 us  [on_device(): jnp.concatenate([constraint_term.reshape(device_count, -1, lanes), variab...]
    reshape x2 -> x0, local copies, waits for them, and re-layouts: 3.5 us -> none  [the longest x1 1.79 us: on_device(): variable_term.reshape(device_count, -1, lanes)]
    unnamed x38 -> x32, local copies, waits for them, and re-layouts: 2.79 us -> 0.08 us
    concatenate x1, other arithmetic: 5.43 us -> 3.13 us  [on_device(): jnp.concatenate([constraint_term.reshape(device_count, -1, lanes), variab...]
    all_to_all x6 -> x8, starting transfers between devices: 43.9 us -> 45.8 us  [the longest x1 11.2 us: on_device(): lax.all_to_all(out_var, DEVICE_AXES, split_axis=0, concat_axis=0, tiled=T...]
  transfers between devices with their start and end apart: 6 -> 8, of which waited for: 6 -> 8; matrix products, arithmetic and copies ran while one was open for 21% -> 18% of each run, Pallas kernels for 0% -> 0%
where the time goes in v3:
time: 205 us; the launch traced here: 204 us
  waiting for transfers between devices  74.8 us (36%)
  starting transfers between devices  45.8 us (22%)
  matrix products  44.1 us (22%)
  local copies, waits for them, and re-layouts  22 us (11%)
  blocking collectives  9.07 us (4%)
  other arithmetic  7.62 us (4%)
    all_to_all x3, waiting for transfers between devices, on_device(): gathered = lax.all_to_all(sent, axis_name, position, position, tiled=True)  22.6 us
    all_to_all x1, waiting for transfers between devices, on_device(): lax.all_to_all(out_con, DEVICE_AXES, split_axis=0, concat_axis=0, tiled=T...  14.1 us
    all_to_all x1, waiting for transfers between devices, on_device(): lax.all_to_all(back_con, DEVICE_AXES, split_axis=0, concat_axis=0, tiled=...  12.9 us
    all_to_all x1, waiting for transfers between devices, on_device(): lax.all_to_all(out_var, DEVICE_AXES, split_axis=0, concat_axis=0, tiled=T...  12.1 us
    all_to_all x1, waiting for transfers between devices, on_device(): lax.all_to_all(back_var, DEVICE_AXES, split_axis=0, concat_axis=0, tiled=...  11.7 us
    all_to_all x1, starting transfers between devices, on_device(): lax.all_to_all(out_var, DEVICE_AXES, split_axis=0, concat_axis=0, tiled=T...  11.2 us
    all_to_all x3, starting transfers between devices, on_device(): gathered = lax.all_to_all(sent, axis_name, position, position, tiled=True)  10.3 us
    all_to_all x1, blocking collectives, on_device(): gathered = lax.all_to_all(sent, axis_name, position, position, tiled=True)  9.07 us
  transfers between devices with their start and end apart: 8, of which 8 were waited for; matrix products, arithmetic and copies ran while one was open for 18% of the time, Pallas kernels for 0%

profile of v3, /device:TPU:0, one launch (start us, length us, event | category | flops | bytes accessed | tf_op | source)
XLA Modules:
  0.0 204.4 jit_solution(11779922485792042366)
XLA Ops:
  4.0 11.2 %all-to-all-start.2 = ((bf16[128,4,768]{2,1,0:T(4,128)(2,1)}), bf16[128,4,768]{2,1,0:T(4,128)(2,1)S(1)}, u32[]{:S(2)}, u32[]{:S(2)}) async-start(bf16[128,4,768]{2,1,0:T(4,128)(2,1)} %reshape.149), calls=%async_computation.2 | async-start | bytes 1572864 | tf_op jit(solution)/shard_map/all_to_all | solution.py:47
  19.5 12.1 %all-to-all-done.2 = bf16[128,4,768]{2,1,0:T(4,128)(2,1)S(1)} async-done(((bf16[128,4,768]{2,1,0:T(4,128)(2,1)}), bf16[128,4,768]{2,1,0:T(4,128)(2,1)S(1)}, u32[]{:S(2)}, u32[]{:S(2)}) %all-to-all-start.2) | async-done | bytes 786464 | tf_op jit(solution)/shard_map/all_to_all | solution.py:47
  31.5 4.6 %all-to-all-start.1 = ((bf16[128,4,768]{2,1,0:T(4,128)(2,1)}), bf16[128,4,768]{2,1,0:T(4,128)(2,1)S(1)}, u32[]{:S(2)}, u32[]{:S(2)}) async-start(bf16[128,4,768]{2,1,0:T(4,128)(2,1)} %reshape.147), calls=%async_computation.1 | async-start | bytes 1572864 | tf_op jit(solution)/shard_map/all_to_all | solution.py:46
  38.4 14.1 %all-to-all-done.1 = bf16[128,4,768]{2,1,0:T(4,128)(2,1)S(1)} async-done(((bf16[128,4,768]{2,1,0:T(4,128)(2,1)}), bf16[128,4,768]{2,1,0:T(4,128)(2,1)S(1)}, u32[]{:S(2)}, u32[]{:S(2)}) %all-to-all-start.1) | async-done | bytes 786464 | tf_op jit(solution)/shard_map/all_to_all | solution.py:46
  52.5 5.9 %all-to-all-start = ((bf16[128,4,768]{2,1,0:T(4,128)(2,1)}), bf16[128,4,768]{2,1,0:T(4,128)(2,1)}, u32[]{:S(2)}, u32[]{:S(2)}) async-start(bf16[128,4,768]{2,1,0:T(4,128)(2,1)} %reshape.145), calls=%async_computation | async-start | bytes 1572864 | tf_op jit(solution)/shard_map/all_to_all | solution.py:48
  58.4 7.7 %fusion.30 = f32[2048,768]{1,0:T(8,128)} fusion(bf16[768,768]{1,0:T(8,128)(2,1)} %param.15, bf16[512,768]{1,0:T(8,128)(2,1)S(1)} %reshape.150, s32[2048]{0:T(1024)} %bitcast.54), kind=kOutput, calls=%fused_computation.46 | convolution fusion | flops 4031250432 | bytes 8265728 | tf_op jit(solution)/shard_map/dot_general | solution.py:69
  66.3 6.4 %fusion.31 = f32[2048,768]{1,0:T(8,128)} fusion(bf16[768,768]{1,0:T(8,128)(2,1)S(1)} %copy-done, bf16[512,768]{1,0:T(8,128)(2,1)S(1)} %reshape.148, s32[2048]{0:T(1024)S(1)} %bitcast.51), kind=kOutput, calls=%fused_computation.47 | convolution fusion | flops 4031250432 | bytes 8265728 | tf_op jit(solution)/shard_map/dot_general | solution.py:68
  75.7 8.1 %convert_reduce_fusion = (f32[768]{0:T(1024)}, bf16[2048,768]{1,0:T(8,128)(2,1)S(1)}) fusion(f32[2048]{0:T(1024)S(1)} %mul.41, f32[768]{0:T(1024)S(1)} %copy-done.15, f32[2048,768]{1,0:T(8,128)} %fusion.31, f32[2048,768]{1,0:T(8,128)} %fusion.30, bf16[512,768]{1,0:T(8,128)(2,1)S(1)} %reshape.146, s32[2048]{0:T(1024)S(1)} %bitcast.55), kind=kOutput, calls=%fused_computation | convolution fusion | flops 1635777792 | bytes 16537600 | tf_op jit(solution)/shard_map/dot_general | solution.py:64
  83.8 2.9 %fusion.28 = bf16[512,768]{1,0:T(8,128)(2,1)} fusion(bf16[2048,768]{1,0:T(8,128)(2,1)S(1)} %get-tuple-element.24, s32[2048]{0:T(1024)S(1)} %bitcast.56), kind=kOutput, calls=%fused_computation.38 | convolution fusion | flops 1614151680 | bytes 3940352 | tf_op jit(solution)/shard_map/dot_general | solution.py:81
  86.7 2.0 fusion.27
  88.8 1.7 convolution_convert_fusion.2
  92.1 2.4 %reshape.152 = bf16[128,4,768]{2,1,0:T(4,128)(2,1)} reshape(bf16[512,768]{1,0:T(8,128)(2,1)} %convolution_convert_fusion.2) | data formatting | bytes 1572864 | tf_op jit(solution)/shard_map/reshape | solution.py:90
  94.4 1.7 concatenate.12
  96.1 2.2 %fusion.84 = f32[768,768]{1,0:T(8,128)S(1)} fusion(bf16[512,768]{1,0:T(8,128)(2,1)} %copy-done.1, bf16[512,768]{1,0:T(8,128)(2,1)} %fusion.28), kind=kOutput, calls=%fused_computation.108 | convolution fusion | flops 603979776 | bytes 3932160 | tf_op jit(solution)/shard_map/dot_general | solution.py:115
  98.3 1.7 concatenate.13
  100.9 3.1 %pad_maximum_fusion = f32[4,2,4,4,80,128]{5,4,3,2,1,0:T(8,128)S(1)} fusion(f32[4,2,4,4,8,128]{5,4,3,2,1,0:T(8,128)S(1)} %bitcast.44, f32[4,2,4,4,36,128]{5,4,3,2,1,0:T(8,128)} %concatenate.13, f32[4,2,4,4,36,128]{5,4,3,2,1,0:T(8,128)} %concatenate.12), kind=kLoop, calls=%fused_computation.2 | loop fusion | flops 2621440 | bytes 10485760 | tf_op jit(solution)/shard_map/concatenate | solution.py:127
  104.6 9.1 %all_to_all.45 = f32[4,2,4,4,80,128]{5,4,3,2,0,1:T(8,128)} all-to-all(f32[4,2,4,4,80,128]{5,4,3,2,0,1:T(8,128)S(1)} %copy.18), channel_id=1, replica_groups=mesh['y'=4,'c'=2,'z'=4,'x'=4] {'c'}, dimensions={1} | all-to-all | bytes 10485760 | tf_op jit(solution)/shard_map/all_to_all | solution.py:138
  113.7 8.2 %all-to-all-start.3 = ((bf16[128,4,768]{2,1,0:T(4,128)(2,1)}), bf16[128,4,768]{2,1,0:T(4,128)(2,1)S(1)}, u32[]{:S(2)}, u32[]{:S(2)}) async-start(bf16[128,4,768]{2,1,0:T(4,128)(2,1)} %reshape.152), calls=%async_computation.3 | async-start | bytes 1572864 | tf_op jit(solution)/shard_map/all_to_all | solution.py:93
  121.9 2.3 %convolution_convert_fusion.1 = bf16[512,768]{1,0:T(8,128)(2,1)S(1)} fusion(bf16[512,768]{1,0:T(8,128)(2,1)} %fusion.28, bf16[768,768]{1,0:T(8,128)(2,1)} %param.15), kind=kOutput, calls=%fused_computation.35 | convolution fusion | flops 604372992 | bytes 2752512 | tf_op jit(solution)/shard_map/dot_general | solution.py:87
  125.3 12.9 %all-to-all-done.3 = bf16[128,4,768]{2,1,0:T(4,128)(2,1)S(1)} async-done(((bf16[128,4,768]{2,1,0:T(4,128)(2,1)}), bf16[128,4,768]{2,1,0:T(4,128)(2,1)S(1)}, u32[]{:S(2)}, u32[]{:S(2)}) %all-to-all-start.3) | async-done | bytes 786464 | tf_op jit(solution)/shard_map/all_to_all | solution.py:93
  138.2 5.7 %all-to-all-start.4 = ((bf16[128,4,768]{2,1,0:T(4,128)(2,1)}), bf16[128,4,768]{2,1,0:T(4,128)(2,1)}, u32[]{:S(2)}, u32[]{:S(2)}) async-start(bf16[128,4,768]{2,1,0:T(4,128)(2,1)} %reshape.154), calls=%async_computation.4 | async-start | bytes 1572864 | tf_op jit(solution)/shard_map/all_to_all | solution.py:94
  143.9 3.1 %reduce_sum.54 = bf16[4,4,4,80,128]{4,3,2,1,0:T(8,128)(2,1)S(1)} reduce(f32[4,2,4,4,80,128]{5,4,3,2,0,1:T(8,128)} %all_to_all.45, f32[]{:T(128)} %constant.50.clone.1), dimensions={1}, to_apply=%region_1.2 | reduce | flops 655360 | bytes 6553604 | tf_op jit(solution)/shard_map/reduce_sum | solution.py:139
  148.2 11.7 %all-to-all-done.4 = bf16[128,4,768]{2,1,0:T(4,128)(2,1)} async-done(((bf16[128,4,768]{2,1,0:T(4,128)(2,1)}), bf16[128,4,768]{2,1,0:T(4,128)(2,1)}, u32[]{:S(2)}, u32[]{:S(2)}) %all-to-all-start.4) | async-done | bytes 786464 | tf_op jit(solution)/shard_map/all_to_all | solution.py:94
  159.9 3.5 %all-to-all-start.6 = ((bf16[4,1,4,4,80,128]{5,4,2,0,1,3:T(8,128)(2,1)}), bf16[4,1,4,4,80,128]{5,4,2,0,1,3:T(8,128)(2,1)S(1)}, u32[]{:S(2)}, u32[]{:S(2)}) async-start(bf16[4,1,4,4,80,128]{5,4,2,0,1,3:T(8,128)(2,1)} %copy.19), calls=%async_computation.6 | async-start | bytes 2621440 | tf_op jit(solution)/shard_map/all_to_all | solution.py:138
  164.5 2.3 %reshape.155 = bf16[512,768]{1,0:T(8,128)(2,1)} reshape(bf16[128,4,768]{2,1,0:T(4,128)(2,1)} %all-to-all-done.4) | data formatting | bytes 1572864 | tf_op jit(solution)/shard_map/reshape | solution.py:104
  166.8 14.8 %all-to-all-done.6 = bf16[4,1,4,4,80,128]{5,4,2,0,1,3:T(8,128)(2,1)S(1)} async-done(((bf16[4,1,4,4,80,128]{5,4,2,0,1,3:T(8,128)(2,1)}), bf16[4,1,4,4,80,128]{5,4,2,0,1,3:T(8,128)(2,1)S(1)}, u32[]{:S(2)}, u32[]{:S(2)}) %all-to-all-start.6) | async-done | bytes 1310752 | tf_op jit(solution)/shard_map/all_to_all | solution.py:138
  182.5 3.5 %all-to-all-start.7 = ((bf16[4,1,4,1,80,128]{5,4,0,3,1,2:T(8,128)(2,1)}), bf16[4,1,4,1,80,128]{5,4,0,3,1,2:T(8,128)(2,1)S(1)}, u32[]{:S(2)}, u32[]{:S(2)}) async-start(bf16[4,1,4,1,80,128]{5,4,0,3,1,2:T(8,128)(2,1)} %copy.20), calls=%async_computation.7 | async-start | bytes 655360 | tf_op jit(solution)/shard_map/all_to_all | solution.py:138
  186.0 2.4 %fusion.29 = bf16[256,768]{1,0:T(8,128)(2,1)} fusion(bf16[512,768]{1,0:T(8,128)(2,1)} %reshape.155, bf16[256,768]{1,0:T(8,128)(2,1)S(1)} %copy-done.14, s32[512]{0:T(512)S(1)} %bitcast.61), kind=kOutput, calls=%fused_computation.44 | convolution fusion | flops 202309632 | bytes 1574912 | tf_op jit(solution)/shard_map/dot_general | solution.py:102
  188.4 4.6 %all-to-all-done.7 = bf16[4,1,4,1,80,128]{5,4,0,3,1,2:T(8,128)(2,1)S(1)} async-done(((bf16[4,1,4,1,80,128]{5,4,0,3,1,2:T(8,128)(2,1)}), bf16[4,1,4,1,80,128]{5,4,0,3,1,2:T(8,128)(2,1)S(1)}, u32[]{:S(2)}, u32[]{:S(2)}) %all-to-all-start.7) | async-done | bytes 327712 | tf_op jit(solution)/shard_map/all_to_all | solution.py:138
  193.7 3.3 %all-to-all-start.8 = ((bf16[4,1,1,1,80,128]{5,4,3,2,1,0:T(8,128)(2,1)}), bf16[4,1,1,1,80,128]{5,4,3,2,1,0:T(8,128)(2,1)S(1)}, u32[]{:S(2)}, u32[]{:S(2)}) async-start(bf16[4,1,1,1,80,128]{5,4,3,2,1,0:T(8,128)(2,1)} %bitcast.10), calls=%async_computation.8 | async-start | bytes 163840 | tf_op jit(solution)/shard_map/all_to_all | solution.py:138
  197.0 2.4 %convolution_convert_fusion.6 = bf16[256,768]{1,0:T(8,128)(2,1)} fusion(bf16[512,768]{1,0:T(8,128)(2,1)} %reshape.153, s32[512]{0:T(512)S(1)} %bitcast.58), kind=kOutput, calls=%fused_computation.45 | convolution fusion | flops 201916416 | bytes 1181696 | tf_op jit(solution)/shard_map/dot_general | solution.py:96
  199.4 3.3 %all-to-all-done.8 = bf16[4,1,1,1,80,128]{5,4,3,2,1,0:T(8,128)(2,1)S(1)} async-done(((bf16[4,1,1,1,80,128]{5,4,3,2,1,0:T(8,128)(2,1)}), bf16[4,1,1,1,80,128]{5,4,3,2,1,0:T(8,128)(2,1)S(1)}, u32[]{:S(2)}, u32[]{:S(2)}) %all-to-all-start.8) | async-done | bytes 81952 | tf_op jit(solution)/shard_map/all_to_all | solution.py:138
  (67 shorter events, 22.7 us)
Async XLA Ops:
  0.6 65.6 %copy-start = (bf16[768,768]{1,0:T(8,128)(2,1)S(1)}, bf16[768,768]{1,0:T(8,128)(2,1)}, u32[]{:S(2)}) copy-start(bf16[768,768]{1,0:T(8,128)(2,1)} %param.14) | copy-start | bytes 3538948
  0.6 14.5 %copy-start.12 = (s32[2,1,128]{2,1,0:T(1,128)S(1)}, s32[2,1,128]{2,1,0:T(1,128)}, u32[]{:S(2)}) copy-start(s32[2,1,128]{2,1,0:T(1,128)} %param.18) | copy-start | bytes 3076
  0.7 14.8 %copy-start.13 = (bf16[256,768]{1,0:T(8,128)(2,1)S(1)}, bf16[256,768]{1,0:T(8,128)(2,1)}, u32[]{:S(2)}) copy-start(bf16[256,768]{1,0:T(8,128)(2,1)} %param.11) | copy-start | bytes 1179652
  1.5 16.9 %copy-start.8 = (s32[1,1,512]{2,1,0:T(1,128)}, s32[1,1,512]{2,1,0:T(1,128)S(1)}, u32[]{:S(2)}) copy-start(s32[1,1,512]{2,1,0:T(1,128)S(1)} %get-tuple-element.22) | copy-start | bytes 6148
  1.5 16.9 %copy-start.10 = (s32[1,1,512]{2,1,0:T(1,128)}, s32[1,1,512]{2,1,0:T(1,128)S(1)}, u32[]{:S(2)}) copy-start(s32[1,1,512]{2,1,0:T(1,128)S(1)} %get-tuple-element.21) | copy-start | bytes 6148
  2.9 16.5 %copy-start.4 = (s32[2,2048]{1,0:T(2,128)S(1)}, s32[2,2048]{1,0:T(2,128)}, u32[]{:S(2)}) copy-start(s32[2,2048]{1,0:T(2,128)} %param.19) | copy-start | bytes 49156
  4.0 27.5 %all-to-all-start.2 = ((bf16[128,4,768]{2,1,0:T(4,128)(2,1)}), bf16[128,4,768]{2,1,0:T(4,128)(2,1)S(1)}, u32[]{:S(2)}, u32[]{:S(2)}) async-start(bf16[128,4,768]{2,1,0:T(4,128)(2,1)} %reshape.149), calls=%async_computation.2 | async-start | bytes 1572864 | tf_op jit(solution)/shard_map/all_to_all | solution.py:47
  19.4 18.7 %copy-start.5 = (s32[1,2048]{1,0:T(1,128)}, s32[1,2048]{1,0:T(1,128)S(1)}, u32[]{:S(2)}) copy-start(s32[1,2048]{1,0:T(1,128)S(1)} %get-tuple-element.19) | copy-start | bytes 24580
  31.5 21.0 %all-to-all-start.1 = ((bf16[128,4,768]{2,1,0:T(4,128)(2,1)}), bf16[128,4,768]{2,1,0:T(4,128)(2,1)S(1)}, u32[]{:S(2)}, u32[]{:S(2)}) async-start(bf16[128,4,768]{2,1,0:T(4,128)(2,1)} %reshape.147), calls=%async_computation.1 | async-start | bytes 1572864 | tf_op jit(solution)/shard_map/all_to_all | solution.py:46
  38.4 27.7 %copy-start.1 = (bf16[512,768]{1,0:T(8,128)(2,1)}, bf16[512,768]{1,0:T(8,128)(2,1)S(1)}, u32[]{:S(2)}) copy-start(bf16[512,768]{1,0:T(8,128)(2,1)S(1)} %reshape.150) | copy-start | bytes 2359300
  52.5 21.7 %all-to-all-start = ((bf16[128,4,768]{2,1,0:T(4,128)(2,1)}), bf16[128,4,768]{2,1,0:T(4,128)(2,1)}, u32[]{:S(2)}, u32[]{:S(2)}) async-start(bf16[128,4,768]{2,1,0:T(4,128)(2,1)} %reshape.145), calls=%async_computation | async-start | bytes 1572864 | tf_op jit(solution)/shard_map/all_to_all | solution.py:48
  66.3 6.5 %copy-start.2 = (bf16[512,768]{1,0:T(8,128)(2,1)}, bf16[512,768]{1,0:T(8,128)(2,1)S(1)}, u32[]{:S(2)}) copy-start(bf16[512,768]{1,0:T(8,128)(2,1)S(1)} %reshape.148) | copy-start | bytes 2359300
  66.3 9.4 %copy-start.6 = (s32[1,2048]{1,0:T(1,128)S(1)}, s32[1,2048]{1,0:T(1,128)}, u32[]{:S(2)}) copy-start(s32[1,2048]{1,0:T(1,128)} %copy-done.5) | copy-start | bytes 24580
  66.3 9.4 %copy-start.15 = (f32[768]{0:T(1024)S(1)}, f32[768]{0:T(1024)}, u32[]{:S(2)}) copy-start(f32[768]{0:T(1024)} %param.16) | copy-start | bytes 9220
  86.7 3.8 %copy-start.3 = (bf16[512,768]{1,0:T(8,128)(2,1)S(1)}, bf16[512,768]{1,0:T(8,128)(2,1)}, u32[]{:S(2)}) copy-start(bf16[512,768]{1,0:T(8,128)(2,1)} %copy-done.2) | copy-start | bytes 2359300
  88.8 2.5 %copy-start.7 = (f32[768]{0:T(1024)S(1)}, f32[768]{0:T(1024)}, u32[]{:S(2)}) copy-start(f32[768]{0:T(1024)} %get-tuple-element.23) | copy-start | bytes 9220
  113.7 24.5 %all-to-all-start.3 = ((bf16[128,4,768]{2,1,0:T(4,128)(2,1)}), bf16[128,4,768]{2,1,0:T(4,128)(2,1)S(1)}, u32[]{:S(2)}, u32[]{:S(2)}) async-start(bf16[128,4,768]{2,1,0:T(4,128)(2,1)} %reshape.152), calls=%async_computation.3 | async-start | bytes 1572864 | tf_op jit(solution)/shard_map/all_to_all | solution.py:93
  138.2 21.6 %all-to-all-start.4 = ((bf16[128,4,768]{2,1,0:T(4,128)(2,1)}), bf16[128,4,768]{2,1,0:T(4,128)(2,1)}, u32[]{:S(2)}, u32[]{:S(2)}) async-start(bf16[128,4,768]{2,1,0:T(4,128)(2,1)} %reshape.154), calls=%async_computation.4 | async-start | bytes 1572864 | tf_op jit(solution)/shard_map/all_to_all | solution.py:94
  148.2 37.8 %copy-start.11 = (s32[1,1,512]{2,1,0:T(1,128)S(1)}, s32[1,1,512]{2,1,0:T(1,128)}, u32[]{:S(2)}) copy-start(s32[1,1,512]{2,1,0:T(1,128)} %copy-done.10) | copy-start | bytes 6148
  159.9 21.7 %all-to-all-start.6 = ((bf16[4,1,4,4,80,128]{5,4,2,0,1,3:T(8,128)(2,1)}), bf16[4,1,4,4,80,128]{5,4,2,0,1,3:T(8,128)(2,1)S(1)}, u32[]{:S(2)}, u32[]{:S(2)}) async-start(bf16[4,1,4,4,80,128]{5,4,2,0,1,3:T(8,128)(2,1)} %copy.19), calls=%async_computation.6 | async-start | bytes 2621440 | tf_op jit(solution)/shard_map/all_to_all | solution.py:138
  163.4 33.6 %copy-start.9 = (s32[1,1,512]{2,1,0:T(1,128)S(1)}, s32[1,1,512]{2,1,0:T(1,128)}, u32[]{:S(2)}) copy-start(s32[1,1,512]{2,1,0:T(1,128)} %copy-done.8) | copy-start | bytes 6148
  164.5 21.5 %copy-start.14 = (bf16[256,768]{1,0:T(8,128)(2,1)S(1)}, bf16[256,768]{1,0:T(8,128)(2,1)}, u32[]{:S(2)}) copy-start(bf16[256,768]{1,0:T(8,128)(2,1)} %param.13) | copy-start | bytes 1179652
  182.5 10.5 %all-to-all-start.7 = ((bf16[4,1,4,1,80,128]{5,4,0,3,1,2:T(8,128)(2,1)}), bf16[4,1,4,1,80,128]{5,4,0,3,1,2:T(8,128)(2,1)S(1)}, u32[]{:S(2)}, u32[]{:S(2)}) async-start(bf16[4,1,4,1,80,128]{5,4,0,3,1,2:T(8,128)(2,1)} %copy.20), calls=%async_computation.7 | async-start | bytes 655360 | tf_op jit(solution)/shard_map/all_to_all | solution.py:138
  193.7 9.0 %all-to-all-start.8 = ((bf16[4,1,1,1,80,128]{5,4,3,2,1,0:T(8,128)(2,1)}), bf16[4,1,1,1,80,128]{5,4,3,2,1,0:T(8,128)(2,1)S(1)}, u32[]{:S(2)}, u32[]{:S(2)}) async-start(bf16[4,1,1,1,80,128]{5,4,3,2,1,0:T(8,128)(2,1)} %bitcast.10), calls=%async_computation.8 | async-start | bytes 163840 | tf_op jit(solution)/shard_map/all_to_all | solution.py:138

commit v4 on v3

--- a/solution.py
+++ b/solution.py
@@ -33,20 +33,16 @@
     master_rows = constraint_features.shape[0]
     select_con = one_hot_table(send_rows[0, 0], master_rows)
     select_var = one_hot_table(send_rows[1, 0], master_rows)
-    out_con = pick_rows(select_con, constraint_features).reshape(
-        device_count, slot_cap, embedding_width
+    out_con = pick_rows(select_con, constraint_features)
+    out_var = pick_rows(select_var, variable_features)
+    out_cot = pick_rows(select_var, variable_cotangent)
+    outgoing = jnp.concatenate([out_con, out_var, out_cot], axis=1).reshape(
+        device_count, slot_cap, 3 * embedding_width
     )
-    out_var = pick_rows(select_var, variable_features).reshape(
-        device_count, slot_cap, embedding_width
-    )
-    out_cot = pick_rows(select_var, variable_cotangent).reshape(
-        device_count, slot_cap, embedding_width
-    )
-    constraint_mirror_rows, variable_mirror_rows, cotangent_mirror_rows = (
-        lax.all_to_all(out_con, DEVICE_AXES, split_axis=0, concat_axis=0, tiled=True),
-        lax.all_to_all(out_var, DEVICE_AXES, split_axis=0, concat_axis=0, tiled=True),
-        lax.all_to_all(out_cot, DEVICE_AXES, split_axis=0, concat_axis=0, tiled=True),
-    )
+    incoming = lax.all_to_all(outgoing, DEVICE_AXES, split_axis=0, concat_axis=0, tiled=True)
+    constraint_mirror_rows = incoming[:, :, :embedding_width]
+    variable_mirror_rows = incoming[:, :, embedding_width : 2 * embedding_width]
+    cotangent_mirror_rows = incoming[:, :, 2 * embedding_width :]
     constraint_mirror_rows = constraint_mirror_rows.reshape(replica_rows, embedding_width)
     variable_mirror_rows = variable_mirror_rows.reshape(replica_rows, embedding_width)
     cotangent_mirror_rows = cotangent_mirror_rows.reshape(replica_rows, embedding_width)
@@ -87,12 +83,12 @@
     back_var = jnp.dot(
         variable_projection_gradient, variable_weight.T, preferred_element_type=jnp.float32
     ).astype(jnp.bfloat16)
-    back_con = back_con.reshape(device_count, slot_cap, embedding_width)
-    back_var = back_var.reshape(device_count, slot_cap, embedding_width)
-    home_con, home_var = (
-        lax.all_to_all(back_con, DEVICE_AXES, split_axis=0, concat_axis=0, tiled=True),
-        lax.all_to_all(back_var, DEVICE_AXES, split_axis=0, concat_axis=0, tiled=True),
+    backward = jnp.concatenate([back_con, back_var], axis=1).reshape(
+        device_count, slot_cap, 2 * embedding_width
     )
+    homes = lax.all_to_all(backward, DEVICE_AXES, split_axis=0, concat_axis=0, tiled=True)
+    home_con = homes[:, :, :embedding_width]
+    home_var = homes[:, :, embedding_width:]
     grad_con = lax.dot_general(
         select_con,
         home_con.reshape(replica_rows, embedding_width),

time: 205 us -> 193 us (0.941)
  starting transfers between devices: 45.8 us -> 26.8 us
  local copies, waits for them, and re-layouts: 22 us -> 25 us
  matrix products: 44.1 us -> 46.7 us
  other arithmetic: 7.62 us -> 9.91 us
    all_to_all x5 -> x2, starting transfers between devices: 35.5 us -> 15.8 us  [the longest x1 11.2 us: on_device(): lax.all_to_all(outgoing, DEVICE_AXES, split_axis=0, concat_axis=0, tiled=...]
    slice x1 -> x3, local copies, waits for them, and re-layouts: 0.81 us -> 4.21 us  [the longest x1 1.97 us: on_device(): cotangent_mirror_rows = incoming[:, :, 2 * embedding_width:]]
    reshape x5 -> x2, local copies, waits for them, and re-layouts: 6.66 us -> 3.52 us  [the longest x1 2.15 us: on_device(): jnp.concatenate([out_con, out_var, out_cot], axis=1)]
    all_to_all x5 -> x2, waiting for transfers between devices: 52.2 us -> 49.6 us  [the longest x1 27.8 us: on_device(): lax.all_to_all(outgoing, DEVICE_AXES, split_axis=0, concat_axis=0, tiled=...]
  transfers between devices with their start and end apart: 8 -> 5, of which waited for: 8 -> 5; matrix products, arithmetic and copies ran while one was open for 18% -> 8% of each run, Pallas kernels for 0% -> 0%
where the time goes in v4:
time: 193 us; the launch traced here: 192 us
  waiting for transfers between devices  73.2 us (38%)
  matrix products  46.7 us (24%)
  starting transfers between devices  26.8 us (14%)
  local copies, waits for them, and re-layouts  25 us (13%)
  other arithmetic  9.91 us (5%)
  blocking collectives  9.07 us (5%)
    all_to_all x1, waiting for transfers between devices, on_device(): lax.all_to_all(outgoing, DEVICE_AXES, split_axis=0, concat_axis=0, tiled=...  27.8 us
    all_to_all x3, waiting for transfers between devices, on_device(): gathered = lax.all_to_all(sent, axis_name, position, position, tiled=True)  23.7 us
    all_to_all x1, waiting for transfers between devices, on_device(): lax.all_to_all(backward, DEVICE_AXES, split_axis=0, concat_axis=0, tiled=...  21.8 us
    all_to_all x1, starting transfers between devices, on_device(): lax.all_to_all(outgoing, DEVICE_AXES, split_axis=0, concat_axis=0, tiled=...  11.2 us
    all_to_all x3, starting transfers between devices, on_device(): gathered = lax.all_to_all(sent, axis_name, position, position, tiled=True)  11 us
    all_to_all x1, blocking collectives, on_device(): gathered = lax.all_to_all(sent, axis_name, position, position, tiled=True)  9.07 us
    dot_general x1, matrix products, on_device(): jnp.dot(edge_var, variable_weight, preferred_element_type=jnp.float32)  7.79 us
    dot_general x1, matrix products, on_device(): jnp.dot(table_var, cotangent_mirror_rows, preferred_element_type=jnp.floa...  7.53 us
  transfers between devices with their start and end apart: 5, of which 5 were waited for; matrix products, arithmetic and copies ran while one was open for 8% of the time, Pallas kernels for 0%

profile of v4, /device:TPU:0, one launch (start us, length us, event | category | flops | bytes accessed | tf_op | source)
XLA Modules:
  0.0 191.7 jit_solution(10822691241125828575)
XLA Ops:
  1.4 1.4 convolution_convert_fusion.3
  5.9 2.1 %reshape.136 = bf16[128,4,2304]{2,1,0:T(4,128)(2,1)} reshape(bf16[512,2304]{1,0:T(8,128)(2,1)S(1)} %pad_maximum_fusion.1) | data formatting | bytes 4718592 | tf_op jit(solution)/shard_map/reshape | solution.py:39
  8.0 11.2 %all-to-all-start = ((bf16[128,4,2304]{2,1,0:T(4,128)(2,1)}), bf16[128,4,2304]{2,1,0:T(4,128)(2,1)S(1)}, u32[]{:S(2)}, u32[]{:S(2)}) async-start(bf16[128,4,2304]{2,1,0:T(4,128)(2,1)} %reshape.136), calls=%async_computation | async-start | bytes 4718592 | tf_op jit(solution)/shard_map/all_to_all | solution.py:42
  23.9 27.8 %all-to-all-done = bf16[128,4,2304]{2,1,0:T(4,128)(2,1)S(1)} async-done(((bf16[128,4,2304]{2,1,0:T(4,128)(2,1)}), bf16[128,4,2304]{2,1,0:T(4,128)(2,1)S(1)}, u32[]{:S(2)}, u32[]{:S(2)}) %all-to-all-start) | async-done | bytes 2359328 | tf_op jit(solution)/shard_map/all_to_all | solution.py:42
  51.6 2.0 %fusion.81 = (bf16[128,4,768]{2,1,0:T(4,128)(2,1)}, bf16[128,4,768]{2,1,0:T(4,128)(2,1)}, bf16[128,4,768]{2,1,0:T(4,128)(2,1)}) fusion(bf16[128,4,2304]{2,1,0:T(4,128)(2,1)S(1)} %all-to-all-done), kind=kLoop, calls=%fused_computation.107 | loop fusion | bytes 4718592 | tf_op jit(solution)/shard_map/slice | solution.py:45
  53.6 2.3 %reshape.137 = bf16[512,768]{1,0:T(8,128)(2,1)} reshape(bf16[128,4,768]{2,1,0:T(4,128)(2,1)} %get-tuple-element.17) | data formatting | bytes 1572864 | tf_op jit(solution)/shard_map/reshape | solution.py:48
  55.9 1.6 reshape.139
  57.7 6.5 %fusion.31 = f32[2048,768]{1,0:T(8,128)} fusion(bf16[768,768]{1,0:T(8,128)(2,1)S(1)} %copy-done, bf16[512,768]{1,0:T(8,128)(2,1)S(1)} %reshape.138, s32[2048]{0:T(1024)S(1)} %bitcast.51), kind=kOutput, calls=%fused_computation.49 | convolution fusion | flops 4031250432 | bytes 8265728 | tf_op jit(solution)/shard_map/dot_general | solution.py:64
  64.2 7.8 %fusion.30 = f32[2048,768]{1,0:T(8,128)} fusion(bf16[768,768]{1,0:T(8,128)(2,1)} %param.15, bf16[512,768]{1,0:T(8,128)(2,1)S(1)} %reshape.139, s32[2048]{0:T(1024)} %bitcast.54), kind=kOutput, calls=%fused_computation.48 | convolution fusion | flops 4031250432 | bytes 8265728 | tf_op jit(solution)/shard_map/dot_general | solution.py:65
  72.0 7.5 %convert_reduce_fusion = (f32[768]{0:T(1024)S(1)}, bf16[2048,768]{1,0:T(8,128)(2,1)S(1)}) fusion(f32[2048]{0:T(1024)S(1)} %mul.41, f32[768]{0:T(1024)} %param.16, f32[2048,768]{1,0:T(8,128)} %fusion.31, f32[2048,768]{1,0:T(8,128)} %fusion.30, bf16[512,768]{1,0:T(8,128)(2,1)S(1)} %copy-done.4, s32[2048]{0:T(1024)} %bitcast.55), kind=kOutput, calls=%fused_computation | convolution fusion | flops 1635777792 | bytes 16537600 | tf_op jit(solution)/shard_map/dot_general | solution.py:60
  79.5 3.0 %fusion.28 = bf16[512,768]{1,0:T(8,128)(2,1)} fusion(bf16[2048,768]{1,0:T(8,128)(2,1)S(1)} %get-tuple-element.29, s32[2048]{0:T(1024)S(1)} %bitcast.56), kind=kOutput, calls=%fused_computation.40 | convolution fusion | flops 1614151680 | bytes 3940352 | tf_op jit(solution)/shard_map/dot_general | solution.py:77
  82.5 2.9 %fusion.27 = bf16[512,768]{1,0:T(8,128)(2,1)} fusion(bf16[2048,768]{1,0:T(8,128)(2,1)S(1)} %get-tuple-element.29, s32[2048]{0:T(1024)S(1)} %bitcast.52), kind=kOutput, calls=%fused_computation.39 | convolution fusion | flops 1614151680 | bytes 3940352 | tf_op jit(solution)/shard_map/dot_general | solution.py:74
  86.2 2.2 %fusion.85 = f32[768,768]{1,0:T(8,128)S(1)} fusion(bf16[512,768]{1,0:T(8,128)(2,1)} %copy-done.2, bf16[512,768]{1,0:T(8,128)(2,1)} %fusion.27), kind=kOutput, calls=%fused_computation.111 | convolution fusion | flops 603979776 | bytes 3932160 | tf_op jit(solution)/shard_map/dot_general | solution.py:105
  88.3 1.7 concatenate.20
  90.0 2.2 %fusion.86 = f32[768,768]{1,0:T(8,128)S(1)} fusion(bf16[512,768]{1,0:T(8,128)(2,1)} %copy-done.1, bf16[512,768]{1,0:T(8,128)(2,1)} %fusion.28), kind=kOutput, calls=%fused_computation.112 | convolution fusion | flops 603979776 | bytes 3932160 | tf_op jit(solution)/shard_map/dot_general | solution.py:111
  92.2 1.7 concatenate.21
  94.8 3.1 %pad_maximum_fusion = f32[4,2,4,4,80,128]{5,4,3,2,1,0:T(8,128)S(1)} fusion(f32[4,2,4,4,8,128]{5,4,3,2,1,0:T(8,128)S(1)} %bitcast.44, f32[4,2,4,4,36,128]{5,4,3,2,1,0:T(8,128)} %concatenate.21, f32[4,2,4,4,36,128]{5,4,3,2,1,0:T(8,128)} %concatenate.20), kind=kLoop, calls=%fused_computation.2 | loop fusion | flops 2621440 | bytes 10485760 | tf_op jit(solution)/shard_map/concatenate | solution.py:123
  98.5 9.1 %all_to_all.30 = f32[4,2,4,4,80,128]{5,4,3,2,0,1:T(8,128)} all-to-all(f32[4,2,4,4,80,128]{5,4,3,2,0,1:T(8,128)S(1)} %copy.18), channel_id=1, replica_groups=mesh['y'=4,'c'=2,'z'=4,'x'=4] {'c'}, dimensions={1} | all-to-all | bytes 10485760 | tf_op jit(solution)/shard_map/all_to_all | solution.py:134
  107.6 3.1 %reduce_sum.54 = bf16[4,4,4,80,128]{4,3,2,1,0:T(8,128)(2,1)S(1)} reduce(f32[4,2,4,4,80,128]{5,4,3,2,0,1:T(8,128)} %all_to_all.30, f32[]{:T(128)} %constant.50.clone.1), dimensions={1}, to_apply=%region_1.2 | reduce | flops 655360 | bytes 6553604 | tf_op jit(solution)/shard_map/reduce_sum | solution.py:135
  111.9 3.5 %all-to-all-start.3 = ((bf16[4,1,4,4,80,128]{5,4,2,0,1,3:T(8,128)(2,1)}), bf16[4,1,4,4,80,128]{5,4,2,0,1,3:T(8,128)(2,1)S(1)}, u32[]{:S(2)}, u32[]{:S(2)}) async-start(bf16[4,1,4,4,80,128]{5,4,2,0,1,3:T(8,128)(2,1)} %copy.19), calls=%async_computation.3 | async-start | bytes 2621440 | tf_op jit(solution)/shard_map/all_to_all | solution.py:134
  115.4 1.7 convolution_convert_fusion.2
  117.2 16.7 %all-to-all-done.3 = bf16[4,1,4,4,80,128]{5,4,2,0,1,3:T(8,128)(2,1)S(1)} async-done(((bf16[4,1,4,4,80,128]{5,4,2,0,1,3:T(8,128)(2,1)}), bf16[4,1,4,4,80,128]{5,4,2,0,1,3:T(8,128)(2,1)S(1)}, u32[]{:S(2)}, u32[]{:S(2)}) %all-to-all-start.3) | async-done | bytes 1310752 | tf_op jit(solution)/shard_map/all_to_all | solution.py:134
  134.8 3.6 %all-to-all-start.4 = ((bf16[4,1,4,1,80,128]{5,4,0,3,1,2:T(8,128)(2,1)}), bf16[4,1,4,1,80,128]{5,4,0,3,1,2:T(8,128)(2,1)S(1)}, u32[]{:S(2)}, u32[]{:S(2)}) async-start(bf16[4,1,4,1,80,128]{5,4,0,3,1,2:T(8,128)(2,1)} %copy.20), calls=%async_computation.4 | async-start | bytes 655360 | tf_op jit(solution)/shard_map/all_to_all | solution.py:134
  138.4 3.3 %convolution_convert_fusion.1 = bf16[512,768]{1,0:T(8,128)(2,1)} fusion(bf16[512,768]{1,0:T(8,128)(2,1)} %fusion.28, bf16[768,768]{1,0:T(8,128)(2,1)} %param.15), kind=kOutput, calls=%fused_computation.37 | convolution fusion | flops 604372992 | bytes 2752512 | tf_op jit(solution)/shard_map/dot_general | solution.py:83
  141.7 3.8 %all-to-all-done.4 = bf16[4,1,4,1,80,128]{5,4,0,3,1,2:T(8,128)(2,1)S(1)} async-done(((bf16[4,1,4,1,80,128]{5,4,0,3,1,2:T(8,128)(2,1)}), bf16[4,1,4,1,80,128]{5,4,0,3,1,2:T(8,128)(2,1)S(1)}, u32[]{:S(2)}, u32[]{:S(2)}) %all-to-all-start.4) | async-done | bytes 327712 | tf_op jit(solution)/shard_map/all_to_all | solution.py:134
  146.2 3.9 %all-to-all-start.5 = ((bf16[4,1,1,1,80,128]{5,4,3,2,1,0:T(8,128)(2,1)}), bf16[4,1,1,1,80,128]{5,4,3,2,1,0:T(8,128)(2,1)}, u32[]{:S(2)}, u32[]{:S(2)}) async-start(bf16[4,1,1,1,80,128]{5,4,3,2,1,0:T(8,128)(2,1)} %bitcast.10), calls=%async_computation.5 | async-start | bytes 163840 | tf_op jit(solution)/shard_map/all_to_all | solution.py:134
  152.7 3.1 %all-to-all-done.5 = bf16[4,1,1,1,80,128]{5,4,3,2,1,0:T(8,128)(2,1)} async-done(((bf16[4,1,1,1,80,128]{5,4,3,2,1,0:T(8,128)(2,1)}), bf16[4,1,1,1,80,128]{5,4,3,2,1,0:T(8,128)(2,1)}, u32[]{:S(2)}, u32[]{:S(2)}) %all-to-all-start.5) | async-done | bytes 81952 | tf_op jit(solution)/shard_map/all_to_all | solution.py:134
  155.9 4.6 %all-to-all-start.1 = ((bf16[128,4,1536]{2,1,0:T(4,128)(2,1)}), bf16[128,4,1536]{2,1,0:T(4,128)(2,1)S(1)}, u32[]{:S(2)}, u32[]{:S(2)}) async-start(bf16[128,4,1536]{2,1,0:T(4,128)(2,1)} %reshape.141), calls=%async_computation.1 | async-start | bytes 3145728 | tf_op jit(solution)/shard_map/all_to_all | solution.py:89
  163.2 21.8 %all-to-all-done.1 = bf16[128,4,1536]{2,1,0:T(4,128)(2,1)S(1)} async-done(((bf16[128,4,1536]{2,1,0:T(4,128)(2,1)}), bf16[128,4,1536]{2,1,0:T(4,128)(2,1)S(1)}, u32[]{:S(2)}, u32[]{:S(2)}) %all-to-all-start.1) | async-done | bytes 1572896 | tf_op jit(solution)/shard_map/all_to_all | solution.py:89
  185.0 1.4 fusion.82
  186.4 1.6 reshape.143
  188.0 2.2 %fusion.29 = bf16[256,768]{1,0:T(8,128)(2,1)} fusion(bf16[512,768]{1,0:T(8,128)(2,1)S(1)} %reshape.143, bf16[256,768]{1,0:T(8,128)(2,1)} %param.13, s32[512]{0:T(512)S(1)} %bitcast.61), kind=kOutput, calls=%fused_computation.46 | convolution fusion | flops 202309632 | bytes 1574912 | tf_op jit(solution)/shard_map/dot_general | solution.py:98
  (58 shorter events, 20.4 us)
Async XLA Ops:
  0.6 57.1 %copy-start = (bf16[768,768]{1,0:T(8,128)(2,1)S(1)}, bf16[768,768]{1,0:T(8,128)(2,1)}, u32[]{:S(2)}) copy-start(bf16[768,768]{1,0:T(8,128)(2,1)} %param.14) | copy-start | bytes 3538948
  1.4 2.8 %copy-start.9 = (s32[1,1,512]{2,1,0:T(1,128)}, s32[1,1,512]{2,1,0:T(1,128)S(1)}, u32[]{:S(2)}) copy-start(s32[1,1,512]{2,1,0:T(1,128)S(1)} %get-tuple-element.26) | copy-start | bytes 6148
  1.4 2.8 %copy-start.11 = (s32[1,1,512]{2,1,0:T(1,128)}, s32[1,1,512]{2,1,0:T(1,128)S(1)}, u32[]{:S(2)}) copy-start(s32[1,1,512]{2,1,0:T(1,128)S(1)} %get-tuple-element.27) | copy-start | bytes 6148
  8.0 11.2 %copy-start.13 = (s32[2,1,128]{2,1,0:T(1,128)S(1)}, s32[2,1,128]{2,1,0:T(1,128)}, u32[]{:S(2)}) copy-start(s32[2,1,128]{2,1,0:T(1,128)} %param.18) | copy-start | bytes 3076
  8.0 43.6 %all-to-all-start = ((bf16[128,4,2304]{2,1,0:T(4,128)(2,1)}), bf16[128,4,2304]{2,1,0:T(4,128)(2,1)S(1)}, u32[]{:S(2)}, u32[]{:S(2)}) async-start(bf16[128,4,2304]{2,1,0:T(4,128)(2,1)} %reshape.136), calls=%async_computation | async-start | bytes 4718592 | tf_op jit(solution)/shard_map/all_to_all | solution.py:42
  21.9 2.0 %copy-start.7 = (s32[1,2048]{1,0:T(1,128)}, s32[1,2048]{1,0:T(1,128)S(1)}, u32[]{:S(2)}) copy-start(s32[1,2048]{1,0:T(1,128)S(1)} %get-tuple-element.24) | copy-start | bytes 24580
  53.6 3.9 %copy-start.3 = (bf16[128,4,768]{2,1,0:T(4,128)(2,1)S(1)}, bf16[128,4,768]{2,1,0:T(4,128)(2,1)}, u32[]{:S(2)}) copy-start(bf16[128,4,768]{2,1,0:T(4,128)(2,1)} %get-tuple-element.19) | copy-start | bytes 2359300
  57.5 6.7 %copy-start.1 = (bf16[512,768]{1,0:T(8,128)(2,1)}, bf16[512,768]{1,0:T(8,128)(2,1)S(1)}, u32[]{:S(2)}) copy-start(bf16[512,768]{1,0:T(8,128)(2,1)S(1)} %reshape.139) | copy-start | bytes 2359300
  57.7 6.5 %copy-start.2 = (bf16[512,768]{1,0:T(8,128)(2,1)}, bf16[512,768]{1,0:T(8,128)(2,1)S(1)}, u32[]{:S(2)}) copy-start(bf16[512,768]{1,0:T(8,128)(2,1)S(1)} %reshape.138) | copy-start | bytes 2359300
  64.2 7.8 %copy-start.4 = (bf16[512,768]{1,0:T(8,128)(2,1)S(1)}, bf16[512,768]{1,0:T(8,128)(2,1)}, u32[]{:S(2)}) copy-start(bf16[512,768]{1,0:T(8,128)(2,1)} %reshape.137) | copy-start | bytes 2359300
  72.0 7.5 %copy-start.8 = (s32[1,2048]{1,0:T(1,128)S(1)}, s32[1,2048]{1,0:T(1,128)}, u32[]{:S(2)}) copy-start(s32[1,2048]{1,0:T(1,128)} %copy-done.7) | copy-start | bytes 24580
  110.7 4.8 %copy-start.6 = (bf16[512,768]{1,0:T(8,128)(2,1)S(1)}, bf16[512,768]{1,0:T(8,128)(2,1)}, u32[]{:S(2)}) copy-start(bf16[512,768]{1,0:T(8,128)(2,1)} %fusion.27) | copy-start | bytes 2359300
  111.9 22.0 %all-to-all-start.3 = ((bf16[4,1,4,4,80,128]{5,4,2,0,1,3:T(8,128)(2,1)}), bf16[4,1,4,4,80,128]{5,4,2,0,1,3:T(8,128)(2,1)S(1)}, u32[]{:S(2)}, u32[]{:S(2)}) async-start(bf16[4,1,4,4,80,128]{5,4,2,0,1,3:T(8,128)(2,1)} %copy.19), calls=%async_computation.3 | async-start | bytes 2621440 | tf_op jit(solution)/shard_map/all_to_all | solution.py:134
  134.8 15.3 %copy-start.5 = (bf16[512,768]{1,0:T(8,128)(2,1)S(1)}, bf16[512,768]{1,0:T(8,128)(2,1)}, u32[]{:S(2)}) copy-start(bf16[512,768]{1,0:T(8,128)(2,1)} %convolution_convert_fusion.2) | copy-start | bytes 2359300
  134.8 10.7 %all-to-all-start.4 = ((bf16[4,1,4,1,80,128]{5,4,0,3,1,2:T(8,128)(2,1)}), bf16[4,1,4,1,80,128]{5,4,0,3,1,2:T(8,128)(2,1)S(1)}, u32[]{:S(2)}, u32[]{:S(2)}) async-start(bf16[4,1,4,1,80,128]{5,4,0,3,1,2:T(8,128)(2,1)} %copy.20), calls=%async_computation.4 | async-start | bytes 655360 | tf_op jit(solution)/shard_map/all_to_all | solution.py:134
  146.2 9.7 %all-to-all-start.5 = ((bf16[4,1,1,1,80,128]{5,4,3,2,1,0:T(8,128)(2,1)}), bf16[4,1,1,1,80,128]{5,4,3,2,1,0:T(8,128)(2,1)}, u32[]{:S(2)}, u32[]{:S(2)}) async-start(bf16[4,1,1,1,80,128]{5,4,3,2,1,0:T(8,128)(2,1)} %bitcast.10), calls=%async_computation.5 | async-start | bytes 163840 | tf_op jit(solution)/shard_map/all_to_all | solution.py:134
  155.9 29.1 %all-to-all-start.1 = ((bf16[128,4,1536]{2,1,0:T(4,128)(2,1)}), bf16[128,4,1536]{2,1,0:T(4,128)(2,1)S(1)}, u32[]{:S(2)}, u32[]{:S(2)}) async-start(bf16[128,4,1536]{2,1,0:T(4,128)(2,1)} %reshape.141), calls=%async_computation.1 | async-start | bytes 3145728 | tf_op jit(solution)/shard_map/all_to_all | solution.py:89
  160.5 27.5 %copy-start.12 = (s32[1,1,512]{2,1,0:T(1,128)S(1)}, s32[1,1,512]{2,1,0:T(1,128)}, u32[]{:S(2)}) copy-start(s32[1,1,512]{2,1,0:T(1,128)} %copy-done.11) | copy-start | bytes 6148
  186.4 4.0 %copy-start.10 = (s32[1,1,512]{2,1,0:T(1,128)S(1)}, s32[1,1,512]{2,1,0:T(1,128)}, u32[]{:S(2)}) copy-start(s32[1,1,512]{2,1,0:T(1,128)} %copy-done.9) | copy-start | bytes 6148

commit v5 on v4

--- a/solution.py
+++ b/solution.py
@@ -36,16 +36,6 @@
     out_con = pick_rows(select_con, constraint_features)
     out_var = pick_rows(select_var, variable_features)
     out_cot = pick_rows(select_var, variable_cotangent)
-    outgoing = jnp.concatenate([out_con, out_var, out_cot], axis=1).reshape(
-        device_count, slot_cap, 3 * embedding_width
-    )
-    incoming = lax.all_to_all(outgoing, DEVICE_AXES, split_axis=0, concat_axis=0, tiled=True)
-    constraint_mirror_rows = incoming[:, :, :embedding_width]
-    variable_mirror_rows = incoming[:, :, embedding_width : 2 * embedding_width]
-    cotangent_mirror_rows = incoming[:, :, 2 * embedding_width :]
-    constraint_mirror_rows = constraint_mirror_rows.reshape(replica_rows, embedding_width)
-    variable_mirror_rows = variable_mirror_rows.reshape(replica_rows, embedding_width)
-    cotangent_mirror_rows = cotangent_mirror_rows.reshape(replica_rows, embedding_width)
     slot_pos = lax.broadcasted_iota(jnp.int32, (2, replica_rows), 1) % slot_cap
     slot_live = jnp.where(
         slot_pos < jnp.repeat(recv_count[:, 0], slot_cap, axis=1), 1.0, 0.0
@@ -55,16 +45,32 @@
     live_con = jnp.dot(table_con, slot_live[0], preferred_element_type=jnp.float32)
     live_var = jnp.dot(table_var, slot_live[1], preferred_element_type=jnp.float32)
     edge_active_mask = live_con * live_var
-    edge_con = pick_rows(table_con, constraint_mirror_rows)
-    edge_var = pick_rows(table_var, variable_mirror_rows)
-    upstream_gradient = jnp.dot(
-        table_var, cotangent_mirror_rows, preferred_element_type=jnp.float32
-    )
-    pre_act = (
-        jnp.dot(edge_con, constraint_weight, preferred_element_type=jnp.float32)
-        + jnp.dot(edge_var, variable_weight, preferred_element_type=jnp.float32)
-        + bias[None, :]
-    )
+    half = embedding_width // 2
+    mirrors = []
+    pre_act = bias[None, :]
+    upstream_parts = []
+    for lo in (0, half):
+        cols = slice(lo, lo + half)
+        outgoing = jnp.concatenate(
+            [out_con[:, cols], out_var[:, cols], out_cot[:, cols]], axis=1
+        ).reshape(device_count, slot_cap, 3 * half)
+        incoming = lax.all_to_all(outgoing, DEVICE_AXES, split_axis=0, concat_axis=0, tiled=True)
+        incoming = incoming.reshape(replica_rows, 3 * half)
+        con_part = incoming[:, :half]
+        var_part = incoming[:, half : 2 * half]
+        cot_part = incoming[:, 2 * half :]
+        mirrors.append((con_part, var_part))
+        edge_con = pick_rows(table_con, con_part)
+        edge_var = pick_rows(table_var, var_part)
+        upstream_parts.append(
+            jnp.dot(table_var, cot_part, preferred_element_type=jnp.float32)
+        )
+        pre_act = (
+            pre_act
+            + jnp.dot(edge_con, constraint_weight[cols], preferred_element_type=jnp.float32)
+            + jnp.dot(edge_var, variable_weight[cols], preferred_element_type=jnp.float32)
+        )
+    upstream_gradient = jnp.concatenate(upstream_parts, axis=1)
     sigmoid_pre = jax.nn.sigmoid(pre_act)
     message_derivative = sigmoid_pre * (1.0 + pre_act * (1.0 - sigmoid_pre))
     edge_delta = (upstream_gradient * message_derivative * edge_active_mask[:, None]).astype(
@@ -102,17 +108,25 @@
         preferred_element_type=jnp.float32,
     )
     grad_var = variable_cotangent.astype(jnp.float32) + grad_var
-    constraint_term = lax.dot_general(
-        constraint_mirror_rows,
-        constraint_projection_gradient,
-        sum_dims,
-        preferred_element_type=jnp.float32,
+    constraint_term = jnp.concatenate(
+        [
+            lax.dot_general(
+                con_part, constraint_projection_gradient, sum_dims,
+                preferred_element_type=jnp.float32,
+            )
+            for con_part, _ in mirrors
+        ],
+        axis=0,
     )
-    variable_term = lax.dot_general(
-        variable_mirror_rows,
-        variable_projection_gradient,
-        sum_dims,
-        preferred_element_type=jnp.float32,
+    variable_term = jnp.concatenate(
+        [
+            lax.dot_general(
+                var_part, variable_projection_gradient, sum_dims,
+                preferred_element_type=jnp.float32,
+            )
+            for _, var_part in mirrors
+        ],
+        axis=0,
     )
     term_bias = jnp.sum(edge_delta.astype(jnp.float32), axis=0)
     factor = float(device_count * edge_slots.shape[1]) ** (-0.5)

time: 193 us -> 213 us (1.10)
  matrix products: 46.7 us -> 60.9 us
  local copies, waits for them, and re-layouts: 25 us -> 18.3 us
  waiting for transfers between devices: 73.2 us -> 78.3 us
  starting transfers between devices: 26.8 us -> 30.9 us
  other arithmetic: 9.91 us -> 13.1 us
    dot_general x5 -> x10, matrix products: 26.1 us -> 41.6 us  [the longest x2 18.4 us: on_device(): jnp.dot(edge_var, variable_weight[cols], preferred_element_type=jnp.float32)]
    concatenate x1 -> x4, other arithmetic: 0.15 us -> 5 us  [the longest x1 3.21 us: on_device(): jnp.concatenate([lax.dot_general(con_part, constraint_projection_gradient...]
    all_to_all x1 -> x2, starting transfers between devices: 11.2 us -> 16 us  [on_device(): lax.all_to_all(outgoing, DEVICE_AXES, split_axis=0, concat_axis=0, tiled=...]
    all_to_all x1 -> x2, waiting for transfers between devices: 27.8 us -> 32.1 us  [on_device(): lax.all_to_all(outgoing, DEVICE_AXES, split_axis=0, concat_axis=0, tiled=...]
    slice x2 -> x3, local copies, waits for them, and re-layouts: 2.79 us -> 0.26 us  [the longest x1 0.16 us: on_device(): out_con[:, cols]]
    concatenate x3, local copies, waits for them, and re-layouts: 3.99 us -> 6.41 us  [on_device(): jnp.concatenate([constraint_term.reshape(device_count, -1, lanes), variab...]
    reshape x4, local copies, waits for them, and re-layouts: 6.22 us -> 3.9 us  [the longest x2 2.41 us: on_device(): outgoing = jnp.concatenate([out_con[:, cols], out_var[:, cols], out_cot[:...]
  transfers between devices with their start and end apart: 5 -> 6, of which waited for: 5 -> 6; matrix products, arithmetic and copies ran while one was open for 8% -> 8% of each run, Pallas kernels for 0% -> 0%
where the time goes in v5:
time: 213 us; the launch traced here: 212 us
  waiting for transfers between devices  78.3 us (37%)
  matrix products  60.9 us (29%)
  starting transfers between devices  30.9 us (15%)
  local copies, waits for them, and re-layouts  18.3 us (9%)
  other arithmetic  13.1 us (6%)
  blocking collectives  9.07 us (4%)
    all_to_all x2, waiting for transfers between devices, on_device(): lax.all_to_all(outgoing, DEVICE_AXES, split_axis=0, concat_axis=0, tiled=...  32.1 us
    all_to_all x3, waiting for transfers between devices, on_device(): gathered = lax.all_to_all(sent, axis_name, position, position, tiled=True)  23.5 us
    all_to_all x1, waiting for transfers between devices, on_device(): lax.all_to_all(backward, DEVICE_AXES, split_axis=0, concat_axis=0, tiled=...  22.7 us
    dot_general x2, matrix products, on_device(): jnp.dot(edge_var, variable_weight[cols], preferred_element_type=jnp.float32)  18.4 us
    all_to_all x2, starting transfers between devices, on_device(): lax.all_to_all(outgoing, DEVICE_AXES, split_axis=0, concat_axis=0, tiled=...  16 us
    dot_general x2, matrix products, on_device(): jnp.dot(edge_con, constraint_weight[cols], preferred_element_type=jnp.flo...  11.8 us
    all_to_all x3, starting transfers between devices, on_device(): gathered = lax.all_to_all(sent, axis_name, position, position, tiled=True)  10.3 us
    all_to_all x1, blocking collectives, on_device(): gathered = lax.all_to_all(sent, axis_name, position, position, tiled=True)  9.07 us
  transfers between devices with their start and end apart: 6, of which 6 were waited for; matrix products, arithmetic and copies ran while one was open for 8% of the time, Pallas kernels for 0%

profile of v5, /device:TPU:0, one launch (start us, length us, event | category | flops | bytes accessed | tf_op | source)
XLA Modules:
  0.0 211.6 jit_solution(16500284743390076187)
XLA Ops:
  5.3 11.2 %all-to-all-start.1 = ((bf16[128,4,1152]{2,1,0:T(4,128)(2,1)}), bf16[128,4,1152]{2,1,0:T(4,128)(2,1)S(1)}, u32[]{:S(2)}, u32[]{:S(2)}) async-start(bf16[128,4,1152]{2,1,0:T(4,128)(2,1)} %reshape.138), calls=%async_computation.1 | async-start | bytes 2359296 | tf_op jit(solution)/shard_map/all_to_all | solution.py:57
  18.1 18.8 %all-to-all-done.1 = bf16[128,4,1152]{2,1,0:T(4,128)(2,1)S(1)} async-done(((bf16[128,4,1152]{2,1,0:T(4,128)(2,1)}), bf16[128,4,1152]{2,1,0:T(4,128)(2,1)S(1)}, u32[]{:S(2)}, u32[]{:S(2)}) %all-to-all-start.1) | async-done | bytes 1179680 | tf_op jit(solution)/shard_map/all_to_all | solution.py:57
  36.9 4.8 %all-to-all-start = ((bf16[128,4,1152]{2,1,0:T(4,128)(2,1)}), bf16[128,4,1152]{2,1,0:T(4,128)(2,1)S(1)}, u32[]{:S(2)}, u32[]{:S(2)}) async-start(bf16[128,4,1152]{2,1,0:T(4,128)(2,1)} %reshape.136), calls=%async_computation | async-start | bytes 2359296 | tf_op jit(solution)/shard_map/all_to_all | solution.py:57
  44.9 3.7 %fusion.6 = f32[2048,384]{0,1:T(8,128)} fusion(s32[2048]{0:T(1024)S(1)} %bitcast.50, bf16[512,1152]{1,0:T(8,128)(2,1)} %reshape.139), kind=kOutput, calls=%fused_computation.13 | convolution fusion | flops 808452096 | bytes 3547136 | tf_op jit(solution)/shard_map/dot_general | solution.py:66
  48.6 13.3 %all-to-all-done = bf16[128,4,1152]{2,1,0:T(4,128)(2,1)S(1)} async-done(((bf16[128,4,1152]{2,1,0:T(4,128)(2,1)}), bf16[128,4,1152]{2,1,0:T(4,128)(2,1)S(1)}, u32[]{:S(2)}, u32[]{:S(2)}) %all-to-all-start) | async-done | bytes 1179680 | tf_op jit(solution)/shard_map/all_to_all | solution.py:57
  62.2 2.7 %fusion.7 = f32[2048,384]{0,1:T(8,128)} fusion(s32[2048]{0:T(1024)S(1)} %bitcast.51, bf16[512,1152]{1,0:T(8,128)(2,1)S(1)} %reshape.137), kind=kOutput, calls=%fused_computation.14 | convolution fusion | flops 808452096 | bytes 3547136 | tf_op jit(solution)/shard_map/dot_general | solution.py:66
  64.9 5.9 %fusion.47 = f32[2048,768]{0,1:T(8,128)} fusion(s32[2048]{0:T(1024)S(1)} %bitcast.46, bf16[768,768]{1,0:T(8,128)(2,1)} %param.14, bf16[512,1152]{1,0:T(8,128)(2,1)S(1)} %copy-done.2), kind=kOutput, calls=%fused_computation.57 | convolution fusion | flops 2017198080 | bytes 7282688 | tf_op jit(solution)/shard_map/dot_general | solution.py:70
  70.8 5.9 %fusion.48 = f32[2048,768]{0,1:T(8,128)} fusion(s32[2048]{0:T(1024)S(1)} %bitcast.47, bf16[768,768]{1,0:T(8,128)(2,1)} %param.14, bf16[512,1152]{1,0:T(8,128)(2,1)S(1)} %reshape.137), kind=kOutput, calls=%fused_computation.58 | convolution fusion | flops 2017198080 | bytes 7282688 | tf_op jit(solution)/shard_map/dot_general | solution.py:70
  76.7 6.0 %fusion.46 = f32[2048,768]{0,1:T(8,128)} fusion(s32[2048]{0:T(1024)S(1)} %bitcast.52, bf16[768,768]{1,0:T(8,128)(2,1)} %param.15, bf16[512,1152]{1,0:T(8,128)(2,1)S(1)} %reshape.137), kind=kOutput, calls=%fused_computation.56 | convolution fusion | flops 2017198080 | bytes 7282688 | tf_op jit(solution)/shard_map/dot_general | solution.py:71
  82.7 12.4 %convert_reduce_fusion = (f32[768]{0:T(1024)S(1)}, bf16[2048,768]{0,1:T(8,128)(2,1)}) fusion(f32[2048]{0:T(1024)S(1)} %mul.41, bf16[768,768]{1,0:T(8,128)(2,1)} %param.15, s32[2048]{0:T(1024)S(1)} %bitcast.53, bf16[512,1152]{1,0:T(8,128)(2,1)S(1)} %copy-done.2, f32[2048,768]{0,1:T(8,128)} %fusion.47, f32[2048,768]{0,1:T(8,128)} %fusion.46, ...), kind=kOutput, calls=%fused_computation.3 | convolution fusion | flops 2043936000 | bytes 29318144 | tf_op jit(solution)/shard_map/dot_general | solution.py:71
  95.0 4.3 %fusion.50 = bf16[512,768]{1,0:T(8,128)(2,1)S(1)} fusion(bf16[2048,768]{0,1:T(8,128)(2,1)} %get-tuple-element.32, s32[2048]{0:T(1024)S(1)} %bitcast.54), kind=kOutput, calls=%fused_computation.62 | convolution fusion | flops 1614151680 | bytes 3940352 | tf_op jit(solution)/shard_map/dot_general | solution.py:83
  99.4 2.3 %fusion.49 = bf16[512,768]{1,0:T(8,128)(2,1)S(1)} fusion(bf16[2048,768]{0,1:T(8,128)(2,1)S(1)} %copy-done.13, s32[2048]{0:T(1024)S(1)} %bitcast.48), kind=kOutput, calls=%fused_computation.61 | convolution fusion | flops 1614151680 | bytes 3940352 | tf_op jit(solution)/shard_map/dot_general | solution.py:80
  103.7 2.5 %fusion.62 = f32[384,768]{1,0:T(8,128)} fusion(bf16[512,768]{1,0:T(8,128)(2,1)S(1)} %fusion.49, bf16[512,1152]{1,0:T(8,128)(2,1)} %reshape.139), kind=kOutput, calls=%fused_computation.85 | convolution fusion | flops 301989888 | bytes 2359296 | tf_op jit(solution)/shard_map/dot_general | solution.py:113
  106.2 1.5 fusion.70
  107.9 1.6 pad_maximum_fusion.2
  109.5 2.5 %concatenate.37 = f32[4,2,4,4,36,128]{5,4,3,2,1,0:T(8,128)S(1)} reshape(f32[768,768]{1,0:T(8,128)} %pad_maximum_fusion.2) | data formatting | bytes 4718592 | tf_op jit(solution)/shard_map/concatenate | solution.py:137
  111.9 3.2 %pad_maximum_fusion.1 = f32[768,768]{1,0:T(8,128)} fusion(f32[384,768]{1,0:T(8,128)} %fusion.62, f32[384,768]{1,0:T(8,128)} %fusion.70), kind=kLoop, calls=%fused_computation.23 | loop fusion | flops 589824 | bytes 4718592 | tf_op jit(solution)/shard_map/concatenate | solution.py:111
  115.2 3.4 %concatenate.35 = f32[4,2,4,4,36,128]{5,4,3,2,1,0:T(8,128)} reshape(f32[768,768]{1,0:T(8,128)} %pad_maximum_fusion.1) | data formatting | bytes 4718592 | tf_op jit(solution)/shard_map/concatenate | solution.py:137
  118.6 2.4 %pad_maximum_fusion = f32[4,2,4,4,80,128]{5,4,3,2,1,0:T(8,128)S(1)} fusion(f32[4,2,4,4,8,128]{5,4,3,2,1,0:T(8,128)S(1)} %bitcast.39, f32[4,2,4,4,36,128]{5,4,3,2,1,0:T(8,128)S(1)} %concatenate.37, f32[4,2,4,4,36,128]{5,4,3,2,1,0:T(8,128)} %concatenate.35), kind=kLoop, calls=%fused_computation.4 | loop fusion | flops 2621440 | bytes 10485760 | tf_op jit(solution)/shard_map/concatenate | solution.py:137
  121.6 9.1 %all_to_all.35 = f32[4,2,4,4,80,128]{5,4,3,2,0,1:T(8,128)} all-to-all(f32[4,2,4,4,80,128]{5,4,3,2,0,1:T(8,128)S(1)} %copy.34), channel_id=1, replica_groups=mesh['y'=4,'c'=2,'z'=4,'x'=4] {'c'}, dimensions={1} | all-to-all | bytes 10485760 | tf_op jit(solution)/shard_map/all_to_all | solution.py:148
  130.6 3.1 %reduce_sum.54 = bf16[4,4,4,80,128]{4,3,2,1,0:T(8,128)(2,1)S(1)} reduce(f32[4,2,4,4,80,128]{5,4,3,2,0,1:T(8,128)} %all_to_all.35, f32[]{:T(128)} %constant.50.clone.1), dimensions={1}, to_apply=%region_1.2 | reduce | flops 655360 | bytes 6553604 | tf_op jit(solution)/shard_map/reduce_sum | solution.py:149
  134.9 3.5 %all-to-all-start.4 = ((bf16[4,1,4,4,80,128]{5,4,2,0,1,3:T(8,128)(2,1)}), bf16[4,1,4,4,80,128]{5,4,2,0,1,3:T(8,128)(2,1)S(1)}, u32[]{:S(2)}, u32[]{:S(2)}) async-start(bf16[4,1,4,4,80,128]{5,4,2,0,1,3:T(8,128)(2,1)} %copy.35), calls=%async_computation.4 | async-start | bytes 2621440 | tf_op jit(solution)/shard_map/all_to_all | solution.py:148
  138.5 2.1 convolution_convert_fusion.1
  140.6 16.3 %all-to-all-done.4 = bf16[4,1,4,4,80,128]{5,4,2,0,1,3:T(8,128)(2,1)S(1)} async-done(((bf16[4,1,4,4,80,128]{5,4,2,0,1,3:T(8,128)(2,1)}), bf16[4,1,4,4,80,128]{5,4,2,0,1,3:T(8,128)(2,1)S(1)}, u32[]{:S(2)}, u32[]{:S(2)}) %all-to-all-start.4) | async-done | bytes 1310752 | tf_op jit(solution)/shard_map/all_to_all | solution.py:148
  157.9 3.5 %all-to-all-start.5 = ((bf16[4,1,4,1,80,128]{5,4,0,3,1,2:T(8,128)(2,1)}), bf16[4,1,4,1,80,128]{5,4,0,3,1,2:T(8,128)(2,1)S(1)}, u32[]{:S(2)}, u32[]{:S(2)}) async-start(bf16[4,1,4,1,80,128]{5,4,0,3,1,2:T(8,128)(2,1)} %copy.36), calls=%async_computation.5 | async-start | bytes 655360 | tf_op jit(solution)/shard_map/all_to_all | solution.py:148
  161.4 3.0 %convolution_convert_fusion = bf16[512,768]{1,0:T(8,128)(2,1)} fusion(bf16[512,768]{1,0:T(8,128)(2,1)S(1)} %copy-done.6, bf16[768,768]{1,0:T(8,128)(2,1)} %param.15), kind=kOutput, calls=%fused_computation.59 | convolution fusion | flops 604372992 | bytes 2752512 | tf_op jit(solution)/shard_map/dot_general | solution.py:89
  164.3 4.1 %all-to-all-done.5 = bf16[4,1,4,1,80,128]{5,4,0,3,1,2:T(8,128)(2,1)S(1)} async-done(((bf16[4,1,4,1,80,128]{5,4,0,3,1,2:T(8,128)(2,1)}), bf16[4,1,4,1,80,128]{5,4,0,3,1,2:T(8,128)(2,1)S(1)}, u32[]{:S(2)}, u32[]{:S(2)}) %all-to-all-start.5) | async-done | bytes 327712 | tf_op jit(solution)/shard_map/all_to_all | solution.py:148
  169.1 3.3 %all-to-all-start.6 = ((bf16[4,1,1,1,80,128]{5,4,3,2,1,0:T(8,128)(2,1)}), bf16[4,1,1,1,80,128]{5,4,3,2,1,0:T(8,128)(2,1)S(1)}, u32[]{:S(2)}, u32[]{:S(2)}) async-start(bf16[4,1,1,1,80,128]{5,4,3,2,1,0:T(8,128)(2,1)} %bitcast.10), calls=%async_computation.6 | async-start | bytes 163840 | tf_op jit(solution)/shard_map/all_to_all | solution.py:148
  175.0 3.0 %all-to-all-done.6 = bf16[4,1,1,1,80,128]{5,4,3,2,1,0:T(8,128)(2,1)S(1)} async-done(((bf16[4,1,1,1,80,128]{5,4,3,2,1,0:T(8,128)(2,1)}), bf16[4,1,1,1,80,128]{5,4,3,2,1,0:T(8,128)(2,1)S(1)}, u32[]{:S(2)}, u32[]{:S(2)}) %all-to-all-start.6) | async-done | bytes 81952 | tf_op jit(solution)/shard_map/all_to_all | solution.py:148
  178.1 4.6 %all-to-all-start.2 = ((bf16[128,4,1536]{2,1,0:T(4,128)(2,1)}), bf16[128,4,1536]{2,1,0:T(4,128)(2,1)S(1)}, u32[]{:S(2)}, u32[]{:S(2)}) async-start(bf16[128,4,1536]{2,1,0:T(4,128)(2,1)} %reshape.141), calls=%async_computation.2 | async-start | bytes 3145728 | tf_op jit(solution)/shard_map/all_to_all | solution.py:95
  184.5 22.7 %all-to-all-done.2 = bf16[128,4,1536]{2,1,0:T(4,128)(2,1)S(1)} async-done(((bf16[128,4,1536]{2,1,0:T(4,128)(2,1)}), bf16[128,4,1536]{2,1,0:T(4,128)(2,1)S(1)}, u32[]{:S(2)}, u32[]{:S(2)}) %all-to-all-start.2) | async-done | bytes 1572896 | tf_op jit(solution)/shard_map/all_to_all | solution.py:95
  207.9 2.2 %fusion.51 = bf16[256,768]{1,0:T(8,128)(2,1)} fusion(bf16[512,768]{1,0:T(8,128)(2,1)S(1)} %reshape.143, bf16[256,768]{1,0:T(8,128)(2,1)} %param.13, s32[512]{0:T(512)S(1)} %bitcast.59), kind=kOutput, calls=%fused_computation.68 | convolution fusion | flops 202309632 | bytes 1574912 | tf_op jit(solution)/shard_map/dot_general | solution.py:104
  (69 shorter events, 21.8 us)
Async XLA Ops:
  0.6 2.3 %copy-start = (bf16[256,768]{1,0:T(8,128)(2,1)S(1)}, bf16[256,768]{1,0:T(8,128)(2,1)}, u32[]{:S(2)}) copy-start(bf16[256,768]{1,0:T(8,128)(2,1)} %param.12) | copy-start | bytes 1179652
  0.6 2.7 %copy-start.11 = (bf16[256,768]{1,0:T(8,128)(2,1)S(1)}, bf16[256,768]{1,0:T(8,128)(2,1)}, u32[]{:S(2)}) copy-start(bf16[256,768]{1,0:T(8,128)(2,1)} %param.11) | copy-start | bytes 1179652
  4.1 12.4 %copy-start.10 = (s32[2,1,128]{2,1,0:T(1,128)S(1)}, s32[2,1,128]{2,1,0:T(1,128)}, u32[]{:S(2)}) copy-start(s32[2,1,128]{2,1,0:T(1,128)} %param.18) | copy-start | bytes 3076
  5.3 31.6 %all-to-all-start.1 = ((bf16[128,4,1152]{2,1,0:T(4,128)(2,1)}), bf16[128,4,1152]{2,1,0:T(4,128)(2,1)S(1)}, u32[]{:S(2)}, u32[]{:S(2)}) async-start(bf16[128,4,1152]{2,1,0:T(4,128)(2,1)} %reshape.138), calls=%async_computation.1 | async-start | bytes 2359296 | tf_op jit(solution)/shard_map/all_to_all | solution.py:57
  16.8 24.9 %copy-start.9 = (s32[2,2048]{1,0:T(2,128)S(1)}, s32[2,2048]{1,0:T(2,128)}, u32[]{:S(2)}) copy-start(s32[2,2048]{1,0:T(2,128)} %param.19) | copy-start | bytes 49156
  36.9 25.0 %all-to-all-start = ((bf16[128,4,1152]{2,1,0:T(4,128)(2,1)}), bf16[128,4,1152]{2,1,0:T(4,128)(2,1)S(1)}, u32[]{:S(2)}, u32[]{:S(2)}) async-start(bf16[128,4,1152]{2,1,0:T(4,128)(2,1)} %reshape.136), calls=%async_computation | async-start | bytes 2359296 | tf_op jit(solution)/shard_map/all_to_all | solution.py:57
  62.2 14.5 %copy-start.3 = (bf16[512,1152]{1,0:T(8,128)(2,1)}, bf16[512,1152]{1,0:T(8,128)(2,1)S(1)}, u32[]{:S(2)}) copy-start(bf16[512,1152]{1,0:T(8,128)(2,1)S(1)} %reshape.137) | copy-start | bytes 3538948
  62.2 2.7 %copy-start.2 = (bf16[512,1152]{1,0:T(8,128)(2,1)S(1)}, bf16[512,1152]{1,0:T(8,128)(2,1)}, u32[]{:S(2)}) copy-start(bf16[512,1152]{1,0:T(8,128)(2,1)} %reshape.139) | copy-start | bytes 3538948
  76.7 6.0 %copy-start.12 = (f32[768]{0:T(1024)S(1)}, f32[768]{0:T(1024)}, u32[]{:S(2)}) copy-start(f32[768]{0:T(1024)} %param.16) | copy-start | bytes 9220
  95.0 4.3 %copy-start.13 = (bf16[2048,768]{0,1:T(8,128)(2,1)S(1)}, bf16[2048,768]{0,1:T(8,128)(2,1)}, u32[]{:S(2)}) copy-start(bf16[2048,768]{0,1:T(8,128)(2,1)} %get-tuple-element.32) | copy-start | bytes 9437188
  99.3 2.8 %copy-start.5 = (bf16[512,768]{1,0:T(8,128)(2,1)}, bf16[512,768]{1,0:T(8,128)(2,1)S(1)}, u32[]{:S(2)}) copy-start(bf16[512,768]{1,0:T(8,128)(2,1)S(1)} %fusion.50) | copy-start | bytes 2359300
  101.6 4.6 %copy-start.7 = (bf16[512,768]{1,0:T(8,128)(2,1)}, bf16[512,768]{1,0:T(8,128)(2,1)S(1)}, u32[]{:S(2)}) copy-start(bf16[512,768]{1,0:T(8,128)(2,1)S(1)} %fusion.49) | copy-start | bytes 2359300
  101.6 1.6 copy-start.4
  133.7 4.8 %copy-start.8 = (bf16[512,768]{1,0:T(8,128)(2,1)S(1)}, bf16[512,768]{1,0:T(8,128)(2,1)}, u32[]{:S(2)}) copy-start(bf16[512,768]{1,0:T(8,128)(2,1)} %copy-done.7) | copy-start | bytes 2359300
  134.9 22.0 %all-to-all-start.4 = ((bf16[4,1,4,4,80,128]{5,4,2,0,1,3:T(8,128)(2,1)}), bf16[4,1,4,4,80,128]{5,4,2,0,1,3:T(8,128)(2,1)S(1)}, u32[]{:S(2)}, u32[]{:S(2)}) async-start(bf16[4,1,4,4,80,128]{5,4,2,0,1,3:T(8,128)(2,1)} %copy.35), calls=%async_computation.4 | async-start | bytes 2621440 | tf_op jit(solution)/shard_map/all_to_all | solution.py:148
  140.6 20.8 %copy-start.6 = (bf16[512,768]{1,0:T(8,128)(2,1)S(1)}, bf16[512,768]{1,0:T(8,128)(2,1)}, u32[]{:S(2)}) copy-start(bf16[512,768]{1,0:T(8,128)(2,1)} %copy-done.5) | copy-start | bytes 2359300
  157.9 10.5 %all-to-all-start.5 = ((bf16[4,1,4,1,80,128]{5,4,0,3,1,2:T(8,128)(2,1)}), bf16[4,1,4,1,80,128]{5,4,0,3,1,2:T(8,128)(2,1)S(1)}, u32[]{:S(2)}, u32[]{:S(2)}) async-start(bf16[4,1,4,1,80,128]{5,4,0,3,1,2:T(8,128)(2,1)} %copy.36), calls=%async_computation.5 | async-start | bytes 655360 | tf_op jit(solution)/shard_map/all_to_all | solution.py:148
  169.1 9.0 %all-to-all-start.6 = ((bf16[4,1,1,1,80,128]{5,4,3,2,1,0:T(8,128)(2,1)}), bf16[4,1,1,1,80,128]{5,4,3,2,1,0:T(8,128)(2,1)S(1)}, u32[]{:S(2)}, u32[]{:S(2)}) async-start(bf16[4,1,1,1,80,128]{5,4,3,2,1,0:T(8,128)(2,1)} %bitcast.10), calls=%async_computation.6 | async-start | bytes 163840 | tf_op jit(solution)/shard_map/all_to_all | solution.py:148
  178.1 29.1 %all-to-all-start.2 = ((bf16[128,4,1536]{2,1,0:T(4,128)(2,1)}), bf16[128,4,1536]{2,1,0:T(4,128)(2,1)S(1)}, u32[]{:S(2)}, u32[]{:S(2)}) async-start(bf16[128,4,1536]{2,1,0:T(4,128)(2,1)} %reshape.141), calls=%async_computation.2 | async-start | bytes 3145728 | tf_op jit(solution)/shard_map/all_to_all | solution.py:95
  207.7 3.9 %copy-start.1 = (bf16[256,768]{1,0:T(8,128)(2,1)S(1)}, bf16[256,768]{1,0:T(8,128)(2,1)}, u32[]{:S(2)}) copy-start(bf16[256,768]{1,0:T(8,128)(2,1)} %param.12) | copy-start | bytes 1179652

commit v6 on v4

--- a/solution.py
+++ b/solution.py
@@ -130,9 +130,15 @@
     )
     summed = partials.reshape(*(lax.axis_size(name) for name in DEVICE_AXES), -1, lanes)
     for axis_name, position in (("c", 1), ("x", 3), ("z", 2), ("y", 0)):
+        ring = lax.axis_size(axis_name)
+        me = lax.axis_index(axis_name)
         sent = summed if axis_name == "c" else summed.astype(jnp.bfloat16)
-        gathered = lax.all_to_all(sent, axis_name, position, position, tiled=True)
-        summed = jnp.sum(gathered.astype(jnp.float32), axis=position, keepdims=True)
+        total = lax.dynamic_slice_in_dim(summed, me, 1, position)
+        for shift in range(1, ring):
+            chunk = lax.dynamic_slice_in_dim(sent, (me + shift) % ring, 1, position)
+            pairs = [(i, (i + shift) % ring) for i in range(ring)]
+            total = total + lax.ppermute(chunk, axis_name, pairs).astype(jnp.float32)
+        summed = total
     summed = summed.reshape(-1, lanes)
     term_rows = share * embedding_width // lanes
     sum_con = summed[:term_rows].reshape(share, embedding_width)

time: 193 us -> 169 us (0.88)
  waiting for transfers between devices: 73.2 us -> 53.9 us
  blocking collectives: 9.07 us -> 0 us
  local copies, waits for them, and re-layouts: 25 us -> 29 us
  matrix products: 46.7 us -> 44.2 us
  starting transfers between devices: 26.8 us -> 29.1 us
    all_to_all x3 -> x0, waiting for transfers between devices: 23.7 us -> none  [on_device(): gathered = lax.all_to_all(sent, axis_name, position, position, tiled=True)]
    ppermute x0 -> x10, starting transfers between devices: none -> 13.3 us  [on_device(): total = total + lax.ppermute(chunk, axis_name, pairs).astype(jnp.float32)]
    all_to_all x3 -> x0, starting transfers between devices: 11 us -> none  [on_device(): gathered = lax.all_to_all(sent, axis_name, position, position, tiled=True)]
    all_to_all x1 -> x0, blocking collectives: 9.07 us -> none  [on_device(): gathered = lax.all_to_all(sent, axis_name, position, position, tiled=True)]
    convert_element_type x0 -> x3, other arithmetic: none -> 7.08 us  [on_device(): sent = summed if axis_name == 'c' else summed.astype(jnp.bfloat16)]
    ppermute x0 -> x10, waiting for transfers between devices: none -> 6.7 us  [on_device(): total = total + lax.ppermute(chunk, axis_name, pairs).astype(jnp.float32)]
    reduce_sum x4 -> x0, other arithmetic: 4.85 us -> none  [on_device(): summed = jnp.sum(gathered.astype(jnp.float32), axis=position, keepdims=True)]
    dynamic_slice x0 -> x4, local copies, waits for them, and re-layouts: none -> 3.39 us  [on_device(): chunk = lax.dynamic_slice_in_dim(sent, (me + shift) % ring, 1, position)]
  transfers between devices with their start and end apart: 5 -> 12, of which waited for: 5 -> 7; matrix products, arithmetic and copies ran while one was open for 8% -> 12% of each run, Pallas kernels for 0% -> 0%
where the time goes in v6:
time: 169 us; the launch traced here: 168 us
  waiting for transfers between devices  53.9 us (32%)
  matrix products  44.2 us (26%)
  starting transfers between devices  29.1 us (17%)
  local copies, waits for them, and re-layouts  29 us (17%)
  other arithmetic  11 us (7%)
    all_to_all x1, waiting for transfers between devices, on_device(): lax.all_to_all(outgoing, DEVICE_AXES, split_axis=0, concat_axis=0, tiled=...  27.7 us
    all_to_all x1, waiting for transfers between devices, on_device(): lax.all_to_all(backward, DEVICE_AXES, split_axis=0, concat_axis=0, tiled=...  19.5 us
    ppermute x10, starting transfers between devices, on_device(): total = total + lax.ppermute(chunk, axis_name, pairs).astype(jnp.float32)  13.3 us
    all_to_all x1, starting transfers between devices, on_device(): lax.all_to_all(outgoing, DEVICE_AXES, split_axis=0, concat_axis=0, tiled=...  11.2 us
    dot_general x1, matrix products, on_device(): jnp.dot(edge_con, constraint_weight, preferred_element_type=jnp.float32)  7.72 us
    dot_general x1, matrix products, on_device(): jnp.dot(table_var, cotangent_mirror_rows, preferred_element_type=jnp.floa...  7.52 us
    dot_general x1, matrix products, on_device(): jnp.dot(edge_var, variable_weight, preferred_element_type=jnp.float32)  7.23 us
    convert_element_type x3, other arithmetic, on_device(): sent = summed if axis_name == 'c' else summed.astype(jnp.bfloat16)  7.08 us
  transfers between devices with their start and end apart: 12, of which 7 were waited for; matrix products, arithmetic and copies ran while one was open for 12% of the time, Pallas kernels for 0%

profile of v6, /device:TPU:0, one launch (start us, length us, event | category | flops | bytes accessed | tf_op | source)
XLA Modules:
  0.0 168.2 jit_solution(10516705356225600292)
XLA Ops:
  1.4 1.4 convolution_convert_fusion.3
  2.9 1.4 convolution_convert_fusion.4
  4.3 1.4 convolution_convert_fusion.5
  5.9 2.2 %reshape.104 = bf16[128,4,2304]{2,1,0:T(4,128)(2,1)} reshape(bf16[512,2304]{1,0:T(8,128)(2,1)S(1)} %pad_maximum_fusion.1) | data formatting | bytes 4718592 | tf_op jit(solution)/shard_map/reshape | solution.py:39
  8.0 11.2 %all-to-all-start = ((bf16[128,4,2304]{2,1,0:T(4,128)(2,1)}), bf16[128,4,2304]{2,1,0:T(4,128)(2,1)S(1)}, u32[]{:S(2)}, u32[]{:S(2)}) async-start(bf16[128,4,2304]{2,1,0:T(4,128)(2,1)} %reshape.104), calls=%async_computation | async-start | bytes 4718592 | tf_op jit(solution)/shard_map/all_to_all | solution.py:42
  23.9 27.7 %all-to-all-done = bf16[128,4,2304]{2,1,0:T(4,128)(2,1)S(1)} async-done(((bf16[128,4,2304]{2,1,0:T(4,128)(2,1)}), bf16[128,4,2304]{2,1,0:T(4,128)(2,1)S(1)}, u32[]{:S(2)}, u32[]{:S(2)}) %all-to-all-start) | async-done | bytes 2359328 | tf_op jit(solution)/shard_map/all_to_all | solution.py:42
  51.6 2.0 %fusion.84 = (bf16[128,4,768]{2,1,0:T(4,128)(2,1)}, bf16[128,4,768]{2,1,0:T(4,128)(2,1)}, bf16[128,4,768]{2,1,0:T(4,128)(2,1)}) fusion(bf16[128,4,2304]{2,1,0:T(4,128)(2,1)S(1)} %all-to-all-done), kind=kLoop, calls=%fused_computation.122 | loop fusion | bytes 4718592 | tf_op jit(solution)/shard_map/slice | solution.py:45
  53.6 1.6 reshape.106
  55.3 1.9 %reshape.107 = bf16[512,768]{1,0:T(8,128)(2,1)S(1)} reshape(bf16[128,4,768]{2,1,0:T(4,128)(2,1)} %get-tuple-element.24) | data formatting | bytes 1572864 | tf_op jit(solution)/shard_map/reshape | solution.py:47
  58.3 7.7 %fusion.31 = f32[2048,768]{1,0:T(8,128)} fusion(bf16[768,768]{1,0:T(8,128)(2,1)} %param.14, bf16[512,768]{1,0:T(8,128)(2,1)S(1)} %reshape.106, s32[2048]{0:T(1024)S(1)} %bitcast.44), kind=kOutput, calls=%fused_computation.49 | convolution fusion | flops 4031250432 | bytes 8265728 | tf_op jit(solution)/shard_map/dot_general | solution.py:64
  66.0 7.2 %fusion.30 = f32[2048,768]{1,0:T(8,128)} fusion(bf16[768,768]{1,0:T(8,128)(2,1)S(1)} %copy-done, bf16[512,768]{1,0:T(8,128)(2,1)S(1)} %reshape.107, s32[2048]{0:T(1024)} %bitcast.47), kind=kOutput, calls=%fused_computation.48 | convolution fusion | flops 4031250432 | bytes 8265728 | tf_op jit(solution)/shard_map/dot_general | solution.py:65
  73.2 7.5 %convert_reduce_fusion = (f32[768]{0:T(1024)S(1)}, bf16[2048,768]{1,0:T(8,128)(2,1)S(1)}) fusion(f32[2048]{0:T(1024)S(1)} %mul.41, f32[768]{0:T(1024)} %param.16, f32[2048,768]{1,0:T(8,128)} %fusion.31, f32[2048,768]{1,0:T(8,128)} %fusion.30, bf16[512,768]{1,0:T(8,128)(2,1)S(1)} %copy-done.5, s32[2048]{0:T(1024)} %bitcast.48), kind=kOutput, calls=%fused_computation | convolution fusion | flops 1635777792 | bytes 16537600 | tf_op jit(solution)/shard_map/dot_general | solution.py:60
  80.8 2.9 %fusion.28 = bf16[512,768]{1,0:T(8,128)(2,1)} fusion(bf16[2048,768]{1,0:T(8,128)(2,1)S(1)} %get-tuple-element.44, s32[2048]{0:T(1024)S(1)} %bitcast.49), kind=kOutput, calls=%fused_computation.41 | convolution fusion | flops 1614151680 | bytes 3940352 | tf_op jit(solution)/shard_map/dot_general | solution.py:77
  83.7 2.9 %fusion.27 = bf16[512,768]{1,0:T(8,128)(2,1)} fusion(bf16[2048,768]{1,0:T(8,128)(2,1)S(1)} %get-tuple-element.44, s32[2048]{0:T(1024)S(1)} %bitcast.45), kind=kOutput, calls=%fused_computation.40 | convolution fusion | flops 1614151680 | bytes 3940352 | tf_op jit(solution)/shard_map/dot_general | solution.py:74
  87.4 2.2 %fusion.89 = f32[768,768]{1,0:T(8,128)S(1)} fusion(bf16[512,768]{1,0:T(8,128)(2,1)} %copy-done.3, bf16[512,768]{1,0:T(8,128)(2,1)} %fusion.28), kind=kOutput, calls=%fused_computation.127 | convolution fusion | flops 603979776 | bytes 3932160 | tf_op jit(solution)/shard_map/dot_general | solution.py:111
  89.5 1.7 %concatenate.21 = f32[4,2,4,4,36,128]{5,4,3,2,1,0:T(8,128)} reshape(f32[768,768]{1,0:T(8,128)S(1)} %fusion.89) | data formatting | bytes 4718592 | tf_op jit(solution)/shard_map/concatenate | solution.py:123
  91.2 2.2 %fusion.88 = f32[768,768]{1,0:T(8,128)S(1)} fusion(bf16[512,768]{1,0:T(8,128)(2,1)} %copy-done.2, bf16[512,768]{1,0:T(8,128)(2,1)} %fusion.27), kind=kOutput, calls=%fused_computation.126 | convolution fusion | flops 603979776 | bytes 3932160 | tf_op jit(solution)/shard_map/dot_general | solution.py:105
  93.4 1.7 %concatenate.20 = f32[4,2,4,4,36,128]{5,4,3,2,1,0:T(8,128)} reshape(f32[768,768]{1,0:T(8,128)S(1)} %fusion.88) | data formatting | bytes 4718592 | tf_op jit(solution)/shard_map/concatenate | solution.py:123
  96.0 3.1 %pad_maximum_fusion = f32[4,2,4,4,80,128]{5,4,3,2,1,0:T(8,128)S(1)} fusion(f32[4,2,4,4,8,128]{5,4,3,2,1,0:T(8,128)S(1)} %bitcast.38, f32[4,2,4,4,36,128]{5,4,3,2,1,0:T(8,128)} %concatenate.21, f32[4,2,4,4,36,128]{5,4,3,2,1,0:T(8,128)} %concatenate.20), kind=kLoop, calls=%fused_computation.2 | loop fusion | flops 2621440 | bytes 10485760 | tf_op jit(solution)/shard_map/concatenate | solution.py:123
  99.2 1.7 %constant_dynamic-slice_fusion.9 = f32[4,1,4,4,80,128]{5,4,3,2,1,0:T(8,128)} fusion(f32[4,2,4,4,80,128]{5,4,3,2,1,0:T(8,128)S(1)} %pad_maximum_fusion, s32[]{:T(128)S(6)} %select_n.117), kind=kLoop, calls=%fused_computation.85 | loop fusion | bytes 5242884 | tf_op jit(solution)/shard_map/dynamic_slice | solution.py:138
  105.9 4.6 %all-to-all-start.1 = ((bf16[128,4,1536]{2,1,0:T(4,128)(2,1)}), bf16[128,4,1536]{2,1,0:T(4,128)(2,1)S(1)}, u32[]{:S(2)}, u32[]{:S(2)}) async-start(bf16[128,4,1536]{2,1,0:T(4,128)(2,1)} %reshape.109), calls=%async_computation.1 | async-start | bytes 3145728 | tf_op jit(solution)/shard_map/all_to_all | solution.py:89
  110.6 4.6 %fusion.83 = (bf16[4,1,4,4,80,128]{5,4,3,2,1,0:T(8,128)(2,1)S(1)}, f32[4,1,4,4,80,128]{5,4,3,2,1,0:T(8,128)}) fusion(f32[4,1,4,4,80,128]{5,4,3,2,1,0:T(8,128)} %collective-permute-done, f32[4,2,4,4,80,128]{5,4,3,2,1,0:T(8,128)} %copy-done.1, s32[]{:T(128)S(6)} %select_n.115), kind=kLoop, calls=%fused_computation.121 | loop fusion | flops 1310720 | bytes 9175044 | tf_op jit(solution)/shard_map/convert_element_type | solution.py:135
  116.1 2.1 %collective-permute-start.3 = (bf16[4,1,4,1,80,128]{5,4,3,2,1,0:T(8,128)(2,1)}, bf16[4,1,4,1,80,128]{5,4,3,2,1,0:T(8,128)(2,1)}, u32[]{:S(2)}, u32[]{:S(2)}) collective-permute-start(bf16[4,1,4,1,80,128]{5,4,3,2,1,0:T(8,128)(2,1)} %get-tuple-element.29), channel_id=1, source_target_pairs={{0,3},{1,0},{2,1},{3,2},{4,7},{5,4},{6,5},{7,6},{8,11},{9,8},{10,9... | collective-permute-start | bytes 983048 | tf_op jit(solution)/shard_map/ppermute | solution.py:140
  119.9 19.5 %all-to-all-done.1 = bf16[128,4,1536]{2,1,0:T(4,128)(2,1)S(1)} async-done(((bf16[128,4,1536]{2,1,0:T(4,128)(2,1)}), bf16[128,4,1536]{2,1,0:T(4,128)(2,1)S(1)}, u32[]{:S(2)}, u32[]{:S(2)}) %all-to-all-start.1) | async-done | bytes 1572896 | tf_op jit(solution)/shard_map/all_to_all | solution.py:89
  139.4 1.4 fusion.85
  140.8 2.3 %reshape.111 = bf16[512,768]{1,0:T(8,128)(2,1)} reshape(bf16[128,4,768]{2,1,0:T(4,128)(2,1)} %get-tuple-element.26) | data formatting | bytes 1572864 | tf_op jit(solution)/shard_map/reshape | solution.py:100
  143.9 1.6 fusion.82
  146.2 3.5 %collective-permute-start.6 = (bf16[4,1,1,1,80,128]{5,4,3,2,1,0:T(8,128)(2,1)}, bf16[4,1,1,1,80,128]{5,4,3,2,1,0:T(8,128)(2,1)S(1)}, u32[]{:S(2)}, u32[]{:S(2)}) collective-permute-start(bf16[4,1,1,1,80,128]{5,4,3,2,1,0:T(8,128)(2,1)} %get-tuple-element.32), channel_id=1, source_target_pairs={{0,12},{4,0},{8,4},{12,8},{1,13},{5,1},{9,5},{13,9},{2,14},{6,2},{... | collective-permute-start | bytes 245768 | tf_op jit(solution)/shard_map/ppermute | solution.py:140
  151.1 2.5 %fusion.29 = bf16[256,768]{1,0:T(8,128)(2,1)} fusion(bf16[512,768]{1,0:T(8,128)(2,1)} %reshape.111, bf16[256,768]{1,0:T(8,128)(2,1)} %param.13, s32[512]{0:T(512)S(1)} %bitcast.54), kind=kOutput, calls=%fused_computation.46 | convolution fusion | flops 202309632 | bytes 1574912 | tf_op jit(solution)/shard_map/dot_general | solution.py:98
  153.8 2.2 %collective-permute-done.5 = bf16[4,1,1,1,80,128]{5,4,3,2,1,0:T(8,128)(2,1)} collective-permute-done((bf16[4,1,1,1,80,128]{5,4,3,2,1,0:T(8,128)(2,1)}, bf16[4,1,1,1,80,128]{5,4,3,2,1,0:T(8,128)(2,1)}, u32[]{:S(2)}, u32[]{:S(2)}) %collective-permute-start.5) | collective-permute-done | bytes 81952 | tf_op jit(solution)/shard_map/ppermute | solution.py:140
  157.8 2.9 %collective-permute-start.9 = (bf16[1,1,1,1,80,128]{5,4,3,2,1,0:T(8,128)(2,1)S(1)}, bf16[1,1,1,1,80,128]{5,4,3,2,1,0:T(8,128)(2,1)S(1)}, u32[]{:S(2)}, u32[]{:S(2)}) collective-permute-start(bf16[1,1,1,1,80,128]{5,4,3,2,1,0:T(8,128)(2,1)S(1)} %get-tuple-element.35), channel_id=1, source_target_pairs={{0,96},{32,0},{64,32},{96,64},{1,97},{33,1},{65,33},{97,65},{2,98}... | collective-permute-start | bytes 61448 | tf_op jit(solution)/shard_map/ppermute | solution.py:140
  163.6 2.4 %collective-permute-done.8 = bf16[1,1,1,1,80,128]{5,4,3,2,1,0:T(8,128)(2,1)S(1)} collective-permute-done((bf16[1,1,1,1,80,128]{5,4,3,2,1,0:T(8,128)(2,1)S(1)}, bf16[1,1,1,1,80,128]{5,4,3,2,1,0:T(8,128)(2,1)S(1)}, u32[]{:S(2)}, u32[]{:S(2)}) %collective-permute-start.8) | collective-permute-done | bytes 20512 | tf_op jit(solution)/shard_map/ppermute | solution.py:140
  (76 shorter events, 26.1 us)
Async XLA Ops:
  0.6 65.4 %copy-start = (bf16[768,768]{1,0:T(8,128)(2,1)S(1)}, bf16[768,768]{1,0:T(8,128)(2,1)}, u32[]{:S(2)}) copy-start(bf16[768,768]{1,0:T(8,128)(2,1)} %param.15) | copy-start | bytes 3538948
  1.4 2.8 %copy-start.10 = (s32[1,1,512]{2,1,0:T(1,128)}, s32[1,1,512]{2,1,0:T(1,128)S(1)}, u32[]{:S(2)}) copy-start(s32[1,1,512]{2,1,0:T(1,128)S(1)} %get-tuple-element.41) | copy-start | bytes 6148
  1.4 2.8 %copy-start.12 = (s32[1,1,512]{2,1,0:T(1,128)}, s32[1,1,512]{2,1,0:T(1,128)S(1)}, u32[]{:S(2)}) copy-start(s32[1,1,512]{2,1,0:T(1,128)S(1)} %get-tuple-element.42) | copy-start | bytes 6148
  8.0 11.2 %copy-start.14 = (s32[2,1,128]{2,1,0:T(1,128)S(1)}, s32[2,1,128]{2,1,0:T(1,128)}, u32[]{:S(2)}) copy-start(s32[2,1,128]{2,1,0:T(1,128)} %param.18) | copy-start | bytes 3076
  8.0 43.6 %all-to-all-start = ((bf16[128,4,2304]{2,1,0:T(4,128)(2,1)}), bf16[128,4,2304]{2,1,0:T(4,128)(2,1)S(1)}, u32[]{:S(2)}, u32[]{:S(2)}) async-start(bf16[128,4,2304]{2,1,0:T(4,128)(2,1)} %reshape.104), calls=%async_computation | async-start | bytes 4718592 | tf_op jit(solution)/shard_map/all_to_all | solution.py:42
  21.9 2.0 %copy-start.8 = (s32[1,2048]{1,0:T(1,128)}, s32[1,2048]{1,0:T(1,128)S(1)}, u32[]{:S(2)}) copy-start(s32[1,2048]{1,0:T(1,128)S(1)} %get-tuple-element.39) | copy-start | bytes 24580
  53.6 3.5 %copy-start.4 = (bf16[128,4,768]{2,1,0:T(4,128)(2,1)S(1)}, bf16[128,4,768]{2,1,0:T(4,128)(2,1)}, u32[]{:S(2)}) copy-start(bf16[128,4,768]{2,1,0:T(4,128)(2,1)} %get-tuple-element.23) | copy-start | bytes 2359300
  55.2 10.7 %copy-start.2 = (bf16[512,768]{1,0:T(8,128)(2,1)}, bf16[512,768]{1,0:T(8,128)(2,1)S(1)}, u32[]{:S(2)}) copy-start(bf16[512,768]{1,0:T(8,128)(2,1)S(1)} %reshape.106) | copy-start | bytes 2359300
  57.1 8.9 %copy-start.3 = (bf16[512,768]{1,0:T(8,128)(2,1)}, bf16[512,768]{1,0:T(8,128)(2,1)S(1)}, u32[]{:S(2)}) copy-start(bf16[512,768]{1,0:T(8,128)(2,1)S(1)} %reshape.107) | copy-start | bytes 2359300
  66.0 7.2 %copy-start.5 = (bf16[512,768]{1,0:T(8,128)(2,1)S(1)}, bf16[512,768]{1,0:T(8,128)(2,1)}, u32[]{:S(2)}) copy-start(bf16[512,768]{1,0:T(8,128)(2,1)} %reshape.105) | copy-start | bytes 2359300
  73.2 7.5 %copy-start.9 = (s32[1,2048]{1,0:T(1,128)S(1)}, s32[1,2048]{1,0:T(1,128)}, u32[]{:S(2)}) copy-start(s32[1,2048]{1,0:T(1,128)} %copy-done.8) | copy-start | bytes 24580
  99.2 3.4 %copy-start.1 = (f32[4,2,4,4,80,128]{5,4,3,2,1,0:T(8,128)}, f32[4,2,4,4,80,128]{5,4,3,2,1,0:T(8,128)S(1)}, u32[]{:S(2)}) copy-start(f32[4,2,4,4,80,128]{5,4,3,2,1,0:T(8,128)S(1)} %pad_maximum_fusion) | copy-start | bytes 15728644
  99.2 1.7 %copy-start.6 = (bf16[512,768]{1,0:T(8,128)(2,1)S(1)}, bf16[512,768]{1,0:T(8,128)(2,1)}, u32[]{:S(2)}) copy-start(bf16[512,768]{1,0:T(8,128)(2,1)} %fusion.28) | copy-start | bytes 2359300
  100.9 1.7 %copy-start.7 = (bf16[512,768]{1,0:T(8,128)(2,1)S(1)}, bf16[512,768]{1,0:T(8,128)(2,1)}, u32[]{:S(2)}) copy-start(bf16[512,768]{1,0:T(8,128)(2,1)} %fusion.27) | copy-start | bytes 2359300
  100.9 2.7 %copy-start.15 = (bf16[768,768]{1,0:T(8,128)(2,1)S(1)}, bf16[768,768]{1,0:T(8,128)(2,1)}, u32[]{:S(2)}) copy-start(bf16[768,768]{1,0:T(8,128)(2,1)} %param.14) | copy-start | bytes 3538948
  100.9 9.7 %collective-permute-start = (f32[4,1,4,4,80,128]{5,4,3,2,1,0:T(8,128)}, f32[4,1,4,4,80,128]{5,4,3,2,1,0:T(8,128)}, u32[]{:S(2)}, u32[]{:S(2)}) collective-permute-start(f32[4,1,4,4,80,128]{5,4,3,2,1,0:T(8,128)} %constant_dynamic-slice_fusion.9), channel_id=1, source_target_pairs={{0,16},{16,0},{1,17},{17,1},{2,18},{18,2},{3,19},{19,3},{4,20},{20... | collective-permute-start | bytes 7864328 | tf_op jit(solution)/shard_map/ppermute | solution.py:140
  105.9 33.5 %all-to-all-start.1 = ((bf16[128,4,1536]{2,1,0:T(4,128)(2,1)}), bf16[128,4,1536]{2,1,0:T(4,128)(2,1)S(1)}, u32[]{:S(2)}, u32[]{:S(2)}) async-start(bf16[128,4,1536]{2,1,0:T(4,128)(2,1)} %reshape.109), calls=%async_computation.1 | async-start | bytes 3145728 | tf_op jit(solution)/shard_map/all_to_all | solution.py:89
  116.1 27.0 %collective-permute-start.3 = (bf16[4,1,4,1,80,128]{5,4,3,2,1,0:T(8,128)(2,1)}, bf16[4,1,4,1,80,128]{5,4,3,2,1,0:T(8,128)(2,1)}, u32[]{:S(2)}, u32[]{:S(2)}) collective-permute-start(bf16[4,1,4,1,80,128]{5,4,3,2,1,0:T(8,128)(2,1)} %get-tuple-element.29), channel_id=1, source_target_pairs={{0,3},{1,0},{2,1},{3,2},{4,7},{5,4},{6,5},{7,6},{8,11},{9,8},{10,9... | collective-permute-start | bytes 983048 | tf_op jit(solution)/shard_map/ppermute | solution.py:140
  118.2 24.9 %collective-permute-start.2 = (bf16[4,1,4,1,80,128]{5,4,3,2,1,0:T(8,128)(2,1)}, bf16[4,1,4,1,80,128]{5,4,3,2,1,0:T(8,128)(2,1)}, u32[]{:S(2)}, u32[]{:S(2)}) collective-permute-start(bf16[4,1,4,1,80,128]{5,4,3,2,1,0:T(8,128)(2,1)} %get-tuple-element.30), channel_id=1, source_target_pairs={{0,2},{1,3},{2,0},{3,1},{4,6},{5,7},{6,4},{7,5},{8,10},{9,11},{10,... | collective-permute-start | bytes 983048 | tf_op jit(solution)/shard_map/ppermute | solution.py:140
  119.0 24.9 %collective-permute-start.1 = (bf16[4,1,4,1,80,128]{5,4,3,2,1,0:T(8,128)(2,1)}, bf16[4,1,4,1,80,128]{5,4,3,2,1,0:T(8,128)(2,1)}, u32[]{:S(2)}, u32[]{:S(2)}) collective-permute-start(bf16[4,1,4,1,80,128]{5,4,3,2,1,0:T(8,128)(2,1)} %get-tuple-element.28), channel_id=1, source_target_pairs={{0,1},{1,2},{2,3},{3,0},{4,5},{5,6},{6,7},{7,4},{8,9},{9,10},{10,1... | collective-permute-start | bytes 983048 | tf_op jit(solution)/shard_map/ppermute | solution.py:140
  119.9 31.2 %copy-start.13 = (s32[1,1,512]{2,1,0:T(1,128)S(1)}, s32[1,1,512]{2,1,0:T(1,128)}, u32[]{:S(2)}) copy-start(s32[1,1,512]{2,1,0:T(1,128)} %copy-done.12) | copy-start | bytes 6148
  143.9 18.5 %copy-start.11 = (s32[1,1,512]{2,1,0:T(1,128)S(1)}, s32[1,1,512]{2,1,0:T(1,128)}, u32[]{:S(2)}) copy-start(s32[1,1,512]{2,1,0:T(1,128)} %copy-done.10) | copy-start | bytes 6148
  146.2 7.6 %collective-permute-start.6 = (bf16[4,1,1,1,80,128]{5,4,3,2,1,0:T(8,128)(2,1)}, bf16[4,1,1,1,80,128]{5,4,3,2,1,0:T(8,128)(2,1)S(1)}, u32[]{:S(2)}, u32[]{:S(2)}) collective-permute-start(bf16[4,1,1,1,80,128]{5,4,3,2,1,0:T(8,128)(2,1)} %get-tuple-element.32), channel_id=1, source_target_pairs={{0,12},{4,0},{8,4},{12,8},{1,13},{5,1},{9,5},{13,9},{2,14},{6,2},{... | collective-permute-start | bytes 245768 | tf_op jit(solution)/shard_map/ppermute | solution.py:140
  149.7 6.3 %collective-permute-start.5 = (bf16[4,1,1,1,80,128]{5,4,3,2,1,0:T(8,128)(2,1)}, bf16[4,1,1,1,80,128]{5,4,3,2,1,0:T(8,128)(2,1)}, u32[]{:S(2)}, u32[]{:S(2)}) collective-permute-start(bf16[4,1,1,1,80,128]{5,4,3,2,1,0:T(8,128)(2,1)} %get-tuple-element.33), channel_id=1, source_target_pairs={{0,8},{4,12},{8,0},{12,4},{1,9},{5,13},{9,1},{13,5},{2,10},{6,14},... | collective-permute-start | bytes 245768 | tf_op jit(solution)/shard_map/ppermute | solution.py:140
  150.0 6.8 %collective-permute-start.4 = (bf16[4,1,1,1,80,128]{5,4,3,2,1,0:T(8,128)(2,1)}, bf16[4,1,1,1,80,128]{5,4,3,2,1,0:T(8,128)(2,1)}, u32[]{:S(2)}, u32[]{:S(2)}) collective-permute-start(bf16[4,1,1,1,80,128]{5,4,3,2,1,0:T(8,128)(2,1)} %get-tuple-element.31), channel_id=1, source_target_pairs={{0,4},{4,8},{8,12},{12,0},{1,5},{5,9},{9,13},{13,1},{2,6},{6,10},{... | collective-permute-start | bytes 245768 | tf_op jit(solution)/shard_map/ppermute | solution.py:140
  157.8 5.8 %collective-permute-start.9 = (bf16[1,1,1,1,80,128]{5,4,3,2,1,0:T(8,128)(2,1)S(1)}, bf16[1,1,1,1,80,128]{5,4,3,2,1,0:T(8,128)(2,1)S(1)}, u32[]{:S(2)}, u32[]{:S(2)}) collective-permute-start(bf16[1,1,1,1,80,128]{5,4,3,2,1,0:T(8,128)(2,1)S(1)} %get-tuple-element.35), channel_id=1, source_target_pairs={{0,96},{32,0},{64,32},{96,64},{1,97},{33,1},{65,33},{97,65},{2,98}... | collective-permute-start | bytes 61448 | tf_op jit(solution)/shard_map/ppermute | solution.py:140
  160.7 5.3 %collective-permute-start.8 = (bf16[1,1,1,1,80,128]{5,4,3,2,1,0:T(8,128)(2,1)S(1)}, bf16[1,1,1,1,80,128]{5,4,3,2,1,0:T(8,128)(2,1)S(1)}, u32[]{:S(2)}, u32[]{:S(2)}) collective-permute-start(bf16[1,1,1,1,80,128]{5,4,3,2,1,0:T(8,128)(2,1)S(1)} %get-tuple-element.36), channel_id=1, source_target_pairs={{0,64},{32,96},{64,0},{96,32},{1,65},{33,97},{65,1},{97,33},{2,66}... | collective-permute-start | bytes 61448 | tf_op jit(solution)/shard_map/ppermute | solution.py:140
  161.5 5.0 %collective-permute-start.7 = (bf16[1,1,1,1,80,128]{5,4,3,2,1,0:T(8,128)(2,1)S(1)}, bf16[1,1,1,1,80,128]{5,4,3,2,1,0:T(8,128)(2,1)S(1)}, u32[]{:S(2)}, u32[]{:S(2)}) collective-permute-start(bf16[1,1,1,1,80,128]{5,4,3,2,1,0:T(8,128)(2,1)S(1)} %get-tuple-element.34), channel_id=1, source_target_pairs={{0,32},{32,64},{64,96},{96,0},{1,33},{33,65},{65,97},{97,1},{2,34}... | collective-permute-start | bytes 61448 | tf_op jit(solution)/shard_map/ppermute | solution.py:140

commit v7 on v6

--- a/solution.py
+++ b/solution.py
@@ -86,22 +86,6 @@
     backward = jnp.concatenate([back_con, back_var], axis=1).reshape(
         device_count, slot_cap, 2 * embedding_width
     )
-    homes = lax.all_to_all(backward, DEVICE_AXES, split_axis=0, concat_axis=0, tiled=True)
-    home_con = homes[:, :, :embedding_width]
-    home_var = homes[:, :, embedding_width:]
-    grad_con = lax.dot_general(
-        select_con,
-        home_con.reshape(replica_rows, embedding_width),
-        sum_dims,
-        preferred_element_type=jnp.float32,
-    )
-    grad_var = lax.dot_general(
-        select_var,
-        home_var.reshape(replica_rows, embedding_width),
-        sum_dims,
-        preferred_element_type=jnp.float32,
-    )
-    grad_var = variable_cotangent.astype(jnp.float32) + grad_var
     constraint_term = lax.dot_general(
         constraint_mirror_rows,
         constraint_projection_gradient,
@@ -130,6 +114,11 @@
     )
     summed = partials.reshape(*(lax.axis_size(name) for name in DEVICE_AXES), -1, lanes)
     for axis_name, position in (("c", 1), ("x", 3), ("z", 2), ("y", 0)):
+        if axis_name == "x":
+            backward, summed = lax.optimization_barrier((backward, summed))
+            homes = lax.all_to_all(backward, DEVICE_AXES, split_axis=0, concat_axis=0, tiled=True)
+            home_con = homes[:, :, :embedding_width]
+            home_var = homes[:, :, embedding_width:]
         ring = lax.axis_size(axis_name)
         me = lax.axis_index(axis_name)
         sent = summed if axis_name == "c" else summed.astype(jnp.bfloat16)
@@ -140,6 +129,19 @@
             total = total + lax.ppermute(chunk, axis_name, pairs).astype(jnp.float32)
         summed = total
     summed = summed.reshape(-1, lanes)
+    grad_con = lax.dot_general(
+        select_con,
+        home_con.reshape(replica_rows, embedding_width),
+        sum_dims,
+        preferred_element_type=jnp.float32,
+    )
+    grad_var = lax.dot_general(
+        select_var,
+        home_var.reshape(replica_rows, embedding_width),
+        sum_dims,
+        preferred_element_type=jnp.float32,
+    )
+    grad_var = variable_cotangent.astype(jnp.float32) + grad_var
     term_rows = share * embedding_width // lanes
     sum_con = summed[:term_rows].reshape(share, embedding_width)
     sum_var = summed[term_rows : 2 * term_rows].reshape(share, embedding_width)

time: 169 us -> 170 us (level)
  waiting for transfers between devices: 53.9 us -> 56.5 us
  starting transfers between devices: 29.1 us -> 26.9 us
  local copies, waits for them, and re-layouts: 29 us -> 30.8 us
    ppermute x10, waiting for transfers between devices: 6.7 us -> 28.8 us  [on_device(): total = total + lax.ppermute(chunk, axis_name, pairs).astype(jnp.float32)]
    all_to_all x1, waiting for transfers between devices: 19.5 us -> 0.01 us  [on_device(): lax.all_to_all(backward, DEVICE_AXES, split_axis=0, concat_axis=0, tiled=...]
    ppermute x10, starting transfers between devices: 13.3 us -> 8.72 us  [on_device(): total = total + lax.ppermute(chunk, axis_name, pairs).astype(jnp.float32)]
    convert_element_type x3, other arithmetic: 7.08 us -> 3.39 us  [on_device(): sent = summed if axis_name == 'c' else summed.astype(jnp.bfloat16)]
    add x1 -> x2, other arithmetic: 0.01 us -> 3.62 us  [on_device(): total = total + lax.ppermute(chunk, axis_name, pairs).astype(jnp.float32)]
    unnamed x32 -> x36, local copies, waits for them, and re-layouts: 1.92 us -> 4.52 us
    all_to_all x1, starting transfers between devices: 4.64 us -> 6.98 us  [on_device(): lax.all_to_all(backward, DEVICE_AXES, split_axis=0, concat_axis=0, tiled=...]
    reshape x1, local copies, waits for them, and re-layouts: 2.27 us -> 0.18 us  [on_device(): home_var.reshape(replica_rows, embedding_width)]
  transfers between devices with their start and end apart: 12 -> 12, of which waited for: 7 -> 10; matrix products, arithmetic and copies ran while one was open for 12% -> 8% of each run, Pallas kernels for 0% -> 0%
where the time goes in v7:
time: 170 us; the launch traced here: 169 us
  waiting for transfers between devices  56.5 us (33%)
  matrix products  43 us (25%)
  local copies, waits for them, and re-layouts  30.8 us (18%)
  starting transfers between devices  26.9 us (16%)
  other arithmetic  10.9 us (6%)
    ppermute x10, waiting for transfers between devices, on_device(): total = total + lax.ppermute(chunk, axis_name, pairs).astype(jnp.float32)  28.8 us
    all_to_all x1, waiting for transfers between devices, on_device(): lax.all_to_all(outgoing, DEVICE_AXES, split_axis=0, concat_axis=0, tiled=...  27.7 us
    all_to_all x1, starting transfers between devices, on_device(): lax.all_to_all(outgoing, DEVICE_AXES, split_axis=0, concat_axis=0, tiled=...  11.2 us
    ppermute x10, starting transfers between devices, on_device(): total = total + lax.ppermute(chunk, axis_name, pairs).astype(jnp.float32)  8.72 us
    dot_general x1, matrix products, on_device(): jnp.dot(edge_con, constraint_weight, preferred_element_type=jnp.float32)  7.72 us
    dot_general x1, matrix products, on_device(): jnp.dot(table_var, cotangent_mirror_rows, preferred_element_type=jnp.floa...  7.54 us
    dot_general x1, matrix products, on_device(): jnp.dot(edge_var, variable_weight, preferred_element_type=jnp.float32)  7.22 us
    all_to_all x1, starting transfers between devices, on_device(): lax.all_to_all(backward, DEVICE_AXES, split_axis=0, concat_axis=0, tiled=...  6.98 us
  transfers between devices with their start and end apart: 12, of which 10 were waited for; matrix products, arithmetic and copies ran while one was open for 8% of the time, Pallas kernels for 0%

profile of v7, /device:TPU:0, one launch (start us, length us, event | category | flops | bytes accessed | tf_op | source)
XLA Modules:
  0.0 169.2 jit_solution(12690964455831621609)
XLA Ops:
  5.9 2.1 %reshape.104 = bf16[128,4,2304]{2,1,0:T(4,128)(2,1)} reshape(bf16[512,2304]{1,0:T(8,128)(2,1)S(1)} %pad_maximum_fusion.1) | data formatting | bytes 4718592 | tf_op jit(solution)/shard_map/reshape | solution.py:39
  8.0 11.2 %all-to-all-start = ((bf16[128,4,2304]{2,1,0:T(4,128)(2,1)}), bf16[128,4,2304]{2,1,0:T(4,128)(2,1)S(1)}, u32[]{:S(2)}, u32[]{:S(2)}) async-start(bf16[128,4,2304]{2,1,0:T(4,128)(2,1)} %reshape.104), calls=%async_computation | async-start | bytes 4718592 | tf_op jit(solution)/shard_map/all_to_all | solution.py:42
  23.9 27.7 %all-to-all-done = bf16[128,4,2304]{2,1,0:T(4,128)(2,1)S(1)} async-done(((bf16[128,4,2304]{2,1,0:T(4,128)(2,1)}), bf16[128,4,2304]{2,1,0:T(4,128)(2,1)S(1)}, u32[]{:S(2)}, u32[]{:S(2)}) %all-to-all-start) | async-done | bytes 2359328 | tf_op jit(solution)/shard_map/all_to_all | solution.py:42
  51.6 2.0 %fusion.83 = (bf16[128,4,768]{2,1,0:T(4,128)(2,1)}, bf16[128,4,768]{2,1,0:T(4,128)(2,1)}, bf16[128,4,768]{2,1,0:T(4,128)(2,1)}) fusion(bf16[128,4,2304]{2,1,0:T(4,128)(2,1)S(1)} %all-to-all-done), kind=kLoop, calls=%fused_computation.121 | loop fusion | bytes 4718592 | tf_op jit(solution)/shard_map/slice | solution.py:45
  53.6 1.6 reshape.106
  55.2 1.9 %reshape.107 = bf16[512,768]{1,0:T(8,128)(2,1)S(1)} reshape(bf16[128,4,768]{2,1,0:T(4,128)(2,1)} %get-tuple-element.26) | data formatting | bytes 1572864 | tf_op jit(solution)/shard_map/reshape | solution.py:47
  58.3 7.7 %fusion.31 = f32[2048,768]{1,0:T(8,128)} fusion(bf16[768,768]{1,0:T(8,128)(2,1)} %param.14, bf16[512,768]{1,0:T(8,128)(2,1)S(1)} %reshape.106, s32[2048]{0:T(1024)S(1)} %bitcast.44), kind=kOutput, calls=%fused_computation.49 | convolution fusion | flops 4031250432 | bytes 8265728 | tf_op jit(solution)/shard_map/dot_general | solution.py:64
  66.0 7.2 %fusion.30 = f32[2048,768]{1,0:T(8,128)} fusion(bf16[768,768]{1,0:T(8,128)(2,1)S(1)} %copy-done, bf16[512,768]{1,0:T(8,128)(2,1)S(1)} %reshape.107, s32[2048]{0:T(1024)} %bitcast.47), kind=kOutput, calls=%fused_computation.48 | convolution fusion | flops 4031250432 | bytes 8265728 | tf_op jit(solution)/shard_map/dot_general | solution.py:65
  73.2 7.5 %convert_reduce_fusion = (f32[768]{0:T(1024)S(1)}, bf16[2048,768]{1,0:T(8,128)(2,1)S(1)}) fusion(f32[2048]{0:T(1024)S(1)} %mul.41, f32[768]{0:T(1024)} %param.16, f32[2048,768]{1,0:T(8,128)} %fusion.31, f32[2048,768]{1,0:T(8,128)} %fusion.30, bf16[512,768]{1,0:T(8,128)(2,1)S(1)} %copy-done.6, s32[2048]{0:T(1024)} %bitcast.48), kind=kOutput, calls=%fused_computation | convolution fusion | flops 1635777792 | bytes 16537600 | tf_op jit(solution)/shard_map/dot_general | solution.py:60
  80.8 2.9 %fusion.28 = bf16[512,768]{1,0:T(8,128)(2,1)} fusion(bf16[2048,768]{1,0:T(8,128)(2,1)S(1)} %get-tuple-element.46, s32[2048]{0:T(1024)S(1)} %bitcast.49), kind=kOutput, calls=%fused_computation.41 | convolution fusion | flops 1614151680 | bytes 3940352 | tf_op jit(solution)/shard_map/dot_general | solution.py:77
  83.7 2.9 %fusion.27 = bf16[512,768]{1,0:T(8,128)(2,1)} fusion(bf16[2048,768]{1,0:T(8,128)(2,1)S(1)} %get-tuple-element.46, s32[2048]{0:T(1024)S(1)} %bitcast.45), kind=kOutput, calls=%fused_computation.40 | convolution fusion | flops 1614151680 | bytes 3940352 | tf_op jit(solution)/shard_map/dot_general | solution.py:74
  87.4 2.2 %fusion.88 = f32[768,768]{1,0:T(8,128)S(1)} fusion(bf16[512,768]{1,0:T(8,128)(2,1)} %copy-done.4, bf16[512,768]{1,0:T(8,128)(2,1)} %fusion.28), kind=kOutput, calls=%fused_computation.126 | convolution fusion | flops 603979776 | bytes 3932160 | tf_op jit(solution)/shard_map/dot_general | solution.py:95
  89.6 1.7 concatenate.21
  91.2 2.2 %fusion.87 = f32[768,768]{1,0:T(8,128)S(1)} fusion(bf16[512,768]{1,0:T(8,128)(2,1)} %copy-done.3, bf16[512,768]{1,0:T(8,128)(2,1)} %fusion.27), kind=kOutput, calls=%fused_computation.125 | convolution fusion | flops 603979776 | bytes 3932160 | tf_op jit(solution)/shard_map/dot_general | solution.py:89
  93.4 1.7 %concatenate.20 = f32[4,2,4,4,36,128]{5,4,3,2,1,0:T(8,128)} reshape(f32[768,768]{1,0:T(8,128)S(1)} %fusion.87) | data formatting | bytes 4718592 | tf_op jit(solution)/shard_map/concatenate | solution.py:107
  96.0 3.1 %pad_maximum_fusion = f32[4,2,4,4,80,128]{5,4,3,2,1,0:T(8,128)S(1)} fusion(f32[4,2,4,4,8,128]{5,4,3,2,1,0:T(8,128)S(1)} %bitcast.38, f32[4,2,4,4,36,128]{5,4,3,2,1,0:T(8,128)} %concatenate.21, f32[4,2,4,4,36,128]{5,4,3,2,1,0:T(8,128)} %concatenate.20), kind=kLoop, calls=%fused_computation.2 | loop fusion | flops 2621440 | bytes 10485760 | tf_op jit(solution)/shard_map/concatenate | solution.py:107
  99.2 2.3 %copy-done.1 = f32[4,2,4,4,80,128]{5,4,3,2,1,0:T(8,128)} copy-done((f32[4,2,4,4,80,128]{5,4,3,2,1,0:T(8,128)}, f32[4,2,4,4,80,128]{5,4,3,2,1,0:T(8,128)S(1)}, u32[]{:S(2)}) %copy-start.1) | copy-done | bytes 5242904
  101.5 1.8 %constant_dynamic-slice_fusion.9 = f32[4,1,4,4,80,128]{5,4,3,2,1,0:T(8,128)} fusion(f32[4,2,4,4,80,128]{5,4,3,2,1,0:T(8,128)S(1)} %pad_maximum_fusion, s32[]{:T(128)S(6)} %select_n.117), kind=kLoop, calls=%fused_computation.85 | loop fusion | bytes 5242884 | tf_op jit(solution)/shard_map/dynamic_slice | solution.py:127
  108.5 2.8 %dynamic-slice_add_fusion = f32[4,1,4,4,80,128]{5,4,3,2,1,0:T(8,128)S(1)} fusion(f32[4,1,4,4,80,128]{5,4,3,2,1,0:T(8,128)} %collective-permute-done, f32[4,2,4,4,80,128]{5,4,3,2,1,0:T(8,128)} %copy-done.1, s32[]{:T(128)S(6)} %select_n.115), kind=kLoop, calls=%fused_computation.14 | loop fusion | flops 655360 | bytes 7864324 | tf_op jit(solution)/shard_map/add | solution.py:129
  111.4 1.5 copy-done.2
  113.9 1.6 collective-permute-start.3
  116.9 7.0 %all-to-all-start.1 = ((bf16[128,4,1536]{2,1,0:T(4,128)(2,1)}), bf16[128,4,1536]{2,1,0:T(4,128)(2,1)S(1)}, u32[]{:S(2)}, u32[]{:S(2)}) async-start(bf16[128,4,1536]{2,1,0:T(4,128)(2,1)} %reshape.109), calls=%async_computation.1 | async-start | bytes 3145728 | tf_op jit(solution)/shard_map/all_to_all | solution.py:119
  123.9 6.3 %collective-permute-done.3 = bf16[4,1,4,1,80,128]{5,4,3,2,1,0:T(8,128)(2,1)} collective-permute-done((bf16[4,1,4,1,80,128]{5,4,3,2,1,0:T(8,128)(2,1)}, bf16[4,1,4,1,80,128]{5,4,3,2,1,0:T(8,128)(2,1)}, u32[]{:S(2)}, u32[]{:S(2)}) %collective-permute-start.3) | collective-permute-done | bytes 327712 | tf_op jit(solution)/shard_map/ppermute | solution.py:129
  130.3 3.7 %collective-permute-done.1 = bf16[4,1,4,1,80,128]{5,4,3,2,1,0:T(8,128)(2,1)} collective-permute-done((bf16[4,1,4,1,80,128]{5,4,3,2,1,0:T(8,128)(2,1)S(1)}, bf16[4,1,4,1,80,128]{5,4,3,2,1,0:T(8,128)(2,1)}, u32[]{:S(2)}, u32[]{:S(2)}) %collective-permute-start.1) | collective-permute-done | bytes 327712 | tf_op jit(solution)/shard_map/ppermute | solution.py:129
  133.9 1.5 fusion.82
  137.4 1.7 %collective-permute-start.5 = (bf16[4,1,1,1,80,128]{5,4,3,2,1,0:T(8,128)(2,1)}, bf16[4,1,1,1,80,128]{5,4,3,2,1,0:T(8,128)(2,1)}, u32[]{:S(2)}, u32[]{:S(2)}) collective-permute-start(bf16[4,1,1,1,80,128]{5,4,3,2,1,0:T(8,128)(2,1)} %get-tuple-element.35), channel_id=1, source_target_pairs={{0,8},{4,12},{8,0},{12,4},{1,9},{5,13},{9,1},{13,5},{2,10},{6,14},... | collective-permute-start | bytes 245768 | tf_op jit(solution)/shard_map/ppermute | solution.py:129
  139.1 8.2 %collective-permute-done.6 = bf16[4,1,1,1,80,128]{5,4,3,2,1,0:T(8,128)(2,1)S(1)} collective-permute-done((bf16[4,1,1,1,80,128]{5,4,3,2,1,0:T(8,128)(2,1)}, bf16[4,1,1,1,80,128]{5,4,3,2,1,0:T(8,128)(2,1)S(1)}, u32[]{:S(2)}, u32[]{:S(2)}) %collective-permute-start.6) | collective-permute-done | bytes 81952 | tf_op jit(solution)/shard_map/ppermute | solution.py:129
  147.3 2.6 %collective-permute-done.5 = bf16[4,1,1,1,80,128]{5,4,3,2,1,0:T(8,128)(2,1)} collective-permute-done((bf16[4,1,1,1,80,128]{5,4,3,2,1,0:T(8,128)(2,1)}, bf16[4,1,1,1,80,128]{5,4,3,2,1,0:T(8,128)(2,1)}, u32[]{:S(2)}, u32[]{:S(2)}) %collective-permute-start.5) | collective-permute-done | bytes 81952 | tf_op jit(solution)/shard_map/ppermute | solution.py:129
  149.9 1.7 %collective-permute-done.4 = bf16[4,1,1,1,80,128]{5,4,3,2,1,0:T(8,128)(2,1)} collective-permute-done((bf16[4,1,1,1,80,128]{5,4,3,2,1,0:T(8,128)(2,1)}, bf16[4,1,1,1,80,128]{5,4,3,2,1,0:T(8,128)(2,1)}, u32[]{:S(2)}, u32[]{:S(2)}) %collective-permute-start.4) | collective-permute-done | bytes 81952 | tf_op jit(solution)/shard_map/ppermute | solution.py:129
  151.6 1.6 fusion.81
  157.1 2.9 %collective-permute-done.8 = bf16[1,1,1,1,80,128]{5,4,3,2,1,0:T(8,128)(2,1)S(1)} collective-permute-done((bf16[1,1,1,1,80,128]{5,4,3,2,1,0:T(8,128)(2,1)S(1)}, bf16[1,1,1,1,80,128]{5,4,3,2,1,0:T(8,128)(2,1)S(1)}, u32[]{:S(2)}, u32[]{:S(2)}) %collective-permute-start.8) | collective-permute-done | bytes 20512 | tf_op jit(solution)/shard_map/ppermute | solution.py:129
  164.8 1.6 reshape.111
  (81 shorter events, 33.5 us)
Async XLA Ops:
  0.6 65.3 %copy-start = (bf16[768,768]{1,0:T(8,128)(2,1)S(1)}, bf16[768,768]{1,0:T(8,128)(2,1)}, u32[]{:S(2)}) copy-start(bf16[768,768]{1,0:T(8,128)(2,1)} %param.15) | copy-start | bytes 3538948
  1.4 2.8 %copy-start.11 = (s32[1,1,512]{2,1,0:T(1,128)}, s32[1,1,512]{2,1,0:T(1,128)S(1)}, u32[]{:S(2)}) copy-start(s32[1,1,512]{2,1,0:T(1,128)S(1)} %get-tuple-element.44) | copy-start | bytes 6148
  1.4 2.8 %copy-start.13 = (s32[1,1,512]{2,1,0:T(1,128)}, s32[1,1,512]{2,1,0:T(1,128)S(1)}, u32[]{:S(2)}) copy-start(s32[1,1,512]{2,1,0:T(1,128)S(1)} %get-tuple-element.43) | copy-start | bytes 6148
  8.0 11.2 %copy-start.15 = (s32[2,1,128]{2,1,0:T(1,128)S(1)}, s32[2,1,128]{2,1,0:T(1,128)}, u32[]{:S(2)}) copy-start(s32[2,1,128]{2,1,0:T(1,128)} %param.18) | copy-start | bytes 3076
  8.0 43.6 %all-to-all-start = ((bf16[128,4,2304]{2,1,0:T(4,128)(2,1)}), bf16[128,4,2304]{2,1,0:T(4,128)(2,1)S(1)}, u32[]{:S(2)}, u32[]{:S(2)}) async-start(bf16[128,4,2304]{2,1,0:T(4,128)(2,1)} %reshape.104), calls=%async_computation | async-start | bytes 4718592 | tf_op jit(solution)/shard_map/all_to_all | solution.py:42
  21.9 2.0 %copy-start.9 = (s32[1,2048]{1,0:T(1,128)}, s32[1,2048]{1,0:T(1,128)S(1)}, u32[]{:S(2)}) copy-start(s32[1,2048]{1,0:T(1,128)S(1)} %get-tuple-element.41) | copy-start | bytes 24580
  53.6 3.5 %copy-start.5 = (bf16[128,4,768]{2,1,0:T(4,128)(2,1)S(1)}, bf16[128,4,768]{2,1,0:T(4,128)(2,1)}, u32[]{:S(2)}) copy-start(bf16[128,4,768]{2,1,0:T(4,128)(2,1)} %get-tuple-element.25) | copy-start | bytes 2359300
  55.2 10.7 %copy-start.3 = (bf16[512,768]{1,0:T(8,128)(2,1)}, bf16[512,768]{1,0:T(8,128)(2,1)S(1)}, u32[]{:S(2)}) copy-start(bf16[512,768]{1,0:T(8,128)(2,1)S(1)} %reshape.106) | copy-start | bytes 2359300
  57.1 8.9 %copy-start.4 = (bf16[512,768]{1,0:T(8,128)(2,1)}, bf16[512,768]{1,0:T(8,128)(2,1)S(1)}, u32[]{:S(2)}) copy-start(bf16[512,768]{1,0:T(8,128)(2,1)S(1)} %reshape.107) | copy-start | bytes 2359300
  66.0 7.2 %copy-start.6 = (bf16[512,768]{1,0:T(8,128)(2,1)S(1)}, bf16[512,768]{1,0:T(8,128)(2,1)}, u32[]{:S(2)}) copy-start(bf16[512,768]{1,0:T(8,128)(2,1)} %reshape.105) | copy-start | bytes 2359300
  73.2 7.5 %copy-start.10 = (s32[1,2048]{1,0:T(1,128)S(1)}, s32[1,2048]{1,0:T(1,128)}, u32[]{:S(2)}) copy-start(s32[1,2048]{1,0:T(1,128)} %copy-done.9) | copy-start | bytes 24580
  99.2 2.3 %copy-start.1 = (f32[4,2,4,4,80,128]{5,4,3,2,1,0:T(8,128)}, f32[4,2,4,4,80,128]{5,4,3,2,1,0:T(8,128)S(1)}, u32[]{:S(2)}) copy-start(f32[4,2,4,4,80,128]{5,4,3,2,1,0:T(8,128)S(1)} %pad_maximum_fusion) | copy-start | bytes 15728644
  101.5 1.8 %copy-start.7 = (bf16[512,768]{1,0:T(8,128)(2,1)S(1)}, bf16[512,768]{1,0:T(8,128)(2,1)}, u32[]{:S(2)}) copy-start(bf16[512,768]{1,0:T(8,128)(2,1)} %fusion.28) | copy-start | bytes 2359300
  103.3 1.1 copy-start.8
  103.3 5.3 %collective-permute-start = (f32[4,1,4,4,80,128]{5,4,3,2,1,0:T(8,128)}, f32[4,1,4,4,80,128]{5,4,3,2,1,0:T(8,128)}, u32[]{:S(2)}, u32[]{:S(2)}) collective-permute-start(f32[4,1,4,4,80,128]{5,4,3,2,1,0:T(8,128)} %constant_dynamic-slice_fusion.9), channel_id=1, source_target_pairs={{0,16},{16,0},{1,17},{17,1},{2,18},{18,2},{3,19},{19,3},{4,20},{20... | collective-permute-start | bytes 7864328 | tf_op jit(solution)/shard_map/ppermute | solution.py:129
  103.3 1.5 copy-start.16
  111.3 1.5 copy-start.2
  113.9 16.4 %collective-permute-start.3 = (bf16[4,1,4,1,80,128]{5,4,3,2,1,0:T(8,128)(2,1)}, bf16[4,1,4,1,80,128]{5,4,3,2,1,0:T(8,128)(2,1)}, u32[]{:S(2)}, u32[]{:S(2)}) collective-permute-start(bf16[4,1,4,1,80,128]{5,4,3,2,1,0:T(8,128)(2,1)} %get-tuple-element.31), channel_id=1, source_target_pairs={{0,3},{1,0},{2,1},{3,2},{4,7},{5,4},{6,5},{7,6},{8,11},{9,8},{10,9... | collective-permute-start | bytes 983048 | tf_op jit(solution)/shard_map/ppermute | solution.py:129
  115.5 14.8 %collective-permute-start.2 = (bf16[4,1,4,1,80,128]{5,4,3,2,1,0:T(8,128)(2,1)S(1)}, bf16[4,1,4,1,80,128]{5,4,3,2,1,0:T(8,128)(2,1)}, u32[]{:S(2)}, u32[]{:S(2)}) collective-permute-start(bf16[4,1,4,1,80,128]{5,4,3,2,1,0:T(8,128)(2,1)S(1)} %get-tuple-element.32), channel_id=1, source_target_pairs={{0,2},{1,3},{2,0},{3,1},{4,6},{5,7},{6,4},{7,5},{8,10},{9,11},{10,... | collective-permute-start | bytes 983048 | tf_op jit(solution)/shard_map/ppermute | solution.py:129
  116.9 17.0 %collective-permute-start.1 = (bf16[4,1,4,1,80,128]{5,4,3,2,1,0:T(8,128)(2,1)S(1)}, bf16[4,1,4,1,80,128]{5,4,3,2,1,0:T(8,128)(2,1)}, u32[]{:S(2)}, u32[]{:S(2)}) collective-permute-start(bf16[4,1,4,1,80,128]{5,4,3,2,1,0:T(8,128)(2,1)S(1)} %get-tuple-element.30), channel_id=1, source_target_pairs={{0,1},{1,2},{2,3},{3,0},{4,5},{5,6},{6,7},{7,4},{8,9},{9,10},{10,1... | collective-permute-start | bytes 983048 | tf_op jit(solution)/shard_map/ppermute | solution.py:129
  116.9 46.5 %all-to-all-start.1 = ((bf16[128,4,1536]{2,1,0:T(4,128)(2,1)}), bf16[128,4,1536]{2,1,0:T(4,128)(2,1)S(1)}, u32[]{:S(2)}, u32[]{:S(2)}) async-start(bf16[128,4,1536]{2,1,0:T(4,128)(2,1)} %reshape.109), calls=%async_computation.1 | async-start | bytes 3145728 | tf_op jit(solution)/shard_map/all_to_all | solution.py:119
  135.5 31.0 %copy-start.14 = (s32[1,1,512]{2,1,0:T(1,128)S(1)}, s32[1,1,512]{2,1,0:T(1,128)}, u32[]{:S(2)}) copy-start(s32[1,1,512]{2,1,0:T(1,128)} %copy-done.13) | copy-start | bytes 6148
  136.2 11.1 %collective-permute-start.6 = (bf16[4,1,1,1,80,128]{5,4,3,2,1,0:T(8,128)(2,1)}, bf16[4,1,1,1,80,128]{5,4,3,2,1,0:T(8,128)(2,1)S(1)}, u32[]{:S(2)}, u32[]{:S(2)}) collective-permute-start(bf16[4,1,1,1,80,128]{5,4,3,2,1,0:T(8,128)(2,1)} %get-tuple-element.34), channel_id=1, source_target_pairs={{0,12},{4,0},{8,4},{12,8},{1,13},{5,1},{9,5},{13,9},{2,14},{6,2},{... | collective-permute-start | bytes 245768 | tf_op jit(solution)/shard_map/ppermute | solution.py:129
  137.4 12.5 %collective-permute-start.5 = (bf16[4,1,1,1,80,128]{5,4,3,2,1,0:T(8,128)(2,1)}, bf16[4,1,1,1,80,128]{5,4,3,2,1,0:T(8,128)(2,1)}, u32[]{:S(2)}, u32[]{:S(2)}) collective-permute-start(bf16[4,1,1,1,80,128]{5,4,3,2,1,0:T(8,128)(2,1)} %get-tuple-element.35), channel_id=1, source_target_pairs={{0,8},{4,12},{8,0},{12,4},{1,9},{5,13},{9,1},{13,5},{2,10},{6,14},... | collective-permute-start | bytes 245768 | tf_op jit(solution)/shard_map/ppermute | solution.py:129
  139.1 12.5 %collective-permute-start.4 = (bf16[4,1,1,1,80,128]{5,4,3,2,1,0:T(8,128)(2,1)}, bf16[4,1,1,1,80,128]{5,4,3,2,1,0:T(8,128)(2,1)}, u32[]{:S(2)}, u32[]{:S(2)}) collective-permute-start(bf16[4,1,1,1,80,128]{5,4,3,2,1,0:T(8,128)(2,1)} %get-tuple-element.33), channel_id=1, source_target_pairs={{0,4},{4,8},{8,12},{12,0},{1,5},{5,9},{9,13},{13,1},{2,6},{6,10},{... | collective-permute-start | bytes 245768 | tf_op jit(solution)/shard_map/ppermute | solution.py:129
  153.3 3.8 %collective-permute-start.9 = (bf16[1,1,1,1,80,128]{5,4,3,2,1,0:T(8,128)(2,1)S(1)}, bf16[1,1,1,1,80,128]{5,4,3,2,1,0:T(8,128)(2,1)S(1)}, u32[]{:S(2)}, u32[]{:S(2)}) collective-permute-start(bf16[1,1,1,1,80,128]{5,4,3,2,1,0:T(8,128)(2,1)S(1)} %get-tuple-element.37), channel_id=1, source_target_pairs={{0,96},{32,0},{64,32},{96,64},{1,97},{33,1},{65,33},{97,65},{2,98}... | collective-permute-start | bytes 61448 | tf_op jit(solution)/shard_map/ppermute | solution.py:129
  154.7 5.3 %collective-permute-start.8 = (bf16[1,1,1,1,80,128]{5,4,3,2,1,0:T(8,128)(2,1)S(1)}, bf16[1,1,1,1,80,128]{5,4,3,2,1,0:T(8,128)(2,1)S(1)}, u32[]{:S(2)}, u32[]{:S(2)}) collective-permute-start(bf16[1,1,1,1,80,128]{5,4,3,2,1,0:T(8,128)(2,1)S(1)} %get-tuple-element.38), channel_id=1, source_target_pairs={{0,64},{32,96},{64,0},{96,32},{1,65},{33,97},{65,1},{97,33},{2,66}... | collective-permute-start | bytes 61448 | tf_op jit(solution)/shard_map/ppermute | solution.py:129
  155.8 5.0 %collective-permute-start.7 = (bf16[1,1,1,1,80,128]{5,4,3,2,1,0:T(8,128)(2,1)S(1)}, bf16[1,1,1,1,80,128]{5,4,3,2,1,0:T(8,128)(2,1)S(1)}, u32[]{:S(2)}, u32[]{:S(2)}) collective-permute-start(bf16[1,1,1,1,80,128]{5,4,3,2,1,0:T(8,128)(2,1)S(1)} %get-tuple-element.36), channel_id=1, source_target_pairs={{0,32},{32,64},{64,96},{96,0},{1,33},{33,65},{65,97},{97,1},{2,34}... | collective-permute-start | bytes 61448 | tf_op jit(solution)/shard_map/ppermute | solution.py:129
  164.8 3.1 %copy-start.12 = (s32[1,1,512]{2,1,0:T(1,128)S(1)}, s32[1,1,512]{2,1,0:T(1,128)}, u32[]{:S(2)}) copy-start(s32[1,1,512]{2,1,0:T(1,128)} %copy-done.11) | copy-start | bytes 6148
  164.8 3.1 %copy-start.17 = (bf16[256,768]{1,0:T(8,128)(2,1)S(1)}, bf16[256,768]{1,0:T(8,128)(2,1)}, u32[]{:S(2)}) copy-start(bf16[256,768]{1,0:T(8,128)(2,1)} %param.13) | copy-start | bytes 1179652

commit v8 on v7

--- a/solution.py
+++ b/solution.py
@@ -43,9 +43,6 @@
     constraint_mirror_rows = incoming[:, :, :embedding_width]
     variable_mirror_rows = incoming[:, :, embedding_width : 2 * embedding_width]
     cotangent_mirror_rows = incoming[:, :, 2 * embedding_width :]
-    constraint_mirror_rows = constraint_mirror_rows.reshape(replica_rows, embedding_width)
-    variable_mirror_rows = variable_mirror_rows.reshape(replica_rows, embedding_width)
-    cotangent_mirror_rows = cotangent_mirror_rows.reshape(replica_rows, embedding_width)
     slot_pos = lax.broadcasted_iota(jnp.int32, (2, replica_rows), 1) % slot_cap
     slot_live = jnp.where(
         slot_pos < jnp.repeat(recv_count[:, 0], slot_cap, axis=1), 1.0, 0.0
@@ -55,10 +52,17 @@
     live_con = jnp.dot(table_con, slot_live[0], preferred_element_type=jnp.float32)
     live_var = jnp.dot(table_var, slot_live[1], preferred_element_type=jnp.float32)
     edge_active_mask = live_con * live_var
-    edge_con = pick_rows(table_con, constraint_mirror_rows)
-    edge_var = pick_rows(table_var, variable_mirror_rows)
-    upstream_gradient = jnp.dot(
-        table_var, cotangent_mirror_rows, preferred_element_type=jnp.float32
+    slot_dims = (((1, 2), (0, 1)), ((), ()))
+    table_con3 = table_con.reshape(-1, device_count, slot_cap)
+    table_var3 = table_var.reshape(-1, device_count, slot_cap)
+    edge_con = lax.dot_general(
+        table_con3, constraint_mirror_rows, slot_dims, preferred_element_type=jnp.float32
+    ).astype(jnp.bfloat16)
+    edge_var = lax.dot_general(
+        table_var3, variable_mirror_rows, slot_dims, preferred_element_type=jnp.float32
+    ).astype(jnp.bfloat16)
+    upstream_gradient = lax.dot_general(
+        table_var3, cotangent_mirror_rows, slot_dims, preferred_element_type=jnp.float32
     )
     pre_act = (
         jnp.dot(edge_con, constraint_weight, preferred_element_type=jnp.float32)
@@ -88,14 +92,14 @@
     )
     constraint_term = lax.dot_general(
         constraint_mirror_rows,
-        constraint_projection_gradient,
-        sum_dims,
+        constraint_projection_gradient.reshape(device_count, slot_cap, embedding_width),
+        (((0, 1), (0, 1)), ((), ())),
         preferred_element_type=jnp.float32,
     )
     variable_term = lax.dot_general(
         variable_mirror_rows,
-        variable_projection_gradient,
-        sum_dims,
+        variable_projection_gradient.reshape(device_count, slot_cap, embedding_width),
+        (((0, 1), (0, 1)), ((), ())),
         preferred_element_type=jnp.float32,
     )
     term_bias = jnp.sum(edge_delta.astype(jnp.float32), axis=0)
@@ -130,15 +134,15 @@
         summed = total
     summed = summed.reshape(-1, lanes)
     grad_con = lax.dot_general(
-        select_con,
-        home_con.reshape(replica_rows, embedding_width),
-        sum_dims,
+        select_con.reshape(device_count, slot_cap, -1),
+        home_con,
+        (((0, 1), (0, 1)), ((), ())),
         preferred_element_type=jnp.float32,
     )
     grad_var = lax.dot_general(
-        select_var,
-        home_var.reshape(replica_rows, embedding_width),
-        sum_dims,
+        select_var.reshape(device_count, slot_cap, -1),
+        home_var,
+        (((0, 1), (0, 1)), ((), ())),
         preferred_element_type=jnp.float32,
     )
     grad_var = variable_cotangent.astype(jnp.float32) + grad_var

time: 170 us -> 166 us (0.976)
  local copies, waits for them, and re-layouts: 30.8 us -> 27.4 us
    reshape x5 -> x2, local copies, waits for them, and re-layouts: 6.41 us -> 3.46 us  [the longest x1 2.37 us: on_device(): constraint_projection_gradient.reshape(device_count, slot_cap, embedding_...]
    unnamed x36 -> x34, local copies, waits for them, and re-layouts: 4.52 us -> 4.58 us
  transfers between devices with their start and end apart: 12 -> 12, of which waited for: 10 -> 10; matrix products, arithmetic and copies ran while one was open for 8% -> 9% of each run, Pallas kernels for 0% -> 0%
where the time goes in v8:
time: 166 us; the launch traced here: 165 us
  waiting for transfers between devices  55.6 us (33%)
  matrix products  43 us (26%)
  local copies, waits for them, and re-layouts  27.4 us (17%)
  starting transfers between devices  26.9 us (16%)
  other arithmetic  11.5 us (7%)
    ppermute x10, waiting for transfers between devices, on_device(): total = total + lax.ppermute(chunk, axis_name, pairs).astype(jnp.float32)  28.4 us
    all_to_all x1, waiting for transfers between devices, on_device(): lax.all_to_all(outgoing, DEVICE_AXES, split_axis=0, concat_axis=0, tiled=...  27.1 us
    all_to_all x1, starting transfers between devices, on_device(): lax.all_to_all(outgoing, DEVICE_AXES, split_axis=0, concat_axis=0, tiled=...  11.2 us
    ppermute x10, starting transfers between devices, on_device(): total = total + lax.ppermute(chunk, axis_name, pairs).astype(jnp.float32)  8.79 us
    dot_general x1, matrix products, on_device(): jnp.dot(edge_con, constraint_weight, preferred_element_type=jnp.float32)  8.66 us
    dot_general x1, matrix products, on_device(): lax.dot_general(table_var3, cotangent_mirror_rows, slot_dims, preferred_e...  7.86 us
    dot_general x1, matrix products, on_device(): jnp.dot(edge_var, variable_weight, preferred_element_type=jnp.float32)  7.04 us
    all_to_all x1, starting transfers between devices, on_device(): lax.all_to_all(backward, DEVICE_AXES, split_axis=0, concat_axis=0, tiled=...  6.98 us
  transfers between devices with their start and end apart: 12, of which 10 were waited for; matrix products, arithmetic and copies ran while one was open for 9% of the time, Pallas kernels for 0%

profile of v8, /device:TPU:0, one launch (start us, length us, event | category | flops | bytes accessed | tf_op | source)
XLA Modules:
  0.0 165.4 jit_solution(1725650726544047749)
XLA Ops:
  5.9 2.2 %reshape.133 = bf16[128,4,2304]{2,1,0:T(4,128)(2,1)} reshape(bf16[512,2304]{1,0:T(8,128)(2,1)S(1)} %pad_maximum_fusion.1) | data formatting | bytes 4718592 | tf_op jit(solution)/shard_map/reshape | solution.py:39
  8.0 11.2 %all-to-all-start = ((bf16[128,4,2304]{2,1,0:T(4,128)(2,1)}), bf16[128,4,2304]{2,1,0:T(4,128)(2,1)S(1)}, u32[]{:S(2)}, u32[]{:S(2)}) async-start(bf16[128,4,2304]{2,1,0:T(4,128)(2,1)} %reshape.133), calls=%async_computation | async-start | bytes 4718592 | tf_op jit(solution)/shard_map/all_to_all | solution.py:42
  24.5 27.1 %all-to-all-done = bf16[128,4,2304]{2,1,0:T(4,128)(2,1)S(1)} async-done(((bf16[128,4,2304]{2,1,0:T(4,128)(2,1)}), bf16[128,4,2304]{2,1,0:T(4,128)(2,1)S(1)}, u32[]{:S(2)}, u32[]{:S(2)}) %all-to-all-start) | async-done | bytes 2359328 | tf_op jit(solution)/shard_map/all_to_all | solution.py:42
  51.6 2.0 %fusion.99 = (bf16[128,4,768]{2,1,0:T(4,128)(2,1)}, bf16[128,4,768]{2,1,0:T(4,128)(2,1)}, bf16[128,4,768]{2,1,0:T(4,128)(2,1)}) fusion(bf16[128,4,2304]{2,1,0:T(4,128)(2,1)S(1)} %all-to-all-done), kind=kLoop, calls=%fused_computation.147 | loop fusion | bytes 4718592 | tf_op jit(solution)/shard_map/slice | solution.py:45
  53.6 8.7 %fusion.35 = f32[2048,768]{1,0:T(8,128)} fusion(bf16[768,768]{1,0:T(8,128)(2,1)} %param.14, s32[128,4]{0,1:T(4,128)} %multiply_add_fusion, s32[2048]{0:T(1024)} %bitcast.63, bf16[128,4,768]{2,1,0:T(4,128)(2,1)} %get-tuple-element.28), kind=kOutput, calls=%fused_computation.58 | convolution fusion | flops 4031250432 | bytes 8267776 | tf_op jit(solution)/shard_map/dot_general | solution.py:68
  62.3 7.0 %fusion.36 = f32[2048,768]{1,0:T(8,128)} fusion(bf16[768,768]{1,0:T(8,128)(2,1)S(1)} %copy-done, s32[128,4]{0,1:T(4,128)S(1)} %copy-done.12, s32[2048]{0:T(1024)S(1)} %bitcast.66, bf16[128,4,768]{2,1,0:T(4,128)(2,1)S(1)} %copy-done.3), kind=kOutput, calls=%fused_computation.59 | convolution fusion | flops 4031250432 | bytes 8267776 | tf_op jit(solution)/shard_map/dot_general | solution.py:69
  69.4 7.9 %convert_reduce_fusion = (f32[768]{0:T(1024)S(1)}, bf16[2048,768]{1,0:T(8,128)(2,1)S(1)}) fusion(f32[2048]{0:T(1024)S(1)} %mul.41, f32[768]{0:T(1024)S(1)} %copy-done.16, f32[2048,768]{1,0:T(8,128)} %fusion.35, f32[2048,768]{1,0:T(8,128)} %fusion.36, bf16[128,4,768]{2,1,0:T(4,128)(2,1)S(1)} %copy-done.4, s32[128,4]{0,1:T(4,128)S(1)} %copy-done.12, ...), kind=kOutput, calls=%fused_computation.5 | convolution fusion | flops 1635777792 | bytes 16539648 | tf_op jit(solution)/shard_map/dot_general | solution.py:64
  77.2 2.0 %fusion.30 = bf16[512,768]{1,0:T(8,128)(2,1)S(1)} fusion(bf16[2048,768]{1,0:T(8,128)(2,1)S(1)} %get-tuple-element.48, s32[2048]{0:T(1024)S(1)} %bitcast.68), kind=kOutput, calls=%fused_computation.48 | convolution fusion | flops 1614151680 | bytes 3940352 | tf_op jit(solution)/shard_map/dot_general | solution.py:81
  79.3 2.9 %fusion.31 = bf16[512,768]{1,0:T(8,128)(2,1)} fusion(bf16[2048,768]{1,0:T(8,128)(2,1)S(1)} %get-tuple-element.48, s32[2048]{0:T(1024)S(1)} %bitcast.64), kind=kOutput, calls=%fused_computation.49 | convolution fusion | flops 1614151680 | bytes 3940352 | tf_op jit(solution)/shard_map/dot_general | solution.py:78
  84.1 2.2 %convolution_bitcast_fusion = f32[768,768]{1,0:T(8,128)S(1)} fusion(bf16[128,4,768]{2,1,0:T(4,128)(2,1)} %reshape.137, bf16[128,4,768]{2,1,0:T(4,128)(2,1)} %get-tuple-element.29), kind=kOutput, calls=%fused_computation.43 | convolution fusion | flops 603979776 | bytes 3932160 | tf_op jit(solution)/shard_map/dot_general | solution.py:99
  86.3 1.7 %concatenate.21 = f32[4,2,4,4,36,128]{5,4,3,2,1,0:T(8,128)} reshape(f32[768,768]{1,0:T(8,128)S(1)} %convolution_bitcast_fusion) | data formatting | bytes 4718592 | tf_op jit(solution)/shard_map/concatenate | solution.py:111
  88.0 2.4 %reshape.136 = bf16[128,4,768]{2,1,0:T(4,128)(2,1)} reshape(bf16[512,768]{1,0:T(8,128)(2,1)} %fusion.31) | data formatting | bytes 1572864 | tf_op jit(solution)/shard_map/reshape | solution.py:95
  90.3 2.2 %convolution_bitcast_fusion.1 = f32[768,768]{1,0:T(8,128)S(1)} fusion(bf16[128,4,768]{2,1,0:T(4,128)(2,1)} %reshape.136, bf16[128,4,768]{2,1,0:T(4,128)(2,1)} %get-tuple-element.28), kind=kOutput, calls=%fused_computation.44 | convolution fusion | flops 603979776 | bytes 3932160 | tf_op jit(solution)/shard_map/dot_general | solution.py:93
  92.5 1.7 %concatenate.20 = f32[4,2,4,4,36,128]{5,4,3,2,1,0:T(8,128)} reshape(f32[768,768]{1,0:T(8,128)S(1)} %convolution_bitcast_fusion.1) | data formatting | bytes 4718592 | tf_op jit(solution)/shard_map/concatenate | solution.py:111
  95.1 3.1 %pad_maximum_fusion = f32[4,2,4,4,80,128]{5,4,3,2,1,0:T(8,128)S(1)} fusion(f32[4,2,4,4,8,128]{5,4,3,2,1,0:T(8,128)S(1)} %bitcast.57, f32[4,2,4,4,36,128]{5,4,3,2,1,0:T(8,128)} %concatenate.21, f32[4,2,4,4,36,128]{5,4,3,2,1,0:T(8,128)} %concatenate.20), kind=kLoop, calls=%fused_computation.6 | loop fusion | flops 2621440 | bytes 10485760 | tf_op jit(solution)/shard_map/concatenate | solution.py:111
  98.3 2.3 %copy-done.1 = f32[4,2,4,4,80,128]{5,4,3,2,1,0:T(8,128)} copy-done((f32[4,2,4,4,80,128]{5,4,3,2,1,0:T(8,128)}, f32[4,2,4,4,80,128]{5,4,3,2,1,0:T(8,128)S(1)}, u32[]{:S(2)}) %copy-start.1) | copy-done | bytes 5242904
  100.6 1.8 %constant_dynamic-slice_fusion.9 = f32[4,1,4,4,80,128]{5,4,3,2,1,0:T(8,128)} fusion(f32[4,2,4,4,80,128]{5,4,3,2,1,0:T(8,128)S(1)} %pad_maximum_fusion, s32[]{:T(128)S(6)} %select_n.132), kind=kLoop, calls=%fused_computation.108 | loop fusion | bytes 5242884 | tf_op jit(solution)/shard_map/dynamic_slice | solution.py:131
  106.2 1.5 collective-permute-done
  107.6 2.8 %dynamic-slice_add_fusion = f32[4,1,4,4,80,128]{5,4,3,2,1,0:T(8,128)S(1)} fusion(f32[4,1,4,4,80,128]{5,4,3,2,1,0:T(8,128)} %collective-permute-done, f32[4,2,4,4,80,128]{5,4,3,2,1,0:T(8,128)} %copy-done.1, s32[]{:T(128)S(6)} %select_n.130), kind=kLoop, calls=%fused_computation.17 | loop fusion | flops 655360 | bytes 7864324 | tf_op jit(solution)/shard_map/add | solution.py:133
  110.5 1.5 copy-done.2
  113.0 1.6 collective-permute-start.3
  116.1 7.0 %all-to-all-start.1 = ((bf16[128,4,1536]{2,1,0:T(4,128)(2,1)}), bf16[128,4,1536]{2,1,0:T(4,128)(2,1)S(1)}, u32[]{:S(2)}, u32[]{:S(2)}) async-start(bf16[128,4,1536]{2,1,0:T(4,128)(2,1)} %reshape.135), calls=%async_computation.1 | async-start | bytes 3145728 | tf_op jit(solution)/shard_map/all_to_all | solution.py:123
  123.1 6.4 %collective-permute-done.3 = bf16[4,1,4,1,80,128]{5,4,3,2,1,0:T(8,128)(2,1)} collective-permute-done((bf16[4,1,4,1,80,128]{5,4,3,2,1,0:T(8,128)(2,1)}, bf16[4,1,4,1,80,128]{5,4,3,2,1,0:T(8,128)(2,1)}, u32[]{:S(2)}, u32[]{:S(2)}) %collective-permute-start.3) | collective-permute-done | bytes 327712 | tf_op jit(solution)/shard_map/ppermute | solution.py:133
  129.5 3.6 %collective-permute-done.1 = bf16[4,1,4,1,80,128]{5,4,3,2,1,0:T(8,128)(2,1)} collective-permute-done((bf16[4,1,4,1,80,128]{5,4,3,2,1,0:T(8,128)(2,1)S(1)}, bf16[4,1,4,1,80,128]{5,4,3,2,1,0:T(8,128)(2,1)}, u32[]{:S(2)}, u32[]{:S(2)}) %collective-permute-start.1) | collective-permute-done | bytes 327712 | tf_op jit(solution)/shard_map/ppermute | solution.py:133
  133.1 1.5 fusion.98
  136.6 1.7 %collective-permute-start.5 = (bf16[4,1,1,1,80,128]{5,4,3,2,1,0:T(8,128)(2,1)}, bf16[4,1,1,1,80,128]{5,4,3,2,1,0:T(8,128)(2,1)}, u32[]{:S(2)}, u32[]{:S(2)}) collective-permute-start(bf16[4,1,1,1,80,128]{5,4,3,2,1,0:T(8,128)(2,1)} %get-tuple-element.37), channel_id=1, source_target_pairs={{0,8},{4,12},{8,0},{12,4},{1,9},{5,13},{9,1},{13,5},{2,10},{6,14},... | collective-permute-start | bytes 245768 | tf_op jit(solution)/shard_map/ppermute | solution.py:133
  138.2 8.2 %collective-permute-done.6 = bf16[4,1,1,1,80,128]{5,4,3,2,1,0:T(8,128)(2,1)S(1)} collective-permute-done((bf16[4,1,1,1,80,128]{5,4,3,2,1,0:T(8,128)(2,1)}, bf16[4,1,1,1,80,128]{5,4,3,2,1,0:T(8,128)(2,1)S(1)}, u32[]{:S(2)}, u32[]{:S(2)}) %collective-permute-start.6) | collective-permute-done | bytes 81952 | tf_op jit(solution)/shard_map/ppermute | solution.py:133
  146.5 2.7 %collective-permute-done.5 = bf16[4,1,1,1,80,128]{5,4,3,2,1,0:T(8,128)(2,1)} collective-permute-done((bf16[4,1,1,1,80,128]{5,4,3,2,1,0:T(8,128)(2,1)}, bf16[4,1,1,1,80,128]{5,4,3,2,1,0:T(8,128)(2,1)}, u32[]{:S(2)}, u32[]{:S(2)}) %collective-permute-start.5) | collective-permute-done | bytes 81952 | tf_op jit(solution)/shard_map/ppermute | solution.py:133
  149.2 1.6 collective-permute-done.4
  150.8 1.6 fusion.97
  152.4 1.5 collective-permute-start.9
  156.3 2.9 %collective-permute-done.8 = bf16[1,1,1,1,80,128]{5,4,3,2,1,0:T(8,128)(2,1)S(1)} collective-permute-done((bf16[1,1,1,1,80,128]{5,4,3,2,1,0:T(8,128)(2,1)S(1)}, bf16[1,1,1,1,80,128]{5,4,3,2,1,0:T(8,128)(2,1)S(1)}, u32[]{:S(2)}, u32[]{:S(2)}) %collective-permute-start.8) | collective-permute-done | bytes 20512 | tf_op jit(solution)/shard_map/ppermute | solution.py:133
  (81 shorter events, 29.9 us)
Async XLA Ops:
  0.6 61.6 %copy-start = (bf16[768,768]{1,0:T(8,128)(2,1)S(1)}, bf16[768,768]{1,0:T(8,128)(2,1)}, u32[]{:S(2)}) copy-start(bf16[768,768]{1,0:T(8,128)(2,1)} %param.15) | copy-start | bytes 3538948
  8.0 11.2 %copy-start.13 = (s32[2,1,128]{2,1,0:T(1,128)S(1)}, s32[2,1,128]{2,1,0:T(1,128)}, u32[]{:S(2)}) copy-start(s32[2,1,128]{2,1,0:T(1,128)} %param.18) | copy-start | bytes 3076
  8.0 43.6 %all-to-all-start = ((bf16[128,4,2304]{2,1,0:T(4,128)(2,1)}), bf16[128,4,2304]{2,1,0:T(4,128)(2,1)S(1)}, u32[]{:S(2)}, u32[]{:S(2)}) async-start(bf16[128,4,2304]{2,1,0:T(4,128)(2,1)} %reshape.133), calls=%async_computation | async-start | bytes 4718592 | tf_op jit(solution)/shard_map/all_to_all | solution.py:42
  21.9 2.0 %copy-start.8 = (s32[1,2048]{1,0:T(1,128)}, s32[1,2048]{1,0:T(1,128)S(1)}, u32[]{:S(2)}) copy-start(s32[1,2048]{1,0:T(1,128)S(1)} %get-tuple-element.44) | copy-start | bytes 24580
  21.9 2.0 %copy-start.10 = (s32[1,2048]{1,0:T(1,128)}, s32[1,2048]{1,0:T(1,128)S(1)}, u32[]{:S(2)}) copy-start(s32[1,2048]{1,0:T(1,128)S(1)} %get-tuple-element.43) | copy-start | bytes 24580
  53.6 8.7 %copy-start.3 = (bf16[128,4,768]{2,1,0:T(4,128)(2,1)S(1)}, bf16[128,4,768]{2,1,0:T(4,128)(2,1)}, u32[]{:S(2)}) copy-start(bf16[128,4,768]{2,1,0:T(4,128)(2,1)} %get-tuple-element.29) | copy-start | bytes 2359300
  53.6 8.7 %copy-start.11 = (s32[1,2048]{1,0:T(1,128)S(1)}, s32[1,2048]{1,0:T(1,128)}, u32[]{:S(2)}) copy-start(s32[1,2048]{1,0:T(1,128)} %copy-done.10) | copy-start | bytes 24580
  53.6 8.7 %copy-start.12 = (s32[128,4]{0,1:T(4,128)S(1)}, s32[128,4]{0,1:T(4,128)}, u32[]{:S(2)}) copy-start(s32[128,4]{0,1:T(4,128)} %multiply_add_fusion) | copy-start | bytes 6148
  62.3 7.1 %copy-start.4 = (bf16[128,4,768]{2,1,0:T(4,128)(2,1)S(1)}, bf16[128,4,768]{2,1,0:T(4,128)(2,1)}, u32[]{:S(2)}) copy-start(bf16[128,4,768]{2,1,0:T(4,128)(2,1)} %get-tuple-element.27) | copy-start | bytes 2359300
  62.3 7.1 %copy-start.16 = (f32[768]{0:T(1024)S(1)}, f32[768]{0:T(1024)}, u32[]{:S(2)}) copy-start(f32[768]{0:T(1024)} %param.16) | copy-start | bytes 9220
  77.2 2.1 %copy-start.9 = (s32[1,2048]{1,0:T(1,128)S(1)}, s32[1,2048]{1,0:T(1,128)}, u32[]{:S(2)}) copy-start(s32[1,2048]{1,0:T(1,128)} %copy-done.8) | copy-start | bytes 24580
  79.3 3.7 %copy-start.5 = (bf16[512,768]{1,0:T(8,128)(2,1)}, bf16[512,768]{1,0:T(8,128)(2,1)S(1)}, u32[]{:S(2)}) copy-start(bf16[512,768]{1,0:T(8,128)(2,1)S(1)} %fusion.30) | copy-start | bytes 2359300
  98.3 2.3 %copy-start.1 = (f32[4,2,4,4,80,128]{5,4,3,2,1,0:T(8,128)}, f32[4,2,4,4,80,128]{5,4,3,2,1,0:T(8,128)S(1)}, u32[]{:S(2)}) copy-start(f32[4,2,4,4,80,128]{5,4,3,2,1,0:T(8,128)S(1)} %pad_maximum_fusion) | copy-start | bytes 15728644
  100.6 1.8 %copy-start.6 = (bf16[512,768]{1,0:T(8,128)(2,1)S(1)}, bf16[512,768]{1,0:T(8,128)(2,1)}, u32[]{:S(2)}) copy-start(bf16[512,768]{1,0:T(8,128)(2,1)} %copy-done.5) | copy-start | bytes 2359300
  102.4 1.1 copy-start.7
  102.4 5.3 %collective-permute-start = (f32[4,1,4,4,80,128]{5,4,3,2,1,0:T(8,128)}, f32[4,1,4,4,80,128]{5,4,3,2,1,0:T(8,128)}, u32[]{:S(2)}, u32[]{:S(2)}) collective-permute-start(f32[4,1,4,4,80,128]{5,4,3,2,1,0:T(8,128)} %constant_dynamic-slice_fusion.9), channel_id=1, source_target_pairs={{0,16},{16,0},{1,17},{17,1},{2,18},{18,2},{3,19},{19,3},{4,20},{20... | collective-permute-start | bytes 7864328 | tf_op jit(solution)/shard_map/ppermute | solution.py:133
  102.4 1.5 copy-start.14
  110.5 1.5 copy-start.2
  113.0 16.4 %collective-permute-start.3 = (bf16[4,1,4,1,80,128]{5,4,3,2,1,0:T(8,128)(2,1)}, bf16[4,1,4,1,80,128]{5,4,3,2,1,0:T(8,128)(2,1)}, u32[]{:S(2)}, u32[]{:S(2)}) collective-permute-start(bf16[4,1,4,1,80,128]{5,4,3,2,1,0:T(8,128)(2,1)} %get-tuple-element.33), channel_id=1, source_target_pairs={{0,3},{1,0},{2,1},{3,2},{4,7},{5,4},{6,5},{7,6},{8,11},{9,8},{10,9... | collective-permute-start | bytes 983048 | tf_op jit(solution)/shard_map/ppermute | solution.py:133
  114.6 14.8 %collective-permute-start.2 = (bf16[4,1,4,1,80,128]{5,4,3,2,1,0:T(8,128)(2,1)S(1)}, bf16[4,1,4,1,80,128]{5,4,3,2,1,0:T(8,128)(2,1)}, u32[]{:S(2)}, u32[]{:S(2)}) collective-permute-start(bf16[4,1,4,1,80,128]{5,4,3,2,1,0:T(8,128)(2,1)S(1)} %get-tuple-element.34), channel_id=1, source_target_pairs={{0,2},{1,3},{2,0},{3,1},{4,6},{5,7},{6,4},{7,5},{8,10},{9,11},{10,... | collective-permute-start | bytes 983048 | tf_op jit(solution)/shard_map/ppermute | solution.py:133
  116.1 17.0 %collective-permute-start.1 = (bf16[4,1,4,1,80,128]{5,4,3,2,1,0:T(8,128)(2,1)S(1)}, bf16[4,1,4,1,80,128]{5,4,3,2,1,0:T(8,128)(2,1)}, u32[]{:S(2)}, u32[]{:S(2)}) collective-permute-start(bf16[4,1,4,1,80,128]{5,4,3,2,1,0:T(8,128)(2,1)S(1)} %get-tuple-element.32), channel_id=1, source_target_pairs={{0,1},{1,2},{2,3},{3,0},{4,5},{5,6},{6,7},{7,4},{8,9},{9,10},{10,1... | collective-permute-start | bytes 983048 | tf_op jit(solution)/shard_map/ppermute | solution.py:133
  116.1 46.6 %all-to-all-start.1 = ((bf16[128,4,1536]{2,1,0:T(4,128)(2,1)}), bf16[128,4,1536]{2,1,0:T(4,128)(2,1)S(1)}, u32[]{:S(2)}, u32[]{:S(2)}) async-start(bf16[128,4,1536]{2,1,0:T(4,128)(2,1)} %reshape.135), calls=%async_computation.1 | async-start | bytes 3145728 | tf_op jit(solution)/shard_map/all_to_all | solution.py:123
  135.3 11.1 %collective-permute-start.6 = (bf16[4,1,1,1,80,128]{5,4,3,2,1,0:T(8,128)(2,1)}, bf16[4,1,1,1,80,128]{5,4,3,2,1,0:T(8,128)(2,1)S(1)}, u32[]{:S(2)}, u32[]{:S(2)}) collective-permute-start(bf16[4,1,1,1,80,128]{5,4,3,2,1,0:T(8,128)(2,1)} %get-tuple-element.36), channel_id=1, source_target_pairs={{0,12},{4,0},{8,4},{12,8},{1,13},{5,1},{9,5},{13,9},{2,14},{6,2},{... | collective-permute-start | bytes 245768 | tf_op jit(solution)/shard_map/ppermute | solution.py:133
  136.6 12.6 %collective-permute-start.5 = (bf16[4,1,1,1,80,128]{5,4,3,2,1,0:T(8,128)(2,1)}, bf16[4,1,1,1,80,128]{5,4,3,2,1,0:T(8,128)(2,1)}, u32[]{:S(2)}, u32[]{:S(2)}) collective-permute-start(bf16[4,1,1,1,80,128]{5,4,3,2,1,0:T(8,128)(2,1)} %get-tuple-element.37), channel_id=1, source_target_pairs={{0,8},{4,12},{8,0},{12,4},{1,9},{5,13},{9,1},{13,5},{2,10},{6,14},... | collective-permute-start | bytes 245768 | tf_op jit(solution)/shard_map/ppermute | solution.py:133
  138.2 12.5 %collective-permute-start.4 = (bf16[4,1,1,1,80,128]{5,4,3,2,1,0:T(8,128)(2,1)}, bf16[4,1,1,1,80,128]{5,4,3,2,1,0:T(8,128)(2,1)}, u32[]{:S(2)}, u32[]{:S(2)}) collective-permute-start(bf16[4,1,1,1,80,128]{5,4,3,2,1,0:T(8,128)(2,1)} %get-tuple-element.35), channel_id=1, source_target_pairs={{0,4},{4,8},{8,12},{12,0},{1,5},{5,9},{9,13},{13,1},{2,6},{6,10},{... | collective-permute-start | bytes 245768 | tf_op jit(solution)/shard_map/ppermute | solution.py:133
  152.4 11.9 %copy-start.15 = (bf16[256,768]{1,0:T(8,128)(2,1)S(1)}, bf16[256,768]{1,0:T(8,128)(2,1)}, u32[]{:S(2)}) copy-start(bf16[256,768]{1,0:T(8,128)(2,1)} %param.13) | copy-start | bytes 1179652
  152.4 3.9 %collective-permute-start.9 = (bf16[1,1,1,1,80,128]{5,4,3,2,1,0:T(8,128)(2,1)S(1)}, bf16[1,1,1,1,80,128]{5,4,3,2,1,0:T(8,128)(2,1)S(1)}, u32[]{:S(2)}, u32[]{:S(2)}) collective-permute-start(bf16[1,1,1,1,80,128]{5,4,3,2,1,0:T(8,128)(2,1)S(1)} %get-tuple-element.39), channel_id=1, source_target_pairs={{0,96},{32,0},{64,32},{96,64},{1,97},{33,1},{65,33},{97,65},{2,98}... | collective-permute-start | bytes 61448 | tf_op jit(solution)/shard_map/ppermute | solution.py:133
  153.9 5.3 %collective-permute-start.8 = (bf16[1,1,1,1,80,128]{5,4,3,2,1,0:T(8,128)(2,1)S(1)}, bf16[1,1,1,1,80,128]{5,4,3,2,1,0:T(8,128)(2,1)S(1)}, u32[]{:S(2)}, u32[]{:S(2)}) collective-permute-start(bf16[1,1,1,1,80,128]{5,4,3,2,1,0:T(8,128)(2,1)S(1)} %get-tuple-element.40), channel_id=1, source_target_pairs={{0,64},{32,96},{64,0},{96,32},{1,65},{33,97},{65,1},{97,33},{2,66}... | collective-permute-start | bytes 61448 | tf_op jit(solution)/shard_map/ppermute | solution.py:133
  155.1 5.0 %collective-permute-start.7 = (bf16[1,1,1,1,80,128]{5,4,3,2,1,0:T(8,128)(2,1)S(1)}, bf16[1,1,1,1,80,128]{5,4,3,2,1,0:T(8,128)(2,1)S(1)}, u32[]{:S(2)}, u32[]{:S(2)}) collective-permute-start(bf16[1,1,1,1,80,128]{5,4,3,2,1,0:T(8,128)(2,1)S(1)} %get-tuple-element.38), channel_id=1, source_target_pairs={{0,32},{32,64},{64,96},{96,0},{1,33},{33,65},{65,97},{97,1},{2,34}... | collective-permute-start | bytes 61448 | tf_op jit(solution)/shard_map/ppermute | solution.py:133

commit v9 on v8

--- a/solution.py
+++ b/solution.py
@@ -33,10 +33,16 @@
     master_rows = constraint_features.shape[0]
     select_con = one_hot_table(send_rows[0, 0], master_rows)
     select_var = one_hot_table(send_rows[1, 0], master_rows)
-    out_con = pick_rows(select_con, constraint_features)
-    out_var = pick_rows(select_var, variable_features)
-    out_cot = pick_rows(select_var, variable_cotangent)
-    outgoing = jnp.concatenate([out_con, out_var, out_cot], axis=1).reshape(
+    rows_con = send_rows[0, 0]
+    rows_var = send_rows[1, 0]
+    outgoing = jnp.concatenate(
+        [
+            jnp.take(constraint_features, rows_con, axis=0, mode="clip"),
+            jnp.take(variable_features, rows_var, axis=0, mode="clip"),
+            jnp.take(variable_cotangent, rows_var, axis=0, mode="clip"),
+        ],
+        axis=1,
+    ).reshape(
         device_count, slot_cap, 3 * embedding_width
     )
     incoming = lax.all_to_all(outgoing, DEVICE_AXES, split_axis=0, concat_axis=0, tiled=True)

time: 166 us -> 172 us (1.036)
  local copies, waits for them, and re-layouts: 27.4 us -> 36.9 us
  matrix products: 43 us -> 38.8 us
    gather x0 -> x3, local copies, waits for them, and re-layouts: none -> 9.59 us  [the longest x1 4.18 us: on_device(): jnp.take(variable_cotangent, rows_var, axis=0, mode='clip')]
    dot_general x3 -> x0, matrix products: 4.23 us -> none  [pick_rows(): jnp.dot(table, values, preferred_element_type=jnp.float32)]
    unnamed x34 -> x40, local copies, waits for them, and re-layouts: 4.58 us -> 5.2 us
  transfers between devices with their start and end apart: 12 -> 12, of which waited for: 10 -> 10; matrix products, arithmetic and copies ran while one was open for 9% -> 8% of each run, Pallas kernels for 0% -> 0%
where the time goes in v9:
time: 172 us
  waiting for transfers between devices  55 us (32%)
  matrix products  38.8 us (23%)
  local copies, waits for them, and re-layouts  36.9 us (21%)
  starting transfers between devices  27.2 us (16%)
  other arithmetic  12.6 us (7%)
    ppermute x10, waiting for transfers between devices, on_device(): total = total + lax.ppermute(chunk, axis_name, pairs).astype(jnp.float32)  28.1 us
    all_to_all x1, waiting for transfers between devices, on_device(): lax.all_to_all(outgoing, DEVICE_AXES, split_axis=0, concat_axis=0, tiled=...  26.9 us
    all_to_all x1, starting transfers between devices, on_device(): lax.all_to_all(outgoing, DEVICE_AXES, split_axis=0, concat_axis=0, tiled=...  11.4 us
    ppermute x10, starting transfers between devices, on_device(): total = total + lax.ppermute(chunk, axis_name, pairs).astype(jnp.float32)  8.86 us
    dot_general x1, matrix products, on_device(): jnp.dot(edge_con, constraint_weight, preferred_element_type=jnp.float32)  8.66 us
    dot_general x1, matrix products, on_device(): lax.dot_general(table_var3, cotangent_mirror_rows, slot_dims, preferred_e...  7.9 us
    dot_general x1, matrix products, on_device(): jnp.dot(edge_var, variable_weight, preferred_element_type=jnp.float32)  7.05 us
    all_to_all x1, starting transfers between devices, on_device(): lax.all_to_all(backward, DEVICE_AXES, split_axis=0, concat_axis=0, tiled=...  6.98 us
  transfers between devices with their start and end apart: 12, of which 10 were waited for; matrix products, arithmetic and copies ran while one was open for 8% of the time, Pallas kernels for 0%

profile of v9, /device:TPU:0, one launch (start us, length us, event | category | flops | bytes accessed | tf_op | source)
XLA Modules:
  0.0 171.6 jit_solution(10315453198667231863)
XLA Ops:
  1.5 4.2 %gather_fusion.2 = bf16[512,768]{1,0:T(8,128)(2,1)} fusion(bf16[256,768]{1,0:T(8,128)(2,1)} %param.13, s32[1024]{0:T(1024)S(1)} %pad_clamp_fusion), kind=kCustom, calls=%fused_computation.2 | custom fusion | bytes 1574912 | tf_op jit(solution)/shard_map/jit(_take)/gather | solution.py:42
  5.7 2.7 %gather_fusion.1 = bf16[512,768]{1,0:T(8,128)(2,1)} fusion(bf16[256,768]{1,0:T(8,128)(2,1)S(1)} %copy-done.1, s32[1024]{0:T(1024)S(1)} %pad_clamp_fusion), kind=kCustom, calls=%fused_computation.1 | custom fusion | bytes 1574912 | tf_op jit(solution)/shard_map/jit(_take)/gather | solution.py:41
  8.4 2.7 %gather_fusion = bf16[512,768]{1,0:T(8,128)(2,1)} fusion(bf16[256,768]{1,0:T(8,128)(2,1)S(1)} %copy-done.2, s32[1024]{0:T(1024)S(1)} %pad_clamp_fusion.1), kind=kCustom, calls=%fused_computation | custom fusion | bytes 1574912 | tf_op jit(solution)/shard_map/jit(_take)/gather | solution.py:40
  11.1 1.8 %pad_maximum_fusion.1 = bf16[512,2304]{1,0:T(8,128)(2,1)S(1)} fusion(bf16[512,768]{1,0:T(8,128)(2,1)} %gather_fusion.2, bf16[512,768]{1,0:T(8,128)(2,1)} %gather_fusion.1, bf16[512,768]{1,0:T(8,128)(2,1)} %gather_fusion), kind=kLoop, calls=%fused_computation.21 | loop fusion | flops 7077888 | bytes 4718592 | tf_op jit(solution)/shard_map/concatenate | solution.py:38
  12.9 2.1 %reshape.135 = bf16[128,4,2304]{2,1,0:T(4,128)(2,1)} reshape(bf16[512,2304]{1,0:T(8,128)(2,1)S(1)} %pad_maximum_fusion.1) | data formatting | bytes 4718592 | tf_op jit(solution)/shard_map/reshape | solution.py:45
  15.0 11.4 %all-to-all-start = ((bf16[128,4,2304]{2,1,0:T(4,128)(2,1)}), bf16[128,4,2304]{2,1,0:T(4,128)(2,1)S(1)}, u32[]{:S(2)}, u32[]{:S(2)}) async-start(bf16[128,4,2304]{2,1,0:T(4,128)(2,1)} %reshape.135), calls=%async_computation | async-start | bytes 4718592 | tf_op jit(solution)/shard_map/all_to_all | solution.py:48
  31.6 26.9 %all-to-all-done = bf16[128,4,2304]{2,1,0:T(4,128)(2,1)S(1)} async-done(((bf16[128,4,2304]{2,1,0:T(4,128)(2,1)}), bf16[128,4,2304]{2,1,0:T(4,128)(2,1)S(1)}, u32[]{:S(2)}, u32[]{:S(2)}) %all-to-all-start) | async-done | bytes 2359328 | tf_op jit(solution)/shard_map/all_to_all | solution.py:48
  58.6 2.0 %fusion.84 = (bf16[128,4,768]{2,1,0:T(4,128)(2,1)}, bf16[128,4,768]{2,1,0:T(4,128)(2,1)}, bf16[128,4,768]{2,1,0:T(4,128)(2,1)}) fusion(bf16[128,4,2304]{2,1,0:T(4,128)(2,1)S(1)} %all-to-all-done), kind=kLoop, calls=%fused_computation.130 | loop fusion | bytes 4718592 | tf_op jit(solution)/shard_map/slice | solution.py:51
  60.6 8.7 %fusion.35 = f32[2048,768]{1,0:T(8,128)} fusion(bf16[768,768]{1,0:T(8,128)(2,1)} %param.14, s32[128,4]{0,1:T(4,128)} %multiply_add_fusion, s32[2048]{0:T(1024)} %bitcast.62, bf16[128,4,768]{2,1,0:T(4,128)(2,1)} %get-tuple-element.28), kind=kOutput, calls=%fused_computation.58 | convolution fusion | flops 4031250432 | bytes 8267776 | tf_op jit(solution)/shard_map/dot_general | solution.py:74
  69.3 7.0 %fusion.36 = f32[2048,768]{1,0:T(8,128)} fusion(bf16[768,768]{1,0:T(8,128)(2,1)S(1)} %copy-done, s32[128,4]{0,1:T(4,128)S(1)} %copy-done.16, s32[2048]{0:T(1024)S(1)} %bitcast.65, bf16[128,4,768]{2,1,0:T(4,128)(2,1)S(1)} %copy-done.6), kind=kOutput, calls=%fused_computation.59 | convolution fusion | flops 4031250432 | bytes 8267776 | tf_op jit(solution)/shard_map/dot_general | solution.py:75
  76.3 7.9 %convert_reduce_fusion = (f32[768]{0:T(1024)S(1)}, bf16[2048,768]{1,0:T(8,128)(2,1)S(1)}) fusion(f32[2048]{0:T(1024)S(1)} %mul.41, f32[768]{0:T(1024)S(1)} %copy-done.19, f32[2048,768]{1,0:T(8,128)} %fusion.35, f32[2048,768]{1,0:T(8,128)} %fusion.36, bf16[128,4,768]{2,1,0:T(4,128)(2,1)S(1)} %copy-done.7, s32[128,4]{0,1:T(4,128)S(1)} %copy-done.16, ...), kind=kOutput, calls=%fused_computation.8 | convolution fusion | flops 1635777792 | bytes 16539648 | tf_op jit(solution)/shard_map/dot_general | solution.py:70
  84.2 2.0 %fusion.30 = bf16[512,768]{1,0:T(8,128)(2,1)S(1)} fusion(bf16[2048,768]{1,0:T(8,128)(2,1)S(1)} %get-tuple-element.48, s32[2048]{0:T(1024)S(1)} %bitcast.67), kind=kOutput, calls=%fused_computation.51 | convolution fusion | flops 1614151680 | bytes 3940352 | tf_op jit(solution)/shard_map/dot_general | solution.py:87
  86.3 2.9 %fusion.31 = bf16[512,768]{1,0:T(8,128)(2,1)} fusion(bf16[2048,768]{1,0:T(8,128)(2,1)S(1)} %get-tuple-element.48, s32[2048]{0:T(1024)S(1)} %bitcast.63), kind=kOutput, calls=%fused_computation.52 | convolution fusion | flops 1614151680 | bytes 3940352 | tf_op jit(solution)/shard_map/dot_general | solution.py:84
  91.1 2.2 %convolution_bitcast_fusion = f32[768,768]{1,0:T(8,128)S(1)} fusion(bf16[128,4,768]{2,1,0:T(4,128)(2,1)} %reshape.139, bf16[128,4,768]{2,1,0:T(4,128)(2,1)} %get-tuple-element.29), kind=kOutput, calls=%fused_computation.46 | convolution fusion | flops 603979776 | bytes 3932160 | tf_op jit(solution)/shard_map/dot_general | solution.py:105
  93.3 1.7 concatenate.21
  95.0 2.4 %reshape.138 = bf16[128,4,768]{2,1,0:T(4,128)(2,1)} reshape(bf16[512,768]{1,0:T(8,128)(2,1)} %fusion.31) | data formatting | bytes 1572864 | tf_op jit(solution)/shard_map/reshape | solution.py:101
  97.3 2.2 %convolution_bitcast_fusion.1 = f32[768,768]{1,0:T(8,128)S(1)} fusion(bf16[128,4,768]{2,1,0:T(4,128)(2,1)} %reshape.138, bf16[128,4,768]{2,1,0:T(4,128)(2,1)} %get-tuple-element.28), kind=kOutput, calls=%fused_computation.47 | convolution fusion | flops 603979776 | bytes 3932160 | tf_op jit(solution)/shard_map/dot_general | solution.py:99
  99.5 1.7 %concatenate.20 = f32[4,2,4,4,36,128]{5,4,3,2,1,0:T(8,128)} reshape(f32[768,768]{1,0:T(8,128)S(1)} %convolution_bitcast_fusion.1) | data formatting | bytes 4718592 | tf_op jit(solution)/shard_map/concatenate | solution.py:117
  102.1 3.1 %pad_maximum_fusion = f32[4,2,4,4,80,128]{5,4,3,2,1,0:T(8,128)S(1)} fusion(f32[4,2,4,4,8,128]{5,4,3,2,1,0:T(8,128)S(1)} %bitcast.54, f32[4,2,4,4,36,128]{5,4,3,2,1,0:T(8,128)} %concatenate.21, f32[4,2,4,4,36,128]{5,4,3,2,1,0:T(8,128)} %concatenate.20), kind=kLoop, calls=%fused_computation.9 | loop fusion | flops 2621440 | bytes 10485760 | tf_op jit(solution)/shard_map/concatenate | solution.py:117
  105.3 2.3 %copy-done.4 = f32[4,2,4,4,80,128]{5,4,3,2,1,0:T(8,128)} copy-done((f32[4,2,4,4,80,128]{5,4,3,2,1,0:T(8,128)}, f32[4,2,4,4,80,128]{5,4,3,2,1,0:T(8,128)S(1)}, u32[]{:S(2)}) %copy-start.4) | copy-done | bytes 5242904
  107.6 1.8 %constant_dynamic-slice_fusion.9 = f32[4,1,4,4,80,128]{5,4,3,2,1,0:T(8,128)} fusion(f32[4,2,4,4,80,128]{5,4,3,2,1,0:T(8,128)S(1)} %pad_maximum_fusion, s32[]{:T(128)S(6)} %select_n.126), kind=kLoop, calls=%fused_computation.97 | loop fusion | bytes 5242884 | tf_op jit(solution)/shard_map/dynamic_slice | solution.py:137
  114.6 2.8 %dynamic-slice_add_fusion = f32[4,1,4,4,80,128]{5,4,3,2,1,0:T(8,128)S(1)} fusion(f32[4,1,4,4,80,128]{5,4,3,2,1,0:T(8,128)} %collective-permute-done, f32[4,2,4,4,80,128]{5,4,3,2,1,0:T(8,128)} %copy-done.4, s32[]{:T(128)S(6)} %select_n.124), kind=kLoop, calls=%fused_computation.20 | loop fusion | flops 655360 | bytes 7864324 | tf_op jit(solution)/shard_map/add | solution.py:139
  120.0 1.6 collective-permute-start.3
  123.0 7.0 %all-to-all-start.1 = ((bf16[128,4,1536]{2,1,0:T(4,128)(2,1)}), bf16[128,4,1536]{2,1,0:T(4,128)(2,1)S(1)}, u32[]{:S(2)}, u32[]{:S(2)}) async-start(bf16[128,4,1536]{2,1,0:T(4,128)(2,1)} %reshape.137), calls=%async_computation.1 | async-start | bytes 3145728 | tf_op jit(solution)/shard_map/all_to_all | solution.py:129
  130.1 6.4 %collective-permute-done.3 = bf16[4,1,4,1,80,128]{5,4,3,2,1,0:T(8,128)(2,1)} collective-permute-done((bf16[4,1,4,1,80,128]{5,4,3,2,1,0:T(8,128)(2,1)}, bf16[4,1,4,1,80,128]{5,4,3,2,1,0:T(8,128)(2,1)}, u32[]{:S(2)}, u32[]{:S(2)}) %collective-permute-start.3) | collective-permute-done | bytes 327712 | tf_op jit(solution)/shard_map/ppermute | solution.py:139
  136.4 3.6 %collective-permute-done.1 = bf16[4,1,4,1,80,128]{5,4,3,2,1,0:T(8,128)(2,1)} collective-permute-done((bf16[4,1,4,1,80,128]{5,4,3,2,1,0:T(8,128)(2,1)S(1)}, bf16[4,1,4,1,80,128]{5,4,3,2,1,0:T(8,128)(2,1)}, u32[]{:S(2)}, u32[]{:S(2)}) %collective-permute-start.1) | collective-permute-done | bytes 327712 | tf_op jit(solution)/shard_map/ppermute | solution.py:139
  140.1 2.4 %fusion.83 = (bf16[4,1,4,1,80,128]{5,4,3,2,1,0:T(8,128)(2,1)S(1)}, f32[4,1,4,1,80,128]{5,4,3,2,1,0:T(8,128)}) fusion(bf16[4,1,4,1,80,128]{5,4,3,2,1,0:T(8,128)(2,1)} %collective-permute-done.3, bf16[4,1,4,1,80,128]{5,4,3,2,1,0:T(8,128)(2,1)} %collective-permute-done.2, bf16[4,1,4,1,80,128]{5,4,3,2,1,0:T(8,128)(2,1)} %collective-permute-done.1, ...), kind=kLoop, calls=%fused_computation.129 | loop fusion | flops 1146880 | bytes 2621444 | tf_op jit(solution)/shard_map/convert_element_type | solution.py:134
  143.8 1.7 collective-permute-start.5
  145.5 8.1 %collective-permute-done.6 = bf16[4,1,1,1,80,128]{5,4,3,2,1,0:T(8,128)(2,1)S(1)} collective-permute-done((bf16[4,1,1,1,80,128]{5,4,3,2,1,0:T(8,128)(2,1)S(1)}, bf16[4,1,1,1,80,128]{5,4,3,2,1,0:T(8,128)(2,1)S(1)}, u32[]{:S(2)}, u32[]{:S(2)}) %collective-permute-start.6) | collective-permute-done | bytes 81952 | tf_op jit(solution)/shard_map/ppermute | solution.py:139
  153.6 2.5 %collective-permute-done.5 = bf16[4,1,1,1,80,128]{5,4,3,2,1,0:T(8,128)(2,1)S(1)} collective-permute-done((bf16[4,1,1,1,80,128]{5,4,3,2,1,0:T(8,128)(2,1)S(1)}, bf16[4,1,1,1,80,128]{5,4,3,2,1,0:T(8,128)(2,1)S(1)}, u32[]{:S(2)}, u32[]{:S(2)}) %collective-permute-start.5) | collective-permute-done | bytes 81952 | tf_op jit(solution)/shard_map/ppermute | solution.py:139
  156.1 1.6 collective-permute-done.4
  163.2 2.9 %collective-permute-done.8 = bf16[1,1,1,1,80,128]{5,4,3,2,1,0:T(8,128)(2,1)S(1)} collective-permute-done((bf16[1,1,1,1,80,128]{5,4,3,2,1,0:T(8,128)(2,1)S(1)}, bf16[1,1,1,1,80,128]{5,4,3,2,1,0:T(8,128)(2,1)S(1)}, u32[]{:S(2)}, u32[]{:S(2)}) %collective-permute-start.8) | collective-permute-done | bytes 20512 | tf_op jit(solution)/shard_map/ppermute | solution.py:139
  (89 shorter events, 30.2 us)
Async XLA Ops:
  0.6 68.6 %copy-start = (bf16[768,768]{1,0:T(8,128)(2,1)S(1)}, bf16[768,768]{1,0:T(8,128)(2,1)}, u32[]{:S(2)}) copy-start(bf16[768,768]{1,0:T(8,128)(2,1)} %param.15) | copy-start | bytes 3538948
  1.5 4.2 %copy-start.1 = (bf16[256,768]{1,0:T(8,128)(2,1)S(1)}, bf16[256,768]{1,0:T(8,128)(2,1)}, u32[]{:S(2)}) copy-start(bf16[256,768]{1,0:T(8,128)(2,1)} %param.12) | copy-start | bytes 1179652
  5.7 2.7 %copy-start.2 = (bf16[256,768]{1,0:T(8,128)(2,1)S(1)}, bf16[256,768]{1,0:T(8,128)(2,1)}, u32[]{:S(2)}) copy-start(bf16[256,768]{1,0:T(8,128)(2,1)} %param.11) | copy-start | bytes 1179652
  15.0 11.4 %copy-start.17 = (s32[2,1,128]{2,1,0:T(1,128)S(1)}, s32[2,1,128]{2,1,0:T(1,128)}, u32[]{:S(2)}) copy-start(s32[2,1,128]{2,1,0:T(1,128)} %param.18) | copy-start | bytes 3076
  15.0 43.6 %all-to-all-start = ((bf16[128,4,2304]{2,1,0:T(4,128)(2,1)}), bf16[128,4,2304]{2,1,0:T(4,128)(2,1)S(1)}, u32[]{:S(2)}, u32[]{:S(2)}) async-start(bf16[128,4,2304]{2,1,0:T(4,128)(2,1)} %reshape.135), calls=%async_computation | async-start | bytes 4718592 | tf_op jit(solution)/shard_map/all_to_all | solution.py:48
  29.0 2.0 %copy-start.12 = (s32[1,2048]{1,0:T(1,128)}, s32[1,2048]{1,0:T(1,128)S(1)}, u32[]{:S(2)}) copy-start(s32[1,2048]{1,0:T(1,128)S(1)} %get-tuple-element.44) | copy-start | bytes 24580
  29.0 2.0 %copy-start.14 = (s32[1,2048]{1,0:T(1,128)}, s32[1,2048]{1,0:T(1,128)S(1)}, u32[]{:S(2)}) copy-start(s32[1,2048]{1,0:T(1,128)S(1)} %get-tuple-element.43) | copy-start | bytes 24580
  60.6 8.7 %copy-start.6 = (bf16[128,4,768]{2,1,0:T(4,128)(2,1)S(1)}, bf16[128,4,768]{2,1,0:T(4,128)(2,1)}, u32[]{:S(2)}) copy-start(bf16[128,4,768]{2,1,0:T(4,128)(2,1)} %get-tuple-element.29) | copy-start | bytes 2359300
  60.6 8.7 %copy-start.15 = (s32[1,2048]{1,0:T(1,128)S(1)}, s32[1,2048]{1,0:T(1,128)}, u32[]{:S(2)}) copy-start(s32[1,2048]{1,0:T(1,128)} %copy-done.14) | copy-start | bytes 24580
  60.6 8.7 %copy-start.16 = (s32[128,4]{0,1:T(4,128)S(1)}, s32[128,4]{0,1:T(4,128)}, u32[]{:S(2)}) copy-start(s32[128,4]{0,1:T(4,128)} %multiply_add_fusion) | copy-start | bytes 6148
  69.3 7.1 %copy-start.7 = (bf16[128,4,768]{2,1,0:T(4,128)(2,1)S(1)}, bf16[128,4,768]{2,1,0:T(4,128)(2,1)}, u32[]{:S(2)}) copy-start(bf16[128,4,768]{2,1,0:T(4,128)(2,1)} %get-tuple-element.27) | copy-start | bytes 2359300
  69.3 7.1 %copy-start.19 = (f32[768]{0:T(1024)S(1)}, f32[768]{0:T(1024)}, u32[]{:S(2)}) copy-start(f32[768]{0:T(1024)} %param.16) | copy-start | bytes 9220
  84.2 2.0 %copy-start.13 = (s32[1,2048]{1,0:T(1,128)S(1)}, s32[1,2048]{1,0:T(1,128)}, u32[]{:S(2)}) copy-start(s32[1,2048]{1,0:T(1,128)} %copy-done.12) | copy-start | bytes 24580
  86.3 3.7 %copy-start.8 = (bf16[512,768]{1,0:T(8,128)(2,1)}, bf16[512,768]{1,0:T(8,128)(2,1)S(1)}, u32[]{:S(2)}) copy-start(bf16[512,768]{1,0:T(8,128)(2,1)S(1)} %fusion.30) | copy-start | bytes 2359300
  105.3 2.3 %copy-start.4 = (f32[4,2,4,4,80,128]{5,4,3,2,1,0:T(8,128)}, f32[4,2,4,4,80,128]{5,4,3,2,1,0:T(8,128)S(1)}, u32[]{:S(2)}) copy-start(f32[4,2,4,4,80,128]{5,4,3,2,1,0:T(8,128)S(1)} %pad_maximum_fusion) | copy-start | bytes 15728644
  107.6 1.8 %copy-start.9 = (bf16[512,768]{1,0:T(8,128)(2,1)S(1)}, bf16[512,768]{1,0:T(8,128)(2,1)}, u32[]{:S(2)}) copy-start(bf16[512,768]{1,0:T(8,128)(2,1)} %copy-done.8) | copy-start | bytes 2359300
  109.4 1.1 copy-start.10
  109.4 5.3 %collective-permute-start = (f32[4,1,4,4,80,128]{5,4,3,2,1,0:T(8,128)}, f32[4,1,4,4,80,128]{5,4,3,2,1,0:T(8,128)}, u32[]{:S(2)}, u32[]{:S(2)}) collective-permute-start(f32[4,1,4,4,80,128]{5,4,3,2,1,0:T(8,128)} %constant_dynamic-slice_fusion.9), channel_id=1, source_target_pairs={{0,16},{16,0},{1,17},{17,1},{2,18},{18,2},{3,19},{19,3},{4,20},{20... | collective-permute-start | bytes 7864328 | tf_op jit(solution)/shard_map/ppermute | solution.py:139
  109.4 1.5 copy-start.18
  117.4 1.5 copy-start.5
  120.0 16.4 %collective-permute-start.3 = (bf16[4,1,4,1,80,128]{5,4,3,2,1,0:T(8,128)(2,1)}, bf16[4,1,4,1,80,128]{5,4,3,2,1,0:T(8,128)(2,1)}, u32[]{:S(2)}, u32[]{:S(2)}) collective-permute-start(bf16[4,1,4,1,80,128]{5,4,3,2,1,0:T(8,128)(2,1)} %get-tuple-element.33), channel_id=1, source_target_pairs={{0,3},{1,0},{2,1},{3,2},{4,7},{5,4},{6,5},{7,6},{8,11},{9,8},{10,9... | collective-permute-start | bytes 983048 | tf_op jit(solution)/shard_map/ppermute | solution.py:139
  121.6 14.8 %collective-permute-start.2 = (bf16[4,1,4,1,80,128]{5,4,3,2,1,0:T(8,128)(2,1)S(1)}, bf16[4,1,4,1,80,128]{5,4,3,2,1,0:T(8,128)(2,1)}, u32[]{:S(2)}, u32[]{:S(2)}) collective-permute-start(bf16[4,1,4,1,80,128]{5,4,3,2,1,0:T(8,128)(2,1)S(1)} %get-tuple-element.34), channel_id=1, source_target_pairs={{0,2},{1,3},{2,0},{3,1},{4,6},{5,7},{6,4},{7,5},{8,10},{9,11},{10,... | collective-permute-start | bytes 983048 | tf_op jit(solution)/shard_map/ppermute | solution.py:139
  123.0 17.0 %collective-permute-start.1 = (bf16[4,1,4,1,80,128]{5,4,3,2,1,0:T(8,128)(2,1)S(1)}, bf16[4,1,4,1,80,128]{5,4,3,2,1,0:T(8,128)(2,1)}, u32[]{:S(2)}, u32[]{:S(2)}) collective-permute-start(bf16[4,1,4,1,80,128]{5,4,3,2,1,0:T(8,128)(2,1)S(1)} %get-tuple-element.32), channel_id=1, source_target_pairs={{0,1},{1,2},{2,3},{3,0},{4,5},{5,6},{6,7},{7,4},{8,9},{9,10},{10,1... | collective-permute-start | bytes 983048 | tf_op jit(solution)/shard_map/ppermute | solution.py:139
  123.0 45.7 %all-to-all-start.1 = ((bf16[128,4,1536]{2,1,0:T(4,128)(2,1)}), bf16[128,4,1536]{2,1,0:T(4,128)(2,1)S(1)}, u32[]{:S(2)}, u32[]{:S(2)}) async-start(bf16[128,4,1536]{2,1,0:T(4,128)(2,1)} %reshape.137), calls=%async_computation.1 | async-start | bytes 3145728 | tf_op jit(solution)/shard_map/all_to_all | solution.py:129
  142.5 11.1 %collective-permute-start.6 = (bf16[4,1,1,1,80,128]{5,4,3,2,1,0:T(8,128)(2,1)S(1)}, bf16[4,1,1,1,80,128]{5,4,3,2,1,0:T(8,128)(2,1)S(1)}, u32[]{:S(2)}, u32[]{:S(2)}) collective-permute-start(bf16[4,1,1,1,80,128]{5,4,3,2,1,0:T(8,128)(2,1)S(1)} %get-tuple-element.36), channel_id=1, source_target_pairs={{0,12},{4,0},{8,4},{12,8},{1,13},{5,1},{9,5},{13,9},{2,14},{6,2},{... | collective-permute-start | bytes 245768 | tf_op jit(solution)/shard_map/ppermute | solution.py:139
  143.8 12.3 %collective-permute-start.5 = (bf16[4,1,1,1,80,128]{5,4,3,2,1,0:T(8,128)(2,1)S(1)}, bf16[4,1,1,1,80,128]{5,4,3,2,1,0:T(8,128)(2,1)S(1)}, u32[]{:S(2)}, u32[]{:S(2)}) collective-permute-start(bf16[4,1,1,1,80,128]{5,4,3,2,1,0:T(8,128)(2,1)S(1)} %get-tuple-element.37), channel_id=1, source_target_pairs={{0,8},{4,12},{8,0},{12,4},{1,9},{5,13},{9,1},{13,5},{2,10},{6,14},... | collective-permute-start | bytes 245768 | tf_op jit(solution)/shard_map/ppermute | solution.py:139
  145.5 12.2 %collective-permute-start.4 = (bf16[4,1,1,1,80,128]{5,4,3,2,1,0:T(8,128)(2,1)S(1)}, bf16[4,1,1,1,80,128]{5,4,3,2,1,0:T(8,128)(2,1)S(1)}, u32[]{:S(2)}, u32[]{:S(2)}) collective-permute-start(bf16[4,1,1,1,80,128]{5,4,3,2,1,0:T(8,128)(2,1)S(1)} %get-tuple-element.35), channel_id=1, source_target_pairs={{0,4},{4,8},{8,12},{12,0},{1,5},{5,9},{9,13},{13,1},{2,6},{6,10},{... | collective-permute-start | bytes 245768 | tf_op jit(solution)/shard_map/ppermute | solution.py:139
  157.7 0.6 copy-start.11
  158.3 12.2 %copy-start.3 = (bf16[256,768]{1,0:T(8,128)(2,1)S(1)}, bf16[256,768]{1,0:T(8,128)(2,1)}, u32[]{:S(2)}) copy-start(bf16[256,768]{1,0:T(8,128)(2,1)} %param.13) | copy-start | bytes 1179652
  159.4 3.9 %collective-permute-start.9 = (bf16[1,1,1,1,80,128]{5,4,3,2,1,0:T(8,128)(2,1)S(1)}, bf16[1,1,1,1,80,128]{5,4,3,2,1,0:T(8,128)(2,1)S(1)}, u32[]{:S(2)}, u32[]{:S(2)}) collective-permute-start(bf16[1,1,1,1,80,128]{5,4,3,2,1,0:T(8,128)(2,1)S(1)} %get-tuple-element.39), channel_id=1, source_target_pairs={{0,96},{32,0},{64,32},{96,64},{1,97},{33,1},{65,33},{97,65},{2,98}... | collective-permute-start | bytes 61448 | tf_op jit(solution)/shard_map/ppermute | solution.py:139
  160.8 5.3 %collective-permute-start.8 = (bf16[1,1,1,1,80,128]{5,4,3,2,1,0:T(8,128)(2,1)S(1)}, bf16[1,1,1,1,80,128]{5,4,3,2,1,0:T(8,128)(2,1)S(1)}, u32[]{:S(2)}, u32[]{:S(2)}) collective-permute-start(bf16[1,1,1,1,80,128]{5,4,3,2,1,0:T(8,128)(2,1)S(1)} %get-tuple-element.40), channel_id=1, source_target_pairs={{0,64},{32,96},{64,0},{96,32},{1,65},{33,97},{65,1},{97,33},{2,66}... | collective-permute-start | bytes 61448 | tf_op jit(solution)/shard_map/ppermute | solution.py:139
  162.0 5.0 %collective-permute-start.7 = (bf16[1,1,1,1,80,128]{5,4,3,2,1,0:T(8,128)(2,1)S(1)}, bf16[1,1,1,1,80,128]{5,4,3,2,1,0:T(8,128)(2,1)S(1)}, u32[]{:S(2)}, u32[]{:S(2)}) collective-permute-start(bf16[1,1,1,1,80,128]{5,4,3,2,1,0:T(8,128)(2,1)S(1)} %get-tuple-element.38), channel_id=1, source_target_pairs={{0,32},{32,64},{64,96},{96,0},{1,33},{33,65},{65,97},{97,1},{2,34}... | collective-permute-start | bytes 61448 | tf_op jit(solution)/shard_map/ppermute | solution.py:139

commit v10 on v8

--- a/solution.py
+++ b/solution.py
@@ -116,22 +116,27 @@
         ],
         axis=1,
     )
-    summed = partials.reshape(*(lax.axis_size(name) for name in DEVICE_AXES), -1, lanes)
+    grid = partials.reshape(*(lax.axis_size(name) for name in DEVICE_AXES), -1, lanes)
+    pieces = [grid[..., :40, :], grid[..., 40:, :]]
     for axis_name, position in (("c", 1), ("x", 3), ("z", 2), ("y", 0)):
         if axis_name == "x":
-            backward, summed = lax.optimization_barrier((backward, summed))
+            backward, pieces = lax.optimization_barrier((backward, pieces))
             homes = lax.all_to_all(backward, DEVICE_AXES, split_axis=0, concat_axis=0, tiled=True)
             home_con = homes[:, :, :embedding_width]
             home_var = homes[:, :, embedding_width:]
         ring = lax.axis_size(axis_name)
         me = lax.axis_index(axis_name)
-        sent = summed if axis_name == "c" else summed.astype(jnp.bfloat16)
-        total = lax.dynamic_slice_in_dim(summed, me, 1, position)
-        for shift in range(1, ring):
-            chunk = lax.dynamic_slice_in_dim(sent, (me + shift) % ring, 1, position)
-            pairs = [(i, (i + shift) % ring) for i in range(ring)]
-            total = total + lax.ppermute(chunk, axis_name, pairs).astype(jnp.float32)
-        summed = total
+        reduced = []
+        for piece in pieces:
+            sent = piece if axis_name == "c" else piece.astype(jnp.bfloat16)
+            total = lax.dynamic_slice_in_dim(piece, me, 1, position)
+            for shift in range(1, ring):
+                chunk = lax.dynamic_slice_in_dim(sent, (me + shift) % ring, 1, position)
+                pairs = [(i, (i + shift) % ring) for i in range(ring)]
+                total = total + lax.ppermute(chunk, axis_name, pairs).astype(jnp.float32)
+            reduced.append(total)
+        pieces = reduced
+    summed = jnp.concatenate(pieces, axis=-2)
     summed = summed.reshape(-1, lanes)
     grad_con = lax.dot_general(
         select_con.reshape(device_count, slot_cap, -1),

time: 166 us -> 178 us (1.072)
  starting transfers between devices: 26.9 us -> 45.7 us
  waiting for transfers between devices: 55.6 us -> 46.7 us
    ppermute x10 -> x20, starting transfers between devices: 8.79 us -> 27 us  [on_device(): total = total + lax.ppermute(chunk, axis_name, pairs).astype(jnp.float32)]
    ppermute x10 -> x20, waiting for transfers between devices: 28.4 us -> 19.6 us  [on_device(): total = total + lax.ppermute(chunk, axis_name, pairs).astype(jnp.float32)]
    dynamic_slice x4 -> x6, local copies, waits for them, and re-layouts: 3.29 us -> 0.2 us  [on_device(): chunk = lax.dynamic_slice_in_dim(sent, (me + shift) % ring, 1, position)]
    reshape x1, local copies, waits for them, and re-layouts: 1.34 us -> 3.86 us  [on_device(): jnp.concatenate([back_con, back_var], axis=1)]
    add x2 -> x4, other arithmetic: 3.62 us -> 5.71 us  [on_device(): total = total + lax.ppermute(chunk, axis_name, pairs).astype(jnp.float32)]
    convert_element_type x3 -> x6, other arithmetic: 3.39 us -> 1.37 us  [on_device(): sent = piece if axis_name == 'c' else piece.astype(jnp.bfloat16)]
    unnamed x34 -> x40, local copies, waits for them, and re-layouts: 4.58 us -> 6.08 us
  transfers between devices with their start and end apart: 12 -> 22, of which waited for: 10 -> 5; matrix products, arithmetic and copies ran while one was open for 9% -> 14% of each run, Pallas kernels for 0% -> 0%
where the time goes in v10:
time: 178 us; the launch traced here: 177 us
  waiting for transfers between devices  46.7 us (26%)
  starting transfers between devices  45.7 us (26%)
  matrix products  44.6 us (25%)
  local copies, waits for them, and re-layouts  26.9 us (15%)
  other arithmetic  12.4 us (7%)
    all_to_all x1, waiting for transfers between devices, on_device(): lax.all_to_all(outgoing, DEVICE_AXES, split_axis=0, concat_axis=0, tiled=...  27.1 us
    ppermute x20, starting transfers between devices, on_device(): total = total + lax.ppermute(chunk, axis_name, pairs).astype(jnp.float32)  27 us
    ppermute x20, waiting for transfers between devices, on_device(): total = total + lax.ppermute(chunk, axis_name, pairs).astype(jnp.float32)  19.6 us
    all_to_all x1, starting transfers between devices, on_device(): lax.all_to_all(outgoing, DEVICE_AXES, split_axis=0, concat_axis=0, tiled=...  11.2 us
    dot_general x1, matrix products, on_device(): jnp.dot(edge_con, constraint_weight, preferred_element_type=jnp.float32)  8.72 us
    dot_general x1, matrix products, on_device(): lax.dot_general(table_var3, cotangent_mirror_rows, slot_dims, preferred_e...  8.46 us
    all_to_all x1, starting transfers between devices, on_device(): lax.all_to_all(backward, DEVICE_AXES, split_axis=0, concat_axis=0, tiled=...  7.48 us
    dot_general x1, matrix products, on_device(): jnp.dot(edge_var, variable_weight, preferred_element_type=jnp.float32)  7.12 us
  transfers between devices with their start and end apart: 22, of which 5 were waited for; matrix products, arithmetic and copies ran while one was open for 14% of the time, Pallas kernels for 0%

profile of v10, /device:TPU:0, one launch (start us, length us, event | category | flops | bytes accessed | tf_op | source)
XLA Modules:
  0.0 177.3 jit_solution(15826760311127268199)
XLA Ops:
  2.9 1.4 convolution_convert_fusion.3
  5.9 2.2 %reshape.133 = bf16[128,4,2304]{2,1,0:T(4,128)(2,1)} reshape(bf16[512,2304]{1,0:T(8,128)(2,1)S(1)} %pad_maximum_fusion) | data formatting | bytes 4718592 | tf_op jit(solution)/shard_map/reshape | solution.py:39
  8.1 11.2 %all-to-all-start = ((bf16[128,4,2304]{2,1,0:T(4,128)(2,1)}), bf16[128,4,2304]{2,1,0:T(4,128)(2,1)S(1)}, u32[]{:S(2)}, u32[]{:S(2)}) async-start(bf16[128,4,2304]{2,1,0:T(4,128)(2,1)} %reshape.133), calls=%async_computation | async-start | bytes 4718592 | tf_op jit(solution)/shard_map/all_to_all | solution.py:42
  24.5 27.1 %all-to-all-done = bf16[128,4,2304]{2,1,0:T(4,128)(2,1)S(1)} async-done(((bf16[128,4,2304]{2,1,0:T(4,128)(2,1)}), bf16[128,4,2304]{2,1,0:T(4,128)(2,1)S(1)}, u32[]{:S(2)}, u32[]{:S(2)}) %all-to-all-start) | async-done | bytes 2359328 | tf_op jit(solution)/shard_map/all_to_all | solution.py:42
  51.6 2.0 %fusion.110 = (bf16[128,4,768]{2,1,0:T(4,128)(2,1)}, bf16[128,4,768]{2,1,0:T(4,128)(2,1)}, bf16[128,4,768]{2,1,0:T(4,128)(2,1)}) fusion(bf16[128,4,2304]{2,1,0:T(4,128)(2,1)S(1)} %all-to-all-done), kind=kLoop, calls=%fused_computation.177 | loop fusion | bytes 4718592 | tf_op jit(solution)/shard_map/slice | solution.py:45
  53.6 8.7 %fusion.41 = f32[2048,768]{1,0:T(8,128)} fusion(bf16[768,768]{1,0:T(8,128)(2,1)} %param.14, s32[128,4]{0,1:T(4,128)} %multiply_add_fusion, s32[2048]{0:T(1024)} %bitcast.64, bf16[128,4,768]{2,1,0:T(4,128)(2,1)} %get-tuple-element.36), kind=kOutput, calls=%fused_computation.70 | convolution fusion | flops 4031250432 | bytes 8267776 | tf_op jit(solution)/shard_map/dot_general | solution.py:68
  62.4 7.1 %fusion.42 = f32[2048,768]{1,0:T(8,128)} fusion(bf16[768,768]{1,0:T(8,128)(2,1)S(1)} %copy-done, s32[128,4]{0,1:T(4,128)S(1)} %copy-done.14, s32[2048]{0:T(1024)S(1)} %bitcast.67, bf16[128,4,768]{2,1,0:T(4,128)(2,1)S(1)} %copy-done.3), kind=kOutput, calls=%fused_computation.71 | convolution fusion | flops 4031250432 | bytes 8267776 | tf_op jit(solution)/shard_map/dot_general | solution.py:69
  69.5 8.5 %convert_reduce_fusion = (f32[768]{0:T(1024)}, bf16[2048,768]{1,0:T(8,128)(2,1)S(1)}) fusion(f32[2048]{0:T(1024)S(1)} %mul.41, f32[768]{0:T(1024)S(1)} %copy-done.18, f32[2048,768]{1,0:T(8,128)} %fusion.41, f32[2048,768]{1,0:T(8,128)} %fusion.42, bf16[128,4,768]{2,1,0:T(4,128)(2,1)S(1)} %copy-done.4, s32[128,4]{0,1:T(4,128)S(1)} %copy-done.14, ...), kind=kOutput, calls=%fused_computation.5 | convolution fusion | flops 1635777792 | bytes 16539648 | tf_op jit(solution)/shard_map/dot_general | solution.py:64
  78.0 1.6 copy-done.19
  79.6 2.0 %fusion.30 = bf16[512,768]{1,0:T(8,128)(2,1)S(1)} fusion(bf16[2048,768]{1,0:T(8,128)(2,1)S(1)} %get-tuple-element.65, s32[2048]{0:T(1024)S(1)} %bitcast.69), kind=kOutput, calls=%fused_computation.54 | convolution fusion | flops 1614151680 | bytes 3940352 | tf_op jit(solution)/shard_map/dot_general | solution.py:81
  83.6 2.2 %convolution_bitcast_fusion = f32[768,768]{1,0:T(8,128)S(1)} fusion(bf16[128,4,768]{2,1,0:T(4,128)(2,1)} %reshape.137, bf16[128,4,768]{2,1,0:T(4,128)(2,1)} %get-tuple-element.37), kind=kOutput, calls=%fused_computation.49 | convolution fusion | flops 603979776 | bytes 3932160 | tf_op jit(solution)/shard_map/dot_general | solution.py:99
  85.8 1.7 concatenate.28
  88.5 2.6 %fusion.35 = f32[4,1,4,4,40,128]{5,4,3,2,1,0:T(8,128)} fusion(s32[]{:T(128)S(6)} %select_n.166, f32[4,2,4,4,36,128]{5,4,3,2,1,0:T(8,128)} %concatenate.28, f32[4,2,4,4,8,128]{5,4,3,2,1,0:T(8,128)S(1)} %bitcast.58), kind=kLoop, calls=%fused_computation.62 | loop fusion | flops 327680 | bytes 4194308 | tf_op jit(solution)/shard_map/concatenate | solution.py:111
  91.2 3.9 %fusion.31 = bf16[512,768]{1,0:T(8,128)(2,1)S(1)} fusion(bf16[2048,768]{1,0:T(8,128)(2,1)} %copy-done.19, s32[2048]{0:T(1024)S(1)} %bitcast.65), kind=kOutput, calls=%fused_computation.55 | convolution fusion | flops 1614151680 | bytes 3940352 | tf_op jit(solution)/shard_map/dot_general | solution.py:78
  97.0 2.2 %convolution_bitcast_fusion.1 = f32[768,768]{1,0:T(8,128)S(1)} fusion(bf16[128,4,768]{2,1,0:T(4,128)(2,1)} %reshape.136, bf16[128,4,768]{2,1,0:T(4,128)(2,1)} %get-tuple-element.36), kind=kOutput, calls=%fused_computation.50 | convolution fusion | flops 603979776 | bytes 3932160 | tf_op jit(solution)/shard_map/dot_general | solution.py:93
  99.2 1.7 concatenate.27
  100.9 3.8 %fusion.37 = (f32[4,1,4,4,40,128]{5,4,3,2,1,0:T(8,128)S(1)}, f32[4,1,4,4,40,128]{5,4,3,2,1,0:T(8,128)}) fusion(f32[4,1,4,4,40,128]{5,4,3,2,1,0:T(8,128)} %collective-permute-done.1, s32[]{:T(128)S(6)} %select_n.164, f32[4,2,4,4,36,128]{5,4,3,2,1,0:T(8,128)} %concatenate.28, f32[4,2,4,4,8,128]{5,4,3,2,1,0:T(8,128)} %bitcast.59, s32[]{:T(128)S(6)} %select_n.166, ...), kind=kLoop, calls=%fused_computation.64 | loop fusion | flops 983040 | bytes 9175048 | tf_op jit(solution)/shard_map/add | solution.py:136
  108.9 3.9 %reshape.135 = bf16[128,4,1536]{2,1,0:T(4,128)(2,1)} reshape(bf16[512,1536]{1,0:T(8,128)(2,1)} %pad_maximum_fusion.1) | data formatting | bytes 3145728 | tf_op jit(solution)/shard_map/reshape | solution.py:90
  112.8 1.9 %fusion.34 = f32[4,1,4,4,40,128]{5,4,3,2,1,0:T(8,128)S(1)} fusion(f32[4,1,4,4,40,128]{5,4,3,2,1,0:T(8,128)} %collective-permute-done, s32[]{:T(128)S(6)} %select_n.164, f32[4,2,4,4,36,128]{5,4,3,2,1,0:T(8,128)} %concatenate.27, f32[4,2,4,4,36,128]{5,4,3,2,1,0:T(8,128)} %concatenate.28), kind=kLoop, calls=%fused_computation.61 | loop fusion | flops 655360 | bytes 7340036 | tf_op jit(solution)/shard_map/add | solution.py:136
  115.9 1.7 collective-permute-start.4
  117.6 1.4 collective-permute-start.3
  119.4 7.5 %all-to-all-start.1 = ((bf16[128,4,1536]{2,1,0:T(4,128)(2,1)}), bf16[128,4,1536]{2,1,0:T(4,128)(2,1)}, u32[]{:S(2)}, u32[]{:S(2)}) async-start(bf16[128,4,1536]{2,1,0:T(4,128)(2,1)} %reshape.135), calls=%async_computation.1 | async-start | bytes 3145728 | tf_op jit(solution)/shard_map/all_to_all | solution.py:124
  127.0 2.4 %collective-permute-start.13 = (bf16[4,1,4,1,40,128]{5,4,3,2,1,0:T(8,128)(2,1)S(1)}, bf16[4,1,4,1,40,128]{5,4,3,2,1,0:T(8,128)(2,1)S(1)}, u32[]{:S(2)}, u32[]{:S(2)}) collective-permute-start(bf16[4,1,4,1,40,128]{5,4,3,2,1,0:T(8,128)(2,1)S(1)} %get-tuple-element.41), channel_id=1, source_target_pairs={{0,3},{1,0},{2,1},{3,2},{4,7},{5,4},{6,5},{7,6},{8,11},{9,8},{10,9... | collective-permute-start | bytes 491528 | tf_op jit(solution)/shard_map/ppermute | solution.py:136
  132.2 3.4 %collective-permute-start.7 = (bf16[4,1,1,1,40,128]{5,4,3,2,1,0:T(8,128)(2,1)S(1)}, bf16[4,1,1,1,40,128]{5,4,3,2,1,0:T(8,128)(2,1)S(1)}, u32[]{:S(2)}, u32[]{:S(2)}) collective-permute-start(bf16[4,1,1,1,40,128]{5,4,3,2,1,0:T(8,128)(2,1)S(1)} %get-tuple-element.50), channel_id=1, source_target_pairs={{0,12},{4,0},{8,4},{12,8},{1,13},{5,1},{9,5},{13,9},{2,14},{6,2},{... | collective-permute-start | bytes 122888 | tf_op jit(solution)/shard_map/ppermute | solution.py:136
  136.0 12.6 %collective-permute-done.13 = bf16[4,1,4,1,40,128]{5,4,3,2,1,0:T(8,128)(2,1)S(1)} collective-permute-done((bf16[4,1,4,1,40,128]{5,4,3,2,1,0:T(8,128)(2,1)S(1)}, bf16[4,1,4,1,40,128]{5,4,3,2,1,0:T(8,128)(2,1)S(1)}, u32[]{:S(2)}, u32[]{:S(2)}) %collective-permute-start.13) | collective-permute-done | bytes 163872 | tf_op jit(solution)/shard_map/ppermute | solution.py:136
  148.6 1.6 collective-permute-start.5
  150.2 2.5 %collective-permute-done.11 = bf16[4,1,4,1,40,128]{5,4,3,2,1,0:T(8,128)(2,1)S(1)} collective-permute-done((bf16[4,1,4,1,40,128]{5,4,3,2,1,0:T(8,128)(2,1)S(1)}, bf16[4,1,4,1,40,128]{5,4,3,2,1,0:T(8,128)(2,1)S(1)}, u32[]{:S(2)}, u32[]{:S(2)}) %collective-permute-start.11) | collective-permute-done | bytes 163872 | tf_op jit(solution)/shard_map/ppermute | solution.py:136
  152.9 3.5 %collective-permute-start.16 = (bf16[4,1,1,1,40,128]{5,4,3,2,1,0:T(8,128)(2,1)S(1)}, bf16[4,1,1,1,40,128]{5,4,3,2,1,0:T(8,128)(2,1)S(1)}, u32[]{:S(2)}, u32[]{:S(2)}) collective-permute-start(bf16[4,1,1,1,40,128]{5,4,3,2,1,0:T(8,128)(2,1)S(1)} %get-tuple-element.47), channel_id=1, source_target_pairs={{0,12},{4,0},{8,4},{12,8},{1,13},{5,1},{9,5},{13,9},{2,14},{6,2},{... | collective-permute-start | bytes 122888 | tf_op jit(solution)/shard_map/ppermute | solution.py:136
  157.9 2.9 %collective-permute-start.10 = (bf16[1,1,1,1,40,128]{5,4,3,2,1,0:T(8,128)(2,1)S(1)}, bf16[1,1,1,1,40,128]{5,4,3,2,1,0:T(8,128)(2,1)S(1)}, u32[]{:S(2)}, u32[]{:S(2)}) collective-permute-start(bf16[1,1,1,1,40,128]{5,4,3,2,1,0:T(8,128)(2,1)S(1)} %get-tuple-element.56), channel_id=1, source_target_pairs={{0,96},{32,0},{64,32},{96,64},{1,97},{33,1},{65,33},{97,65},{2,98}... | collective-permute-start | bytes 30728 | tf_op jit(solution)/shard_map/ppermute | solution.py:136
  162.5 2.8 %collective-permute-start.19 = (bf16[1,1,1,1,40,128]{5,4,3,2,1,0:T(8,128)(2,1)S(1)}, bf16[1,1,1,1,40,128]{5,4,3,2,1,0:T(8,128)(2,1)S(1)}, u32[]{:S(2)}, u32[]{:S(2)}) collective-permute-start(bf16[1,1,1,1,40,128]{5,4,3,2,1,0:T(8,128)(2,1)S(1)} %get-tuple-element.53), channel_id=1, source_target_pairs={{0,96},{32,0},{64,32},{96,64},{1,97},{33,1},{65,33},{97,65},{2,98}... | collective-permute-start | bytes 30728 | tf_op jit(solution)/shard_map/ppermute | solution.py:136
  167.0 3.5 %collective-permute-done.18 = bf16[1,1,1,1,40,128]{5,4,3,2,1,0:T(8,128)(2,1)S(1)} collective-permute-done((bf16[1,1,1,1,40,128]{5,4,3,2,1,0:T(8,128)(2,1)S(1)}, bf16[1,1,1,1,40,128]{5,4,3,2,1,0:T(8,128)(2,1)S(1)}, u32[]{:S(2)}, u32[]{:S(2)}) %collective-permute-start.18) | collective-permute-done | bytes 10272 | tf_op jit(solution)/shard_map/ppermute | solution.py:136
  173.2 1.9 %fusion.111 = (bf16[128,4,768]{2,1,0:T(4,128)(2,1)S(1)}, bf16[128,4,768]{2,1,0:T(4,128)(2,1)S(1)}) fusion(bf16[128,4,1536]{2,1,0:T(4,128)(2,1)} %all-to-all-done.1), kind=kLoop, calls=%fused_computation.178 | loop fusion | bytes 3145728 | tf_op jit(solution)/shard_map/slice | solution.py:126
  (115 shorter events, 32.9 us)
Async XLA Ops:
  0.6 61.7 %copy-start = (bf16[768,768]{1,0:T(8,128)(2,1)S(1)}, bf16[768,768]{1,0:T(8,128)(2,1)}, u32[]{:S(2)}) copy-start(bf16[768,768]{1,0:T(8,128)(2,1)} %param.15) | copy-start | bytes 3538948
  8.1 11.2 %copy-start.15 = (s32[2,1,128]{2,1,0:T(1,128)S(1)}, s32[2,1,128]{2,1,0:T(1,128)}, u32[]{:S(2)}) copy-start(s32[2,1,128]{2,1,0:T(1,128)} %param.18) | copy-start | bytes 3076
  8.1 43.6 %all-to-all-start = ((bf16[128,4,2304]{2,1,0:T(4,128)(2,1)}), bf16[128,4,2304]{2,1,0:T(4,128)(2,1)S(1)}, u32[]{:S(2)}, u32[]{:S(2)}) async-start(bf16[128,4,2304]{2,1,0:T(4,128)(2,1)} %reshape.133), calls=%async_computation | async-start | bytes 4718592 | tf_op jit(solution)/shard_map/all_to_all | solution.py:42
  53.6 8.7 %copy-start.3 = (bf16[128,4,768]{2,1,0:T(4,128)(2,1)S(1)}, bf16[128,4,768]{2,1,0:T(4,128)(2,1)}, u32[]{:S(2)}) copy-start(bf16[128,4,768]{2,1,0:T(4,128)(2,1)} %get-tuple-element.37) | copy-start | bytes 2359300
  53.6 8.7 %copy-start.12 = (s32[1,2048]{1,0:T(1,128)S(1)}, s32[1,2048]{1,0:T(1,128)}, u32[]{:S(2)}) copy-start(s32[1,2048]{1,0:T(1,128)} %copy-done.11) | copy-start | bytes 24580
  53.6 8.7 %copy-start.14 = (s32[128,4]{0,1:T(4,128)S(1)}, s32[128,4]{0,1:T(4,128)}, u32[]{:S(2)}) copy-start(s32[128,4]{0,1:T(4,128)} %multiply_add_fusion) | copy-start | bytes 6148
  62.3 7.1 %copy-start.4 = (bf16[128,4,768]{2,1,0:T(4,128)(2,1)S(1)}, bf16[128,4,768]{2,1,0:T(4,128)(2,1)}, u32[]{:S(2)}) copy-start(bf16[128,4,768]{2,1,0:T(4,128)(2,1)} %get-tuple-element.35) | copy-start | bytes 2359300
  62.4 7.1 %copy-start.18 = (f32[768]{0:T(1024)S(1)}, f32[768]{0:T(1024)}, u32[]{:S(2)}) copy-start(f32[768]{0:T(1024)} %param.16) | copy-start | bytes 9220
  87.5 3.6 %copy-start.10 = (s32[1,2048]{1,0:T(1,128)S(1)}, s32[1,2048]{1,0:T(1,128)}, u32[]{:S(2)}) copy-start(s32[1,2048]{1,0:T(1,128)} %copy-done.9) | copy-start | bytes 24580
  91.1 9.8 %collective-permute-start.1 = (f32[4,1,4,4,40,128]{5,4,3,2,1,0:T(8,128)}, f32[4,1,4,4,40,128]{5,4,3,2,1,0:T(8,128)}, u32[]{:S(2)}, u32[]{:S(2)}) collective-permute-start(f32[4,1,4,4,40,128]{5,4,3,2,1,0:T(8,128)} %fusion.35), channel_id=1, source_target_pairs={{0,16},{16,0},{1,17},{17,1},{2,18},{18,2},{3,19},{19,3},{4,20},{20... | collective-permute-start | bytes 3932168 | tf_op jit(solution)/shard_map/ppermute | solution.py:136
  100.9 4.3 %copy-start.6 = (bf16[512,768]{1,0:T(8,128)(2,1)S(1)}, bf16[512,768]{1,0:T(8,128)(2,1)}, u32[]{:S(2)}) copy-start(bf16[512,768]{1,0:T(8,128)(2,1)} %copy-done.5) | copy-start | bytes 2359300
  104.7 8.1 %collective-permute-start = (f32[4,1,4,4,40,128]{5,4,3,2,1,0:T(8,128)}, f32[4,1,4,4,40,128]{5,4,3,2,1,0:T(8,128)}, u32[]{:S(2)}, u32[]{:S(2)}) collective-permute-start(f32[4,1,4,4,40,128]{5,4,3,2,1,0:T(8,128)} %get-tuple-element.34), channel_id=1, source_target_pairs={{0,16},{16,0},{1,17},{17,1},{2,18},{18,2},{3,19},{19,3},{4,20},{20... | collective-permute-start | bytes 3932168 | tf_op jit(solution)/shard_map/ppermute | solution.py:136
  115.9 14.4 %collective-permute-start.4 = (bf16[4,1,4,1,40,128]{5,4,3,2,1,0:T(8,128)(2,1)S(1)}, bf16[4,1,4,1,40,128]{5,4,3,2,1,0:T(8,128)(2,1)S(1)}, u32[]{:S(2)}, u32[]{:S(2)}) collective-permute-start(bf16[4,1,4,1,40,128]{5,4,3,2,1,0:T(8,128)(2,1)S(1)} %get-tuple-element.44), channel_id=1, source_target_pairs={{0,3},{1,0},{2,1},{3,2},{4,7},{5,4},{6,5},{7,6},{8,11},{9,8},{10,9... | collective-permute-start | bytes 491528 | tf_op jit(solution)/shard_map/ppermute | solution.py:136
  117.6 13.6 %collective-permute-start.3 = (bf16[4,1,4,1,40,128]{5,4,3,2,1,0:T(8,128)(2,1)S(1)}, bf16[4,1,4,1,40,128]{5,4,3,2,1,0:T(8,128)(2,1)S(1)}, u32[]{:S(2)}, u32[]{:S(2)}) collective-permute-start(bf16[4,1,4,1,40,128]{5,4,3,2,1,0:T(8,128)(2,1)S(1)} %get-tuple-element.45), channel_id=1, source_target_pairs={{0,2},{1,3},{2,0},{3,1},{4,6},{5,7},{6,4},{7,5},{8,10},{9,11},{10,... | collective-permute-start | bytes 491528 | tf_op jit(solution)/shard_map/ppermute | solution.py:136
  119.0 12.1 %collective-permute-start.2 = (bf16[4,1,4,1,40,128]{5,4,3,2,1,0:T(8,128)(2,1)S(1)}, bf16[4,1,4,1,40,128]{5,4,3,2,1,0:T(8,128)(2,1)S(1)}, u32[]{:S(2)}, u32[]{:S(2)}) collective-permute-start(bf16[4,1,4,1,40,128]{5,4,3,2,1,0:T(8,128)(2,1)S(1)} %get-tuple-element.43), channel_id=1, source_target_pairs={{0,1},{1,2},{2,3},{3,0},{4,5},{5,6},{6,7},{7,4},{8,9},{9,10},{10,1... | collective-permute-start | bytes 491528 | tf_op jit(solution)/shard_map/ppermute | solution.py:136
  119.4 53.8 %all-to-all-start.1 = ((bf16[128,4,1536]{2,1,0:T(4,128)(2,1)}), bf16[128,4,1536]{2,1,0:T(4,128)(2,1)}, u32[]{:S(2)}, u32[]{:S(2)}) async-start(bf16[128,4,1536]{2,1,0:T(4,128)(2,1)} %reshape.135), calls=%async_computation.1 | async-start | bytes 3145728 | tf_op jit(solution)/shard_map/all_to_all | solution.py:124
  127.0 21.6 %collective-permute-start.13 = (bf16[4,1,4,1,40,128]{5,4,3,2,1,0:T(8,128)(2,1)S(1)}, bf16[4,1,4,1,40,128]{5,4,3,2,1,0:T(8,128)(2,1)S(1)}, u32[]{:S(2)}, u32[]{:S(2)}) collective-permute-start(bf16[4,1,4,1,40,128]{5,4,3,2,1,0:T(8,128)(2,1)S(1)} %get-tuple-element.41), channel_id=1, source_target_pairs={{0,3},{1,0},{2,1},{3,2},{4,7},{5,4},{6,5},{7,6},{8,11},{9,8},{10,9... | collective-permute-start | bytes 491528 | tf_op jit(solution)/shard_map/ppermute | solution.py:136
  129.4 20.8 %collective-permute-start.12 = (bf16[4,1,4,1,40,128]{5,4,3,2,1,0:T(8,128)(2,1)S(1)}, bf16[4,1,4,1,40,128]{5,4,3,2,1,0:T(8,128)(2,1)S(1)}, u32[]{:S(2)}, u32[]{:S(2)}) collective-permute-start(bf16[4,1,4,1,40,128]{5,4,3,2,1,0:T(8,128)(2,1)S(1)} %get-tuple-element.42), channel_id=1, source_target_pairs={{0,2},{1,3},{2,0},{3,1},{4,6},{5,7},{6,4},{7,5},{8,10},{9,11},{10,... | collective-permute-start | bytes 491528 | tf_op jit(solution)/shard_map/ppermute | solution.py:136
  130.3 22.5 %collective-permute-start.11 = (bf16[4,1,4,1,40,128]{5,4,3,2,1,0:T(8,128)(2,1)S(1)}, bf16[4,1,4,1,40,128]{5,4,3,2,1,0:T(8,128)(2,1)S(1)}, u32[]{:S(2)}, u32[]{:S(2)}) collective-permute-start(bf16[4,1,4,1,40,128]{5,4,3,2,1,0:T(8,128)(2,1)S(1)} %get-tuple-element.40), channel_id=1, source_target_pairs={{0,1},{1,2},{2,3},{3,0},{4,5},{5,6},{6,7},{7,4},{8,9},{9,10},{10,1... | collective-permute-start | bytes 491528 | tf_op jit(solution)/shard_map/ppermute | solution.py:136
  132.2 24.4 %collective-permute-start.7 = (bf16[4,1,1,1,40,128]{5,4,3,2,1,0:T(8,128)(2,1)S(1)}, bf16[4,1,1,1,40,128]{5,4,3,2,1,0:T(8,128)(2,1)S(1)}, u32[]{:S(2)}, u32[]{:S(2)}) collective-permute-start(bf16[4,1,1,1,40,128]{5,4,3,2,1,0:T(8,128)(2,1)S(1)} %get-tuple-element.50), channel_id=1, source_target_pairs={{0,12},{4,0},{8,4},{12,8},{1,13},{5,1},{9,5},{13,9},{2,14},{6,2},{... | collective-permute-start | bytes 122888 | tf_op jit(solution)/shard_map/ppermute | solution.py:136
  135.7 22.1 %collective-permute-start.6 = (bf16[4,1,1,1,40,128]{5,4,3,2,1,0:T(8,128)(2,1)S(1)}, bf16[4,1,1,1,40,128]{5,4,3,2,1,0:T(8,128)(2,1)S(1)}, u32[]{:S(2)}, u32[]{:S(2)}) collective-permute-start(bf16[4,1,1,1,40,128]{5,4,3,2,1,0:T(8,128)(2,1)S(1)} %get-tuple-element.51), channel_id=1, source_target_pairs={{0,8},{4,12},{8,0},{12,4},{1,9},{5,13},{9,1},{13,5},{2,10},{6,14},... | collective-permute-start | bytes 122888 | tf_op jit(solution)/shard_map/ppermute | solution.py:136
  148.6 9.2 %collective-permute-start.5 = (bf16[4,1,1,1,40,128]{5,4,3,2,1,0:T(8,128)(2,1)S(1)}, bf16[4,1,1,1,40,128]{5,4,3,2,1,0:T(8,128)(2,1)S(1)}, u32[]{:S(2)}, u32[]{:S(2)}) collective-permute-start(bf16[4,1,1,1,40,128]{5,4,3,2,1,0:T(8,128)(2,1)S(1)} %get-tuple-element.49), channel_id=1, source_target_pairs={{0,4},{4,8},{8,12},{12,0},{1,5},{5,9},{9,13},{13,1},{2,6},{6,10},{... | collective-permute-start | bytes 122888 | tf_op jit(solution)/shard_map/ppermute | solution.py:136
  152.9 8.6 %collective-permute-start.16 = (bf16[4,1,1,1,40,128]{5,4,3,2,1,0:T(8,128)(2,1)S(1)}, bf16[4,1,1,1,40,128]{5,4,3,2,1,0:T(8,128)(2,1)S(1)}, u32[]{:S(2)}, u32[]{:S(2)}) collective-permute-start(bf16[4,1,1,1,40,128]{5,4,3,2,1,0:T(8,128)(2,1)S(1)} %get-tuple-element.47), channel_id=1, source_target_pairs={{0,12},{4,0},{8,4},{12,8},{1,13},{5,1},{9,5},{13,9},{2,14},{6,2},{... | collective-permute-start | bytes 122888 | tf_op jit(solution)/shard_map/ppermute | solution.py:136
  156.3 6.1 %collective-permute-start.15 = (bf16[4,1,1,1,40,128]{5,4,3,2,1,0:T(8,128)(2,1)S(1)}, bf16[4,1,1,1,40,128]{5,4,3,2,1,0:T(8,128)(2,1)S(1)}, u32[]{:S(2)}, u32[]{:S(2)}) collective-permute-start(bf16[4,1,1,1,40,128]{5,4,3,2,1,0:T(8,128)(2,1)S(1)} %get-tuple-element.48), channel_id=1, source_target_pairs={{0,8},{4,12},{8,0},{12,4},{1,9},{5,13},{9,1},{13,5},{2,10},{6,14},... | collective-permute-start | bytes 122888 | tf_op jit(solution)/shard_map/ppermute | solution.py:136
  156.7 5.8 %collective-permute-start.14 = (bf16[4,1,1,1,40,128]{5,4,3,2,1,0:T(8,128)(2,1)S(1)}, bf16[4,1,1,1,40,128]{5,4,3,2,1,0:T(8,128)(2,1)S(1)}, u32[]{:S(2)}, u32[]{:S(2)}) collective-permute-start(bf16[4,1,1,1,40,128]{5,4,3,2,1,0:T(8,128)(2,1)S(1)} %get-tuple-element.46), channel_id=1, source_target_pairs={{0,4},{4,8},{8,12},{12,0},{1,5},{5,9},{9,13},{13,1},{2,6},{6,10},{... | collective-permute-start | bytes 122888 | tf_op jit(solution)/shard_map/ppermute | solution.py:136
  157.9 8.6 %collective-permute-start.10 = (bf16[1,1,1,1,40,128]{5,4,3,2,1,0:T(8,128)(2,1)S(1)}, bf16[1,1,1,1,40,128]{5,4,3,2,1,0:T(8,128)(2,1)S(1)}, u32[]{:S(2)}, u32[]{:S(2)}) collective-permute-start(bf16[1,1,1,1,40,128]{5,4,3,2,1,0:T(8,128)(2,1)S(1)} %get-tuple-element.56), channel_id=1, source_target_pairs={{0,96},{32,0},{64,32},{96,64},{1,97},{33,1},{65,33},{97,65},{2,98}... | collective-permute-start | bytes 30728 | tf_op jit(solution)/shard_map/ppermute | solution.py:136
  160.8 6.1 %collective-permute-start.9 = (bf16[1,1,1,1,40,128]{5,4,3,2,1,0:T(8,128)(2,1)S(1)}, bf16[1,1,1,1,40,128]{5,4,3,2,1,0:T(8,128)(2,1)S(1)}, u32[]{:S(2)}, u32[]{:S(2)}) collective-permute-start(bf16[1,1,1,1,40,128]{5,4,3,2,1,0:T(8,128)(2,1)S(1)} %get-tuple-element.57), channel_id=1, source_target_pairs={{0,64},{32,96},{64,0},{96,32},{1,65},{33,97},{65,1},{97,33},{2,66}... | collective-permute-start | bytes 30728 | tf_op jit(solution)/shard_map/ppermute | solution.py:136
  161.5 5.4 %collective-permute-start.8 = (bf16[1,1,1,1,40,128]{5,4,3,2,1,0:T(8,128)(2,1)S(1)}, bf16[1,1,1,1,40,128]{5,4,3,2,1,0:T(8,128)(2,1)S(1)}, u32[]{:S(2)}, u32[]{:S(2)}) collective-permute-start(bf16[1,1,1,1,40,128]{5,4,3,2,1,0:T(8,128)(2,1)S(1)} %get-tuple-element.55), channel_id=1, source_target_pairs={{0,32},{32,64},{64,96},{96,0},{1,33},{33,65},{65,97},{97,1},{2,34}... | collective-permute-start | bytes 30728 | tf_op jit(solution)/shard_map/ppermute | solution.py:136
  162.5 4.5 %collective-permute-start.19 = (bf16[1,1,1,1,40,128]{5,4,3,2,1,0:T(8,128)(2,1)S(1)}, bf16[1,1,1,1,40,128]{5,4,3,2,1,0:T(8,128)(2,1)S(1)}, u32[]{:S(2)}, u32[]{:S(2)}) collective-permute-start(bf16[1,1,1,1,40,128]{5,4,3,2,1,0:T(8,128)(2,1)S(1)} %get-tuple-element.53), channel_id=1, source_target_pairs={{0,96},{32,0},{64,32},{96,64},{1,97},{33,1},{65,33},{97,65},{2,98}... | collective-permute-start | bytes 30728 | tf_op jit(solution)/shard_map/ppermute | solution.py:136
  165.3 5.2 %collective-permute-start.18 = (bf16[1,1,1,1,40,128]{5,4,3,2,1,0:T(8,128)(2,1)S(1)}, bf16[1,1,1,1,40,128]{5,4,3,2,1,0:T(8,128)(2,1)S(1)}, u32[]{:S(2)}, u32[]{:S(2)}) collective-permute-start(bf16[1,1,1,1,40,128]{5,4,3,2,1,0:T(8,128)(2,1)S(1)} %get-tuple-element.54), channel_id=1, source_target_pairs={{0,64},{32,96},{64,0},{96,32},{1,65},{33,97},{65,1},{97,33},{2,66}... | collective-permute-start | bytes 30728 | tf_op jit(solution)/shard_map/ppermute | solution.py:136
  166.5 4.9 %collective-permute-start.17 = (bf16[1,1,1,1,40,128]{5,4,3,2,1,0:T(8,128)(2,1)S(1)}, bf16[1,1,1,1,40,128]{5,4,3,2,1,0:T(8,128)(2,1)S(1)}, u32[]{:S(2)}, u32[]{:S(2)}) collective-permute-start(bf16[1,1,1,1,40,128]{5,4,3,2,1,0:T(8,128)(2,1)S(1)} %get-tuple-element.52), channel_id=1, source_target_pairs={{0,32},{32,64},{64,96},{96,0},{1,33},{33,65},{65,97},{97,1},{2,34}... | collective-permute-start | bytes 30728 | tf_op jit(solution)/shard_map/ppermute | solution.py:136
  171.4 4.8 %copy-start.17 = (bf16[256,768]{1,0:T(8,128)(2,1)S(1)}, bf16[256,768]{1,0:T(8,128)(2,1)}, u32[]{:S(2)}) copy-start(bf16[256,768]{1,0:T(8,128)(2,1)} %param.13) | copy-start | bytes 1179652
  (10 other events, 13.7 us)

commit v11 on v8

--- a/solution.py
+++ b/solution.py
@@ -106,8 +106,9 @@
     factor = float(device_count * edge_slots.shape[1]) ** (-0.5)
     share = embedding_width // device_count
     lanes = 128
-    bias_rows = jnp.zeros((device_count, 8, lanes), jnp.float32)
-    bias_rows = bias_rows.at[:, 0, :share].set(term_bias.reshape(device_count, share))
+    bias_rows = jnp.pad(
+        term_bias.reshape(device_count, 1, share), ((0, 0), (0, 7), (0, lanes - share))
+    )
     partials = jnp.concatenate(
         [
             constraint_term.reshape(device_count, -1, lanes),
@@ -125,7 +126,7 @@
             home_var = homes[:, :, embedding_width:]
         ring = lax.axis_size(axis_name)
         me = lax.axis_index(axis_name)
-        sent = summed if axis_name == "c" else summed.astype(jnp.bfloat16)
+        sent = summed.astype(jnp.bfloat16)
         total = lax.dynamic_slice_in_dim(summed, me, 1, position)
         for shift in range(1, ring):
             chunk = lax.dynamic_slice_in_dim(sent, (me + shift) % ring, 1, position)

time: 166 us -> 164 us (0.988)
    dynamic_slice x4 -> x3, local copies, waits for them, and re-layouts: 3.29 us -> 1.52 us  [on_device(): chunk = lax.dynamic_slice_in_dim(sent, (me + shift) % ring, 1, position)]
  transfers between devices with their start and end apart: 12 -> 12, of which waited for: 10 -> 9; matrix products, arithmetic and copies ran while one was open for 9% -> 9% of each run, Pallas kernels for 0% -> 0%
where the time goes in v11:
time: 164 us; the launch traced here: 163 us
  waiting for transfers between devices  54.1 us (33%)
  matrix products  43 us (26%)
  starting transfers between devices  27.3 us (17%)
  local copies, waits for them, and re-layouts  26.8 us (16%)
  other arithmetic  11.2 us (7%)
    all_to_all x1, waiting for transfers between devices, on_device(): lax.all_to_all(outgoing, DEVICE_AXES, split_axis=0, concat_axis=0, tiled=...  27.1 us
    ppermute x10, waiting for transfers between devices, on_device(): total = total + lax.ppermute(chunk, axis_name, pairs).astype(jnp.float32)  27 us
    all_to_all x1, starting transfers between devices, on_device(): lax.all_to_all(outgoing, DEVICE_AXES, split_axis=0, concat_axis=0, tiled=...  11.2 us
    ppermute x10, starting transfers between devices, on_device(): total = total + lax.ppermute(chunk, axis_name, pairs).astype(jnp.float32)  9.16 us
    dot_general x1, matrix products, on_device(): jnp.dot(edge_con, constraint_weight, preferred_element_type=jnp.float32)  8.66 us
    dot_general x1, matrix products, on_device(): lax.dot_general(table_var3, cotangent_mirror_rows, slot_dims, preferred_e...  7.86 us
    dot_general x1, matrix products, on_device(): jnp.dot(edge_var, variable_weight, preferred_element_type=jnp.float32)  7.04 us
    all_to_all x1, starting transfers between devices, on_device(): lax.all_to_all(backward, DEVICE_AXES, split_axis=0, concat_axis=0, tiled=...  7.01 us
  transfers between devices with their start and end apart: 12, of which 9 were waited for; matrix products, arithmetic and copies ran while one was open for 9% of the time, Pallas kernels for 0%

profile of v11, /device:TPU:0, one launch (start us, length us, event | category | flops | bytes accessed | tf_op | source)
XLA Modules:
  0.0 163.5 jit_solution(15546199206842194601)
XLA Ops:
  1.5 1.4 convolution_convert_fusion.2
  2.9 1.4 convolution_convert_fusion.3
  5.9 2.2 %reshape.95 = bf16[128,4,2304]{2,1,0:T(4,128)(2,1)} reshape(bf16[512,2304]{1,0:T(8,128)(2,1)S(1)} %pad_maximum_fusion.1) | data formatting | bytes 4718592 | tf_op jit(solution)/shard_map/reshape | solution.py:39
  8.0 11.2 %all-to-all-start = ((bf16[128,4,2304]{2,1,0:T(4,128)(2,1)}), bf16[128,4,2304]{2,1,0:T(4,128)(2,1)S(1)}, u32[]{:S(2)}, u32[]{:S(2)}) async-start(bf16[128,4,2304]{2,1,0:T(4,128)(2,1)} %reshape.95), calls=%async_computation | async-start | bytes 4718592 | tf_op jit(solution)/shard_map/all_to_all | solution.py:42
  24.5 27.1 %all-to-all-done = bf16[128,4,2304]{2,1,0:T(4,128)(2,1)S(1)} async-done(((bf16[128,4,2304]{2,1,0:T(4,128)(2,1)}), bf16[128,4,2304]{2,1,0:T(4,128)(2,1)S(1)}, u32[]{:S(2)}, u32[]{:S(2)}) %all-to-all-start) | async-done | bytes 2359328 | tf_op jit(solution)/shard_map/all_to_all | solution.py:42
  51.6 2.0 %fusion.99 = (bf16[128,4,768]{2,1,0:T(4,128)(2,1)}, bf16[128,4,768]{2,1,0:T(4,128)(2,1)}, bf16[128,4,768]{2,1,0:T(4,128)(2,1)}) fusion(bf16[128,4,2304]{2,1,0:T(4,128)(2,1)S(1)} %all-to-all-done), kind=kLoop, calls=%fused_computation.147 | loop fusion | bytes 4718592 | tf_op jit(solution)/shard_map/slice | solution.py:45
  53.6 8.7 %fusion.35 = f32[2048,768]{1,0:T(8,128)} fusion(bf16[768,768]{1,0:T(8,128)(2,1)} %param.12, s32[128,4]{0,1:T(4,128)} %multiply_add_fusion, s32[2048]{0:T(1024)} %bitcast.63, bf16[128,4,768]{2,1,0:T(4,128)(2,1)} %get-tuple-element.16), kind=kOutput, calls=%fused_computation.59 | convolution fusion | flops 4031250432 | bytes 8267776 | tf_op jit(solution)/shard_map/dot_general | solution.py:68
  62.3 7.0 %fusion.36 = f32[2048,768]{1,0:T(8,128)} fusion(bf16[768,768]{1,0:T(8,128)(2,1)S(1)} %copy-done, s32[128,4]{0,1:T(4,128)S(1)} %copy-done.12, s32[2048]{0:T(1024)S(1)} %bitcast.66, bf16[128,4,768]{2,1,0:T(4,128)(2,1)S(1)} %copy-done.3), kind=kOutput, calls=%fused_computation.60 | convolution fusion | flops 4031250432 | bytes 8267776 | tf_op jit(solution)/shard_map/dot_general | solution.py:69
  69.4 7.9 %convert_reduce_fusion = (f32[768]{0:T(1024)S(1)}, bf16[2048,768]{1,0:T(8,128)(2,1)S(1)}) fusion(f32[2048]{0:T(1024)S(1)} %mul.41, f32[768]{0:T(1024)S(1)} %copy-done.16, f32[2048,768]{1,0:T(8,128)} %fusion.35, f32[2048,768]{1,0:T(8,128)} %fusion.36, bf16[128,4,768]{2,1,0:T(4,128)(2,1)S(1)} %copy-done.4, s32[128,4]{0,1:T(4,128)S(1)} %copy-done.12, ...), kind=kOutput, calls=%fused_computation.5 | convolution fusion | flops 1635777792 | bytes 16539648 | tf_op jit(solution)/shard_map/dot_general | solution.py:64
  77.2 2.0 %fusion.30 = bf16[512,768]{1,0:T(8,128)(2,1)S(1)} fusion(bf16[2048,768]{1,0:T(8,128)(2,1)S(1)} %get-tuple-element.36, s32[2048]{0:T(1024)S(1)} %bitcast.68), kind=kOutput, calls=%fused_computation.49 | convolution fusion | flops 1614151680 | bytes 3940352 | tf_op jit(solution)/shard_map/dot_general | solution.py:81
  79.3 2.9 %fusion.31 = bf16[512,768]{1,0:T(8,128)(2,1)} fusion(bf16[2048,768]{1,0:T(8,128)(2,1)S(1)} %get-tuple-element.36, s32[2048]{0:T(1024)S(1)} %bitcast.64), kind=kOutput, calls=%fused_computation.50 | convolution fusion | flops 1614151680 | bytes 3940352 | tf_op jit(solution)/shard_map/dot_general | solution.py:78
  84.1 2.2 %convolution_bitcast_fusion = f32[768,768]{1,0:T(8,128)S(1)} fusion(bf16[128,4,768]{2,1,0:T(4,128)(2,1)} %reshape.99, bf16[128,4,768]{2,1,0:T(4,128)(2,1)} %get-tuple-element.17), kind=kOutput, calls=%fused_computation.44 | convolution fusion | flops 603979776 | bytes 3932160 | tf_op jit(solution)/shard_map/dot_general | solution.py:99
  86.3 1.7 %concatenate.19 = f32[4,2,4,4,36,128]{5,4,3,2,1,0:T(8,128)} reshape(f32[768,768]{1,0:T(8,128)S(1)} %convolution_bitcast_fusion) | data formatting | bytes 4718592 | tf_op jit(solution)/shard_map/concatenate | solution.py:112
  88.0 2.4 %reshape.98 = bf16[128,4,768]{2,1,0:T(4,128)(2,1)} reshape(bf16[512,768]{1,0:T(8,128)(2,1)} %fusion.31) | data formatting | bytes 1572864 | tf_op jit(solution)/shard_map/reshape | solution.py:95
  90.4 2.2 %convolution_bitcast_fusion.1 = f32[768,768]{1,0:T(8,128)S(1)} fusion(bf16[128,4,768]{2,1,0:T(4,128)(2,1)} %reshape.98, bf16[128,4,768]{2,1,0:T(4,128)(2,1)} %get-tuple-element.16), kind=kOutput, calls=%fused_computation.45 | convolution fusion | flops 603979776 | bytes 3932160 | tf_op jit(solution)/shard_map/dot_general | solution.py:93
  92.5 1.7 %concatenate.18 = f32[4,2,4,4,36,128]{5,4,3,2,1,0:T(8,128)} reshape(f32[768,768]{1,0:T(8,128)S(1)} %convolution_bitcast_fusion.1) | data formatting | bytes 4718592 | tf_op jit(solution)/shard_map/concatenate | solution.py:112
  95.2 3.2 %pad_maximum_fusion = f32[4,2,4,4,80,128]{5,4,3,2,1,0:T(8,128)S(1)} fusion(f32[4,2,4,4,8,128]{5,4,3,2,1,0:T(8,128)S(1)} %bitcast.57, f32[4,2,4,4,36,128]{5,4,3,2,1,0:T(8,128)} %concatenate.19, f32[4,2,4,4,36,128]{5,4,3,2,1,0:T(8,128)} %concatenate.18), kind=kLoop, calls=%fused_computation.6 | loop fusion | flops 2621440 | bytes 10485760 | tf_op jit(solution)/shard_map/concatenate | solution.py:112
  98.4 2.3 %copy-done.1 = f32[4,2,4,4,80,128]{5,4,3,2,1,0:T(8,128)} copy-done((f32[4,2,4,4,80,128]{5,4,3,2,1,0:T(8,128)}, f32[4,2,4,4,80,128]{5,4,3,2,1,0:T(8,128)S(1)}, u32[]{:S(2)}) %copy-start.1) | copy-done | bytes 5242904
  105.7 2.4 %convert_add_fusion = f32[4,1,4,4,80,128]{5,4,3,2,1,0:T(8,128)S(1)} fusion(bf16[4,1,4,4,80,128]{5,4,3,2,1,0:T(8,128)(2,1)} %collective-permute-done, f32[4,2,4,4,80,128]{5,4,3,2,1,0:T(8,128)} %copy-done.1, s32[]{:T(128)S(6)} %select_n.130), kind=kLoop, calls=%fused_computation.18 | loop fusion | flops 1310720 | bytes 6553604 | tf_op jit(solution)/shard_map/add | solution.py:134
  108.1 1.5 copy-done.2
  110.7 1.8 %collective-permute-start.3 = (bf16[4,1,4,1,80,128]{5,4,3,2,1,0:T(8,128)(2,1)}, bf16[4,1,4,1,80,128]{5,4,3,2,1,0:T(8,128)(2,1)}, u32[]{:S(2)}, u32[]{:S(2)}) collective-permute-start(bf16[4,1,4,1,80,128]{5,4,3,2,1,0:T(8,128)(2,1)} %get-tuple-element.21), channel_id=1, source_target_pairs={{0,3},{1,0},{2,1},{3,2},{4,7},{5,4},{6,5},{7,6},{8,11},{9,8},{10,9... | collective-permute-start | bytes 983048 | tf_op jit(solution)/shard_map/ppermute | solution.py:134
  113.7 7.0 %all-to-all-start.1 = ((bf16[128,4,1536]{2,1,0:T(4,128)(2,1)}), bf16[128,4,1536]{2,1,0:T(4,128)(2,1)S(1)}, u32[]{:S(2)}, u32[]{:S(2)}) async-start(bf16[128,4,1536]{2,1,0:T(4,128)(2,1)} %reshape.97), calls=%async_computation.1 | async-start | bytes 3145728 | tf_op jit(solution)/shard_map/all_to_all | solution.py:124
  120.8 6.9 %collective-permute-done.3 = bf16[4,1,4,1,80,128]{5,4,3,2,1,0:T(8,128)(2,1)} collective-permute-done((bf16[4,1,4,1,80,128]{5,4,3,2,1,0:T(8,128)(2,1)}, bf16[4,1,4,1,80,128]{5,4,3,2,1,0:T(8,128)(2,1)}, u32[]{:S(2)}, u32[]{:S(2)}) %collective-permute-start.3) | collective-permute-done | bytes 327712 | tf_op jit(solution)/shard_map/ppermute | solution.py:134
  127.7 3.4 %collective-permute-done.1 = bf16[4,1,4,1,80,128]{5,4,3,2,1,0:T(8,128)(2,1)} collective-permute-done((bf16[4,1,4,1,80,128]{5,4,3,2,1,0:T(8,128)(2,1)S(1)}, bf16[4,1,4,1,80,128]{5,4,3,2,1,0:T(8,128)(2,1)}, u32[]{:S(2)}, u32[]{:S(2)}) %collective-permute-start.1) | collective-permute-done | bytes 327712 | tf_op jit(solution)/shard_map/ppermute | solution.py:134
  131.1 1.5 fusion.98
  134.6 1.7 %collective-permute-start.5 = (bf16[4,1,1,1,80,128]{5,4,3,2,1,0:T(8,128)(2,1)}, bf16[4,1,1,1,80,128]{5,4,3,2,1,0:T(8,128)(2,1)}, u32[]{:S(2)}, u32[]{:S(2)}) collective-permute-start(bf16[4,1,1,1,80,128]{5,4,3,2,1,0:T(8,128)(2,1)} %get-tuple-element.25), channel_id=1, source_target_pairs={{0,8},{4,12},{8,0},{12,4},{1,9},{5,13},{9,1},{13,5},{2,10},{6,14},... | collective-permute-start | bytes 245768 | tf_op jit(solution)/shard_map/ppermute | solution.py:134
  136.2 8.4 %collective-permute-done.6 = bf16[4,1,1,1,80,128]{5,4,3,2,1,0:T(8,128)(2,1)S(1)} collective-permute-done((bf16[4,1,1,1,80,128]{5,4,3,2,1,0:T(8,128)(2,1)}, bf16[4,1,1,1,80,128]{5,4,3,2,1,0:T(8,128)(2,1)S(1)}, u32[]{:S(2)}, u32[]{:S(2)}) %collective-permute-start.6) | collective-permute-done | bytes 81952 | tf_op jit(solution)/shard_map/ppermute | solution.py:134
  144.6 2.6 %collective-permute-done.5 = bf16[4,1,1,1,80,128]{5,4,3,2,1,0:T(8,128)(2,1)} collective-permute-done((bf16[4,1,1,1,80,128]{5,4,3,2,1,0:T(8,128)(2,1)}, bf16[4,1,1,1,80,128]{5,4,3,2,1,0:T(8,128)(2,1)}, u32[]{:S(2)}, u32[]{:S(2)}) %collective-permute-start.5) | collective-permute-done | bytes 81952 | tf_op jit(solution)/shard_map/ppermute | solution.py:134
  147.2 1.6 collective-permute-done.4
  148.8 1.6 fusion.97
  151.7 1.4 collective-permute-start.8
  154.3 2.8 %collective-permute-done.8 = bf16[1,1,1,1,80,128]{5,4,3,2,1,0:T(8,128)(2,1)S(1)} collective-permute-done((bf16[1,1,1,1,80,128]{5,4,3,2,1,0:T(8,128)(2,1)S(1)}, bf16[1,1,1,1,80,128]{5,4,3,2,1,0:T(8,128)(2,1)S(1)}, u32[]{:S(2)}, u32[]{:S(2)}) %collective-permute-start.8) | collective-permute-done | bytes 20512 | tf_op jit(solution)/shard_map/ppermute | solution.py:134
  (81 shorter events, 28.3 us)
Async XLA Ops:
  0.6 61.6 %copy-start = (bf16[768,768]{1,0:T(8,128)(2,1)S(1)}, bf16[768,768]{1,0:T(8,128)(2,1)}, u32[]{:S(2)}) copy-start(bf16[768,768]{1,0:T(8,128)(2,1)} %param.13) | copy-start | bytes 3538948
  8.0 11.2 %copy-start.13 = (s32[2,1,128]{2,1,0:T(1,128)S(1)}, s32[2,1,128]{2,1,0:T(1,128)}, u32[]{:S(2)}) copy-start(s32[2,1,128]{2,1,0:T(1,128)} %param.16) | copy-start | bytes 3076
  8.0 43.6 %all-to-all-start = ((bf16[128,4,2304]{2,1,0:T(4,128)(2,1)}), bf16[128,4,2304]{2,1,0:T(4,128)(2,1)S(1)}, u32[]{:S(2)}, u32[]{:S(2)}) async-start(bf16[128,4,2304]{2,1,0:T(4,128)(2,1)} %reshape.95), calls=%async_computation | async-start | bytes 4718592 | tf_op jit(solution)/shard_map/all_to_all | solution.py:42
  21.9 2.0 %copy-start.8 = (s32[1,2048]{1,0:T(1,128)}, s32[1,2048]{1,0:T(1,128)S(1)}, u32[]{:S(2)}) copy-start(s32[1,2048]{1,0:T(1,128)S(1)} %get-tuple-element.32) | copy-start | bytes 24580
  21.9 2.0 %copy-start.10 = (s32[1,2048]{1,0:T(1,128)}, s32[1,2048]{1,0:T(1,128)S(1)}, u32[]{:S(2)}) copy-start(s32[1,2048]{1,0:T(1,128)S(1)} %get-tuple-element.31) | copy-start | bytes 24580
  53.6 8.7 %copy-start.3 = (bf16[128,4,768]{2,1,0:T(4,128)(2,1)S(1)}, bf16[128,4,768]{2,1,0:T(4,128)(2,1)}, u32[]{:S(2)}) copy-start(bf16[128,4,768]{2,1,0:T(4,128)(2,1)} %get-tuple-element.17) | copy-start | bytes 2359300
  53.6 8.7 %copy-start.11 = (s32[1,2048]{1,0:T(1,128)S(1)}, s32[1,2048]{1,0:T(1,128)}, u32[]{:S(2)}) copy-start(s32[1,2048]{1,0:T(1,128)} %copy-done.10) | copy-start | bytes 24580
  53.6 8.7 %copy-start.12 = (s32[128,4]{0,1:T(4,128)S(1)}, s32[128,4]{0,1:T(4,128)}, u32[]{:S(2)}) copy-start(s32[128,4]{0,1:T(4,128)} %multiply_add_fusion) | copy-start | bytes 6148
  62.3 7.1 %copy-start.4 = (bf16[128,4,768]{2,1,0:T(4,128)(2,1)S(1)}, bf16[128,4,768]{2,1,0:T(4,128)(2,1)}, u32[]{:S(2)}) copy-start(bf16[128,4,768]{2,1,0:T(4,128)(2,1)} %get-tuple-element.15) | copy-start | bytes 2359300
  62.3 7.1 %copy-start.16 = (f32[768]{0:T(1024)S(1)}, f32[768]{0:T(1024)}, u32[]{:S(2)}) copy-start(f32[768]{0:T(1024)} %param.14) | copy-start | bytes 9220
  77.2 2.1 %copy-start.9 = (s32[1,2048]{1,0:T(1,128)S(1)}, s32[1,2048]{1,0:T(1,128)}, u32[]{:S(2)}) copy-start(s32[1,2048]{1,0:T(1,128)} %copy-done.8) | copy-start | bytes 24580
  79.3 3.7 %copy-start.5 = (bf16[512,768]{1,0:T(8,128)(2,1)}, bf16[512,768]{1,0:T(8,128)(2,1)S(1)}, u32[]{:S(2)}) copy-start(bf16[512,768]{1,0:T(8,128)(2,1)S(1)} %fusion.30) | copy-start | bytes 2359300
  95.2 6.9 %copy-start.6 = (bf16[512,768]{1,0:T(8,128)(2,1)S(1)}, bf16[512,768]{1,0:T(8,128)(2,1)}, u32[]{:S(2)}) copy-start(bf16[512,768]{1,0:T(8,128)(2,1)} %copy-done.5) | copy-start | bytes 2359300
  98.4 2.3 %copy-start.1 = (f32[4,2,4,4,80,128]{5,4,3,2,1,0:T(8,128)}, f32[4,2,4,4,80,128]{5,4,3,2,1,0:T(8,128)S(1)}, u32[]{:S(2)}) copy-start(f32[4,2,4,4,80,128]{5,4,3,2,1,0:T(8,128)S(1)} %pad_maximum_fusion) | copy-start | bytes 15728644
  100.7 2.2 %copy-start.7 = (bf16[512,768]{1,0:T(8,128)(2,1)S(1)}, bf16[512,768]{1,0:T(8,128)(2,1)}, u32[]{:S(2)}) copy-start(bf16[512,768]{1,0:T(8,128)(2,1)} %fusion.31) | copy-start | bytes 2359300
  102.1 3.6 %collective-permute-start = (bf16[4,1,4,4,80,128]{5,4,3,2,1,0:T(8,128)(2,1)}, bf16[4,1,4,4,80,128]{5,4,3,2,1,0:T(8,128)(2,1)}, u32[]{:S(2)}, u32[]{:S(2)}) collective-permute-start(bf16[4,1,4,4,80,128]{5,4,3,2,1,0:T(8,128)(2,1)} %dynamic-slice_convert_fusion), channel_id=1, source_target_pairs={{0,16},{16,0},{1,17},{17,1},{2,18},{18,2},{3,19},{19,3},{4,20},{20... | collective-permute-start | bytes 3932168 | tf_op jit(solution)/shard_map/ppermute | solution.py:134
  102.1 1.3 copy-start.14
  108.1 1.5 copy-start.2
  110.7 17.0 %collective-permute-start.3 = (bf16[4,1,4,1,80,128]{5,4,3,2,1,0:T(8,128)(2,1)}, bf16[4,1,4,1,80,128]{5,4,3,2,1,0:T(8,128)(2,1)}, u32[]{:S(2)}, u32[]{:S(2)}) collective-permute-start(bf16[4,1,4,1,80,128]{5,4,3,2,1,0:T(8,128)(2,1)} %get-tuple-element.21), channel_id=1, source_target_pairs={{0,3},{1,0},{2,1},{3,2},{4,7},{5,4},{6,5},{7,6},{8,11},{9,8},{10,9... | collective-permute-start | bytes 983048 | tf_op jit(solution)/shard_map/ppermute | solution.py:134
  112.4 15.3 %collective-permute-start.2 = (bf16[4,1,4,1,80,128]{5,4,3,2,1,0:T(8,128)(2,1)S(1)}, bf16[4,1,4,1,80,128]{5,4,3,2,1,0:T(8,128)(2,1)}, u32[]{:S(2)}, u32[]{:S(2)}) collective-permute-start(bf16[4,1,4,1,80,128]{5,4,3,2,1,0:T(8,128)(2,1)S(1)} %get-tuple-element.22), channel_id=1, source_target_pairs={{0,2},{1,3},{2,0},{3,1},{4,6},{5,7},{6,4},{7,5},{8,10},{9,11},{10,... | collective-permute-start | bytes 983048 | tf_op jit(solution)/shard_map/ppermute | solution.py:134
  113.7 17.4 %collective-permute-start.1 = (bf16[4,1,4,1,80,128]{5,4,3,2,1,0:T(8,128)(2,1)S(1)}, bf16[4,1,4,1,80,128]{5,4,3,2,1,0:T(8,128)(2,1)}, u32[]{:S(2)}, u32[]{:S(2)}) collective-permute-start(bf16[4,1,4,1,80,128]{5,4,3,2,1,0:T(8,128)(2,1)S(1)} %get-tuple-element.20), channel_id=1, source_target_pairs={{0,1},{1,2},{2,3},{3,0},{4,5},{5,6},{6,7},{7,4},{8,9},{9,10},{10,1... | collective-permute-start | bytes 983048 | tf_op jit(solution)/shard_map/ppermute | solution.py:134
  113.7 47.0 %all-to-all-start.1 = ((bf16[128,4,1536]{2,1,0:T(4,128)(2,1)}), bf16[128,4,1536]{2,1,0:T(4,128)(2,1)S(1)}, u32[]{:S(2)}, u32[]{:S(2)}) async-start(bf16[128,4,1536]{2,1,0:T(4,128)(2,1)} %reshape.97), calls=%async_computation.1 | async-start | bytes 3145728 | tf_op jit(solution)/shard_map/all_to_all | solution.py:124
  133.3 11.3 %collective-permute-start.6 = (bf16[4,1,1,1,80,128]{5,4,3,2,1,0:T(8,128)(2,1)}, bf16[4,1,1,1,80,128]{5,4,3,2,1,0:T(8,128)(2,1)S(1)}, u32[]{:S(2)}, u32[]{:S(2)}) collective-permute-start(bf16[4,1,1,1,80,128]{5,4,3,2,1,0:T(8,128)(2,1)} %get-tuple-element.24), channel_id=1, source_target_pairs={{0,12},{4,0},{8,4},{12,8},{1,13},{5,1},{9,5},{13,9},{2,14},{6,2},{... | collective-permute-start | bytes 245768 | tf_op jit(solution)/shard_map/ppermute | solution.py:134
  134.6 12.6 %collective-permute-start.5 = (bf16[4,1,1,1,80,128]{5,4,3,2,1,0:T(8,128)(2,1)}, bf16[4,1,1,1,80,128]{5,4,3,2,1,0:T(8,128)(2,1)}, u32[]{:S(2)}, u32[]{:S(2)}) collective-permute-start(bf16[4,1,1,1,80,128]{5,4,3,2,1,0:T(8,128)(2,1)} %get-tuple-element.25), channel_id=1, source_target_pairs={{0,8},{4,12},{8,0},{12,4},{1,9},{5,13},{9,1},{13,5},{2,10},{6,14},... | collective-permute-start | bytes 245768 | tf_op jit(solution)/shard_map/ppermute | solution.py:134
  136.2 12.6 %collective-permute-start.4 = (bf16[4,1,1,1,80,128]{5,4,3,2,1,0:T(8,128)(2,1)}, bf16[4,1,1,1,80,128]{5,4,3,2,1,0:T(8,128)(2,1)}, u32[]{:S(2)}, u32[]{:S(2)}) collective-permute-start(bf16[4,1,1,1,80,128]{5,4,3,2,1,0:T(8,128)(2,1)} %get-tuple-element.23), channel_id=1, source_target_pairs={{0,4},{4,8},{8,12},{12,0},{1,5},{5,9},{9,13},{13,1},{2,6},{6,10},{... | collective-permute-start | bytes 245768 | tf_op jit(solution)/shard_map/ppermute | solution.py:134
  150.4 11.9 %copy-start.15 = (bf16[256,768]{1,0:T(8,128)(2,1)S(1)}, bf16[256,768]{1,0:T(8,128)(2,1)}, u32[]{:S(2)}) copy-start(bf16[256,768]{1,0:T(8,128)(2,1)} %param.11) | copy-start | bytes 1179652
  150.5 3.9 %collective-permute-start.9 = (bf16[1,1,1,1,80,128]{5,4,3,2,1,0:T(8,128)(2,1)S(1)}, bf16[1,1,1,1,80,128]{5,4,3,2,1,0:T(8,128)(2,1)S(1)}, u32[]{:S(2)}, u32[]{:S(2)}) collective-permute-start(bf16[1,1,1,1,80,128]{5,4,3,2,1,0:T(8,128)(2,1)S(1)} %get-tuple-element.27), channel_id=1, source_target_pairs={{0,96},{32,0},{64,32},{96,64},{1,97},{33,1},{65,33},{97,65},{2,98}... | collective-permute-start | bytes 61448 | tf_op jit(solution)/shard_map/ppermute | solution.py:134
  151.7 5.4 %collective-permute-start.8 = (bf16[1,1,1,1,80,128]{5,4,3,2,1,0:T(8,128)(2,1)S(1)}, bf16[1,1,1,1,80,128]{5,4,3,2,1,0:T(8,128)(2,1)S(1)}, u32[]{:S(2)}, u32[]{:S(2)}) collective-permute-start(bf16[1,1,1,1,80,128]{5,4,3,2,1,0:T(8,128)(2,1)S(1)} %get-tuple-element.28), channel_id=1, source_target_pairs={{0,64},{32,96},{64,0},{96,32},{1,65},{33,97},{65,1},{97,33},{2,66}... | collective-permute-start | bytes 61448 | tf_op jit(solution)/shard_map/ppermute | solution.py:134
  153.1 5.0 %collective-permute-start.7 = (bf16[1,1,1,1,80,128]{5,4,3,2,1,0:T(8,128)(2,1)S(1)}, bf16[1,1,1,1,80,128]{5,4,3,2,1,0:T(8,128)(2,1)S(1)}, u32[]{:S(2)}, u32[]{:S(2)}) collective-permute-start(bf16[1,1,1,1,80,128]{5,4,3,2,1,0:T(8,128)(2,1)S(1)} %get-tuple-element.26), channel_id=1, source_target_pairs={{0,32},{32,64},{64,96},{96,0},{1,33},{33,65},{65,97},{97,1},{2,34}... | collective-permute-start | bytes 61448 | tf_op jit(solution)/shard_map/ppermute | solution.py:134

commit v12 on v11

--- a/solution.py
+++ b/solution.py
@@ -76,10 +76,10 @@
     )
     sum_dims = (((0,), (0,)), ((), ()))
     constraint_projection_gradient = lax.dot_general(
-        table_con, edge_delta, sum_dims, preferred_element_type=jnp.float32
+        table_con3, edge_delta, sum_dims, preferred_element_type=jnp.float32
     ).astype(jnp.bfloat16)
     variable_projection_gradient = lax.dot_general(
-        table_var, edge_delta, sum_dims, preferred_element_type=jnp.float32
+        table_var3, edge_delta, sum_dims, preferred_element_type=jnp.float32
     ).astype(jnp.bfloat16)
     back_con = jnp.dot(
         constraint_projection_gradient, constraint_weight.T, preferred_element_type=jnp.float32
@@ -87,18 +87,16 @@
     back_var = jnp.dot(
         variable_projection_gradient, variable_weight.T, preferred_element_type=jnp.float32
     ).astype(jnp.bfloat16)
-    backward = jnp.concatenate([back_con, back_var], axis=1).reshape(
-        device_count, slot_cap, 2 * embedding_width
-    )
+    backward = jnp.concatenate([back_con, back_var], axis=2)
     constraint_term = lax.dot_general(
         constraint_mirror_rows,
-        constraint_projection_gradient.reshape(device_count, slot_cap, embedding_width),
+        constraint_projection_gradient,
         (((0, 1), (0, 1)), ((), ())),
         preferred_element_type=jnp.float32,
     )
     variable_term = lax.dot_general(
         variable_mirror_rows,
-        variable_projection_gradient.reshape(device_count, slot_cap, embedding_width),
+        variable_projection_gradient,
         (((0, 1), (0, 1)), ((), ())),
         preferred_element_type=jnp.float32,
     )

time: 164 us -> 161 us (0.982)
  local copies, waits for them, and re-layouts: 26.8 us -> 24.3 us
    reshape x3 -> x0, local copies, waits for them, and re-layouts: 4.84 us -> none  [the longest x1 2.37 us: on_device(): constraint_projection_gradient.reshape(device_count, slot_cap, embedding_...]
    optimization_barrier x0 -> x1, local copies, waits for them, and re-layouts: none -> 2.37 us  [on_device(): backward, summed = lax.optimization_barrier((backward, summed))]
  transfers between devices with their start and end apart: 12 -> 12, of which waited for: 9 -> 10; matrix products, arithmetic and copies ran while one was open for 9% -> 10% of each run, Pallas kernels for 0% -> 0%
where the time goes in v12:
time: 161 us; the launch traced here: 160 us
  waiting for transfers between devices  52.7 us (33%)
  matrix products  44 us (27%)
  starting transfers between devices  27.3 us (17%)
  local copies, waits for them, and re-layouts  24.3 us (15%)
  other arithmetic  10.4 us (6%)
    all_to_all x1, waiting for transfers between devices, on_device(): lax.all_to_all(outgoing, DEVICE_AXES, split_axis=0, concat_axis=0, tiled=...  27.1 us
    ppermute x10, waiting for transfers between devices, on_device(): total = total + lax.ppermute(chunk, axis_name, pairs).astype(jnp.float32)  25.6 us
    all_to_all x1, starting transfers between devices, on_device(): lax.all_to_all(outgoing, DEVICE_AXES, split_axis=0, concat_axis=0, tiled=...  11.2 us
    dot_general x1, matrix products, on_device(): jnp.dot(edge_con, constraint_weight, preferred_element_type=jnp.float32)  9.26 us
    ppermute x10, starting transfers between devices, on_device(): total = total + lax.ppermute(chunk, axis_name, pairs).astype(jnp.float32)  9.15 us
    dot_general x1, matrix products, on_device(): jnp.dot(edge_var, variable_weight, preferred_element_type=jnp.float32)  7.65 us
    dot_general x1, matrix products, on_device(): lax.dot_general(table_var3, cotangent_mirror_rows, slot_dims, preferred_e...  7.09 us
    all_to_all x1, starting transfers between devices, on_device(): lax.all_to_all(backward, DEVICE_AXES, split_axis=0, concat_axis=0, tiled=...  6.97 us
  transfers between devices with their start and end apart: 12, of which 10 were waited for; matrix products, arithmetic and copies ran while one was open for 10% of the time, Pallas kernels for 0%

profile of v12, /device:TPU:0, one launch (start us, length us, event | category | flops | bytes accessed | tf_op | source)
XLA Modules:
  0.0 159.9 jit_solution(15641504787820922932)
XLA Ops:
  1.5 1.4 convolution_convert_fusion.2
  2.9 1.4 convolution_convert_fusion.3
  5.9 2.2 %reshape.86 = bf16[128,4,2304]{2,1,0:T(4,128)(2,1)} reshape(bf16[512,2304]{1,0:T(8,128)(2,1)S(1)} %pad_maximum_fusion.1) | data formatting | bytes 4718592 | tf_op jit(solution)/shard_map/reshape | solution.py:39
  8.0 11.2 %all-to-all-start = ((bf16[128,4,2304]{2,1,0:T(4,128)(2,1)}), bf16[128,4,2304]{2,1,0:T(4,128)(2,1)S(1)}, u32[]{:S(2)}, u32[]{:S(2)}) async-start(bf16[128,4,2304]{2,1,0:T(4,128)(2,1)} %reshape.86), calls=%async_computation | async-start | bytes 4718592 | tf_op jit(solution)/shard_map/all_to_all | solution.py:42
  24.5 27.1 %all-to-all-done = bf16[128,4,2304]{2,1,0:T(4,128)(2,1)S(1)} async-done(((bf16[128,4,2304]{2,1,0:T(4,128)(2,1)}), bf16[128,4,2304]{2,1,0:T(4,128)(2,1)S(1)}, u32[]{:S(2)}, u32[]{:S(2)}) %all-to-all-start) | async-done | bytes 2359328 | tf_op jit(solution)/shard_map/all_to_all | solution.py:42
  51.6 2.0 %fusion.107 = (bf16[128,4,768]{2,1,0:T(4,128)(2,1)}, bf16[128,4,768]{2,1,0:T(4,128)(2,1)}, bf16[128,4,768]{2,1,0:T(4,128)(2,1)}) fusion(bf16[128,4,2304]{2,1,0:T(4,128)(2,1)S(1)} %all-to-all-done), kind=kLoop, calls=%fused_computation.151 | loop fusion | bytes 4718592 | tf_op jit(solution)/shard_map/slice | solution.py:45
  53.6 9.3 %fusion.45 = f32[2048,768]{1,0:T(8,128)} fusion(bf16[768,768]{1,0:T(8,128)(2,1)} %param.12, s32[2048]{0:T(1024)} %bitcast.76, s32[128,4]{0,1:T(4,128)} %multiply_add_fusion, bf16[128,4,768]{2,1,0:T(4,128)(2,1)} %get-tuple-element.16), kind=kOutput, calls=%fused_computation.65 | convolution fusion | flops 4031250432 | bytes 8267776 | tf_op jit(solution)/shard_map/dot_general | solution.py:68
  62.9 7.6 %fusion.46 = f32[2048,768]{1,0:T(8,128)} fusion(bf16[768,768]{1,0:T(8,128)(2,1)S(1)} %copy-done, s32[2048]{0:T(1024)S(1)} %bitcast.79, s32[128,4]{0,1:T(4,128)S(1)} %copy-done.12, bf16[128,4,768]{2,1,0:T(4,128)(2,1)S(1)} %copy-done.4), kind=kOutput, calls=%fused_computation.66 | convolution fusion | flops 4031250432 | bytes 8267776 | tf_op jit(solution)/shard_map/dot_general | solution.py:69
  70.6 7.1 %convert_reduce_fusion = (f32[768]{0:T(1024)S(1)}, bf16[2048,768]{1,0:T(8,128)(2,1)S(1)}) fusion(f32[2048]{0:T(1024)S(1)} %mul.41, f32[768]{0:T(1024)S(1)} %copy-done.16, f32[2048,768]{1,0:T(8,128)} %fusion.45, f32[2048,768]{1,0:T(8,128)} %fusion.46, bf16[128,4,768]{2,1,0:T(4,128)(2,1)S(1)} %copy-done.5, s32[2048]{0:T(1024)S(1)} %bitcast.80, ...), kind=kOutput, calls=%fused_computation.5 | convolution fusion | flops 1635777792 | bytes 16539648 | tf_op jit(solution)/shard_map/dot_general | solution.py:64
  77.7 2.7 %fusion.37 = bf16[128,4,768]{2,0,1:T(8,128)(2,1)} fusion(bf16[2048,768]{1,0:T(8,128)(2,1)S(1)} %get-tuple-element.36, s32[2048]{0:T(1024)S(1)} %bitcast.81, s32[128,4]{0,1:T(4,128)S(1)} %copy-done.12), kind=kOutput, calls=%fused_computation.54 | convolution fusion | flops 1614151680 | bytes 3942400 | tf_op jit(solution)/shard_map/dot_general | solution.py:81
  80.4 2.8 %fusion.34 = bf16[128,4,768]{2,0,1:T(8,128)(2,1)} fusion(bf16[2048,768]{1,0:T(8,128)(2,1)S(1)} %get-tuple-element.36, s32[2048]{0:T(1024)S(1)} %bitcast.77, s32[128,4]{0,1:T(4,128)S(1)} %copy-done.12), kind=kOutput, calls=%fused_computation.53 | convolution fusion | flops 1614151680 | bytes 3942400 | tf_op jit(solution)/shard_map/dot_general | solution.py:78
  84.0 2.2 %convolution_bitcast_fusion = f32[768,768]{1,0:T(8,128)S(1)} fusion(bf16[128,4,768]{2,0,1:T(8,128)(2,1)} %fusion.37, bf16[128,4,768]{2,1,0:T(4,128)(2,1)} %get-tuple-element.17), kind=kOutput, calls=%fused_computation.48 | convolution fusion | flops 603979776 | bytes 3932160 | tf_op jit(solution)/shard_map/dot_general | solution.py:97
  86.2 1.7 %concatenate.19 = f32[4,2,4,4,36,128]{5,4,3,2,1,0:T(8,128)} reshape(f32[768,768]{1,0:T(8,128)S(1)} %convolution_bitcast_fusion) | data formatting | bytes 4718592 | tf_op jit(solution)/shard_map/concatenate | solution.py:110
  87.9 2.2 %convolution_bitcast_fusion.1 = f32[768,768]{1,0:T(8,128)S(1)} fusion(bf16[128,4,768]{2,0,1:T(8,128)(2,1)} %fusion.34, bf16[128,4,768]{2,1,0:T(4,128)(2,1)} %get-tuple-element.16), kind=kOutput, calls=%fused_computation.49 | convolution fusion | flops 603979776 | bytes 3932160 | tf_op jit(solution)/shard_map/dot_general | solution.py:91
  90.1 1.7 %concatenate.18 = f32[4,2,4,4,36,128]{5,4,3,2,1,0:T(8,128)} reshape(f32[768,768]{1,0:T(8,128)S(1)} %convolution_bitcast_fusion.1) | data formatting | bytes 4718592 | tf_op jit(solution)/shard_map/concatenate | solution.py:110
  92.7 3.2 %pad_maximum_fusion = f32[4,2,4,4,80,128]{5,4,3,2,1,0:T(8,128)S(1)} fusion(f32[4,2,4,4,8,128]{5,4,3,2,1,0:T(8,128)S(1)} %bitcast.70, f32[4,2,4,4,36,128]{5,4,3,2,1,0:T(8,128)} %concatenate.19, f32[4,2,4,4,36,128]{5,4,3,2,1,0:T(8,128)} %concatenate.18), kind=kLoop, calls=%fused_computation.6 | loop fusion | flops 2621440 | bytes 10485760 | tf_op jit(solution)/shard_map/concatenate | solution.py:110
  95.9 2.3 %copy-done.1 = f32[4,2,4,4,80,128]{5,4,3,2,1,0:T(8,128)} copy-done((f32[4,2,4,4,80,128]{5,4,3,2,1,0:T(8,128)}, f32[4,2,4,4,80,128]{5,4,3,2,1,0:T(8,128)S(1)}, u32[]{:S(2)}) %copy-start.1) | copy-done | bytes 5242904
  102.6 1.7 %convert_add_fusion = f32[4,1,4,4,80,128]{5,4,3,2,1,0:T(8,128)S(1)} fusion(bf16[4,1,4,4,80,128]{5,4,3,2,1,0:T(8,128)(2,1)} %collective-permute-done, f32[4,2,4,4,80,128]{5,4,3,2,1,0:T(8,128)S(1)} %copy-done.2, s32[]{:T(128)S(6)} %select_n.130), kind=kLoop, calls=%fused_computation.18 | loop fusion | flops 1310720 | bytes 6553604 | tf_op jit(solution)/shard_map/add | solution.py:132
  104.3 1.5 copy-done.3
  106.8 1.7 %collective-permute-start.3 = (bf16[4,1,4,1,80,128]{5,4,3,2,1,0:T(8,128)(2,1)}, bf16[4,1,4,1,80,128]{5,4,3,2,1,0:T(8,128)(2,1)}, u32[]{:S(2)}, u32[]{:S(2)}) collective-permute-start(bf16[4,1,4,1,80,128]{5,4,3,2,1,0:T(8,128)(2,1)} %get-tuple-element.21), channel_id=1, source_target_pairs={{0,3},{1,0},{2,1},{3,2},{4,7},{5,4},{6,5},{7,6},{8,11},{9,8},{10,9... | collective-permute-start | bytes 983048 | tf_op jit(solution)/shard_map/ppermute | solution.py:132
  109.9 2.4 %copy.37 = bf16[128,4,1536]{2,1,0:T(4,128)(2,1)} copy(bf16[128,4,1536]{2,0,1:T(8,128)(2,1)S(1)} %pad_maximum_fusion.2) | data formatting | bytes 3145728 | tf_op jit(solution)/shard_map/optimization_barrier | solution.py:121
  112.2 7.0 %all-to-all-start.1 = ((bf16[128,4,1536]{2,1,0:T(4,128)(2,1)}), bf16[128,4,1536]{2,1,0:T(4,128)(2,1)S(1)}, u32[]{:S(2)}, u32[]{:S(2)}) async-start(bf16[128,4,1536]{2,1,0:T(4,128)(2,1)} %copy.37), calls=%async_computation.1 | async-start | bytes 3145728 | tf_op jit(solution)/shard_map/all_to_all | solution.py:122
  119.3 1.5 collective-permute-done.2
  120.7 6.4 %collective-permute-done.1 = bf16[4,1,4,1,80,128]{5,4,3,2,1,0:T(8,128)(2,1)} collective-permute-done((bf16[4,1,4,1,80,128]{5,4,3,2,1,0:T(8,128)(2,1)S(1)}, bf16[4,1,4,1,80,128]{5,4,3,2,1,0:T(8,128)(2,1)}, u32[]{:S(2)}, u32[]{:S(2)}) %collective-permute-start.1) | collective-permute-done | bytes 327712 | tf_op jit(solution)/shard_map/ppermute | solution.py:132
  127.2 1.5 fusion.106
  130.6 1.7 %collective-permute-start.5 = (bf16[4,1,1,1,80,128]{5,4,3,2,1,0:T(8,128)(2,1)}, bf16[4,1,1,1,80,128]{5,4,3,2,1,0:T(8,128)(2,1)}, u32[]{:S(2)}, u32[]{:S(2)}) collective-permute-start(bf16[4,1,1,1,80,128]{5,4,3,2,1,0:T(8,128)(2,1)} %get-tuple-element.25), channel_id=1, source_target_pairs={{0,8},{4,12},{8,0},{12,4},{1,9},{5,13},{9,1},{13,5},{2,10},{6,14},... | collective-permute-start | bytes 245768 | tf_op jit(solution)/shard_map/ppermute | solution.py:132
  132.3 8.4 %collective-permute-done.6 = bf16[4,1,1,1,80,128]{5,4,3,2,1,0:T(8,128)(2,1)S(1)} collective-permute-done((bf16[4,1,1,1,80,128]{5,4,3,2,1,0:T(8,128)(2,1)}, bf16[4,1,1,1,80,128]{5,4,3,2,1,0:T(8,128)(2,1)S(1)}, u32[]{:S(2)}, u32[]{:S(2)}) %collective-permute-start.6) | collective-permute-done | bytes 81952 | tf_op jit(solution)/shard_map/ppermute | solution.py:132
  140.7 2.6 %collective-permute-done.5 = bf16[4,1,1,1,80,128]{5,4,3,2,1,0:T(8,128)(2,1)} collective-permute-done((bf16[4,1,1,1,80,128]{5,4,3,2,1,0:T(8,128)(2,1)}, bf16[4,1,1,1,80,128]{5,4,3,2,1,0:T(8,128)(2,1)}, u32[]{:S(2)}, u32[]{:S(2)}) %collective-permute-start.5) | collective-permute-done | bytes 81952 | tf_op jit(solution)/shard_map/ppermute | solution.py:132
  143.2 1.7 %collective-permute-done.4 = bf16[4,1,1,1,80,128]{5,4,3,2,1,0:T(8,128)(2,1)} collective-permute-done((bf16[4,1,1,1,80,128]{5,4,3,2,1,0:T(8,128)(2,1)}, bf16[4,1,1,1,80,128]{5,4,3,2,1,0:T(8,128)(2,1)}, u32[]{:S(2)}, u32[]{:S(2)}) %collective-permute-start.4) | collective-permute-done | bytes 81952 | tf_op jit(solution)/shard_map/ppermute | solution.py:132
  145.0 1.6 %fusion.105 = (bf16[4,1,1,1,80,128]{5,4,3,2,1,0:T(8,128)(2,1)S(1)}, f32[4,1,1,1,80,128]{5,4,3,2,1,0:T(8,128)}) fusion(bf16[4,1,1,1,80,128]{5,4,3,2,1,0:T(8,128)(2,1)S(1)} %collective-permute-done.6, bf16[4,1,1,1,80,128]{5,4,3,2,1,0:T(8,128)(2,1)} %collective-permute-done.5, bf16[4,1,1,1,80,128]{5,4,3,2,1,0:T(8,128)(2,1)} %collective-permute-done.4, ...), kind=kLoop, calls=%fused_computation.149 | loop fusion | flops 286720 | bytes 655364 | tf_op jit(solution)/shard_map/convert_element_type | solution.py:127
  147.9 1.6 collective-permute-start.8
  150.5 2.9 %collective-permute-done.8 = bf16[1,1,1,1,80,128]{5,4,3,2,1,0:T(8,128)(2,1)S(1)} collective-permute-done((bf16[1,1,1,1,80,128]{5,4,3,2,1,0:T(8,128)(2,1)S(1)}, bf16[1,1,1,1,80,128]{5,4,3,2,1,0:T(8,128)(2,1)S(1)}, u32[]{:S(2)}, u32[]{:S(2)}) %collective-permute-start.8) | collective-permute-done | bytes 20512 | tf_op jit(solution)/shard_map/ppermute | solution.py:132
  (79 shorter events, 26.5 us)
Async XLA Ops:
  0.6 62.2 %copy-start = (bf16[768,768]{1,0:T(8,128)(2,1)S(1)}, bf16[768,768]{1,0:T(8,128)(2,1)}, u32[]{:S(2)}) copy-start(bf16[768,768]{1,0:T(8,128)(2,1)} %param.13) | copy-start | bytes 3538948
  8.0 11.2 %copy-start.13 = (s32[2,1,128]{2,1,0:T(1,128)S(1)}, s32[2,1,128]{2,1,0:T(1,128)}, u32[]{:S(2)}) copy-start(s32[2,1,128]{2,1,0:T(1,128)} %param.16) | copy-start | bytes 3076
  8.0 43.6 %all-to-all-start = ((bf16[128,4,2304]{2,1,0:T(4,128)(2,1)}), bf16[128,4,2304]{2,1,0:T(4,128)(2,1)S(1)}, u32[]{:S(2)}, u32[]{:S(2)}) async-start(bf16[128,4,2304]{2,1,0:T(4,128)(2,1)} %reshape.86), calls=%async_computation | async-start | bytes 4718592 | tf_op jit(solution)/shard_map/all_to_all | solution.py:42
  21.9 2.0 %copy-start.8 = (s32[1,2048]{1,0:T(1,128)}, s32[1,2048]{1,0:T(1,128)S(1)}, u32[]{:S(2)}) copy-start(s32[1,2048]{1,0:T(1,128)S(1)} %get-tuple-element.32) | copy-start | bytes 24580
  21.9 2.0 %copy-start.10 = (s32[1,2048]{1,0:T(1,128)}, s32[1,2048]{1,0:T(1,128)S(1)}, u32[]{:S(2)}) copy-start(s32[1,2048]{1,0:T(1,128)S(1)} %get-tuple-element.31) | copy-start | bytes 24580
  53.6 9.3 %copy-start.4 = (bf16[128,4,768]{2,1,0:T(4,128)(2,1)S(1)}, bf16[128,4,768]{2,1,0:T(4,128)(2,1)}, u32[]{:S(2)}) copy-start(bf16[128,4,768]{2,1,0:T(4,128)(2,1)} %get-tuple-element.17) | copy-start | bytes 2359300
  53.6 9.3 %copy-start.11 = (s32[1,2048]{1,0:T(1,128)S(1)}, s32[1,2048]{1,0:T(1,128)}, u32[]{:S(2)}) copy-start(s32[1,2048]{1,0:T(1,128)} %copy-done.10) | copy-start | bytes 24580
  53.6 9.3 %copy-start.12 = (s32[128,4]{0,1:T(4,128)S(1)}, s32[128,4]{0,1:T(4,128)}, u32[]{:S(2)}) copy-start(s32[128,4]{0,1:T(4,128)} %multiply_add_fusion) | copy-start | bytes 6148
  62.9 7.7 %copy-start.5 = (bf16[128,4,768]{2,1,0:T(4,128)(2,1)S(1)}, bf16[128,4,768]{2,1,0:T(4,128)(2,1)}, u32[]{:S(2)}) copy-start(bf16[128,4,768]{2,1,0:T(4,128)(2,1)} %get-tuple-element.15) | copy-start | bytes 2359300
  62.9 7.7 %copy-start.16 = (f32[768]{0:T(1024)S(1)}, f32[768]{0:T(1024)}, u32[]{:S(2)}) copy-start(f32[768]{0:T(1024)} %param.14) | copy-start | bytes 9220
  77.7 2.8 %copy-start.9 = (s32[1,2048]{1,0:T(1,128)S(1)}, s32[1,2048]{1,0:T(1,128)}, u32[]{:S(2)}) copy-start(s32[1,2048]{1,0:T(1,128)} %copy-done.8) | copy-start | bytes 24580
  92.7 5.9 %copy-start.6 = (bf16[128,4,768]{2,0,1:T(8,128)(2,1)S(1)}, bf16[128,4,768]{2,0,1:T(8,128)(2,1)}, u32[]{:S(2)}) copy-start(bf16[128,4,768]{2,0,1:T(8,128)(2,1)} %fusion.37) | copy-start | bytes 2359300
  95.9 2.3 %copy-start.1 = (f32[4,2,4,4,80,128]{5,4,3,2,1,0:T(8,128)}, f32[4,2,4,4,80,128]{5,4,3,2,1,0:T(8,128)S(1)}, u32[]{:S(2)}) copy-start(f32[4,2,4,4,80,128]{5,4,3,2,1,0:T(8,128)S(1)} %pad_maximum_fusion) | copy-start | bytes 15728644
  98.5 3.2 %collective-permute-start = (bf16[4,1,4,4,80,128]{5,4,3,2,1,0:T(8,128)(2,1)S(1)}, bf16[4,1,4,4,80,128]{5,4,3,2,1,0:T(8,128)(2,1)}, u32[]{:S(2)}, u32[]{:S(2)}) collective-permute-start(bf16[4,1,4,4,80,128]{5,4,3,2,1,0:T(8,128)(2,1)S(1)} %dynamic-slice_convert_fusion), channel_id=1, source_target_pairs={{0,16},{16,0},{1,17},{17,1},{2,18},{18,2},{3,19},{19,3},{4,20},{20... | collective-permute-start | bytes 3932168 | tf_op jit(solution)/shard_map/ppermute | solution.py:132
  98.6 1.1 copy-start.7
  98.6 1.5 copy-start.14
  100.1 2.5 %copy-start.2 = (f32[4,2,4,4,80,128]{5,4,3,2,1,0:T(8,128)S(1)}, f32[4,2,4,4,80,128]{5,4,3,2,1,0:T(8,128)}, u32[]{:S(2)}) copy-start(f32[4,2,4,4,80,128]{5,4,3,2,1,0:T(8,128)} %copy-done.1) | copy-start | bytes 15728644
  104.3 1.5 copy-start.3
  106.8 12.5 %collective-permute-start.3 = (bf16[4,1,4,1,80,128]{5,4,3,2,1,0:T(8,128)(2,1)}, bf16[4,1,4,1,80,128]{5,4,3,2,1,0:T(8,128)(2,1)}, u32[]{:S(2)}, u32[]{:S(2)}) collective-permute-start(bf16[4,1,4,1,80,128]{5,4,3,2,1,0:T(8,128)(2,1)} %get-tuple-element.21), channel_id=1, source_target_pairs={{0,3},{1,0},{2,1},{3,2},{4,7},{5,4},{6,5},{7,6},{8,11},{9,8},{10,9... | collective-permute-start | bytes 983048 | tf_op jit(solution)/shard_map/ppermute | solution.py:132
  108.5 12.2 %collective-permute-start.2 = (bf16[4,1,4,1,80,128]{5,4,3,2,1,0:T(8,128)(2,1)S(1)}, bf16[4,1,4,1,80,128]{5,4,3,2,1,0:T(8,128)(2,1)}, u32[]{:S(2)}, u32[]{:S(2)}) collective-permute-start(bf16[4,1,4,1,80,128]{5,4,3,2,1,0:T(8,128)(2,1)S(1)} %get-tuple-element.22), channel_id=1, source_target_pairs={{0,2},{1,3},{2,0},{3,1},{4,6},{5,7},{6,4},{7,5},{8,10},{9,11},{10,... | collective-permute-start | bytes 983048 | tf_op jit(solution)/shard_map/ppermute | solution.py:132
  109.8 17.3 %collective-permute-start.1 = (bf16[4,1,4,1,80,128]{5,4,3,2,1,0:T(8,128)(2,1)S(1)}, bf16[4,1,4,1,80,128]{5,4,3,2,1,0:T(8,128)(2,1)}, u32[]{:S(2)}, u32[]{:S(2)}) collective-permute-start(bf16[4,1,4,1,80,128]{5,4,3,2,1,0:T(8,128)(2,1)S(1)} %get-tuple-element.20), channel_id=1, source_target_pairs={{0,1},{1,2},{2,3},{3,0},{4,5},{5,6},{6,7},{7,4},{8,9},{9,10},{10,1... | collective-permute-start | bytes 983048 | tf_op jit(solution)/shard_map/ppermute | solution.py:132
  112.2 44.8 %all-to-all-start.1 = ((bf16[128,4,1536]{2,1,0:T(4,128)(2,1)}), bf16[128,4,1536]{2,1,0:T(4,128)(2,1)S(1)}, u32[]{:S(2)}, u32[]{:S(2)}) async-start(bf16[128,4,1536]{2,1,0:T(4,128)(2,1)} %copy.37), calls=%async_computation.1 | async-start | bytes 3145728 | tf_op jit(solution)/shard_map/all_to_all | solution.py:122
  129.4 11.2 %collective-permute-start.6 = (bf16[4,1,1,1,80,128]{5,4,3,2,1,0:T(8,128)(2,1)}, bf16[4,1,1,1,80,128]{5,4,3,2,1,0:T(8,128)(2,1)S(1)}, u32[]{:S(2)}, u32[]{:S(2)}) collective-permute-start(bf16[4,1,1,1,80,128]{5,4,3,2,1,0:T(8,128)(2,1)} %get-tuple-element.24), channel_id=1, source_target_pairs={{0,12},{4,0},{8,4},{12,8},{1,13},{5,1},{9,5},{13,9},{2,14},{6,2},{... | collective-permute-start | bytes 245768 | tf_op jit(solution)/shard_map/ppermute | solution.py:132
  130.6 12.6 %collective-permute-start.5 = (bf16[4,1,1,1,80,128]{5,4,3,2,1,0:T(8,128)(2,1)}, bf16[4,1,1,1,80,128]{5,4,3,2,1,0:T(8,128)(2,1)}, u32[]{:S(2)}, u32[]{:S(2)}) collective-permute-start(bf16[4,1,1,1,80,128]{5,4,3,2,1,0:T(8,128)(2,1)} %get-tuple-element.25), channel_id=1, source_target_pairs={{0,8},{4,12},{8,0},{12,4},{1,9},{5,13},{9,1},{13,5},{2,10},{6,14},... | collective-permute-start | bytes 245768 | tf_op jit(solution)/shard_map/ppermute | solution.py:132
  132.3 12.7 %collective-permute-start.4 = (bf16[4,1,1,1,80,128]{5,4,3,2,1,0:T(8,128)(2,1)}, bf16[4,1,1,1,80,128]{5,4,3,2,1,0:T(8,128)(2,1)}, u32[]{:S(2)}, u32[]{:S(2)}) collective-permute-start(bf16[4,1,1,1,80,128]{5,4,3,2,1,0:T(8,128)(2,1)} %get-tuple-element.23), channel_id=1, source_target_pairs={{0,4},{4,8},{8,12},{12,0},{1,5},{5,9},{9,13},{13,1},{2,6},{6,10},{... | collective-permute-start | bytes 245768 | tf_op jit(solution)/shard_map/ppermute | solution.py:132
  146.6 12.1 %copy-start.15 = (bf16[256,768]{1,0:T(8,128)(2,1)S(1)}, bf16[256,768]{1,0:T(8,128)(2,1)}, u32[]{:S(2)}) copy-start(bf16[256,768]{1,0:T(8,128)(2,1)} %param.11) | copy-start | bytes 1179652
  146.6 3.9 %collective-permute-start.9 = (bf16[1,1,1,1,80,128]{5,4,3,2,1,0:T(8,128)(2,1)S(1)}, bf16[1,1,1,1,80,128]{5,4,3,2,1,0:T(8,128)(2,1)S(1)}, u32[]{:S(2)}, u32[]{:S(2)}) collective-permute-start(bf16[1,1,1,1,80,128]{5,4,3,2,1,0:T(8,128)(2,1)S(1)} %get-tuple-element.27), channel_id=1, source_target_pairs={{0,96},{32,0},{64,32},{96,64},{1,97},{33,1},{65,33},{97,65},{2,98}... | collective-permute-start | bytes 61448 | tf_op jit(solution)/shard_map/ppermute | solution.py:132
  147.9 5.5 %collective-permute-start.8 = (bf16[1,1,1,1,80,128]{5,4,3,2,1,0:T(8,128)(2,1)S(1)}, bf16[1,1,1,1,80,128]{5,4,3,2,1,0:T(8,128)(2,1)S(1)}, u32[]{:S(2)}, u32[]{:S(2)}) collective-permute-start(bf16[1,1,1,1,80,128]{5,4,3,2,1,0:T(8,128)(2,1)S(1)} %get-tuple-element.28), channel_id=1, source_target_pairs={{0,64},{32,96},{64,0},{96,32},{1,65},{33,97},{65,1},{97,33},{2,66}... | collective-permute-start | bytes 61448 | tf_op jit(solution)/shard_map/ppermute | solution.py:132
  149.5 5.0 %collective-permute-start.7 = (bf16[1,1,1,1,80,128]{5,4,3,2,1,0:T(8,128)(2,1)S(1)}, bf16[1,1,1,1,80,128]{5,4,3,2,1,0:T(8,128)(2,1)S(1)}, u32[]{:S(2)}, u32[]{:S(2)}) collective-permute-start(bf16[1,1,1,1,80,128]{5,4,3,2,1,0:T(8,128)(2,1)S(1)} %get-tuple-element.26), channel_id=1, source_target_pairs={{0,32},{32,64},{64,96},{96,0},{1,33},{33,65},{65,97},{97,1},{2,34}... | collective-permute-start | bytes 61448 | tf_op jit(solution)/shard_map/ppermute | solution.py:132

commit v13 on v12

--- a/solution.py
+++ b/solution.py
@@ -31,14 +31,18 @@
     embedding_width = constraint_features.shape[1]
     replica_rows = device_count * slot_cap
     master_rows = constraint_features.shape[0]
-    select_con = one_hot_table(send_rows[0, 0], master_rows)
-    select_var = one_hot_table(send_rows[1, 0], master_rows)
+    slot_shape = (device_count, slot_cap, master_rows)
+    master_ids = lax.broadcasted_iota(jnp.int32, slot_shape, 2)
+    select_con = jnp.where(
+        master_ids == send_rows[0, 0].reshape(device_count, slot_cap, 1), 1.0, 0.0
+    ).astype(jnp.bfloat16)
+    select_var = jnp.where(
+        master_ids == send_rows[1, 0].reshape(device_count, slot_cap, 1), 1.0, 0.0
+    ).astype(jnp.bfloat16)
     out_con = pick_rows(select_con, constraint_features)
     out_var = pick_rows(select_var, variable_features)
     out_cot = pick_rows(select_var, variable_cotangent)
-    outgoing = jnp.concatenate([out_con, out_var, out_cot], axis=1).reshape(
-        device_count, slot_cap, 3 * embedding_width
-    )
+    outgoing = jnp.concatenate([out_con, out_var, out_cot], axis=2)
     incoming = lax.all_to_all(outgoing, DEVICE_AXES, split_axis=0, concat_axis=0, tiled=True)
     constraint_mirror_rows = incoming[:, :, :embedding_width]
     variable_mirror_rows = incoming[:, :, embedding_width : 2 * embedding_width]
@@ -133,13 +137,13 @@
         summed = total
     summed = summed.reshape(-1, lanes)
     grad_con = lax.dot_general(
-        select_con.reshape(device_count, slot_cap, -1),
+        select_con,
         home_con,
         (((0, 1), (0, 1)), ((), ())),
         preferred_element_type=jnp.float32,
     )
     grad_var = lax.dot_general(
-        select_var.reshape(device_count, slot_cap, -1),
+        select_var,
         home_var,
         (((0, 1), (0, 1)), ((), ())),
         preferred_element_type=jnp.float32,

time: 161 us -> 162 us (level)
    concatenate x0 -> x1, local copies, waits for them, and re-layouts: none -> 3.25 us  [on_device(): outgoing = jnp.concatenate([out_con, out_var, out_cot], axis=2)]
    reshape x1 -> x0, local copies, waits for them, and re-layouts: 2.16 us -> none  [on_device(): jnp.concatenate([out_con, out_var, out_cot], axis=1)]
where the time goes in v13:
time: 162 us; the launch traced here: 161 us
  waiting for transfers between devices  52.9 us (33%)
  matrix products  44.1 us (27%)
  starting transfers between devices  27.5 us (17%)
  local copies, waits for them, and re-layouts  25.4 us (16%)
  other arithmetic  10.5 us (6%)
    all_to_all x1, waiting for transfers between devices, on_device(): lax.all_to_all(outgoing, DEVICE_AXES, split_axis=0, concat_axis=0, tiled=...  26.9 us
    ppermute x10, waiting for transfers between devices, on_device(): total = total + lax.ppermute(chunk, axis_name, pairs).astype(jnp.float32)  26 us
    all_to_all x1, starting transfers between devices, on_device(): lax.all_to_all(outgoing, DEVICE_AXES, split_axis=0, concat_axis=0, tiled=...  11.4 us
    dot_general x1, matrix products, on_device(): jnp.dot(edge_con, constraint_weight, preferred_element_type=jnp.float32)  9.25 us
    ppermute x10, starting transfers between devices, on_device(): total = total + lax.ppermute(chunk, axis_name, pairs).astype(jnp.float32)  9.15 us
    dot_general x1, matrix products, on_device(): jnp.dot(edge_var, variable_weight, preferred_element_type=jnp.float32)  7.65 us
    dot_general x1, matrix products, on_device(): lax.dot_general(table_var3, cotangent_mirror_rows, slot_dims, preferred_e...  7.14 us
    all_to_all x1, starting transfers between devices, on_device(): lax.all_to_all(backward, DEVICE_AXES, split_axis=0, concat_axis=0, tiled=...  6.99 us
  transfers between devices with their start and end apart: 12, of which 10 were waited for; matrix products, arithmetic and copies ran while one was open for 10% of the time, Pallas kernels for 0%

profile of v13, /device:TPU:0, one launch (start us, length us, event | category | flops | bytes accessed | tf_op | source)
XLA Modules:
  0.0 161.4 jit_solution(9600940310036002414)
XLA Ops:
  1.6 1.4 convolution_convert_fusion.2
  4.7 1.4 convolution_convert_fusion.4
  6.3 3.2 %copy.36 = bf16[128,4,2304]{2,1,0:T(4,128)(2,1)} copy(bf16[128,4,2304]{2,0,1:T(8,128)(2,1)S(1)} %pad_maximum_fusion.1) | data formatting | bytes 4718592 | tf_op jit(solution)/shard_map/concatenate | solution.py:45
  9.5 11.4 %all-to-all-start = ((bf16[128,4,2304]{2,1,0:T(4,128)(2,1)}), bf16[128,4,2304]{2,1,0:T(4,128)(2,1)S(1)}, u32[]{:S(2)}, u32[]{:S(2)}) async-start(bf16[128,4,2304]{2,1,0:T(4,128)(2,1)} %copy.36), calls=%async_computation | async-start | bytes 4718592 | tf_op jit(solution)/shard_map/all_to_all | solution.py:46
  26.2 26.9 %all-to-all-done = bf16[128,4,2304]{2,1,0:T(4,128)(2,1)S(1)} async-done(((bf16[128,4,2304]{2,1,0:T(4,128)(2,1)}), bf16[128,4,2304]{2,1,0:T(4,128)(2,1)S(1)}, u32[]{:S(2)}, u32[]{:S(2)}) %all-to-all-start) | async-done | bytes 2359328 | tf_op jit(solution)/shard_map/all_to_all | solution.py:46
  53.1 2.0 %fusion.110 = (bf16[128,4,768]{2,1,0:T(4,128)(2,1)}, bf16[128,4,768]{2,1,0:T(4,128)(2,1)}, bf16[128,4,768]{2,1,0:T(4,128)(2,1)}) fusion(bf16[128,4,2304]{2,1,0:T(4,128)(2,1)S(1)} %all-to-all-done), kind=kLoop, calls=%fused_computation.150 | loop fusion | bytes 4718592 | tf_op jit(solution)/shard_map/slice | solution.py:49
  55.1 9.2 %fusion.45 = f32[2048,768]{1,0:T(8,128)} fusion(bf16[768,768]{1,0:T(8,128)(2,1)} %param.12, s32[2048]{0:T(1024)} %bitcast.80, s32[128,4]{0,1:T(4,128)S(1)} %multiply_add_fusion, bf16[128,4,768]{2,1,0:T(4,128)(2,1)} %get-tuple-element.16), kind=kOutput, calls=%fused_computation.65 | convolution fusion | flops 4031250432 | bytes 8267776 | tf_op jit(solution)/shard_map/dot_general | solution.py:72
  64.4 7.6 %fusion.46 = f32[2048,768]{1,0:T(8,128)} fusion(bf16[768,768]{1,0:T(8,128)(2,1)S(1)} %copy-done, s32[2048]{0:T(1024)S(1)} %bitcast.83, s32[128,4]{0,1:T(4,128)S(1)} %multiply_add_fusion, bf16[128,4,768]{2,1,0:T(4,128)(2,1)S(1)} %copy-done.4), kind=kOutput, calls=%fused_computation.66 | convolution fusion | flops 4031250432 | bytes 8267776 | tf_op jit(solution)/shard_map/dot_general | solution.py:73
  72.0 7.1 %convert_reduce_fusion = (f32[768]{0:T(1024)S(1)}, bf16[2048,768]{1,0:T(8,128)(2,1)S(1)}) fusion(f32[2048]{0:T(1024)S(1)} %copy-done.9, f32[768]{0:T(1024)S(1)} %copy-done.16, f32[2048,768]{1,0:T(8,128)} %fusion.45, f32[2048,768]{1,0:T(8,128)} %fusion.46, bf16[128,4,768]{2,1,0:T(4,128)(2,1)S(1)} %copy-done.5, s32[2048]{0:T(1024)S(1)} %bitcast.84, ...), kind=kOutput, calls=%fused_computation.5 | convolution fusion | flops 1635777792 | bytes 16539648 | tf_op jit(solution)/shard_map/dot_general | solution.py:68
  79.2 2.7 %fusion.37 = bf16[128,4,768]{2,0,1:T(8,128)(2,1)} fusion(bf16[2048,768]{1,0:T(8,128)(2,1)S(1)} %get-tuple-element.34, s32[2048]{0:T(1024)S(1)} %bitcast.85, s32[128,4]{0,1:T(4,128)S(1)} %multiply_add_fusion), kind=kOutput, calls=%fused_computation.54 | convolution fusion | flops 1614151680 | bytes 3942400 | tf_op jit(solution)/shard_map/dot_general | solution.py:85
  81.9 2.8 %fusion.34 = bf16[128,4,768]{2,0,1:T(8,128)(2,1)} fusion(bf16[2048,768]{1,0:T(8,128)(2,1)S(1)} %get-tuple-element.34, s32[2048]{0:T(1024)S(1)} %bitcast.81, s32[128,4]{0,1:T(4,128)S(1)} %multiply_add_fusion), kind=kOutput, calls=%fused_computation.53 | convolution fusion | flops 1614151680 | bytes 3942400 | tf_op jit(solution)/shard_map/dot_general | solution.py:82
  85.5 2.2 %convolution_bitcast_fusion = f32[768,768]{1,0:T(8,128)S(1)} fusion(bf16[128,4,768]{2,0,1:T(8,128)(2,1)} %fusion.37, bf16[128,4,768]{2,1,0:T(4,128)(2,1)} %get-tuple-element.17), kind=kOutput, calls=%fused_computation.48 | convolution fusion | flops 603979776 | bytes 3932160 | tf_op jit(solution)/shard_map/dot_general | solution.py:101
  87.7 1.7 %concatenate.19 = f32[4,2,4,4,36,128]{5,4,3,2,1,0:T(8,128)} reshape(f32[768,768]{1,0:T(8,128)S(1)} %convolution_bitcast_fusion) | data formatting | bytes 4718592 | tf_op jit(solution)/shard_map/concatenate | solution.py:114
  89.4 2.2 %convolution_bitcast_fusion.1 = f32[768,768]{1,0:T(8,128)S(1)} fusion(bf16[128,4,768]{2,0,1:T(8,128)(2,1)} %fusion.34, bf16[128,4,768]{2,1,0:T(4,128)(2,1)} %get-tuple-element.16), kind=kOutput, calls=%fused_computation.49 | convolution fusion | flops 603979776 | bytes 3932160 | tf_op jit(solution)/shard_map/dot_general | solution.py:95
  91.6 1.7 %concatenate.18 = f32[4,2,4,4,36,128]{5,4,3,2,1,0:T(8,128)} reshape(f32[768,768]{1,0:T(8,128)S(1)} %convolution_bitcast_fusion.1) | data formatting | bytes 4718592 | tf_op jit(solution)/shard_map/concatenate | solution.py:114
  94.2 3.2 %pad_maximum_fusion = f32[4,2,4,4,80,128]{5,4,3,2,1,0:T(8,128)S(1)} fusion(f32[4,2,4,4,8,128]{5,4,3,2,1,0:T(8,128)S(1)} %bitcast.74, f32[4,2,4,4,36,128]{5,4,3,2,1,0:T(8,128)} %concatenate.19, f32[4,2,4,4,36,128]{5,4,3,2,1,0:T(8,128)} %concatenate.18), kind=kLoop, calls=%fused_computation.6 | loop fusion | flops 2621440 | bytes 10485760 | tf_op jit(solution)/shard_map/concatenate | solution.py:114
  97.4 2.3 %copy-done.1 = f32[4,2,4,4,80,128]{5,4,3,2,1,0:T(8,128)} copy-done((f32[4,2,4,4,80,128]{5,4,3,2,1,0:T(8,128)}, f32[4,2,4,4,80,128]{5,4,3,2,1,0:T(8,128)S(1)}, u32[]{:S(2)}) %copy-start.1) | copy-done | bytes 5242904
  104.1 1.7 %convert_add_fusion = f32[4,1,4,4,80,128]{5,4,3,2,1,0:T(8,128)S(1)} fusion(bf16[4,1,4,4,80,128]{5,4,3,2,1,0:T(8,128)(2,1)} %collective-permute-done, f32[4,2,4,4,80,128]{5,4,3,2,1,0:T(8,128)S(1)} %copy-done.2, s32[]{:T(128)S(6)} %select_n.123), kind=kLoop, calls=%fused_computation.18 | loop fusion | flops 1310720 | bytes 6553604 | tf_op jit(solution)/shard_map/add | solution.py:136
  105.8 1.5 copy-done.3
  108.3 1.7 %collective-permute-start.3 = (bf16[4,1,4,1,80,128]{5,4,3,2,1,0:T(8,128)(2,1)}, bf16[4,1,4,1,80,128]{5,4,3,2,1,0:T(8,128)(2,1)}, u32[]{:S(2)}, u32[]{:S(2)}) collective-permute-start(bf16[4,1,4,1,80,128]{5,4,3,2,1,0:T(8,128)(2,1)} %get-tuple-element.21), channel_id=1, source_target_pairs={{0,3},{1,0},{2,1},{3,2},{4,7},{5,4},{6,5},{7,6},{8,11},{9,8},{10,9... | collective-permute-start | bytes 983048 | tf_op jit(solution)/shard_map/ppermute | solution.py:136
  111.3 2.4 %copy.46 = bf16[128,4,1536]{2,1,0:T(4,128)(2,1)} copy(bf16[128,4,1536]{2,0,1:T(8,128)(2,1)S(1)} %pad_maximum_fusion.2) | data formatting | bytes 3145728 | tf_op jit(solution)/shard_map/optimization_barrier | solution.py:125
  113.7 7.0 %all-to-all-start.1 = ((bf16[128,4,1536]{2,1,0:T(4,128)(2,1)}), bf16[128,4,1536]{2,1,0:T(4,128)(2,1)S(1)}, u32[]{:S(2)}, u32[]{:S(2)}) async-start(bf16[128,4,1536]{2,1,0:T(4,128)(2,1)} %copy.46), calls=%async_computation.1 | async-start | bytes 3145728 | tf_op jit(solution)/shard_map/all_to_all | solution.py:126
  120.8 1.5 collective-permute-done.2
  122.2 6.4 %collective-permute-done.1 = bf16[4,1,4,1,80,128]{5,4,3,2,1,0:T(8,128)(2,1)} collective-permute-done((bf16[4,1,4,1,80,128]{5,4,3,2,1,0:T(8,128)(2,1)S(1)}, bf16[4,1,4,1,80,128]{5,4,3,2,1,0:T(8,128)(2,1)}, u32[]{:S(2)}, u32[]{:S(2)}) %collective-permute-start.1) | collective-permute-done | bytes 327712 | tf_op jit(solution)/shard_map/ppermute | solution.py:136
  128.7 1.5 fusion.109
  132.2 1.6 %collective-permute-start.5 = (bf16[4,1,1,1,80,128]{5,4,3,2,1,0:T(8,128)(2,1)}, bf16[4,1,1,1,80,128]{5,4,3,2,1,0:T(8,128)(2,1)}, u32[]{:S(2)}, u32[]{:S(2)}) collective-permute-start(bf16[4,1,1,1,80,128]{5,4,3,2,1,0:T(8,128)(2,1)} %get-tuple-element.25), channel_id=1, source_target_pairs={{0,8},{4,12},{8,0},{12,4},{1,9},{5,13},{9,1},{13,5},{2,10},{6,14},... | collective-permute-start | bytes 245768 | tf_op jit(solution)/shard_map/ppermute | solution.py:136
  133.8 8.4 %collective-permute-done.6 = bf16[4,1,1,1,80,128]{5,4,3,2,1,0:T(8,128)(2,1)S(1)} collective-permute-done((bf16[4,1,1,1,80,128]{5,4,3,2,1,0:T(8,128)(2,1)}, bf16[4,1,1,1,80,128]{5,4,3,2,1,0:T(8,128)(2,1)S(1)}, u32[]{:S(2)}, u32[]{:S(2)}) %collective-permute-start.6) | collective-permute-done | bytes 81952 | tf_op jit(solution)/shard_map/ppermute | solution.py:136
  142.2 2.6 %collective-permute-done.5 = bf16[4,1,1,1,80,128]{5,4,3,2,1,0:T(8,128)(2,1)} collective-permute-done((bf16[4,1,1,1,80,128]{5,4,3,2,1,0:T(8,128)(2,1)}, bf16[4,1,1,1,80,128]{5,4,3,2,1,0:T(8,128)(2,1)}, u32[]{:S(2)}, u32[]{:S(2)}) %collective-permute-start.5) | collective-permute-done | bytes 81952 | tf_op jit(solution)/shard_map/ppermute | solution.py:136
  144.7 1.7 %collective-permute-done.4 = bf16[4,1,1,1,80,128]{5,4,3,2,1,0:T(8,128)(2,1)} collective-permute-done((bf16[4,1,1,1,80,128]{5,4,3,2,1,0:T(8,128)(2,1)}, bf16[4,1,1,1,80,128]{5,4,3,2,1,0:T(8,128)(2,1)}, u32[]{:S(2)}, u32[]{:S(2)}) %collective-permute-start.4) | collective-permute-done | bytes 81952 | tf_op jit(solution)/shard_map/ppermute | solution.py:136
  146.5 1.6 %fusion.108 = (bf16[4,1,1,1,80,128]{5,4,3,2,1,0:T(8,128)(2,1)S(1)}, f32[4,1,1,1,80,128]{5,4,3,2,1,0:T(8,128)}) fusion(bf16[4,1,1,1,80,128]{5,4,3,2,1,0:T(8,128)(2,1)S(1)} %collective-permute-done.6, bf16[4,1,1,1,80,128]{5,4,3,2,1,0:T(8,128)(2,1)} %collective-permute-done.5, bf16[4,1,1,1,80,128]{5,4,3,2,1,0:T(8,128)(2,1)} %collective-permute-done.4, ...), kind=kLoop, calls=%fused_computation.148 | loop fusion | flops 286720 | bytes 655364 | tf_op jit(solution)/shard_map/convert_element_type | solution.py:131
  149.4 1.6 collective-permute-start.8
  152.0 2.9 %collective-permute-done.8 = bf16[1,1,1,1,80,128]{5,4,3,2,1,0:T(8,128)(2,1)S(1)} collective-permute-done((bf16[1,1,1,1,80,128]{5,4,3,2,1,0:T(8,128)(2,1)S(1)}, bf16[1,1,1,1,80,128]{5,4,3,2,1,0:T(8,128)(2,1)S(1)}, u32[]{:S(2)}, u32[]{:S(2)}) %collective-permute-start.8) | collective-permute-done | bytes 20512 | tf_op jit(solution)/shard_map/ppermute | solution.py:136
  (79 shorter events, 26.9 us)
Async XLA Ops:
  0.6 63.7 %copy-start = (bf16[768,768]{1,0:T(8,128)(2,1)S(1)}, bf16[768,768]{1,0:T(8,128)(2,1)}, u32[]{:S(2)}) copy-start(bf16[768,768]{1,0:T(8,128)(2,1)} %param.13) | copy-start | bytes 3538948
  9.5 11.4 %copy-start.14 = (s32[2,1,128]{2,1,0:T(1,128)S(1)}, s32[2,1,128]{2,1,0:T(1,128)}, u32[]{:S(2)}) copy-start(s32[2,1,128]{2,1,0:T(1,128)} %param.16) | copy-start | bytes 3076
  9.5 43.6 %all-to-all-start = ((bf16[128,4,2304]{2,1,0:T(4,128)(2,1)}), bf16[128,4,2304]{2,1,0:T(4,128)(2,1)S(1)}, u32[]{:S(2)}, u32[]{:S(2)}) async-start(bf16[128,4,2304]{2,1,0:T(4,128)(2,1)} %copy.36), calls=%async_computation | async-start | bytes 4718592 | tf_op jit(solution)/shard_map/all_to_all | solution.py:46
  23.5 1.0 copy-start.10
  23.5 2.0 %copy-start.12 = (s32[1,2048]{1,0:T(1,128)}, s32[1,2048]{1,0:T(1,128)S(1)}, u32[]{:S(2)}) copy-start(s32[1,2048]{1,0:T(1,128)S(1)} %get-tuple-element.31) | copy-start | bytes 24580
  55.1 9.3 %copy-start.4 = (bf16[128,4,768]{2,1,0:T(4,128)(2,1)S(1)}, bf16[128,4,768]{2,1,0:T(4,128)(2,1)}, u32[]{:S(2)}) copy-start(bf16[128,4,768]{2,1,0:T(4,128)(2,1)} %get-tuple-element.17) | copy-start | bytes 2359300
  55.1 9.3 %copy-start.13 = (s32[1,2048]{1,0:T(1,128)S(1)}, s32[1,2048]{1,0:T(1,128)}, u32[]{:S(2)}) copy-start(s32[1,2048]{1,0:T(1,128)} %copy-done.12) | copy-start | bytes 24580
  64.3 7.7 %copy-start.5 = (bf16[128,4,768]{2,1,0:T(4,128)(2,1)S(1)}, bf16[128,4,768]{2,1,0:T(4,128)(2,1)}, u32[]{:S(2)}) copy-start(bf16[128,4,768]{2,1,0:T(4,128)(2,1)} %get-tuple-element.15) | copy-start | bytes 2359300
  64.3 7.7 %copy-start.9 = (f32[2048]{0:T(1024)S(1)}, f32[2048]{0:T(1024)}, u32[]{:S(2)}) copy-start(f32[2048]{0:T(1024)} %mul.41) | copy-start | bytes 24580
  64.4 7.7 %copy-start.16 = (f32[768]{0:T(1024)S(1)}, f32[768]{0:T(1024)}, u32[]{:S(2)}) copy-start(f32[768]{0:T(1024)} %param.14) | copy-start | bytes 9220
  79.2 2.8 %copy-start.11 = (s32[1,2048]{1,0:T(1,128)S(1)}, s32[1,2048]{1,0:T(1,128)}, u32[]{:S(2)}) copy-start(s32[1,2048]{1,0:T(1,128)} %copy-done.10) | copy-start | bytes 24580
  94.2 5.9 %copy-start.6 = (bf16[128,4,768]{2,0,1:T(8,128)(2,1)S(1)}, bf16[128,4,768]{2,0,1:T(8,128)(2,1)}, u32[]{:S(2)}) copy-start(bf16[128,4,768]{2,0,1:T(8,128)(2,1)} %fusion.37) | copy-start | bytes 2359300
  97.4 2.3 %copy-start.1 = (f32[4,2,4,4,80,128]{5,4,3,2,1,0:T(8,128)}, f32[4,2,4,4,80,128]{5,4,3,2,1,0:T(8,128)S(1)}, u32[]{:S(2)}) copy-start(f32[4,2,4,4,80,128]{5,4,3,2,1,0:T(8,128)S(1)} %pad_maximum_fusion) | copy-start | bytes 15728644
  100.0 3.2 %collective-permute-start = (bf16[4,1,4,4,80,128]{5,4,3,2,1,0:T(8,128)(2,1)S(1)}, bf16[4,1,4,4,80,128]{5,4,3,2,1,0:T(8,128)(2,1)}, u32[]{:S(2)}, u32[]{:S(2)}) collective-permute-start(bf16[4,1,4,4,80,128]{5,4,3,2,1,0:T(8,128)(2,1)S(1)} %dynamic-slice_convert_fusion), channel_id=1, source_target_pairs={{0,16},{16,0},{1,17},{17,1},{2,18},{18,2},{3,19},{19,3},{4,20},{20... | collective-permute-start | bytes 3932168 | tf_op jit(solution)/shard_map/ppermute | solution.py:136
  100.1 1.1 copy-start.7
  100.1 1.5 copy-start.15
  101.6 2.5 %copy-start.2 = (f32[4,2,4,4,80,128]{5,4,3,2,1,0:T(8,128)S(1)}, f32[4,2,4,4,80,128]{5,4,3,2,1,0:T(8,128)}, u32[]{:S(2)}) copy-start(f32[4,2,4,4,80,128]{5,4,3,2,1,0:T(8,128)} %copy-done.1) | copy-start | bytes 15728644
  105.8 1.5 copy-start.3
  108.3 12.5 %collective-permute-start.3 = (bf16[4,1,4,1,80,128]{5,4,3,2,1,0:T(8,128)(2,1)}, bf16[4,1,4,1,80,128]{5,4,3,2,1,0:T(8,128)(2,1)}, u32[]{:S(2)}, u32[]{:S(2)}) collective-permute-start(bf16[4,1,4,1,80,128]{5,4,3,2,1,0:T(8,128)(2,1)} %get-tuple-element.21), channel_id=1, source_target_pairs={{0,3},{1,0},{2,1},{3,2},{4,7},{5,4},{6,5},{7,6},{8,11},{9,8},{10,9... | collective-permute-start | bytes 983048 | tf_op jit(solution)/shard_map/ppermute | solution.py:136
  110.0 12.2 %collective-permute-start.2 = (bf16[4,1,4,1,80,128]{5,4,3,2,1,0:T(8,128)(2,1)S(1)}, bf16[4,1,4,1,80,128]{5,4,3,2,1,0:T(8,128)(2,1)}, u32[]{:S(2)}, u32[]{:S(2)}) collective-permute-start(bf16[4,1,4,1,80,128]{5,4,3,2,1,0:T(8,128)(2,1)S(1)} %get-tuple-element.22), channel_id=1, source_target_pairs={{0,2},{1,3},{2,0},{3,1},{4,6},{5,7},{6,4},{7,5},{8,10},{9,11},{10,... | collective-permute-start | bytes 983048 | tf_op jit(solution)/shard_map/ppermute | solution.py:136
  111.3 17.3 %collective-permute-start.1 = (bf16[4,1,4,1,80,128]{5,4,3,2,1,0:T(8,128)(2,1)S(1)}, bf16[4,1,4,1,80,128]{5,4,3,2,1,0:T(8,128)(2,1)}, u32[]{:S(2)}, u32[]{:S(2)}) collective-permute-start(bf16[4,1,4,1,80,128]{5,4,3,2,1,0:T(8,128)(2,1)S(1)} %get-tuple-element.20), channel_id=1, source_target_pairs={{0,1},{1,2},{2,3},{3,0},{4,5},{5,6},{6,7},{7,4},{8,9},{9,10},{10,1... | collective-permute-start | bytes 983048 | tf_op jit(solution)/shard_map/ppermute | solution.py:136
  113.7 44.9 %all-to-all-start.1 = ((bf16[128,4,1536]{2,1,0:T(4,128)(2,1)}), bf16[128,4,1536]{2,1,0:T(4,128)(2,1)S(1)}, u32[]{:S(2)}, u32[]{:S(2)}) async-start(bf16[128,4,1536]{2,1,0:T(4,128)(2,1)} %copy.46), calls=%async_computation.1 | async-start | bytes 3145728 | tf_op jit(solution)/shard_map/all_to_all | solution.py:126
  130.9 11.3 %collective-permute-start.6 = (bf16[4,1,1,1,80,128]{5,4,3,2,1,0:T(8,128)(2,1)}, bf16[4,1,1,1,80,128]{5,4,3,2,1,0:T(8,128)(2,1)S(1)}, u32[]{:S(2)}, u32[]{:S(2)}) collective-permute-start(bf16[4,1,1,1,80,128]{5,4,3,2,1,0:T(8,128)(2,1)} %get-tuple-element.24), channel_id=1, source_target_pairs={{0,12},{4,0},{8,4},{12,8},{1,13},{5,1},{9,5},{13,9},{2,14},{6,2},{... | collective-permute-start | bytes 245768 | tf_op jit(solution)/shard_map/ppermute | solution.py:136
  132.2 12.6 %collective-permute-start.5 = (bf16[4,1,1,1,80,128]{5,4,3,2,1,0:T(8,128)(2,1)}, bf16[4,1,1,1,80,128]{5,4,3,2,1,0:T(8,128)(2,1)}, u32[]{:S(2)}, u32[]{:S(2)}) collective-permute-start(bf16[4,1,1,1,80,128]{5,4,3,2,1,0:T(8,128)(2,1)} %get-tuple-element.25), channel_id=1, source_target_pairs={{0,8},{4,12},{8,0},{12,4},{1,9},{5,13},{9,1},{13,5},{2,10},{6,14},... | collective-permute-start | bytes 245768 | tf_op jit(solution)/shard_map/ppermute | solution.py:136
  133.8 12.7 %collective-permute-start.4 = (bf16[4,1,1,1,80,128]{5,4,3,2,1,0:T(8,128)(2,1)}, bf16[4,1,1,1,80,128]{5,4,3,2,1,0:T(8,128)(2,1)}, u32[]{:S(2)}, u32[]{:S(2)}) collective-permute-start(bf16[4,1,1,1,80,128]{5,4,3,2,1,0:T(8,128)(2,1)} %get-tuple-element.23), channel_id=1, source_target_pairs={{0,4},{4,8},{8,12},{12,0},{1,5},{5,9},{9,13},{13,1},{2,6},{6,10},{... | collective-permute-start | bytes 245768 | tf_op jit(solution)/shard_map/ppermute | solution.py:136
  148.1 12.2 %copy-start.8 = (bf16[256,768]{1,0:T(8,128)(2,1)S(1)}, bf16[256,768]{1,0:T(8,128)(2,1)}, u32[]{:S(2)}) copy-start(bf16[256,768]{1,0:T(8,128)(2,1)} %param.11) | copy-start | bytes 1179652
  148.1 3.9 %collective-permute-start.9 = (bf16[1,1,1,1,80,128]{5,4,3,2,1,0:T(8,128)(2,1)S(1)}, bf16[1,1,1,1,80,128]{5,4,3,2,1,0:T(8,128)(2,1)S(1)}, u32[]{:S(2)}, u32[]{:S(2)}) collective-permute-start(bf16[1,1,1,1,80,128]{5,4,3,2,1,0:T(8,128)(2,1)S(1)} %get-tuple-element.27), channel_id=1, source_target_pairs={{0,96},{32,0},{64,32},{96,64},{1,97},{33,1},{65,33},{97,65},{2,98}... | collective-permute-start | bytes 61448 | tf_op jit(solution)/shard_map/ppermute | solution.py:136
  149.4 5.5 %collective-permute-start.8 = (bf16[1,1,1,1,80,128]{5,4,3,2,1,0:T(8,128)(2,1)S(1)}, bf16[1,1,1,1,80,128]{5,4,3,2,1,0:T(8,128)(2,1)S(1)}, u32[]{:S(2)}, u32[]{:S(2)}) collective-permute-start(bf16[1,1,1,1,80,128]{5,4,3,2,1,0:T(8,128)(2,1)S(1)} %get-tuple-element.28), channel_id=1, source_target_pairs={{0,64},{32,96},{64,0},{96,32},{1,65},{33,97},{65,1},{97,33},{2,66}... | collective-permute-start | bytes 61448 | tf_op jit(solution)/shard_map/ppermute | solution.py:136
  151.0 5.0 %collective-permute-start.7 = (bf16[1,1,1,1,80,128]{5,4,3,2,1,0:T(8,128)(2,1)S(1)}, bf16[1,1,1,1,80,128]{5,4,3,2,1,0:T(8,128)(2,1)S(1)}, u32[]{:S(2)}, u32[]{:S(2)}) collective-permute-start(bf16[1,1,1,1,80,128]{5,4,3,2,1,0:T(8,128)(2,1)S(1)} %get-tuple-element.26), channel_id=1, source_target_pairs={{0,32},{32,64},{64,96},{96,0},{1,33},{33,65},{65,97},{97,1},{2,34}... | collective-permute-start | bytes 61448 | tf_op jit(solution)/shard_map/ppermute | solution.py:136

commit v14 on v12

--- a/solution.py
+++ b/solution.py
@@ -109,9 +109,9 @@
     )
     partials = jnp.concatenate(
         [
-            constraint_term.reshape(device_count, -1, lanes),
-            variable_term.reshape(device_count, -1, lanes),
-            bias_rows,
+            constraint_term.astype(jnp.bfloat16).reshape(device_count, -1, lanes),
+            variable_term.astype(jnp.bfloat16).reshape(device_count, -1, lanes),
+            bias_rows.astype(jnp.bfloat16),
         ],
         axis=1,
     )
@@ -125,7 +125,7 @@
         ring = lax.axis_size(axis_name)
         me = lax.axis_index(axis_name)
         sent = summed.astype(jnp.bfloat16)
-        total = lax.dynamic_slice_in_dim(summed, me, 1, position)
+        total = lax.dynamic_slice_in_dim(summed, me, 1, position).astype(jnp.float32)
         for shift in range(1, ring):
             chunk = lax.dynamic_slice_in_dim(sent, (me + shift) % ring, 1, position)
             pairs = [(i, (i + shift) % ring) for i in range(ring)]

time: 161 us -> 161 us (level)
  matrix products: 44 us -> 45.7 us
    concatenate x2, local copies, waits for them, and re-layouts: 3.43 us -> 6.08 us  [on_device(): jnp.concatenate([constraint_term.astype(jnp.bfloat16).reshape(device_coun...]
    unnamed x34 -> x36, local copies, waits for them, and re-layouts: 5.47 us -> 3.83 us
where the time goes in v14:
time: 161 us; the launch traced here: 160 us
  waiting for transfers between devices  52.7 us (33%)
  matrix products  45.7 us (28%)
  starting transfers between devices  27.3 us (17%)
  local copies, waits for them, and re-layouts  23.7 us (15%)
  other arithmetic  9.53 us (6%)
    all_to_all x1, waiting for transfers between devices, on_device(): lax.all_to_all(outgoing, DEVICE_AXES, split_axis=0, concat_axis=0, tiled=...  27.1 us
    ppermute x10, waiting for transfers between devices, on_device(): total = total + lax.ppermute(chunk, axis_name, pairs).astype(jnp.float32)  25.6 us
    all_to_all x1, starting transfers between devices, on_device(): lax.all_to_all(outgoing, DEVICE_AXES, split_axis=0, concat_axis=0, tiled=...  11.2 us
    dot_general x1, matrix products, on_device(): jnp.dot(edge_con, constraint_weight, preferred_element_type=jnp.float32)  9.27 us
    ppermute x10, starting transfers between devices, on_device(): total = total + lax.ppermute(chunk, axis_name, pairs).astype(jnp.float32)  9.14 us
    dot_general x1, matrix products, on_device(): jnp.dot(edge_var, variable_weight, preferred_element_type=jnp.float32)  7.66 us
    dot_general x1, matrix products, on_device(): lax.dot_general(table_var3, cotangent_mirror_rows, slot_dims, preferred_e...  7.15 us
    all_to_all x1, starting transfers between devices, on_device(): lax.all_to_all(backward, DEVICE_AXES, split_axis=0, concat_axis=0, tiled=...  7 us
  transfers between devices with their start and end apart: 12, of which 10 were waited for; matrix products, arithmetic and copies ran while one was open for 10% of the time, Pallas kernels for 0%

profile of v14, /device:TPU:0, one launch (start us, length us, event | category | flops | bytes accessed | tf_op | source)
XLA Modules:
  0.0 160.1 jit_solution(4336404597436963545)
XLA Ops:
  1.5 1.4 convolution_convert_fusion.2
  2.9 1.4 convolution_convert_fusion.3
  5.9 2.1 %reshape.87 = bf16[128,4,2304]{2,1,0:T(4,128)(2,1)} reshape(bf16[512,2304]{1,0:T(8,128)(2,1)S(1)} %pad_maximum_fusion.1) | data formatting | bytes 4718592 | tf_op jit(solution)/shard_map/reshape | solution.py:39
  8.0 11.2 %all-to-all-start = ((bf16[128,4,2304]{2,1,0:T(4,128)(2,1)}), bf16[128,4,2304]{2,1,0:T(4,128)(2,1)S(1)}, u32[]{:S(2)}, u32[]{:S(2)}) async-start(bf16[128,4,2304]{2,1,0:T(4,128)(2,1)} %reshape.87), calls=%async_computation | async-start | bytes 4718592 | tf_op jit(solution)/shard_map/all_to_all | solution.py:42
  24.5 27.1 %all-to-all-done = bf16[128,4,2304]{2,1,0:T(4,128)(2,1)S(1)} async-done(((bf16[128,4,2304]{2,1,0:T(4,128)(2,1)}), bf16[128,4,2304]{2,1,0:T(4,128)(2,1)S(1)}, u32[]{:S(2)}, u32[]{:S(2)}) %all-to-all-start) | async-done | bytes 2359328 | tf_op jit(solution)/shard_map/all_to_all | solution.py:42
  51.6 1.9 %fusion.107 = (bf16[128,4,768]{2,1,0:T(4,128)(2,1)}, bf16[128,4,768]{2,1,0:T(4,128)(2,1)}, bf16[128,4,768]{2,1,0:T(4,128)(2,1)}) fusion(bf16[128,4,2304]{2,1,0:T(4,128)(2,1)S(1)} %all-to-all-done), kind=kLoop, calls=%fused_computation.150 | loop fusion | bytes 4718592 | tf_op jit(solution)/shard_map/slice | solution.py:45
  53.6 9.3 %fusion.45 = f32[2048,768]{1,0:T(8,128)} fusion(bf16[768,768]{1,0:T(8,128)(2,1)} %param.12, s32[2048]{0:T(1024)} %bitcast.74, s32[128,4]{0,1:T(4,128)} %multiply_add_fusion, bf16[128,4,768]{2,1,0:T(4,128)(2,1)} %get-tuple-element.16), kind=kOutput, calls=%fused_computation.63 | convolution fusion | flops 4031250432 | bytes 8267776 | tf_op jit(solution)/shard_map/dot_general | solution.py:68
  62.9 7.7 %fusion.46 = f32[2048,768]{1,0:T(8,128)} fusion(bf16[768,768]{1,0:T(8,128)(2,1)S(1)} %copy-done, s32[2048]{0:T(1024)S(1)} %bitcast.77, s32[128,4]{0,1:T(4,128)S(1)} %copy-done.11, bf16[128,4,768]{2,1,0:T(4,128)(2,1)S(1)} %copy-done.5), kind=kOutput, calls=%fused_computation.64 | convolution fusion | flops 4031250432 | bytes 8267776 | tf_op jit(solution)/shard_map/dot_general | solution.py:69
  70.5 7.1 %fusion.110 = (bf16[768]{0:T(1024)(128)(2,1)S(1)}, bf16[2048,768]{1,0:T(8,128)(2,1)S(1)}) fusion(f32[2048]{0:T(1024)S(1)} %mul.41, f32[768]{0:T(1024)S(1)} %copy-done.15, f32[2048,768]{1,0:T(8,128)} %fusion.45, f32[2048,768]{1,0:T(8,128)} %fusion.46, bf16[128,4,768]{2,1,0:T(4,128)(2,1)S(1)} %copy-done.6, s32[2048]{0:T(1024)S(1)} %bitcast.78, ...), kind=kOutput, calls=%fused_computation.153 | convolution fusion | flops 1634204928 | bytes 16538112 | tf_op jit(solution)/shard_map/dot_general | solution.py:64
  77.7 2.7 %fusion.37 = bf16[128,4,768]{2,0,1:T(8,128)(2,1)} fusion(bf16[2048,768]{1,0:T(8,128)(2,1)S(1)} %get-tuple-element.36, s32[2048]{0:T(1024)S(1)} %bitcast.79, s32[128,4]{0,1:T(4,128)S(1)} %copy-done.11), kind=kOutput, calls=%fused_computation.52 | convolution fusion | flops 1614151680 | bytes 3942400 | tf_op jit(solution)/shard_map/dot_general | solution.py:81
  80.5 2.8 %fusion.34 = bf16[128,4,768]{2,0,1:T(8,128)(2,1)} fusion(bf16[2048,768]{1,0:T(8,128)(2,1)S(1)} %get-tuple-element.36, s32[2048]{0:T(1024)S(1)} %bitcast.75, s32[128,4]{0,1:T(4,128)S(1)} %copy-done.11), kind=kOutput, calls=%fused_computation.51 | convolution fusion | flops 1614151680 | bytes 3942400 | tf_op jit(solution)/shard_map/dot_general | solution.py:78
  83.4 3.0 %bitcast_convert_fusion.2 = bf16[768,768]{1,0:T(8,128)(2,1)} fusion(bf16[128,4,768]{2,0,1:T(8,128)(2,1)} %fusion.37, bf16[128,4,768]{2,1,0:T(4,128)(2,1)S(1)} %copy-done.5), kind=kOutput, calls=%fused_computation.18 | convolution fusion | flops 604569600 | bytes 2752512 | tf_op jit(solution)/shard_map/dot_general | solution.py:97
  86.5 2.6 %concatenate.19 = bf16[4,2,4,4,36,128]{5,4,3,2,1,0:T(8,128)(2,1)S(1)} reshape(bf16[768,768]{1,0:T(8,128)(2,1)} %bitcast_convert_fusion.2) | data formatting | bytes 2359296 | tf_op jit(solution)/shard_map/concatenate | solution.py:110
  89.1 3.0 %bitcast_convert_fusion.3 = bf16[768,768]{1,0:T(8,128)(2,1)} fusion(bf16[128,4,768]{2,0,1:T(8,128)(2,1)} %fusion.34, bf16[128,4,768]{2,1,0:T(4,128)(2,1)S(1)} %copy-done.4), kind=kOutput, calls=%fused_computation.19 | convolution fusion | flops 604569600 | bytes 2752512 | tf_op jit(solution)/shard_map/dot_general | solution.py:91
  92.1 3.5 %concatenate.18 = bf16[4,2,4,4,36,128]{5,4,3,2,1,0:T(8,128)(2,1)} reshape(bf16[768,768]{1,0:T(8,128)(2,1)} %bitcast_convert_fusion.3) | data formatting | bytes 2359296 | tf_op jit(solution)/shard_map/concatenate | solution.py:110
  95.6 2.3 %pad_maximum_fusion = bf16[4,2,4,4,80,128]{5,4,3,2,1,0:T(8,128)(2,1)S(1)} fusion(bf16[4,2,4,4,8,128]{5,4,3,2,1,0:T(8,128)(2,1)S(1)} %bitcast.69, bf16[4,2,4,4,36,128]{5,4,3,2,1,0:T(8,128)(2,1)S(1)} %concatenate.19, bf16[4,2,4,4,36,128]{5,4,3,2,1,0:T(8,128)(2,1)} %concatenate.18), kind=kLoop, calls=%fused_computation.15 | loop fusion | flops 7864320 | bytes 5242880 | tf_op jit(solution)/shard_map/concatenate | solution.py:110
  97.9 1.5 copy-done.2
  102.9 1.6 %convert_add_fusion = f32[4,1,4,4,80,128]{5,4,3,2,1,0:T(8,128)S(1)} fusion(bf16[4,1,4,4,80,128]{5,4,3,2,1,0:T(8,128)(2,1)} %collective-permute-done, bf16[4,2,4,4,80,128]{5,4,3,2,1,0:T(8,128)(2,1)S(1)} %copy-done.3, s32[]{:T(128)S(6)} %select_n.130), kind=kLoop, calls=%fused_computation.16 | loop fusion | flops 1966080 | bytes 5242884 | tf_op jit(solution)/shard_map/add | solution.py:132
  104.5 1.5 copy-done.1
  107.1 1.7 %collective-permute-start.3 = (bf16[4,1,4,1,80,128]{5,4,3,2,1,0:T(8,128)(2,1)}, bf16[4,1,4,1,80,128]{5,4,3,2,1,0:T(8,128)(2,1)}, u32[]{:S(2)}, u32[]{:S(2)}) collective-permute-start(bf16[4,1,4,1,80,128]{5,4,3,2,1,0:T(8,128)(2,1)} %get-tuple-element.21), channel_id=1, source_target_pairs={{0,3},{1,0},{2,1},{3,2},{4,7},{5,4},{6,5},{7,6},{8,11},{9,8},{10,9... | collective-permute-start | bytes 983048 | tf_op jit(solution)/shard_map/ppermute | solution.py:132
  110.1 2.4 %copy.37 = bf16[128,4,1536]{2,1,0:T(4,128)(2,1)} copy(bf16[128,4,1536]{2,0,1:T(8,128)(2,1)S(1)} %pad_maximum_fusion.2) | data formatting | bytes 3145728 | tf_op jit(solution)/shard_map/optimization_barrier | solution.py:121
  112.5 7.0 %all-to-all-start.1 = ((bf16[128,4,1536]{2,1,0:T(4,128)(2,1)}), bf16[128,4,1536]{2,1,0:T(4,128)(2,1)S(1)}, u32[]{:S(2)}, u32[]{:S(2)}) async-start(bf16[128,4,1536]{2,1,0:T(4,128)(2,1)} %copy.37), calls=%async_computation.1 | async-start | bytes 3145728 | tf_op jit(solution)/shard_map/all_to_all | solution.py:122
  119.5 1.5 collective-permute-done.2
  121.0 6.4 %collective-permute-done.1 = bf16[4,1,4,1,80,128]{5,4,3,2,1,0:T(8,128)(2,1)} collective-permute-done((bf16[4,1,4,1,80,128]{5,4,3,2,1,0:T(8,128)(2,1)S(1)}, bf16[4,1,4,1,80,128]{5,4,3,2,1,0:T(8,128)(2,1)}, u32[]{:S(2)}, u32[]{:S(2)}) %collective-permute-start.1) | collective-permute-done | bytes 327712 | tf_op jit(solution)/shard_map/ppermute | solution.py:132
  127.4 1.5 fusion.106
  130.9 1.6 %collective-permute-start.5 = (bf16[4,1,1,1,80,128]{5,4,3,2,1,0:T(8,128)(2,1)}, bf16[4,1,1,1,80,128]{5,4,3,2,1,0:T(8,128)(2,1)}, u32[]{:S(2)}, u32[]{:S(2)}) collective-permute-start(bf16[4,1,1,1,80,128]{5,4,3,2,1,0:T(8,128)(2,1)} %get-tuple-element.25), channel_id=1, source_target_pairs={{0,8},{4,12},{8,0},{12,4},{1,9},{5,13},{9,1},{13,5},{2,10},{6,14},... | collective-permute-start | bytes 245768 | tf_op jit(solution)/shard_map/ppermute | solution.py:132
  132.6 8.3 %collective-permute-done.6 = bf16[4,1,1,1,80,128]{5,4,3,2,1,0:T(8,128)(2,1)S(1)} collective-permute-done((bf16[4,1,1,1,80,128]{5,4,3,2,1,0:T(8,128)(2,1)}, bf16[4,1,1,1,80,128]{5,4,3,2,1,0:T(8,128)(2,1)S(1)}, u32[]{:S(2)}, u32[]{:S(2)}) %collective-permute-start.6) | collective-permute-done | bytes 81952 | tf_op jit(solution)/shard_map/ppermute | solution.py:132
  140.9 2.6 %collective-permute-done.5 = bf16[4,1,1,1,80,128]{5,4,3,2,1,0:T(8,128)(2,1)} collective-permute-done((bf16[4,1,1,1,80,128]{5,4,3,2,1,0:T(8,128)(2,1)}, bf16[4,1,1,1,80,128]{5,4,3,2,1,0:T(8,128)(2,1)}, u32[]{:S(2)}, u32[]{:S(2)}) %collective-permute-start.5) | collective-permute-done | bytes 81952 | tf_op jit(solution)/shard_map/ppermute | solution.py:132
  143.5 1.7 %collective-permute-done.4 = bf16[4,1,1,1,80,128]{5,4,3,2,1,0:T(8,128)(2,1)} collective-permute-done((bf16[4,1,1,1,80,128]{5,4,3,2,1,0:T(8,128)(2,1)}, bf16[4,1,1,1,80,128]{5,4,3,2,1,0:T(8,128)(2,1)}, u32[]{:S(2)}, u32[]{:S(2)}) %collective-permute-start.4) | collective-permute-done | bytes 81952 | tf_op jit(solution)/shard_map/ppermute | solution.py:132
  145.2 1.6 %fusion.105 = (bf16[4,1,1,1,80,128]{5,4,3,2,1,0:T(8,128)(2,1)S(1)}, f32[4,1,1,1,80,128]{5,4,3,2,1,0:T(8,128)}) fusion(bf16[4,1,1,1,80,128]{5,4,3,2,1,0:T(8,128)(2,1)S(1)} %collective-permute-done.6, bf16[4,1,1,1,80,128]{5,4,3,2,1,0:T(8,128)(2,1)} %collective-permute-done.5, bf16[4,1,1,1,80,128]{5,4,3,2,1,0:T(8,128)(2,1)} %collective-permute-done.4, ...), kind=kLoop, calls=%fused_computation.148 | loop fusion | flops 286720 | bytes 655364 | tf_op jit(solution)/shard_map/convert_element_type | solution.py:127
  148.2 1.6 collective-permute-start.8
  150.7 2.9 %collective-permute-done.8 = bf16[1,1,1,1,80,128]{5,4,3,2,1,0:T(8,128)(2,1)S(1)} collective-permute-done((bf16[1,1,1,1,80,128]{5,4,3,2,1,0:T(8,128)(2,1)S(1)}, bf16[1,1,1,1,80,128]{5,4,3,2,1,0:T(8,128)(2,1)S(1)}, u32[]{:S(2)}, u32[]{:S(2)}) %collective-permute-start.8) | collective-permute-done | bytes 20512 | tf_op jit(solution)/shard_map/ppermute | solution.py:132
  (81 shorter events, 24.3 us)
Async XLA Ops:
  0.6 62.2 %copy-start = (bf16[768,768]{1,0:T(8,128)(2,1)S(1)}, bf16[768,768]{1,0:T(8,128)(2,1)}, u32[]{:S(2)}) copy-start(bf16[768,768]{1,0:T(8,128)(2,1)} %param.13) | copy-start | bytes 3538948
  8.0 11.2 %copy-start.12 = (s32[2,1,128]{2,1,0:T(1,128)S(1)}, s32[2,1,128]{2,1,0:T(1,128)}, u32[]{:S(2)}) copy-start(s32[2,1,128]{2,1,0:T(1,128)} %param.16) | copy-start | bytes 3076
  8.0 43.6 %all-to-all-start = ((bf16[128,4,2304]{2,1,0:T(4,128)(2,1)}), bf16[128,4,2304]{2,1,0:T(4,128)(2,1)S(1)}, u32[]{:S(2)}, u32[]{:S(2)}) async-start(bf16[128,4,2304]{2,1,0:T(4,128)(2,1)} %reshape.87), calls=%async_computation | async-start | bytes 4718592 | tf_op jit(solution)/shard_map/all_to_all | solution.py:42
  21.9 2.0 %copy-start.7 = (s32[1,2048]{1,0:T(1,128)}, s32[1,2048]{1,0:T(1,128)S(1)}, u32[]{:S(2)}) copy-start(s32[1,2048]{1,0:T(1,128)S(1)} %get-tuple-element.32) | copy-start | bytes 24580
  21.9 2.0 %copy-start.9 = (s32[1,2048]{1,0:T(1,128)}, s32[1,2048]{1,0:T(1,128)S(1)}, u32[]{:S(2)}) copy-start(s32[1,2048]{1,0:T(1,128)S(1)} %get-tuple-element.31) | copy-start | bytes 24580
  53.6 9.3 %copy-start.5 = (bf16[128,4,768]{2,1,0:T(4,128)(2,1)S(1)}, bf16[128,4,768]{2,1,0:T(4,128)(2,1)}, u32[]{:S(2)}) copy-start(bf16[128,4,768]{2,1,0:T(4,128)(2,1)} %get-tuple-element.17) | copy-start | bytes 2359300
  53.6 9.3 %copy-start.10 = (s32[1,2048]{1,0:T(1,128)S(1)}, s32[1,2048]{1,0:T(1,128)}, u32[]{:S(2)}) copy-start(s32[1,2048]{1,0:T(1,128)} %copy-done.9) | copy-start | bytes 24580
  53.6 9.3 %copy-start.11 = (s32[128,4]{0,1:T(4,128)S(1)}, s32[128,4]{0,1:T(4,128)}, u32[]{:S(2)}) copy-start(s32[128,4]{0,1:T(4,128)} %multiply_add_fusion) | copy-start | bytes 6148
  62.8 7.7 %copy-start.6 = (bf16[128,4,768]{2,1,0:T(4,128)(2,1)S(1)}, bf16[128,4,768]{2,1,0:T(4,128)(2,1)}, u32[]{:S(2)}) copy-start(bf16[128,4,768]{2,1,0:T(4,128)(2,1)} %get-tuple-element.15) | copy-start | bytes 2359300
  62.9 7.7 %copy-start.15 = (f32[768]{0:T(1024)S(1)}, f32[768]{0:T(1024)}, u32[]{:S(2)}) copy-start(f32[768]{0:T(1024)} %param.14) | copy-start | bytes 9220
  77.7 2.8 %copy-start.8 = (s32[1,2048]{1,0:T(1,128)S(1)}, s32[1,2048]{1,0:T(1,128)}, u32[]{:S(2)}) copy-start(s32[1,2048]{1,0:T(1,128)} %copy-done.7) | copy-start | bytes 24580
  83.2 5.8 %copy-start.4 = (bf16[128,4,768]{2,1,0:T(4,128)(2,1)S(1)}, bf16[128,4,768]{2,1,0:T(4,128)(2,1)}, u32[]{:S(2)}) copy-start(bf16[128,4,768]{2,1,0:T(4,128)(2,1)} %get-tuple-element.16) | copy-start | bytes 2359300
  95.6 4.1 %copy-start.16 = (bf16[128,4,768]{2,0,1:T(8,128)(2,1)S(1)}, bf16[128,4,768]{2,0,1:T(8,128)(2,1)}, u32[]{:S(2)}) copy-start(bf16[128,4,768]{2,0,1:T(8,128)(2,1)} %fusion.37) | copy-start | bytes 2359300
  97.9 1.5 copy-start.2
  99.5 3.2 %collective-permute-start = (bf16[4,1,4,4,80,128]{5,4,3,2,1,0:T(8,128)(2,1)S(1)}, bf16[4,1,4,4,80,128]{5,4,3,2,1,0:T(8,128)(2,1)}, u32[]{:S(2)}, u32[]{:S(2)}) collective-permute-start(bf16[4,1,4,4,80,128]{5,4,3,2,1,0:T(8,128)(2,1)S(1)} %constant_dynamic-slice_fusion.9), channel_id=1, source_target_pairs={{0,16},{16,0},{1,17},{17,1},{2,18},{18,2},{3,19},{19,3},{4,20},{20... | collective-permute-start | bytes 3932168 | tf_op jit(solution)/shard_map/ppermute | solution.py:132
  99.7 1.3 copy-start.13
  99.7 1.5 copy-start.17
  101.2 1.7 %copy-start.3 = (bf16[4,2,4,4,80,128]{5,4,3,2,1,0:T(8,128)(2,1)S(1)}, bf16[4,2,4,4,80,128]{5,4,3,2,1,0:T(8,128)(2,1)}, u32[]{:S(2)}) copy-start(bf16[4,2,4,4,80,128]{5,4,3,2,1,0:T(8,128)(2,1)} %copy-done.2) | copy-start | bytes 7864324
  104.5 1.5 copy-start.1
  107.1 12.5 %collective-permute-start.3 = (bf16[4,1,4,1,80,128]{5,4,3,2,1,0:T(8,128)(2,1)}, bf16[4,1,4,1,80,128]{5,4,3,2,1,0:T(8,128)(2,1)}, u32[]{:S(2)}, u32[]{:S(2)}) collective-permute-start(bf16[4,1,4,1,80,128]{5,4,3,2,1,0:T(8,128)(2,1)} %get-tuple-element.21), channel_id=1, source_target_pairs={{0,3},{1,0},{2,1},{3,2},{4,7},{5,4},{6,5},{7,6},{8,11},{9,8},{10,9... | collective-permute-start | bytes 983048 | tf_op jit(solution)/shard_map/ppermute | solution.py:132
  108.7 12.2 %collective-permute-start.2 = (bf16[4,1,4,1,80,128]{5,4,3,2,1,0:T(8,128)(2,1)S(1)}, bf16[4,1,4,1,80,128]{5,4,3,2,1,0:T(8,128)(2,1)}, u32[]{:S(2)}, u32[]{:S(2)}) collective-permute-start(bf16[4,1,4,1,80,128]{5,4,3,2,1,0:T(8,128)(2,1)S(1)} %get-tuple-element.22), channel_id=1, source_target_pairs={{0,2},{1,3},{2,0},{3,1},{4,6},{5,7},{6,4},{7,5},{8,10},{9,11},{10,... | collective-permute-start | bytes 983048 | tf_op jit(solution)/shard_map/ppermute | solution.py:132
  110.1 17.3 %collective-permute-start.1 = (bf16[4,1,4,1,80,128]{5,4,3,2,1,0:T(8,128)(2,1)S(1)}, bf16[4,1,4,1,80,128]{5,4,3,2,1,0:T(8,128)(2,1)}, u32[]{:S(2)}, u32[]{:S(2)}) collective-permute-start(bf16[4,1,4,1,80,128]{5,4,3,2,1,0:T(8,128)(2,1)S(1)} %get-tuple-element.20), channel_id=1, source_target_pairs={{0,1},{1,2},{2,3},{3,0},{4,5},{5,6},{6,7},{7,4},{8,9},{9,10},{10,1... | collective-permute-start | bytes 983048 | tf_op jit(solution)/shard_map/ppermute | solution.py:132
  112.5 44.9 %all-to-all-start.1 = ((bf16[128,4,1536]{2,1,0:T(4,128)(2,1)}), bf16[128,4,1536]{2,1,0:T(4,128)(2,1)S(1)}, u32[]{:S(2)}, u32[]{:S(2)}) async-start(bf16[128,4,1536]{2,1,0:T(4,128)(2,1)} %copy.37), calls=%async_computation.1 | async-start | bytes 3145728 | tf_op jit(solution)/shard_map/all_to_all | solution.py:122
  129.7 11.2 %collective-permute-start.6 = (bf16[4,1,1,1,80,128]{5,4,3,2,1,0:T(8,128)(2,1)}, bf16[4,1,1,1,80,128]{5,4,3,2,1,0:T(8,128)(2,1)S(1)}, u32[]{:S(2)}, u32[]{:S(2)}) collective-permute-start(bf16[4,1,1,1,80,128]{5,4,3,2,1,0:T(8,128)(2,1)} %get-tuple-element.24), channel_id=1, source_target_pairs={{0,12},{4,0},{8,4},{12,8},{1,13},{5,1},{9,5},{13,9},{2,14},{6,2},{... | collective-permute-start | bytes 245768 | tf_op jit(solution)/shard_map/ppermute | solution.py:132
  130.9 12.6 %collective-permute-start.5 = (bf16[4,1,1,1,80,128]{5,4,3,2,1,0:T(8,128)(2,1)}, bf16[4,1,1,1,80,128]{5,4,3,2,1,0:T(8,128)(2,1)}, u32[]{:S(2)}, u32[]{:S(2)}) collective-permute-start(bf16[4,1,1,1,80,128]{5,4,3,2,1,0:T(8,128)(2,1)} %get-tuple-element.25), channel_id=1, source_target_pairs={{0,8},{4,12},{8,0},{12,4},{1,9},{5,13},{9,1},{13,5},{2,10},{6,14},... | collective-permute-start | bytes 245768 | tf_op jit(solution)/shard_map/ppermute | solution.py:132
  132.6 12.7 %collective-permute-start.4 = (bf16[4,1,1,1,80,128]{5,4,3,2,1,0:T(8,128)(2,1)}, bf16[4,1,1,1,80,128]{5,4,3,2,1,0:T(8,128)(2,1)}, u32[]{:S(2)}, u32[]{:S(2)}) collective-permute-start(bf16[4,1,1,1,80,128]{5,4,3,2,1,0:T(8,128)(2,1)} %get-tuple-element.23), channel_id=1, source_target_pairs={{0,4},{4,8},{8,12},{12,0},{1,5},{5,9},{9,13},{13,1},{2,6},{6,10},{... | collective-permute-start | bytes 245768 | tf_op jit(solution)/shard_map/ppermute | solution.py:132
  146.8 12.1 %copy-start.14 = (bf16[256,768]{1,0:T(8,128)(2,1)S(1)}, bf16[256,768]{1,0:T(8,128)(2,1)}, u32[]{:S(2)}) copy-start(bf16[256,768]{1,0:T(8,128)(2,1)} %param.11) | copy-start | bytes 1179652
  146.9 3.9 %collective-permute-start.9 = (bf16[1,1,1,1,80,128]{5,4,3,2,1,0:T(8,128)(2,1)S(1)}, bf16[1,1,1,1,80,128]{5,4,3,2,1,0:T(8,128)(2,1)S(1)}, u32[]{:S(2)}, u32[]{:S(2)}) collective-permute-start(bf16[1,1,1,1,80,128]{5,4,3,2,1,0:T(8,128)(2,1)S(1)} %get-tuple-element.27), channel_id=1, source_target_pairs={{0,96},{32,0},{64,32},{96,64},{1,97},{33,1},{65,33},{97,65},{2,98}... | collective-permute-start | bytes 61448 | tf_op jit(solution)/shard_map/ppermute | solution.py:132
  148.2 5.5 %collective-permute-start.8 = (bf16[1,1,1,1,80,128]{5,4,3,2,1,0:T(8,128)(2,1)S(1)}, bf16[1,1,1,1,80,128]{5,4,3,2,1,0:T(8,128)(2,1)S(1)}, u32[]{:S(2)}, u32[]{:S(2)}) collective-permute-start(bf16[1,1,1,1,80,128]{5,4,3,2,1,0:T(8,128)(2,1)S(1)} %get-tuple-element.28), channel_id=1, source_target_pairs={{0,64},{32,96},{64,0},{96,32},{1,65},{33,97},{65,1},{97,33},{2,66}... | collective-permute-start | bytes 61448 | tf_op jit(solution)/shard_map/ppermute | solution.py:132
  149.8 5.0 %collective-permute-start.7 = (bf16[1,1,1,1,80,128]{5,4,3,2,1,0:T(8,128)(2,1)S(1)}, bf16[1,1,1,1,80,128]{5,4,3,2,1,0:T(8,128)(2,1)S(1)}, u32[]{:S(2)}, u32[]{:S(2)}) collective-permute-start(bf16[1,1,1,1,80,128]{5,4,3,2,1,0:T(8,128)(2,1)S(1)} %get-tuple-element.26), channel_id=1, source_target_pairs={{0,32},{32,64},{64,96},{96,0},{1,33},{33,65},{65,97},{97,1},{2,34}... | collective-permute-start | bytes 61448 | tf_op jit(solution)/shard_map/ppermute | solution.py:132

commit v15 on v12

--- a/solution.py
+++ b/solution.py
@@ -34,9 +34,10 @@
     select_con = one_hot_table(send_rows[0, 0], master_rows)
     select_var = one_hot_table(send_rows[1, 0], master_rows)
     out_con = pick_rows(select_con, constraint_features)
-    out_var = pick_rows(select_var, variable_features)
-    out_cot = pick_rows(select_var, variable_cotangent)
-    outgoing = jnp.concatenate([out_con, out_var, out_cot], axis=1).reshape(
+    out_var_cot = pick_rows(
+        select_var, jnp.concatenate([variable_features, variable_cotangent], axis=1)
+    )
+    outgoing = jnp.concatenate([out_con, out_var_cot], axis=1).reshape(
         device_count, slot_cap, 3 * embedding_width
     )
     incoming = lax.all_to_all(outgoing, DEVICE_AXES, split_axis=0, concat_axis=0, tiled=True)

time: 161 us -> 160 us (level)
    dot_general x3 -> x2, matrix products: 4.23 us -> 3.13 us  [pick_rows(): jnp.dot(table, values, preferred_element_type=jnp.float32)]
where the time goes in v15:
time: 160 us; the launch traced here: 159 us
  waiting for transfers between devices  52.7 us (33%)
  matrix products  42.9 us (27%)
  starting transfers between devices  27.3 us (17%)
  local copies, waits for them, and re-layouts  24.3 us (15%)
  other arithmetic  10.4 us (6%)
    all_to_all x1, waiting for transfers between devices, on_device(): lax.all_to_all(outgoing, DEVICE_AXES, split_axis=0, concat_axis=0, tiled=...  27.1 us
    ppermute x10, waiting for transfers between devices, on_device(): total = total + lax.ppermute(chunk, axis_name, pairs).astype(jnp.float32)  25.6 us
    all_to_all x1, starting transfers between devices, on_device(): lax.all_to_all(outgoing, DEVICE_AXES, split_axis=0, concat_axis=0, tiled=...  11.2 us
    dot_general x1, matrix products, on_device(): jnp.dot(edge_con, constraint_weight, preferred_element_type=jnp.float32)  9.26 us
    ppermute x10, starting transfers between devices, on_device(): total = total + lax.ppermute(chunk, axis_name, pairs).astype(jnp.float32)  9.15 us
    dot_general x1, matrix products, on_device(): jnp.dot(edge_var, variable_weight, preferred_element_type=jnp.float32)  7.65 us
    dot_general x1, matrix products, on_device(): lax.dot_general(table_var3, cotangent_mirror_rows, slot_dims, preferred_e...  7.1 us
    all_to_all x1, starting transfers between devices, on_device(): lax.all_to_all(backward, DEVICE_AXES, split_axis=0, concat_axis=0, tiled=...  6.99 us
  transfers between devices with their start and end apart: 12, of which 10 were waited for; matrix products, arithmetic and copies ran while one was open for 10% of the time, Pallas kernels for 0%

profile of v15, /device:TPU:0, one launch (start us, length us, event | category | flops | bytes accessed | tf_op | source)
XLA Modules:
  0.0 158.8 jit_solution(4178267331300021857)
XLA Ops:
  1.5 1.4 convolution_convert_fusion.3
  2.9 1.7 %convolution_convert_fusion = bf16[512,1536]{1,0:T(8,128)(2,1)S(1)} fusion(bf16[256,768]{1,0:T(8,128)(2,1)} %param.11, bf16[256,768]{1,0:T(8,128)(2,1)} %param.10, s32[512]{0:T(512)S(1)} %bitcast.80), kind=kOutput, calls=%fused_computation.17 | convolution fusion | flops 405405696 | bytes 2361344 | tf_op jit(solution)/shard_map/dot_general | solution.py:15
  4.8 2.2 %reshape.86 = bf16[128,4,2304]{2,1,0:T(4,128)(2,1)} reshape(bf16[512,2304]{1,0:T(8,128)(2,1)S(1)} %pad_maximum_fusion.1) | data formatting | bytes 4718592 | tf_op jit(solution)/shard_map/reshape | solution.py:40
  6.9 11.2 %all-to-all-start = ((bf16[128,4,2304]{2,1,0:T(4,128)(2,1)}), bf16[128,4,2304]{2,1,0:T(4,128)(2,1)S(1)}, u32[]{:S(2)}, u32[]{:S(2)}) async-start(bf16[128,4,2304]{2,1,0:T(4,128)(2,1)} %reshape.86), calls=%async_computation | async-start | bytes 4718592 | tf_op jit(solution)/shard_map/all_to_all | solution.py:43
  23.4 27.1 %all-to-all-done = bf16[128,4,2304]{2,1,0:T(4,128)(2,1)S(1)} async-done(((bf16[128,4,2304]{2,1,0:T(4,128)(2,1)}), bf16[128,4,2304]{2,1,0:T(4,128)(2,1)S(1)}, u32[]{:S(2)}, u32[]{:S(2)}) %all-to-all-start) | async-done | bytes 2359328 | tf_op jit(solution)/shard_map/all_to_all | solution.py:43
  50.5 2.0 %fusion.106 = (bf16[128,4,768]{2,1,0:T(4,128)(2,1)}, bf16[128,4,768]{2,1,0:T(4,128)(2,1)}, bf16[128,4,768]{2,1,0:T(4,128)(2,1)}) fusion(bf16[128,4,2304]{2,1,0:T(4,128)(2,1)S(1)} %all-to-all-done), kind=kLoop, calls=%fused_computation.149 | loop fusion | bytes 4718592 | tf_op jit(solution)/shard_map/slice | solution.py:46
  52.5 9.3 %fusion.45 = f32[2048,768]{1,0:T(8,128)} fusion(bf16[768,768]{1,0:T(8,128)(2,1)} %param.12, s32[2048]{0:T(1024)} %bitcast.74, s32[128,4]{0,1:T(4,128)} %multiply_add_fusion, bf16[128,4,768]{2,1,0:T(4,128)(2,1)} %get-tuple-element.16), kind=kOutput, calls=%fused_computation.64 | convolution fusion | flops 4031250432 | bytes 8267776 | tf_op jit(solution)/shard_map/dot_general | solution.py:69
  61.8 7.6 %fusion.46 = f32[2048,768]{1,0:T(8,128)} fusion(bf16[768,768]{1,0:T(8,128)(2,1)S(1)} %copy-done, s32[2048]{0:T(1024)S(1)} %bitcast.77, s32[128,4]{0,1:T(4,128)S(1)} %copy-done.12, bf16[128,4,768]{2,1,0:T(4,128)(2,1)S(1)} %copy-done.4), kind=kOutput, calls=%fused_computation.65 | convolution fusion | flops 4031250432 | bytes 8267776 | tf_op jit(solution)/shard_map/dot_general | solution.py:70
  69.5 7.1 %convert_reduce_fusion = (f32[768]{0:T(1024)S(1)}, bf16[2048,768]{1,0:T(8,128)(2,1)S(1)}) fusion(f32[2048]{0:T(1024)S(1)} %mul.41, f32[768]{0:T(1024)S(1)} %copy-done.16, f32[2048,768]{1,0:T(8,128)} %fusion.45, f32[2048,768]{1,0:T(8,128)} %fusion.46, bf16[128,4,768]{2,1,0:T(4,128)(2,1)S(1)} %copy-done.5, s32[2048]{0:T(1024)S(1)} %bitcast.78, ...), kind=kOutput, calls=%fused_computation.5 | convolution fusion | flops 1635777792 | bytes 16539648 | tf_op jit(solution)/shard_map/dot_general | solution.py:65
  76.6 2.7 %fusion.37 = bf16[128,4,768]{2,0,1:T(8,128)(2,1)} fusion(bf16[2048,768]{1,0:T(8,128)(2,1)S(1)} %get-tuple-element.36, s32[2048]{0:T(1024)S(1)} %bitcast.79, s32[128,4]{0,1:T(4,128)S(1)} %copy-done.12), kind=kOutput, calls=%fused_computation.55 | convolution fusion | flops 1614151680 | bytes 3942400 | tf_op jit(solution)/shard_map/dot_general | solution.py:82
  79.3 2.8 %fusion.34 = bf16[128,4,768]{2,0,1:T(8,128)(2,1)} fusion(bf16[2048,768]{1,0:T(8,128)(2,1)S(1)} %get-tuple-element.36, s32[2048]{0:T(1024)S(1)} %bitcast.75, s32[128,4]{0,1:T(4,128)S(1)} %copy-done.12), kind=kOutput, calls=%fused_computation.54 | convolution fusion | flops 1614151680 | bytes 3942400 | tf_op jit(solution)/shard_map/dot_general | solution.py:79
  82.9 2.2 %convolution_bitcast_fusion = f32[768,768]{1,0:T(8,128)S(1)} fusion(bf16[128,4,768]{2,0,1:T(8,128)(2,1)} %fusion.37, bf16[128,4,768]{2,1,0:T(4,128)(2,1)} %get-tuple-element.17), kind=kOutput, calls=%fused_computation.49 | convolution fusion | flops 603979776 | bytes 3932160 | tf_op jit(solution)/shard_map/dot_general | solution.py:98
  85.1 1.7 %concatenate.23 = f32[4,2,4,4,36,128]{5,4,3,2,1,0:T(8,128)} reshape(f32[768,768]{1,0:T(8,128)S(1)} %convolution_bitcast_fusion) | data formatting | bytes 4718592 | tf_op jit(solution)/shard_map/concatenate | solution.py:111
  86.8 2.2 %convolution_bitcast_fusion.1 = f32[768,768]{1,0:T(8,128)S(1)} fusion(bf16[128,4,768]{2,0,1:T(8,128)(2,1)} %fusion.34, bf16[128,4,768]{2,1,0:T(4,128)(2,1)} %get-tuple-element.16), kind=kOutput, calls=%fused_computation.50 | convolution fusion | flops 603979776 | bytes 3932160 | tf_op jit(solution)/shard_map/dot_general | solution.py:92
  89.0 1.7 %concatenate.22 = f32[4,2,4,4,36,128]{5,4,3,2,1,0:T(8,128)} reshape(f32[768,768]{1,0:T(8,128)S(1)} %convolution_bitcast_fusion.1) | data formatting | bytes 4718592 | tf_op jit(solution)/shard_map/concatenate | solution.py:111
  91.6 3.2 %pad_maximum_fusion = f32[4,2,4,4,80,128]{5,4,3,2,1,0:T(8,128)S(1)} fusion(f32[4,2,4,4,8,128]{5,4,3,2,1,0:T(8,128)S(1)} %bitcast.68, f32[4,2,4,4,36,128]{5,4,3,2,1,0:T(8,128)} %concatenate.23, f32[4,2,4,4,36,128]{5,4,3,2,1,0:T(8,128)} %concatenate.22), kind=kLoop, calls=%fused_computation.6 | loop fusion | flops 2621440 | bytes 10485760 | tf_op jit(solution)/shard_map/concatenate | solution.py:111
  94.8 2.3 %copy-done.1 = f32[4,2,4,4,80,128]{5,4,3,2,1,0:T(8,128)} copy-done((f32[4,2,4,4,80,128]{5,4,3,2,1,0:T(8,128)}, f32[4,2,4,4,80,128]{5,4,3,2,1,0:T(8,128)S(1)}, u32[]{:S(2)}) %copy-start.1) | copy-done | bytes 5242904
  101.5 1.7 %convert_add_fusion = f32[4,1,4,4,80,128]{5,4,3,2,1,0:T(8,128)S(1)} fusion(bf16[4,1,4,4,80,128]{5,4,3,2,1,0:T(8,128)(2,1)} %collective-permute-done, f32[4,2,4,4,80,128]{5,4,3,2,1,0:T(8,128)S(1)} %copy-done.2, s32[]{:T(128)S(6)} %select_n.130), kind=kLoop, calls=%fused_computation.19 | loop fusion | flops 1310720 | bytes 6553604 | tf_op jit(solution)/shard_map/add | solution.py:133
  103.2 1.5 copy-done.3
  105.7 1.7 %collective-permute-start.3 = (bf16[4,1,4,1,80,128]{5,4,3,2,1,0:T(8,128)(2,1)}, bf16[4,1,4,1,80,128]{5,4,3,2,1,0:T(8,128)(2,1)}, u32[]{:S(2)}, u32[]{:S(2)}) collective-permute-start(bf16[4,1,4,1,80,128]{5,4,3,2,1,0:T(8,128)(2,1)} %get-tuple-element.21), channel_id=1, source_target_pairs={{0,3},{1,0},{2,1},{3,2},{4,7},{5,4},{6,5},{7,6},{8,11},{9,8},{10,9... | collective-permute-start | bytes 983048 | tf_op jit(solution)/shard_map/ppermute | solution.py:133
  108.7 2.4 %copy.37 = bf16[128,4,1536]{2,1,0:T(4,128)(2,1)} copy(bf16[128,4,1536]{2,0,1:T(8,128)(2,1)S(1)} %pad_maximum_fusion.2) | data formatting | bytes 3145728 | tf_op jit(solution)/shard_map/optimization_barrier | solution.py:122
  111.1 7.0 %all-to-all-start.1 = ((bf16[128,4,1536]{2,1,0:T(4,128)(2,1)}), bf16[128,4,1536]{2,1,0:T(4,128)(2,1)S(1)}, u32[]{:S(2)}, u32[]{:S(2)}) async-start(bf16[128,4,1536]{2,1,0:T(4,128)(2,1)} %copy.37), calls=%async_computation.1 | async-start | bytes 3145728 | tf_op jit(solution)/shard_map/all_to_all | solution.py:123
  118.2 1.5 collective-permute-done.2
  119.6 6.4 %collective-permute-done.1 = bf16[4,1,4,1,80,128]{5,4,3,2,1,0:T(8,128)(2,1)} collective-permute-done((bf16[4,1,4,1,80,128]{5,4,3,2,1,0:T(8,128)(2,1)S(1)}, bf16[4,1,4,1,80,128]{5,4,3,2,1,0:T(8,128)(2,1)}, u32[]{:S(2)}, u32[]{:S(2)}) %collective-permute-start.1) | collective-permute-done | bytes 327712 | tf_op jit(solution)/shard_map/ppermute | solution.py:133
  126.1 1.5 fusion.105
  129.6 1.6 %collective-permute-start.5 = (bf16[4,1,1,1,80,128]{5,4,3,2,1,0:T(8,128)(2,1)}, bf16[4,1,1,1,80,128]{5,4,3,2,1,0:T(8,128)(2,1)}, u32[]{:S(2)}, u32[]{:S(2)}) collective-permute-start(bf16[4,1,1,1,80,128]{5,4,3,2,1,0:T(8,128)(2,1)} %get-tuple-element.25), channel_id=1, source_target_pairs={{0,8},{4,12},{8,0},{12,4},{1,9},{5,13},{9,1},{13,5},{2,10},{6,14},... | collective-permute-start | bytes 245768 | tf_op jit(solution)/shard_map/ppermute | solution.py:133
  131.2 8.4 %collective-permute-done.6 = bf16[4,1,1,1,80,128]{5,4,3,2,1,0:T(8,128)(2,1)S(1)} collective-permute-done((bf16[4,1,1,1,80,128]{5,4,3,2,1,0:T(8,128)(2,1)}, bf16[4,1,1,1,80,128]{5,4,3,2,1,0:T(8,128)(2,1)S(1)}, u32[]{:S(2)}, u32[]{:S(2)}) %collective-permute-start.6) | collective-permute-done | bytes 81952 | tf_op jit(solution)/shard_map/ppermute | solution.py:133
  139.6 2.6 %collective-permute-done.5 = bf16[4,1,1,1,80,128]{5,4,3,2,1,0:T(8,128)(2,1)} collective-permute-done((bf16[4,1,1,1,80,128]{5,4,3,2,1,0:T(8,128)(2,1)}, bf16[4,1,1,1,80,128]{5,4,3,2,1,0:T(8,128)(2,1)}, u32[]{:S(2)}, u32[]{:S(2)}) %collective-permute-start.5) | collective-permute-done | bytes 81952 | tf_op jit(solution)/shard_map/ppermute | solution.py:133
  142.1 1.7 %collective-permute-done.4 = bf16[4,1,1,1,80,128]{5,4,3,2,1,0:T(8,128)(2,1)} collective-permute-done((bf16[4,1,1,1,80,128]{5,4,3,2,1,0:T(8,128)(2,1)}, bf16[4,1,1,1,80,128]{5,4,3,2,1,0:T(8,128)(2,1)}, u32[]{:S(2)}, u32[]{:S(2)}) %collective-permute-start.4) | collective-permute-done | bytes 81952 | tf_op jit(solution)/shard_map/ppermute | solution.py:133
  143.9 1.6 %fusion.104 = (bf16[4,1,1,1,80,128]{5,4,3,2,1,0:T(8,128)(2,1)S(1)}, f32[4,1,1,1,80,128]{5,4,3,2,1,0:T(8,128)}) fusion(bf16[4,1,1,1,80,128]{5,4,3,2,1,0:T(8,128)(2,1)S(1)} %collective-permute-done.6, bf16[4,1,1,1,80,128]{5,4,3,2,1,0:T(8,128)(2,1)} %collective-permute-done.5, bf16[4,1,1,1,80,128]{5,4,3,2,1,0:T(8,128)(2,1)} %collective-permute-done.4, ...), kind=kLoop, calls=%fused_computation.147 | loop fusion | flops 286720 | bytes 655364 | tf_op jit(solution)/shard_map/convert_element_type | solution.py:128
  146.8 1.6 %collective-permute-start.8 = (bf16[1,1,1,1,80,128]{5,4,3,2,1,0:T(8,128)(2,1)S(1)}, bf16[1,1,1,1,80,128]{5,4,3,2,1,0:T(8,128)(2,1)S(1)}, u32[]{:S(2)}, u32[]{:S(2)}) collective-permute-start(bf16[1,1,1,1,80,128]{5,4,3,2,1,0:T(8,128)(2,1)S(1)} %get-tuple-element.28), channel_id=1, source_target_pairs={{0,64},{32,96},{64,0},{96,32},{1,65},{33,97},{65,1},{97,33},{2,66}... | collective-permute-start | bytes 61448 | tf_op jit(solution)/shard_map/ppermute | solution.py:133
  149.4 2.9 %collective-permute-done.8 = bf16[1,1,1,1,80,128]{5,4,3,2,1,0:T(8,128)(2,1)S(1)} collective-permute-done((bf16[1,1,1,1,80,128]{5,4,3,2,1,0:T(8,128)(2,1)S(1)}, bf16[1,1,1,1,80,128]{5,4,3,2,1,0:T(8,128)(2,1)S(1)}, u32[]{:S(2)}, u32[]{:S(2)}) %collective-permute-start.8) | collective-permute-done | bytes 20512 | tf_op jit(solution)/shard_map/ppermute | solution.py:133
  (78 shorter events, 25.2 us)
Async XLA Ops:
  0.6 61.1 %copy-start = (bf16[768,768]{1,0:T(8,128)(2,1)S(1)}, bf16[768,768]{1,0:T(8,128)(2,1)}, u32[]{:S(2)}) copy-start(bf16[768,768]{1,0:T(8,128)(2,1)} %param.13) | copy-start | bytes 3538948
  6.9 11.2 %copy-start.13 = (s32[2,1,128]{2,1,0:T(1,128)S(1)}, s32[2,1,128]{2,1,0:T(1,128)}, u32[]{:S(2)}) copy-start(s32[2,1,128]{2,1,0:T(1,128)} %param.16) | copy-start | bytes 3076
  6.9 43.6 %all-to-all-start = ((bf16[128,4,2304]{2,1,0:T(4,128)(2,1)}), bf16[128,4,2304]{2,1,0:T(4,128)(2,1)S(1)}, u32[]{:S(2)}, u32[]{:S(2)}) async-start(bf16[128,4,2304]{2,1,0:T(4,128)(2,1)} %reshape.86), calls=%async_computation | async-start | bytes 4718592 | tf_op jit(solution)/shard_map/all_to_all | solution.py:43
  20.8 2.0 %copy-start.8 = (s32[1,2048]{1,0:T(1,128)}, s32[1,2048]{1,0:T(1,128)S(1)}, u32[]{:S(2)}) copy-start(s32[1,2048]{1,0:T(1,128)S(1)} %get-tuple-element.32) | copy-start | bytes 24580
  20.8 2.0 %copy-start.10 = (s32[1,2048]{1,0:T(1,128)}, s32[1,2048]{1,0:T(1,128)S(1)}, u32[]{:S(2)}) copy-start(s32[1,2048]{1,0:T(1,128)S(1)} %get-tuple-element.31) | copy-start | bytes 24580
  52.5 9.3 %copy-start.4 = (bf16[128,4,768]{2,1,0:T(4,128)(2,1)S(1)}, bf16[128,4,768]{2,1,0:T(4,128)(2,1)}, u32[]{:S(2)}) copy-start(bf16[128,4,768]{2,1,0:T(4,128)(2,1)} %get-tuple-element.17) | copy-start | bytes 2359300
  52.5 9.3 %copy-start.11 = (s32[1,2048]{1,0:T(1,128)S(1)}, s32[1,2048]{1,0:T(1,128)}, u32[]{:S(2)}) copy-start(s32[1,2048]{1,0:T(1,128)} %copy-done.10) | copy-start | bytes 24580
  52.5 9.3 %copy-start.12 = (s32[128,4]{0,1:T(4,128)S(1)}, s32[128,4]{0,1:T(4,128)}, u32[]{:S(2)}) copy-start(s32[128,4]{0,1:T(4,128)} %multiply_add_fusion) | copy-start | bytes 6148
  61.8 7.7 %copy-start.5 = (bf16[128,4,768]{2,1,0:T(4,128)(2,1)S(1)}, bf16[128,4,768]{2,1,0:T(4,128)(2,1)}, u32[]{:S(2)}) copy-start(bf16[128,4,768]{2,1,0:T(4,128)(2,1)} %get-tuple-element.15) | copy-start | bytes 2359300
  61.8 7.7 %copy-start.16 = (f32[768]{0:T(1024)S(1)}, f32[768]{0:T(1024)}, u32[]{:S(2)}) copy-start(f32[768]{0:T(1024)} %param.14) | copy-start | bytes 9220
  76.6 2.8 %copy-start.9 = (s32[1,2048]{1,0:T(1,128)S(1)}, s32[1,2048]{1,0:T(1,128)}, u32[]{:S(2)}) copy-start(s32[1,2048]{1,0:T(1,128)} %copy-done.8) | copy-start | bytes 24580
  91.6 5.9 %copy-start.6 = (bf16[128,4,768]{2,0,1:T(8,128)(2,1)S(1)}, bf16[128,4,768]{2,0,1:T(8,128)(2,1)}, u32[]{:S(2)}) copy-start(bf16[128,4,768]{2,0,1:T(8,128)(2,1)} %fusion.37) | copy-start | bytes 2359300
  94.8 2.3 %copy-start.1 = (f32[4,2,4,4,80,128]{5,4,3,2,1,0:T(8,128)}, f32[4,2,4,4,80,128]{5,4,3,2,1,0:T(8,128)S(1)}, u32[]{:S(2)}) copy-start(f32[4,2,4,4,80,128]{5,4,3,2,1,0:T(8,128)S(1)} %pad_maximum_fusion) | copy-start | bytes 15728644
  97.4 3.2 %collective-permute-start = (bf16[4,1,4,4,80,128]{5,4,3,2,1,0:T(8,128)(2,1)S(1)}, bf16[4,1,4,4,80,128]{5,4,3,2,1,0:T(8,128)(2,1)}, u32[]{:S(2)}, u32[]{:S(2)}) collective-permute-start(bf16[4,1,4,4,80,128]{5,4,3,2,1,0:T(8,128)(2,1)S(1)} %dynamic-slice_convert_fusion), channel_id=1, source_target_pairs={{0,16},{16,0},{1,17},{17,1},{2,18},{18,2},{3,19},{19,3},{4,20},{20... | collective-permute-start | bytes 3932168 | tf_op jit(solution)/shard_map/ppermute | solution.py:133
  97.5 1.1 copy-start.7
  97.5 1.5 copy-start.14
  99.0 2.5 %copy-start.2 = (f32[4,2,4,4,80,128]{5,4,3,2,1,0:T(8,128)S(1)}, f32[4,2,4,4,80,128]{5,4,3,2,1,0:T(8,128)}, u32[]{:S(2)}) copy-start(f32[4,2,4,4,80,128]{5,4,3,2,1,0:T(8,128)} %copy-done.1) | copy-start | bytes 15728644
  103.2 1.5 copy-start.3
  105.7 12.5 %collective-permute-start.3 = (bf16[4,1,4,1,80,128]{5,4,3,2,1,0:T(8,128)(2,1)}, bf16[4,1,4,1,80,128]{5,4,3,2,1,0:T(8,128)(2,1)}, u32[]{:S(2)}, u32[]{:S(2)}) collective-permute-start(bf16[4,1,4,1,80,128]{5,4,3,2,1,0:T(8,128)(2,1)} %get-tuple-element.21), channel_id=1, source_target_pairs={{0,3},{1,0},{2,1},{3,2},{4,7},{5,4},{6,5},{7,6},{8,11},{9,8},{10,9... | collective-permute-start | bytes 983048 | tf_op jit(solution)/shard_map/ppermute | solution.py:133
  107.4 12.2 %collective-permute-start.2 = (bf16[4,1,4,1,80,128]{5,4,3,2,1,0:T(8,128)(2,1)S(1)}, bf16[4,1,4,1,80,128]{5,4,3,2,1,0:T(8,128)(2,1)}, u32[]{:S(2)}, u32[]{:S(2)}) collective-permute-start(bf16[4,1,4,1,80,128]{5,4,3,2,1,0:T(8,128)(2,1)S(1)} %get-tuple-element.22), channel_id=1, source_target_pairs={{0,2},{1,3},{2,0},{3,1},{4,6},{5,7},{6,4},{7,5},{8,10},{9,11},{10,... | collective-permute-start | bytes 983048 | tf_op jit(solution)/shard_map/ppermute | solution.py:133
  108.7 17.3 %collective-permute-start.1 = (bf16[4,1,4,1,80,128]{5,4,3,2,1,0:T(8,128)(2,1)S(1)}, bf16[4,1,4,1,80,128]{5,4,3,2,1,0:T(8,128)(2,1)}, u32[]{:S(2)}, u32[]{:S(2)}) collective-permute-start(bf16[4,1,4,1,80,128]{5,4,3,2,1,0:T(8,128)(2,1)S(1)} %get-tuple-element.20), channel_id=1, source_target_pairs={{0,1},{1,2},{2,3},{3,0},{4,5},{5,6},{6,7},{7,4},{8,9},{9,10},{10,1... | collective-permute-start | bytes 983048 | tf_op jit(solution)/shard_map/ppermute | solution.py:133
  111.1 44.8 %all-to-all-start.1 = ((bf16[128,4,1536]{2,1,0:T(4,128)(2,1)}), bf16[128,4,1536]{2,1,0:T(4,128)(2,1)S(1)}, u32[]{:S(2)}, u32[]{:S(2)}) async-start(bf16[128,4,1536]{2,1,0:T(4,128)(2,1)} %copy.37), calls=%async_computation.1 | async-start | bytes 3145728 | tf_op jit(solution)/shard_map/all_to_all | solution.py:123
  128.3 11.3 %collective-permute-start.6 = (bf16[4,1,1,1,80,128]{5,4,3,2,1,0:T(8,128)(2,1)}, bf16[4,1,1,1,80,128]{5,4,3,2,1,0:T(8,128)(2,1)S(1)}, u32[]{:S(2)}, u32[]{:S(2)}) collective-permute-start(bf16[4,1,1,1,80,128]{5,4,3,2,1,0:T(8,128)(2,1)} %get-tuple-element.24), channel_id=1, source_target_pairs={{0,12},{4,0},{8,4},{12,8},{1,13},{5,1},{9,5},{13,9},{2,14},{6,2},{... | collective-permute-start | bytes 245768 | tf_op jit(solution)/shard_map/ppermute | solution.py:133
  129.6 12.6 %collective-permute-start.5 = (bf16[4,1,1,1,80,128]{5,4,3,2,1,0:T(8,128)(2,1)}, bf16[4,1,1,1,80,128]{5,4,3,2,1,0:T(8,128)(2,1)}, u32[]{:S(2)}, u32[]{:S(2)}) collective-permute-start(bf16[4,1,1,1,80,128]{5,4,3,2,1,0:T(8,128)(2,1)} %get-tuple-element.25), channel_id=1, source_target_pairs={{0,8},{4,12},{8,0},{12,4},{1,9},{5,13},{9,1},{13,5},{2,10},{6,14},... | collective-permute-start | bytes 245768 | tf_op jit(solution)/shard_map/ppermute | solution.py:133
  131.2 12.7 %collective-permute-start.4 = (bf16[4,1,1,1,80,128]{5,4,3,2,1,0:T(8,128)(2,1)}, bf16[4,1,1,1,80,128]{5,4,3,2,1,0:T(8,128)(2,1)}, u32[]{:S(2)}, u32[]{:S(2)}) collective-permute-start(bf16[4,1,1,1,80,128]{5,4,3,2,1,0:T(8,128)(2,1)} %get-tuple-element.23), channel_id=1, source_target_pairs={{0,4},{4,8},{8,12},{12,0},{1,5},{5,9},{9,13},{13,1},{2,6},{6,10},{... | collective-permute-start | bytes 245768 | tf_op jit(solution)/shard_map/ppermute | solution.py:133
  145.5 12.1 %copy-start.15 = (bf16[256,768]{1,0:T(8,128)(2,1)S(1)}, bf16[256,768]{1,0:T(8,128)(2,1)}, u32[]{:S(2)}) copy-start(bf16[256,768]{1,0:T(8,128)(2,1)} %param.11) | copy-start | bytes 1179652
  145.5 3.9 %collective-permute-start.9 = (bf16[1,1,1,1,80,128]{5,4,3,2,1,0:T(8,128)(2,1)S(1)}, bf16[1,1,1,1,80,128]{5,4,3,2,1,0:T(8,128)(2,1)S(1)}, u32[]{:S(2)}, u32[]{:S(2)}) collective-permute-start(bf16[1,1,1,1,80,128]{5,4,3,2,1,0:T(8,128)(2,1)S(1)} %get-tuple-element.27), channel_id=1, source_target_pairs={{0,96},{32,0},{64,32},{96,64},{1,97},{33,1},{65,33},{97,65},{2,98}... | collective-permute-start | bytes 61448 | tf_op jit(solution)/shard_map/ppermute | solution.py:133
  146.8 5.5 %collective-permute-start.8 = (bf16[1,1,1,1,80,128]{5,4,3,2,1,0:T(8,128)(2,1)S(1)}, bf16[1,1,1,1,80,128]{5,4,3,2,1,0:T(8,128)(2,1)S(1)}, u32[]{:S(2)}, u32[]{:S(2)}) collective-permute-start(bf16[1,1,1,1,80,128]{5,4,3,2,1,0:T(8,128)(2,1)S(1)} %get-tuple-element.28), channel_id=1, source_target_pairs={{0,64},{32,96},{64,0},{96,32},{1,65},{33,97},{65,1},{97,33},{2,66}... | collective-permute-start | bytes 61448 | tf_op jit(solution)/shard_map/ppermute | solution.py:133
  148.4 5.0 %collective-permute-start.7 = (bf16[1,1,1,1,80,128]{5,4,3,2,1,0:T(8,128)(2,1)S(1)}, bf16[1,1,1,1,80,128]{5,4,3,2,1,0:T(8,128)(2,1)S(1)}, u32[]{:S(2)}, u32[]{:S(2)}) collective-permute-start(bf16[1,1,1,1,80,128]{5,4,3,2,1,0:T(8,128)(2,1)S(1)} %get-tuple-element.26), channel_id=1, source_target_pairs={{0,32},{32,64},{64,96},{96,0},{1,33},{33,65},{65,97},{97,1},{2,34}... | collective-permute-start | bytes 61448 | tf_op jit(solution)/shard_map/ppermute | solution.py:133

commit v16 on v15

--- a/solution.py
+++ b/solution.py
@@ -118,7 +118,7 @@
     )
     summed = partials.reshape(*(lax.axis_size(name) for name in DEVICE_AXES), -1, lanes)
     for axis_name, position in (("c", 1), ("x", 3), ("z", 2), ("y", 0)):
-        if axis_name == "x":
+        if axis_name == "z":
             backward, summed = lax.optimization_barrier((backward, summed))
             homes = lax.all_to_all(backward, DEVICE_AXES, split_axis=0, concat_axis=0, tiled=True)
             home_con = homes[:, :, :embedding_width]

time: 160 us -> 170 us (1.062)
  waiting for transfers between devices: 52.7 us -> 68.7 us
  local copies, waits for them, and re-layouts: 24.3 us -> 20.6 us
    ppermute x10, waiting for transfers between devices: 25.6 us -> 41.6 us  [on_device(): total = total + lax.ppermute(chunk, axis_name, pairs).astype(jnp.float32)]
    unnamed x34 -> x30, local copies, waits for them, and re-layouts: 5.47 us -> 2.4 us
    all_to_all x1, starting transfers between devices: 6.99 us -> 4.64 us  [on_device(): lax.all_to_all(backward, DEVICE_AXES, split_axis=0, concat_axis=0, tiled=...]
    ppermute x10, starting transfers between devices: 9.15 us -> 10.9 us  [on_device(): total = total + lax.ppermute(chunk, axis_name, pairs).astype(jnp.float32)]
  transfers between devices with their start and end apart: 12 -> 12, of which waited for: 10 -> 11; matrix products, arithmetic and copies ran while one was open for 10% -> 7% of each run, Pallas kernels for 0% -> 0%
where the time goes in v16:
time: 170 us
  waiting for transfers between devices  68.7 us (40%)
  matrix products  42.9 us (25%)
  starting transfers between devices  26.7 us (16%)
  local copies, waits for them, and re-layouts  20.6 us (12%)
  other arithmetic  9.82 us (6%)
    ppermute x10, waiting for transfers between devices, on_device(): total = total + lax.ppermute(chunk, axis_name, pairs).astype(jnp.float32)  41.6 us
    all_to_all x1, waiting for transfers between devices, on_device(): lax.all_to_all(outgoing, DEVICE_AXES, split_axis=0, concat_axis=0, tiled=...  27.1 us
    all_to_all x1, starting transfers between devices, on_device(): lax.all_to_all(outgoing, DEVICE_AXES, split_axis=0, concat_axis=0, tiled=...  11.2 us
    ppermute x10, starting transfers between devices, on_device(): total = total + lax.ppermute(chunk, axis_name, pairs).astype(jnp.float32)  10.9 us
    dot_general x1, matrix products, on_device(): jnp.dot(edge_con, constraint_weight, preferred_element_type=jnp.float32)  9.26 us
    dot_general x1, matrix products, on_device(): jnp.dot(edge_var, variable_weight, preferred_element_type=jnp.float32)  7.66 us
    dot_general x1, matrix products, on_device(): lax.dot_general(table_var3, cotangent_mirror_rows, slot_dims, preferred_e...  7.11 us
    all_to_all x1, starting transfers between devices, on_device(): lax.all_to_all(backward, DEVICE_AXES, split_axis=0, concat_axis=0, tiled=...  4.64 us
  transfers between devices with their start and end apart: 12, of which 11 were waited for; matrix products, arithmetic and copies ran while one was open for 7% of the time, Pallas kernels for 0%

profile of v16, /device:TPU:0, one launch (start us, length us, event | category | flops | bytes accessed | tf_op | source)
XLA Modules:
  0.0 169.7 jit_solution(13799398698500522948)
XLA Ops:
  2.9 1.7 %convolution_convert_fusion = bf16[512,1536]{1,0:T(8,128)(2,1)S(1)} fusion(bf16[256,768]{1,0:T(8,128)(2,1)} %param.11, bf16[256,768]{1,0:T(8,128)(2,1)} %param.10, s32[512]{0:T(512)S(1)} %bitcast.80), kind=kOutput, calls=%fused_computation.17 | convolution fusion | flops 405405696 | bytes 2361344 | tf_op jit(solution)/shard_map/dot_general | solution.py:15
  4.8 2.2 %reshape.86 = bf16[128,4,2304]{2,1,0:T(4,128)(2,1)} reshape(bf16[512,2304]{1,0:T(8,128)(2,1)S(1)} %pad_maximum_fusion.1) | data formatting | bytes 4718592 | tf_op jit(solution)/shard_map/reshape | solution.py:40
  6.9 11.2 %all-to-all-start = ((bf16[128,4,2304]{2,1,0:T(4,128)(2,1)}), bf16[128,4,2304]{2,1,0:T(4,128)(2,1)S(1)}, u32[]{:S(2)}, u32[]{:S(2)}) async-start(bf16[128,4,2304]{2,1,0:T(4,128)(2,1)} %reshape.86), calls=%async_computation | async-start | bytes 4718592 | tf_op jit(solution)/shard_map/all_to_all | solution.py:43
  23.4 27.1 %all-to-all-done = bf16[128,4,2304]{2,1,0:T(4,128)(2,1)S(1)} async-done(((bf16[128,4,2304]{2,1,0:T(4,128)(2,1)}), bf16[128,4,2304]{2,1,0:T(4,128)(2,1)S(1)}, u32[]{:S(2)}, u32[]{:S(2)}) %all-to-all-start) | async-done | bytes 2359328 | tf_op jit(solution)/shard_map/all_to_all | solution.py:43
  50.5 2.0 %fusion.106 = (bf16[128,4,768]{2,1,0:T(4,128)(2,1)}, bf16[128,4,768]{2,1,0:T(4,128)(2,1)}, bf16[128,4,768]{2,1,0:T(4,128)(2,1)}) fusion(bf16[128,4,2304]{2,1,0:T(4,128)(2,1)S(1)} %all-to-all-done), kind=kLoop, calls=%fused_computation.149 | loop fusion | bytes 4718592 | tf_op jit(solution)/shard_map/slice | solution.py:46
  52.5 9.3 %fusion.45 = f32[2048,768]{1,0:T(8,128)} fusion(bf16[768,768]{1,0:T(8,128)(2,1)} %param.12, s32[2048]{0:T(1024)} %bitcast.74, s32[128,4]{0,1:T(4,128)} %multiply_add_fusion, bf16[128,4,768]{2,1,0:T(4,128)(2,1)} %get-tuple-element.16), kind=kOutput, calls=%fused_computation.64 | convolution fusion | flops 4031250432 | bytes 8267776 | tf_op jit(solution)/shard_map/dot_general | solution.py:69
  61.8 7.7 %fusion.46 = f32[2048,768]{1,0:T(8,128)} fusion(bf16[768,768]{1,0:T(8,128)(2,1)S(1)} %copy-done, s32[2048]{0:T(1024)S(1)} %bitcast.77, s32[128,4]{0,1:T(4,128)S(1)} %copy-done.10, bf16[128,4,768]{2,1,0:T(4,128)(2,1)S(1)} %copy-done.2), kind=kOutput, calls=%fused_computation.65 | convolution fusion | flops 4031250432 | bytes 8267776 | tf_op jit(solution)/shard_map/dot_general | solution.py:70
  69.5 7.1 %convert_reduce_fusion = (f32[768]{0:T(1024)S(1)}, bf16[2048,768]{1,0:T(8,128)(2,1)S(1)}) fusion(f32[2048]{0:T(1024)S(1)} %mul.41, f32[768]{0:T(1024)S(1)} %copy-done.14, f32[2048,768]{1,0:T(8,128)} %fusion.45, f32[2048,768]{1,0:T(8,128)} %fusion.46, bf16[128,4,768]{2,1,0:T(4,128)(2,1)S(1)} %copy-done.3, s32[2048]{0:T(1024)S(1)} %bitcast.78, ...), kind=kOutput, calls=%fused_computation.5 | convolution fusion | flops 1635777792 | bytes 16539648 | tf_op jit(solution)/shard_map/dot_general | solution.py:65
  76.6 2.8 %fusion.37 = bf16[128,4,768]{2,0,1:T(8,128)(2,1)} fusion(bf16[2048,768]{1,0:T(8,128)(2,1)S(1)} %get-tuple-element.36, s32[2048]{0:T(1024)S(1)} %bitcast.79, s32[128,4]{0,1:T(4,128)S(1)} %copy-done.10), kind=kOutput, calls=%fused_computation.55 | convolution fusion | flops 1614151680 | bytes 3942400 | tf_op jit(solution)/shard_map/dot_general | solution.py:82
  79.4 2.7 %fusion.34 = bf16[128,4,768]{2,0,1:T(8,128)(2,1)} fusion(bf16[2048,768]{1,0:T(8,128)(2,1)S(1)} %get-tuple-element.36, s32[2048]{0:T(1024)S(1)} %bitcast.75, s32[128,4]{0,1:T(4,128)S(1)} %copy-done.10), kind=kOutput, calls=%fused_computation.54 | convolution fusion | flops 1614151680 | bytes 3942400 | tf_op jit(solution)/shard_map/dot_general | solution.py:79
  82.9 2.2 %convolution_bitcast_fusion = f32[768,768]{1,0:T(8,128)S(1)} fusion(bf16[128,4,768]{2,0,1:T(8,128)(2,1)} %fusion.37, bf16[128,4,768]{2,1,0:T(4,128)(2,1)} %get-tuple-element.17), kind=kOutput, calls=%fused_computation.49 | convolution fusion | flops 603979776 | bytes 3932160 | tf_op jit(solution)/shard_map/dot_general | solution.py:98
  85.1 1.7 %concatenate.23 = f32[4,2,4,4,36,128]{5,4,3,2,1,0:T(8,128)} reshape(f32[768,768]{1,0:T(8,128)S(1)} %convolution_bitcast_fusion) | data formatting | bytes 4718592 | tf_op jit(solution)/shard_map/concatenate | solution.py:111
  86.8 2.2 %convolution_bitcast_fusion.1 = f32[768,768]{1,0:T(8,128)S(1)} fusion(bf16[128,4,768]{2,0,1:T(8,128)(2,1)} %fusion.34, bf16[128,4,768]{2,1,0:T(4,128)(2,1)} %get-tuple-element.16), kind=kOutput, calls=%fused_computation.50 | convolution fusion | flops 603979776 | bytes 3932160 | tf_op jit(solution)/shard_map/dot_general | solution.py:92
  89.0 1.7 %concatenate.22 = f32[4,2,4,4,36,128]{5,4,3,2,1,0:T(8,128)} reshape(f32[768,768]{1,0:T(8,128)S(1)} %convolution_bitcast_fusion.1) | data formatting | bytes 4718592 | tf_op jit(solution)/shard_map/concatenate | solution.py:111
  91.6 3.2 %pad_maximum_fusion = f32[4,2,4,4,80,128]{5,4,3,2,1,0:T(8,128)S(1)} fusion(f32[4,2,4,4,8,128]{5,4,3,2,1,0:T(8,128)S(1)} %bitcast.68, f32[4,2,4,4,36,128]{5,4,3,2,1,0:T(8,128)} %concatenate.23, f32[4,2,4,4,36,128]{5,4,3,2,1,0:T(8,128)} %concatenate.22), kind=kLoop, calls=%fused_computation.6 | loop fusion | flops 2621440 | bytes 10485760 | tf_op jit(solution)/shard_map/concatenate | solution.py:111
  94.8 2.3 %copy-done.1 = f32[4,2,4,4,80,128]{5,4,3,2,1,0:T(8,128)} copy-done((f32[4,2,4,4,80,128]{5,4,3,2,1,0:T(8,128)}, f32[4,2,4,4,80,128]{5,4,3,2,1,0:T(8,128)S(1)}, u32[]{:S(2)}) %copy-start.1) | copy-done | bytes 5242904
  98.4 2.3 %collective-permute-done = bf16[4,1,4,4,80,128]{5,4,3,2,1,0:T(8,128)(2,1)} collective-permute-done((bf16[4,1,4,4,80,128]{5,4,3,2,1,0:T(8,128)(2,1)S(1)}, bf16[4,1,4,4,80,128]{5,4,3,2,1,0:T(8,128)(2,1)}, u32[]{:S(2)}, u32[]{:S(2)}) %collective-permute-start) | collective-permute-done | bytes 1310752 | tf_op jit(solution)/shard_map/ppermute | solution.py:133
  100.6 2.6 %fusion.105 = (bf16[4,1,4,4,80,128]{5,4,3,2,1,0:T(8,128)(2,1)S(1)}, f32[4,1,4,4,80,128]{5,4,3,2,1,0:T(8,128)S(1)}) fusion(bf16[4,1,4,4,80,128]{5,4,3,2,1,0:T(8,128)(2,1)} %collective-permute-done, f32[4,2,4,4,80,128]{5,4,3,2,1,0:T(8,128)} %copy-done.1, s32[]{:T(128)S(6)} %select_n.130), kind=kLoop, calls=%fused_computation.148 | loop fusion | flops 1966080 | bytes 7864324 | tf_op jit(solution)/shard_map/convert_element_type | solution.py:128
  103.3 1.7 collective-permute-start.3
  105.0 1.4 collective-permute-start.2
  107.4 6.6 %collective-permute-done.3 = bf16[4,1,4,1,80,128]{5,4,3,2,1,0:T(8,128)(2,1)S(1)} collective-permute-done((bf16[4,1,4,1,80,128]{5,4,3,2,1,0:T(8,128)(2,1)S(1)}, bf16[4,1,4,1,80,128]{5,4,3,2,1,0:T(8,128)(2,1)S(1)}, u32[]{:S(2)}, u32[]{:S(2)}) %collective-permute-start.3) | collective-permute-done | bytes 327712 | tf_op jit(solution)/shard_map/ppermute | solution.py:133
  114.0 3.1 %collective-permute-done.2 = bf16[4,1,4,1,80,128]{5,4,3,2,1,0:T(8,128)(2,1)S(1)} collective-permute-done((bf16[4,1,4,1,80,128]{5,4,3,2,1,0:T(8,128)(2,1)S(1)}, bf16[4,1,4,1,80,128]{5,4,3,2,1,0:T(8,128)(2,1)S(1)}, u32[]{:S(2)}, u32[]{:S(2)}) %collective-permute-start.2) | collective-permute-done | bytes 327712 | tf_op jit(solution)/shard_map/ppermute | solution.py:133
  117.1 5.9 %collective-permute-done.1 = bf16[4,1,4,1,80,128]{5,4,3,2,1,0:T(8,128)(2,1)S(1)} collective-permute-done((bf16[4,1,4,1,80,128]{5,4,3,2,1,0:T(8,128)(2,1)S(1)}, bf16[4,1,4,1,80,128]{5,4,3,2,1,0:T(8,128)(2,1)S(1)}, u32[]{:S(2)}, u32[]{:S(2)}) %collective-permute-start.1) | collective-permute-done | bytes 327712 | tf_op jit(solution)/shard_map/ppermute | solution.py:133
  123.1 2.4 %copy.37 = bf16[128,4,1536]{2,1,0:T(4,128)(2,1)} copy(bf16[128,4,1536]{2,0,1:T(8,128)(2,1)S(1)} %pad_maximum_fusion.2) | data formatting | bytes 3145728 | tf_op jit(solution)/shard_map/optimization_barrier | solution.py:122
  125.6 4.6 %all-to-all-start.1 = ((bf16[128,4,1536]{2,1,0:T(4,128)(2,1)}), bf16[128,4,1536]{2,1,0:T(4,128)(2,1)S(1)}, u32[]{:S(2)}, u32[]{:S(2)}) async-start(bf16[128,4,1536]{2,1,0:T(4,128)(2,1)} %copy.37), calls=%async_computation.1 | async-start | bytes 3145728 | tf_op jit(solution)/shard_map/all_to_all | solution.py:123
  131.0 2.8 %collective-permute-start.6 = (bf16[4,1,1,1,80,128]{5,4,3,2,1,0:T(8,128)(2,1)}, bf16[4,1,1,1,80,128]{5,4,3,2,1,0:T(8,128)(2,1)S(1)}, u32[]{:S(2)}, u32[]{:S(2)}) collective-permute-start(bf16[4,1,1,1,80,128]{5,4,3,2,1,0:T(8,128)(2,1)} %get-tuple-element.24), channel_id=1, source_target_pairs={{0,12},{4,0},{8,4},{12,8},{1,13},{5,1},{9,5},{13,9},{2,14},{6,2},{... | collective-permute-start | bytes 245768 | tf_op jit(solution)/shard_map/ppermute | solution.py:133
  135.3 14.5 %collective-permute-done.6 = bf16[4,1,1,1,80,128]{5,4,3,2,1,0:T(8,128)(2,1)S(1)} collective-permute-done((bf16[4,1,1,1,80,128]{5,4,3,2,1,0:T(8,128)(2,1)}, bf16[4,1,1,1,80,128]{5,4,3,2,1,0:T(8,128)(2,1)S(1)}, u32[]{:S(2)}, u32[]{:S(2)}) %collective-permute-start.6) | collective-permute-done | bytes 81952 | tf_op jit(solution)/shard_map/ppermute | solution.py:133
  149.8 2.6 %collective-permute-done.5 = bf16[4,1,1,1,80,128]{5,4,3,2,1,0:T(8,128)(2,1)} collective-permute-done((bf16[4,1,1,1,80,128]{5,4,3,2,1,0:T(8,128)(2,1)}, bf16[4,1,1,1,80,128]{5,4,3,2,1,0:T(8,128)(2,1)}, u32[]{:S(2)}, u32[]{:S(2)}) %collective-permute-start.5) | collective-permute-done | bytes 81952 | tf_op jit(solution)/shard_map/ppermute | solution.py:133
  152.4 2.6 %collective-permute-done.4 = bf16[4,1,1,1,80,128]{5,4,3,2,1,0:T(8,128)(2,1)} collective-permute-done((bf16[4,1,1,1,80,128]{5,4,3,2,1,0:T(8,128)(2,1)}, bf16[4,1,1,1,80,128]{5,4,3,2,1,0:T(8,128)(2,1)}, u32[]{:S(2)}, u32[]{:S(2)}) %collective-permute-start.4) | collective-permute-done | bytes 81952 | tf_op jit(solution)/shard_map/ppermute | solution.py:133
  155.0 1.6 fusion.104
  156.7 1.6 collective-permute-start.9
  160.7 2.9 %collective-permute-done.8 = bf16[1,1,1,1,80,128]{5,4,3,2,1,0:T(8,128)(2,1)S(1)} collective-permute-done((bf16[1,1,1,1,80,128]{5,4,3,2,1,0:T(8,128)(2,1)S(1)}, bf16[1,1,1,1,80,128]{5,4,3,2,1,0:T(8,128)(2,1)S(1)}, u32[]{:S(2)}, u32[]{:S(2)}) %collective-permute-start.8) | collective-permute-done | bytes 20512 | tf_op jit(solution)/shard_map/ppermute | solution.py:133
  (74 shorter events, 22.2 us)
Async XLA Ops:
  0.6 61.1 %copy-start = (bf16[768,768]{1,0:T(8,128)(2,1)S(1)}, bf16[768,768]{1,0:T(8,128)(2,1)}, u32[]{:S(2)}) copy-start(bf16[768,768]{1,0:T(8,128)(2,1)} %param.13) | copy-start | bytes 3538948
  6.9 11.2 %copy-start.11 = (s32[2,1,128]{2,1,0:T(1,128)S(1)}, s32[2,1,128]{2,1,0:T(1,128)}, u32[]{:S(2)}) copy-start(s32[2,1,128]{2,1,0:T(1,128)} %param.16) | copy-start | bytes 3076
  6.9 43.6 %all-to-all-start = ((bf16[128,4,2304]{2,1,0:T(4,128)(2,1)}), bf16[128,4,2304]{2,1,0:T(4,128)(2,1)S(1)}, u32[]{:S(2)}, u32[]{:S(2)}) async-start(bf16[128,4,2304]{2,1,0:T(4,128)(2,1)} %reshape.86), calls=%async_computation | async-start | bytes 4718592 | tf_op jit(solution)/shard_map/all_to_all | solution.py:43
  20.8 2.0 %copy-start.6 = (s32[1,2048]{1,0:T(1,128)}, s32[1,2048]{1,0:T(1,128)S(1)}, u32[]{:S(2)}) copy-start(s32[1,2048]{1,0:T(1,128)S(1)} %get-tuple-element.32) | copy-start | bytes 24580
  20.8 2.0 %copy-start.8 = (s32[1,2048]{1,0:T(1,128)}, s32[1,2048]{1,0:T(1,128)S(1)}, u32[]{:S(2)}) copy-start(s32[1,2048]{1,0:T(1,128)S(1)} %get-tuple-element.31) | copy-start | bytes 24580
  52.5 9.3 %copy-start.2 = (bf16[128,4,768]{2,1,0:T(4,128)(2,1)S(1)}, bf16[128,4,768]{2,1,0:T(4,128)(2,1)}, u32[]{:S(2)}) copy-start(bf16[128,4,768]{2,1,0:T(4,128)(2,1)} %get-tuple-element.17) | copy-start | bytes 2359300
  52.5 9.3 %copy-start.9 = (s32[1,2048]{1,0:T(1,128)S(1)}, s32[1,2048]{1,0:T(1,128)}, u32[]{:S(2)}) copy-start(s32[1,2048]{1,0:T(1,128)} %copy-done.8) | copy-start | bytes 24580
  52.5 9.3 %copy-start.10 = (s32[128,4]{0,1:T(4,128)S(1)}, s32[128,4]{0,1:T(4,128)}, u32[]{:S(2)}) copy-start(s32[128,4]{0,1:T(4,128)} %multiply_add_fusion) | copy-start | bytes 6148
  61.8 7.7 %copy-start.3 = (bf16[128,4,768]{2,1,0:T(4,128)(2,1)S(1)}, bf16[128,4,768]{2,1,0:T(4,128)(2,1)}, u32[]{:S(2)}) copy-start(bf16[128,4,768]{2,1,0:T(4,128)(2,1)} %get-tuple-element.15) | copy-start | bytes 2359300
  61.8 7.7 %copy-start.14 = (f32[768]{0:T(1024)S(1)}, f32[768]{0:T(1024)}, u32[]{:S(2)}) copy-start(f32[768]{0:T(1024)} %param.14) | copy-start | bytes 9220
  76.6 2.8 %copy-start.7 = (s32[1,2048]{1,0:T(1,128)S(1)}, s32[1,2048]{1,0:T(1,128)}, u32[]{:S(2)}) copy-start(s32[1,2048]{1,0:T(1,128)} %copy-done.6) | copy-start | bytes 24580
  91.6 5.9 %copy-start.5 = (bf16[128,4,768]{2,0,1:T(8,128)(2,1)S(1)}, bf16[128,4,768]{2,0,1:T(8,128)(2,1)}, u32[]{:S(2)}) copy-start(bf16[128,4,768]{2,0,1:T(8,128)(2,1)} %fusion.37) | copy-start | bytes 2359300
  94.8 2.3 %copy-start.1 = (f32[4,2,4,4,80,128]{5,4,3,2,1,0:T(8,128)}, f32[4,2,4,4,80,128]{5,4,3,2,1,0:T(8,128)S(1)}, u32[]{:S(2)}) copy-start(f32[4,2,4,4,80,128]{5,4,3,2,1,0:T(8,128)S(1)} %pad_maximum_fusion) | copy-start | bytes 15728644
  97.4 3.2 %collective-permute-start = (bf16[4,1,4,4,80,128]{5,4,3,2,1,0:T(8,128)(2,1)S(1)}, bf16[4,1,4,4,80,128]{5,4,3,2,1,0:T(8,128)(2,1)}, u32[]{:S(2)}, u32[]{:S(2)}) collective-permute-start(bf16[4,1,4,4,80,128]{5,4,3,2,1,0:T(8,128)(2,1)S(1)} %dynamic-slice_convert_fusion), channel_id=1, source_target_pairs={{0,16},{16,0},{1,17},{17,1},{2,18},{18,2},{3,19},{19,3},{4,20},{20... | collective-permute-start | bytes 3932168 | tf_op jit(solution)/shard_map/ppermute | solution.py:133
  98.3 8.1 %copy-start.4 = (bf16[128,4,768]{2,0,1:T(8,128)(2,1)S(1)}, bf16[128,4,768]{2,0,1:T(8,128)(2,1)}, u32[]{:S(2)}) copy-start(bf16[128,4,768]{2,0,1:T(8,128)(2,1)} %fusion.34) | copy-start | bytes 2359300
  98.3 8.1 %copy-start.12 = (bf16[768,768]{1,0:T(8,128)(2,1)S(1)}, bf16[768,768]{1,0:T(8,128)(2,1)}, u32[]{:S(2)}) copy-start(bf16[768,768]{1,0:T(8,128)(2,1)} %param.12) | copy-start | bytes 3538948
  103.3 10.6 %collective-permute-start.3 = (bf16[4,1,4,1,80,128]{5,4,3,2,1,0:T(8,128)(2,1)S(1)}, bf16[4,1,4,1,80,128]{5,4,3,2,1,0:T(8,128)(2,1)S(1)}, u32[]{:S(2)}, u32[]{:S(2)}) collective-permute-start(bf16[4,1,4,1,80,128]{5,4,3,2,1,0:T(8,128)(2,1)S(1)} %get-tuple-element.21), channel_id=1, source_target_pairs={{0,3},{1,0},{2,1},{3,2},{4,7},{5,4},{6,5},{7,6},{8,11},{9,8},{10,9... | collective-permute-start | bytes 983048 | tf_op jit(solution)/shard_map/ppermute | solution.py:133
  105.0 12.1 %collective-permute-start.2 = (bf16[4,1,4,1,80,128]{5,4,3,2,1,0:T(8,128)(2,1)S(1)}, bf16[4,1,4,1,80,128]{5,4,3,2,1,0:T(8,128)(2,1)S(1)}, u32[]{:S(2)}, u32[]{:S(2)}) collective-permute-start(bf16[4,1,4,1,80,128]{5,4,3,2,1,0:T(8,128)(2,1)S(1)} %get-tuple-element.22), channel_id=1, source_target_pairs={{0,2},{1,3},{2,0},{3,1},{4,6},{5,7},{6,4},{7,5},{8,10},{9,11},{10,... | collective-permute-start | bytes 983048 | tf_op jit(solution)/shard_map/ppermute | solution.py:133
  106.4 16.6 %collective-permute-start.1 = (bf16[4,1,4,1,80,128]{5,4,3,2,1,0:T(8,128)(2,1)S(1)}, bf16[4,1,4,1,80,128]{5,4,3,2,1,0:T(8,128)(2,1)S(1)}, u32[]{:S(2)}, u32[]{:S(2)}) collective-permute-start(bf16[4,1,4,1,80,128]{5,4,3,2,1,0:T(8,128)(2,1)S(1)} %get-tuple-element.20), channel_id=1, source_target_pairs={{0,1},{1,2},{2,3},{3,0},{4,5},{5,6},{6,7},{7,4},{8,9},{9,10},{10,1... | collective-permute-start | bytes 983048 | tf_op jit(solution)/shard_map/ppermute | solution.py:133
  125.6 41.4 %all-to-all-start.1 = ((bf16[128,4,1536]{2,1,0:T(4,128)(2,1)}), bf16[128,4,1536]{2,1,0:T(4,128)(2,1)S(1)}, u32[]{:S(2)}, u32[]{:S(2)}) async-start(bf16[128,4,1536]{2,1,0:T(4,128)(2,1)} %copy.37), calls=%async_computation.1 | async-start | bytes 3145728 | tf_op jit(solution)/shard_map/all_to_all | solution.py:123
  131.0 18.8 %collective-permute-start.6 = (bf16[4,1,1,1,80,128]{5,4,3,2,1,0:T(8,128)(2,1)}, bf16[4,1,1,1,80,128]{5,4,3,2,1,0:T(8,128)(2,1)S(1)}, u32[]{:S(2)}, u32[]{:S(2)}) collective-permute-start(bf16[4,1,1,1,80,128]{5,4,3,2,1,0:T(8,128)(2,1)} %get-tuple-element.24), channel_id=1, source_target_pairs={{0,12},{4,0},{8,4},{12,8},{1,13},{5,1},{9,5},{13,9},{2,14},{6,2},{... | collective-permute-start | bytes 245768 | tf_op jit(solution)/shard_map/ppermute | solution.py:133
  133.8 18.6 %collective-permute-start.5 = (bf16[4,1,1,1,80,128]{5,4,3,2,1,0:T(8,128)(2,1)}, bf16[4,1,1,1,80,128]{5,4,3,2,1,0:T(8,128)(2,1)}, u32[]{:S(2)}, u32[]{:S(2)}) collective-permute-start(bf16[4,1,1,1,80,128]{5,4,3,2,1,0:T(8,128)(2,1)} %get-tuple-element.25), channel_id=1, source_target_pairs={{0,8},{4,12},{8,0},{12,4},{1,9},{5,13},{9,1},{13,5},{2,10},{6,14},... | collective-permute-start | bytes 245768 | tf_op jit(solution)/shard_map/ppermute | solution.py:133
  134.2 20.9 %collective-permute-start.4 = (bf16[4,1,1,1,80,128]{5,4,3,2,1,0:T(8,128)(2,1)}, bf16[4,1,1,1,80,128]{5,4,3,2,1,0:T(8,128)(2,1)}, u32[]{:S(2)}, u32[]{:S(2)}) collective-permute-start(bf16[4,1,1,1,80,128]{5,4,3,2,1,0:T(8,128)(2,1)} %get-tuple-element.23), channel_id=1, source_target_pairs={{0,4},{4,8},{8,12},{12,0},{1,5},{5,9},{9,13},{13,1},{2,6},{6,10},{... | collective-permute-start | bytes 245768 | tf_op jit(solution)/shard_map/ppermute | solution.py:133
  156.7 11.9 %copy-start.13 = (bf16[256,768]{1,0:T(8,128)(2,1)S(1)}, bf16[256,768]{1,0:T(8,128)(2,1)}, u32[]{:S(2)}) copy-start(bf16[256,768]{1,0:T(8,128)(2,1)} %param.11) | copy-start | bytes 1179652
  156.7 4.0 %collective-permute-start.9 = (bf16[1,1,1,1,80,128]{5,4,3,2,1,0:T(8,128)(2,1)S(1)}, bf16[1,1,1,1,80,128]{5,4,3,2,1,0:T(8,128)(2,1)S(1)}, u32[]{:S(2)}, u32[]{:S(2)}) collective-permute-start(bf16[1,1,1,1,80,128]{5,4,3,2,1,0:T(8,128)(2,1)S(1)} %get-tuple-element.27), channel_id=1, source_target_pairs={{0,96},{32,0},{64,32},{96,64},{1,97},{33,1},{65,33},{97,65},{2,98}... | collective-permute-start | bytes 61448 | tf_op jit(solution)/shard_map/ppermute | solution.py:133
  158.3 5.3 %collective-permute-start.8 = (bf16[1,1,1,1,80,128]{5,4,3,2,1,0:T(8,128)(2,1)S(1)}, bf16[1,1,1,1,80,128]{5,4,3,2,1,0:T(8,128)(2,1)S(1)}, u32[]{:S(2)}, u32[]{:S(2)}) collective-permute-start(bf16[1,1,1,1,80,128]{5,4,3,2,1,0:T(8,128)(2,1)S(1)} %get-tuple-element.28), channel_id=1, source_target_pairs={{0,64},{32,96},{64,0},{96,32},{1,65},{33,97},{65,1},{97,33},{2,66}... | collective-permute-start | bytes 61448 | tf_op jit(solution)/shard_map/ppermute | solution.py:133
  159.4 5.0 %collective-permute-start.7 = (bf16[1,1,1,1,80,128]{5,4,3,2,1,0:T(8,128)(2,1)S(1)}, bf16[1,1,1,1,80,128]{5,4,3,2,1,0:T(8,128)(2,1)S(1)}, u32[]{:S(2)}, u32[]{:S(2)}) collective-permute-start(bf16[1,1,1,1,80,128]{5,4,3,2,1,0:T(8,128)(2,1)S(1)} %get-tuple-element.26), channel_id=1, source_target_pairs={{0,32},{32,64},{64,96},{96,0},{1,33},{33,65},{65,97},{97,1},{2,34}... | collective-permute-start | bytes 61448 | tf_op jit(solution)/shard_map/ppermute | solution.py:133
